TPU v7x, 32 devices: a whole 2x2x4 slice. The times are simulated.
32 devices in a mesh: dp: 4 (over z), context: 8 (over y, x, core).
Axes of the slice: x: 2, y: 2, z: 4, core: 2. Of those that a mesh axis runs over, the one named last changes fastest.
Arguments:
- queries: bfloat16 [4, 1024, 4096], P('dp', 'context'), may hold values from -12 to 12
- key_rows: bfloat16 [4, 1024, 4096], P('dp', 'context'), may hold values from -12 to 12
- value_rows: bfloat16 [4, 1024, 4096], P('dp', 'context'), may hold values from -6 to 6
- cotangent: bfloat16 [4, 1024, 2048], P('dp', 'context'), may hold values from -6 to 6
- out_weight: bfloat16 [4096, 2048], P(('dp', 'context')), may hold values from -0.09375 to 0.09375
- random_blocks: int32 [4, 14, 3], P('dp'), may hold values from 1 to 14, as said below
Outputs:
- query_grad: bfloat16 [4, 1024, 4096], P('dp', 'context')
- key_grad: bfloat16 [4, 1024, 4096], P('dp', 'context')
- value_grad: bfloat16 [4, 1024, 4096], P('dp', 'context')
Inputs may be any that keep to these rules, and one draw needn't show every extreme that they name: `random_blocks`: row j of a document holds three distinct block numbers, none of them j, j + 1 or j + 2.
All inputs are finite; a program needn't handle non-finite values.
Results may differ from a plain program's by a relative error of at most 0.012.
The roundings to bfloat16 on the way count: a program that leaves them out, or rounds other values in their place, can miss the bound.
Values may be sent and summed in bfloat16 or wider, within the bound.
No kernel may reach another device: no remote copies, remote signals or barrier semaphores. Data moves between devices by JAX's collectives and lax.ppermute only.
A program may use at most 192 MiB of HBM per device.

v0:
```python
import functools
import math

import jax
import jax.numpy as jnp
from jax import lax
from jax.experimental import pallas as pl
from jax.experimental.pallas import tpu as pltpu
from jax.sharding import PartitionSpec as P

HD = 128
BLOCK = 64
RAND = 3
SLOTS = 5 + RAND


def _nt(a, b):
    return lax.dot_general(a, b, (((1,), (1,)), ((), ())), preferred_element_type=jnp.float32)


def _tn(a, b):
    return lax.dot_general(a, b, (((0,), (0,)), ((), ())), preferred_element_type=jnp.float32)


def _nn(a, b):
    return lax.dot_general(a, b, (((1,), (0,)), ((), ())), preferred_element_type=jnp.float32)


def _attention_kernel(rb_ref, q_ref, k_ref, v_ref, u_ref, dq_ref, dk_ref, dv_ref,
                      dk_acc, dv_acc, kg_ref, vg_ref, *, length):
    count = length // BLOCK
    factor = 1.0 / math.sqrt(HD)

    def softmax_grads(qb, ub, keys, values, mask):
        scores = _nt(qb, keys) * factor
        if mask is not None:
            scores = jnp.where(mask, -1e30, scores)
        top = jnp.max(scores, axis=1, keepdims=True)
        expo = jnp.exp(scores - top)
        weights = expo * (1.0 / jnp.sum(expo, axis=1, keepdims=True))
        rounded = weights.astype(jnp.bfloat16)
        attended = _nn(rounded, values)
        row = jnp.sum(ub.astype(jnp.float32) * attended, axis=1, keepdims=True)
        grad_probs = _nt(ub, values)
        grad_scores = (weights * (grad_probs - row) * factor).astype(jnp.bfloat16)
        query_grad = _nn(grad_scores, keys)
        key_grad = _tn(grad_scores, qb)
        value_grad = _tn(rounded, ub)
        return query_grad, key_grad, value_grad

    keys_all = k_ref[...]
    values_all = v_ref[...]
    for index, start in enumerate((0, length - BLOCK)):
        qb = q_ref[start:start + BLOCK, :]
        ub = u_ref[start:start + BLOCK, :]
        query_grad, key_grad, value_grad = softmax_grads(qb, ub, keys_all, values_all, None)
        dq_ref[start:start + BLOCK, :] = query_grad.astype(jnp.bfloat16)
        if index == 0:
            dk_acc[...] = key_grad
            dv_acc[...] = value_grad
        else:
            dk_acc[...] += key_grad
            dv_acc[...] += value_grad

    columns = lax.broadcasted_iota(jnp.int32, (BLOCK, SLOTS * BLOCK), 1) // BLOCK

    def mid_step(m, carry):
        base = (m - 1) * RAND
        lower = jnp.where(m - 1 >= 1, m - 1, m)
        upper = jnp.where(m + 1 <= count - 2, m + 1, m)
        ids = [0, count - 1, lower, m, upper] + [rb_ref[base + r] for r in range(RAND)]
        for slot, block in enumerate(ids):
            row = pl.multiple_of(block * BLOCK, BLOCK)
            kg_ref[slot * BLOCK:(slot + 1) * BLOCK, :] = k_ref[pl.ds(row, BLOCK), :]
            vg_ref[slot * BLOCK:(slot + 1) * BLOCK, :] = v_ref[pl.ds(row, BLOCK), :]
        start = pl.multiple_of(m * BLOCK, BLOCK)
        qb = q_ref[pl.ds(start, BLOCK), :]
        ub = u_ref[pl.ds(start, BLOCK), :]
        mask = ((columns == 2) & (m == 1)) | ((columns == 4) & (m == count - 2))
        query_grad, key_grad, value_grad = softmax_grads(qb, ub, kg_ref[...], vg_ref[...], mask)
        dq_ref[pl.ds(start, BLOCK), :] = query_grad.astype(jnp.bfloat16)
        for slot, block in enumerate(ids):
            row = pl.multiple_of(block * BLOCK, BLOCK)
            dk_acc[pl.ds(row, BLOCK), :] += key_grad[slot * BLOCK:(slot + 1) * BLOCK, :]
            dv_acc[pl.ds(row, BLOCK), :] += value_grad[slot * BLOCK:(slot + 1) * BLOCK, :]
        return carry

    lax.fori_loop(1, count - 1, mid_step, 0)
    dk_ref[...] = dk_acc[...].astype(jnp.bfloat16)
    dv_ref[...] = dv_acc[...].astype(jnp.bfloat16)


def attention_grads(queries, key_rows, value_rows, upstream, random_ids):
    length, width = queries.shape
    heads = width // HD
    spec = pl.BlockSpec((length, HD), lambda h, rb: (0, h))
    out = jax.ShapeDtypeStruct((length, width), jnp.bfloat16)
    return pl.pallas_call(
        functools.partial(_attention_kernel, length=length),
        out_shape=(out, out, out),
        grid_spec=pltpu.PrefetchScalarGridSpec(
            num_scalar_prefetch=1,
            grid=(heads,),
            in_specs=[spec, spec, spec, spec],
            out_specs=[spec, spec, spec],
            scratch_shapes=[
                pltpu.VMEM((length, HD), jnp.float32),
                pltpu.VMEM((length, HD), jnp.float32),
                pltpu.VMEM((SLOTS * BLOCK, HD), jnp.bfloat16),
                pltpu.VMEM((SLOTS * BLOCK, HD), jnp.bfloat16),
            ],
        ),
        compiler_params=pltpu.CompilerParams(dimension_semantics=("arbitrary",)),
    )(random_ids.reshape(-1), queries, key_rows, value_rows, upstream)


def body(queries, key_rows, value_rows, cotangent, out_weight, random_blocks):
    dp = lax.axis_size("dp")
    ctx = lax.axis_size("context")
    local_queries = queries[0]
    local_keys = key_rows[0]
    local_values = value_rows[0]
    local_cotangent = cotangent[0]
    tokens, width = local_queries.shape
    total_heads = width // HD
    rows_per_device = out_weight.shape[0]
    strided = rows_per_device == HD and total_heads == dp * ctx

    if strided:
        head_weight = lax.all_gather(out_weight, "dp", axis=0, tiled=True)
        full_cotangent = lax.all_gather(local_cotangent, "context", axis=0, tiled=True)
        upstream = lax.dot_general(
            full_cotangent, head_weight, (((1,), (1,)), ((), ())),
            preferred_element_type=jnp.float32,
        ).astype(jnp.bfloat16)

        def send(array):
            split = array.reshape(tokens, dp, ctx, HD)
            moved = lax.all_to_all(split, "context", split_axis=2, concat_axis=0, tiled=True)
            return moved.reshape(tokens * ctx, dp * HD)

        def back(array):
            split = array.reshape(tokens * ctx, dp, 1, HD)
            moved = lax.all_to_all(split, "context", split_axis=0, concat_axis=2, tiled=True)
            return moved.reshape(tokens, width)

        head_upstream = upstream
    else:
        upstream = lax.dot_general(
            local_cotangent,
            lax.all_gather(out_weight, ("dp", "context"), axis=0, tiled=True),
            (((1,), (1,)), ((), ())),
            preferred_element_type=jnp.float32,
        ).astype(jnp.bfloat16)

        def send(array):
            return lax.all_to_all(array, "context", split_axis=1, concat_axis=0, tiled=True)

        def back(array):
            return lax.all_to_all(array, "context", split_axis=0, concat_axis=1, tiled=True)

        head_upstream = send(upstream)

    grads = attention_grads(
        send(local_queries), send(local_keys), send(local_values), head_upstream,
        random_blocks[0],
    )
    return tuple(back(grad)[None] for grad in grads)


def solution(mesh):
    return jax.shard_map(
        body,
        mesh=mesh,
        in_specs=(
            P("dp", "context", None),
            P("dp", "context", None),
            P("dp", "context", None),
            P("dp", "context", None),
            P(("dp", "context"), None),
            P("dp", None, None),
        ),
        out_specs=(P("dp", "context", None), P("dp", "context", None), P("dp", "context", None)),
        check_vma=False,
    )
```

profile of v0, /device:TPU:0, one launch (start us, length us, event | category | flops | bytes accessed | tf_op | source)
XLA Modules:
  0.0 226.6 jit_solution(17404798135426928751)
XLA Ops:
  7.2 0.0 all-gather.4.cloned.1.call-start
  7.2 0.7 all-gather.4.cloned.1.call-update
  7.9 0.0 all-gather.6.cloned.1.call-start
  7.9 0.7 all-gather.6.cloned.1.call-update
  8.6 1.5 copy.33
  10.1 0.0 copy-start
  10.1 1.4 copy.24
  11.5 5.2 %all-to-all-start = ((bf16[128,4,8,128]{3,1,0,2:T(4,128)(2,1)}), bf16[128,4,8,128]{3,1,0,2:T(4,128)(2,1)S(1)}, u32[]{:S(2)}, u32[]{:S(2)}) async-start(bf16[128,4,8,128]{3,1,0,2:T(4,128)(2,1)} %copy.24), calls=%async_computation | async-start | bytes 2097152 | tf_op jit(solution)/shard_map/all_to_all | solution.py:139
  16.7 0.0 copy-done
  16.7 0.2 copy.35
  16.9 0.0 copy-start.1
  16.9 1.4 copy.25
  18.3 13.8 %all-to-all-done = bf16[128,4,8,128]{3,1,0,2:T(4,128)(2,1)S(1)} async-done(((bf16[128,4,8,128]{3,1,0,2:T(4,128)(2,1)}), bf16[128,4,8,128]{3,1,0,2:T(4,128)(2,1)S(1)}, u32[]{:S(2)}, u32[]{:S(2)}) %all-to-all-start) | async-done | bytes 1048608 | tf_op jit(solution)/shard_map/all_to_all | solution.py:139
  32.1 3.6 %all-to-all-start.1 = ((bf16[128,4,8,128]{3,1,0,2:T(4,128)(2,1)}), bf16[128,4,8,128]{3,1,0,2:T(4,128)(2,1)S(1)}, u32[]{:S(2)}, u32[]{:S(2)}) async-start(bf16[128,4,8,128]{3,1,0,2:T(4,128)(2,1)} %copy.25), calls=%async_computation.1 | async-start | bytes 2097152 | tf_op jit(solution)/shard_map/all_to_all | solution.py:139
  35.6 0.0 copy-done.1
  35.7 0.2 copy.37
  35.9 0.0 copy-start.4
  35.9 1.4 copy.26
  37.3 13.7 %all-to-all-done.1 = bf16[128,4,8,128]{3,1,0,2:T(4,128)(2,1)S(1)} async-done(((bf16[128,4,8,128]{3,1,0,2:T(4,128)(2,1)}), bf16[128,4,8,128]{3,1,0,2:T(4,128)(2,1)S(1)}, u32[]{:S(2)}, u32[]{:S(2)}) %all-to-all-start.1) | async-done | bytes 1048608 | tf_op jit(solution)/shard_map/all_to_all | solution.py:139
  51.0 3.6 %all-to-all-start.2 = ((bf16[128,4,8,128]{3,1,0,2:T(4,128)(2,1)}), bf16[128,4,8,128]{3,1,0,2:T(4,128)(2,1)S(1)}, u32[]{:S(2)}, u32[]{:S(2)}) async-start(bf16[128,4,8,128]{3,1,0,2:T(4,128)(2,1)} %copy.26), calls=%async_computation.2 | async-start | bytes 2097152 | tf_op jit(solution)/shard_map/all_to_all | solution.py:139
  54.6 0.0 copy-done.4
  54.6 0.1 copy.23
  54.7 0.7 reshape_squeeze.12.rb_ref
  55.3 1.2 copy.44
  56.5 1.2 copy.43
  57.6 12.3 %all-to-all-done.2 = bf16[128,4,8,128]{3,1,0,2:T(4,128)(2,1)S(1)} async-done(((bf16[128,4,8,128]{3,1,0,2:T(4,128)(2,1)}), bf16[128,4,8,128]{3,1,0,2:T(4,128)(2,1)S(1)}, u32[]{:S(2)}, u32[]{:S(2)}) %all-to-all-start.2) | async-done | bytes 1048608 | tf_op jit(solution)/shard_map/all_to_all | solution.py:139
  69.9 1.2 copy.42
  71.1 24.5 %all-gather.6.cloned.1.call-done = bf16[1,1024,2048]{2,1,0:T(8,128)(2,1)} async-done(((bf16[1,128,2048]{2,1,0:T(8,128)(2,1)}), bf16[1,1024,2048]{2,1,0:T(8,128)(2,1)}) %all-gather.6.cloned.1.call-update) | async-done | bytes 4194320 | tf_op jit(solution)/shard_map/all_gather | solution.py:131
  95.6 6.2 %fusion.2.u_ref = bf16[1024,512]{1,0:T(8,128)(2,1)} fusion(bf16[512,2048]{1,0:T(8,128)(2,1)} %all-gather.4.cloned.1.call-done, bf16[1,1024,2048]{2,1,0:T(8,128)(2,1)} %all-gather.6.cloned.1.call-done), kind=kOutput, calls=%fused_computation.2 | convolution fusion | flops 2148007936 | bytes 7340032 | tf_op jit(solution)/shard_map/dot_general | solution.py:132
  101.8 56.5 %shard_map.85 = (bf16[1024,512]{1,0:T(8,128)(2,1)}, bf16[1024,512]{1,0:T(8,128)(2,1)}, bf16[1024,512]{1,0:T(8,128)(2,1)}) custom-call(s32[42]{0:T(128)} %reshape_squeeze.12.rb_ref, bf16[1024,512]{1,0:T(8,128)(2,1)} %bitcast.69, bf16[1024,512]{1,0:T(8,128)(2,1)} %bitcast.70, bf16[1024,512]{1,0:T(8,128)(2,1)} %bitcast.71, bf16[1024,512]{1,0:T(8,128)(2,1)} %fusion.2.u_ref), custom_call_target="tpu_custom_call" | custom-call | tf_op jit(solution)/shard_map/pallas_call | solution.py:98
  158.3 2.2 reshape.33
  160.6 3.6 %all-to-all-start.3 = ((bf16[1024,4,1,128]{3,1,2,0:T(4,128)(2,1)}), bf16[1024,4,1,128]{3,1,2,0:T(4,128)(2,1)S(1)}, u32[]{:S(2)}, u32[]{:S(2)}) async-start(bf16[1024,4,1,128]{3,1,2,0:T(4,128)(2,1)} %bitcast.7), calls=%async_computation.3 | async-start | bytes 2097152 | tf_op jit(solution)/shard_map/all_to_all | solution.py:144
  164.1 0.0 copy-done.3
  164.1 0.0 copy-start.2
  164.1 1.1 reshape.34
  165.3 14.2 %all-to-all-done.3 = bf16[1024,4,1,128]{3,1,2,0:T(4,128)(2,1)S(1)} async-done(((bf16[1024,4,1,128]{3,1,2,0:T(4,128)(2,1)}), bf16[1024,4,1,128]{3,1,2,0:T(4,128)(2,1)S(1)}, u32[]{:S(2)}, u32[]{:S(2)}) %all-to-all-start.3) | async-done | bytes 1048608 | tf_op jit(solution)/shard_map/all_to_all | solution.py:144
  179.5 3.6 %all-to-all-start.4 = ((bf16[1024,4,1,128]{3,1,2,0:T(4,128)(2,1)}), bf16[1024,4,1,128]{3,1,2,0:T(4,128)(2,1)S(1)}, u32[]{:S(2)}, u32[]{:S(2)}) async-start(bf16[1024,4,1,128]{3,1,2,0:T(4,128)(2,1)} %bitcast.10), calls=%async_computation.4 | async-start | bytes 2097152 | tf_op jit(solution)/shard_map/all_to_all | solution.py:144
  183.0 0.0 copy-done.2
  183.0 1.1 reshape.35
  184.2 14.2 %all-to-all-done.4 = bf16[1024,4,1,128]{3,1,2,0:T(4,128)(2,1)S(1)} async-done(((bf16[1024,4,1,128]{3,1,2,0:T(4,128)(2,1)}), bf16[1024,4,1,128]{3,1,2,0:T(4,128)(2,1)S(1)}, u32[]{:S(2)}, u32[]{:S(2)}) %all-to-all-start.4) | async-done | bytes 1048608 | tf_op jit(solution)/shard_map/all_to_all | solution.py:144
  198.4 3.7 %all-to-all-start.5 = ((bf16[1024,4,1,128]{3,1,2,0:T(4,128)(2,1)}), bf16[1024,4,1,128]{3,1,2,0:T(4,128)(2,1)S(1)}, u32[]{:S(2)}, u32[]{:S(2)}) async-start(bf16[1024,4,1,128]{3,1,2,0:T(4,128)(2,1)} %bitcast.13), calls=%async_computation.5 | async-start | bytes 2097152 | tf_op jit(solution)/shard_map/all_to_all | solution.py:144
  202.1 2.2 copy.28
  204.3 2.3 %broadcast_in_dim_reshape.9 = bf16[1,128,4096]{2,1,0:T(8,128)(2,1)} reshape(bf16[128,4,8,1,128]{4,2,1,0,3:T(8,128)(2,1)} %copy.28) | data formatting | bytes 2097152 | tf_op jit(solution)/shard_map/broadcast_in_dim;reshape | solution.py:168
  206.6 1.2 copy.30
  207.8 1.3 broadcast_in_dim_reshape.10
  209.1 8.2 %all-to-all-done.5 = bf16[1024,4,1,128]{3,1,2,0:T(4,128)(2,1)S(1)} async-done(((bf16[1024,4,1,128]{3,1,2,0:T(4,128)(2,1)}), bf16[1024,4,1,128]{3,1,2,0:T(4,128)(2,1)S(1)}, u32[]{:S(2)}, u32[]{:S(2)}) %all-to-all-start.5) | async-done | bytes 1048608 | tf_op jit(solution)/shard_map/all_to_all | solution.py:144
  217.3 1.2 copy.32
  218.5 1.3 broadcast_in_dim_reshape.11
  (2 shorter events, 0.0 us)
Async XLA Ops:
  7.2 63.9 %all-gather.4.cloned.1.call-start = ((), (), s32[]{:S(2)}) async-start(), calls=%async_computation.6 | async-start | bytes 2621440 | tf_op jit(solution)/shard_map/all_gather | solution.py:130
  7.9 87.7 %all-gather.6.cloned.1.call-start = ((), (), s32[]{:S(2)}) async-start(), calls=%async_computation.7 | async-start | bytes 4718592 | tf_op jit(solution)/shard_map/all_gather | solution.py:131
  10.1 6.6 %copy-start = (bf16[1,128,4096]{2,1,0:T(8,128)(2,1)S(1)}, bf16[1,128,4096]{2,1,0:T(8,128)(2,1)}, u32[]{:S(2)}) copy-start(bf16[1,128,4096]{2,1,0:T(8,128)(2,1)} %param.7) | copy-start | bytes 3145732
  11.5 20.6 %all-to-all-start = ((bf16[128,4,8,128]{3,1,0,2:T(4,128)(2,1)}), bf16[128,4,8,128]{3,1,0,2:T(4,128)(2,1)S(1)}, u32[]{:S(2)}, u32[]{:S(2)}) async-start(bf16[128,4,8,128]{3,1,0,2:T(4,128)(2,1)} %copy.24), calls=%async_computation | async-start | bytes 2097152 | tf_op jit(solution)/shard_map/all_to_all | solution.py:139
  16.9 18.7 %copy-start.1 = (bf16[1,128,4096]{2,1,0:T(8,128)(2,1)S(1)}, bf16[1,128,4096]{2,1,0:T(8,128)(2,1)}, u32[]{:S(2)}) copy-start(bf16[1,128,4096]{2,1,0:T(8,128)(2,1)} %param.8) | copy-start | bytes 3145732
  32.1 18.9 %all-to-all-start.1 = ((bf16[128,4,8,128]{3,1,0,2:T(4,128)(2,1)}), bf16[128,4,8,128]{3,1,0,2:T(4,128)(2,1)S(1)}, u32[]{:S(2)}, u32[]{:S(2)}) async-start(bf16[128,4,8,128]{3,1,0,2:T(4,128)(2,1)} %copy.25), calls=%async_computation.1 | async-start | bytes 2097152 | tf_op jit(solution)/shard_map/all_to_all | solution.py:139
  35.9 18.6 %copy-start.4 = (s32[1,14,3]{1,0,2:T(1,128)S(1)}, s32[1,14,3]{1,0,2:T(1,128)}, u32[]{:S(2)}) copy-start(s32[1,14,3]{1,0,2:T(1,128)} %param.11) | copy-start | bytes 508
  51.0 19.0 %all-to-all-start.2 = ((bf16[128,4,8,128]{3,1,0,2:T(4,128)(2,1)}), bf16[128,4,8,128]{3,1,0,2:T(4,128)(2,1)S(1)}, u32[]{:S(2)}, u32[]{:S(2)}) async-start(bf16[128,4,8,128]{3,1,0,2:T(4,128)(2,1)} %copy.26), calls=%async_computation.2 | async-start | bytes 2097152 | tf_op jit(solution)/shard_map/all_to_all | solution.py:139
  158.3 5.8 %copy-start.3 = (bf16[1024,512]{1,0:T(8,128)(2,1)S(1)}, bf16[1024,512]{1,0:T(8,128)(2,1)}, u32[]{:S(2)}) copy-start(bf16[1024,512]{1,0:T(8,128)(2,1)} %get-tuple-element.7) | copy-start | bytes 3145732
  160.6 18.9 %all-to-all-start.3 = ((bf16[1024,4,1,128]{3,1,2,0:T(4,128)(2,1)}), bf16[1024,4,1,128]{3,1,2,0:T(4,128)(2,1)S(1)}, u32[]{:S(2)}, u32[]{:S(2)}) async-start(bf16[1024,4,1,128]{3,1,2,0:T(4,128)(2,1)} %bitcast.7), calls=%async_computation.3 | async-start | bytes 2097152 | tf_op jit(solution)/shard_map/all_to_all | solution.py:144
  164.1 18.9 %copy-start.2 = (bf16[1024,512]{1,0:T(8,128)(2,1)S(1)}, bf16[1024,512]{1,0:T(8,128)(2,1)}, u32[]{:S(2)}) copy-start(bf16[1024,512]{1,0:T(8,128)(2,1)} %get-tuple-element.8) | copy-start | bytes 3145732
  179.5 18.9 %all-to-all-start.4 = ((bf16[1024,4,1,128]{3,1,2,0:T(4,128)(2,1)}), bf16[1024,4,1,128]{3,1,2,0:T(4,128)(2,1)S(1)}, u32[]{:S(2)}, u32[]{:S(2)}) async-start(bf16[1024,4,1,128]{3,1,2,0:T(4,128)(2,1)} %bitcast.10), calls=%async_computation.4 | async-start | bytes 2097152 | tf_op jit(solution)/shard_map/all_to_all | solution.py:144
  198.4 18.9 %all-to-all-start.5 = ((bf16[1024,4,1,128]{3,1,2,0:T(4,128)(2,1)}), bf16[1024,4,1,128]{3,1,2,0:T(4,128)(2,1)S(1)}, u32[]{:S(2)}, u32[]{:S(2)}) async-start(bf16[1024,4,1,128]{3,1,2,0:T(4,128)(2,1)} %bitcast.13), calls=%async_computation.5 | async-start | bytes 2097152 | tf_op jit(solution)/shard_map/all_to_all | solution.py:144
Sparse Core Ops, SparseCore 0:
  9.6 48.6 all-gather.3
  60.1 35.4 all-gather.5
where the time goes:
time: 227 us
  waiting for transfers between devices  102 us (45%)
  Pallas kernels  56.5 us (25%)
  local copies, waits for them, and re-layouts  24.3 us (11%)
  starting transfers between devices  23.2 us (10%)
  between operations  14.2 us (6%)
  matrix products  6.2 us (3%)
    pallas_call x1, Pallas kernels, attention_grads(): pl.pallas_call(functools.partial(_attention_kernel, length=length), out_s...  56.5 us
    all_to_all x3, waiting for transfers between devices, send(): lax.all_to_all(split, 'context', split_axis=2, concat_axis=0, tiled=True)  39.8 us
    all_to_all x3, waiting for transfers between devices, back(): lax.all_to_all(split, 'context', split_axis=0, concat_axis=2, tiled=True)  36.6 us
    all_gather x1, waiting for transfers between devices, body(): lax.all_gather(local_cotangent, 'context', axis=0, tiled=True)  24.5 us
    all_to_all x3, starting transfers between devices, send(): lax.all_to_all(split, 'context', split_axis=2, concat_axis=0, tiled=True)  12.3 us
    all_to_all x3, starting transfers between devices, back(): lax.all_to_all(split, 'context', split_axis=0, concat_axis=2, tiled=True)  10.9 us
    dot_general x1, matrix products, body(): lax.dot_general(full_cotangent, head_weight, (((1,), (1,)), ((), ())), pr...  6.2 us
    unnamed x17, local copies, waits for them, and re-layouts  5.52 us
  transfers between devices with their start and end apart: 8, of which 7 were waited for; matrix products, arithmetic and copies ran while one was open for 9% of the time, Pallas kernels for 0%

commit v1 on v0

--- a/solution.py
+++ b/solution.py
@@ -26,9 +26,10 @@
     return lax.dot_general(a, b, (((1,), (0,)), ((), ())), preferred_element_type=jnp.float32)
 
 
-def _attention_kernel(rb_ref, q_ref, k_ref, v_ref, u_ref, dq_ref, dk_ref, dv_ref,
-                      dk_acc, dv_acc, kg_ref, vg_ref, *, length):
+def _attention_kernel(rb_ref, x_ref, u_ref, o_ref, dk_acc, dv_acc, kg_ref, vg_ref, *, length):
     count = length // BLOCK
+    q_ref, k_ref, v_ref = (x_ref.at[:, i * HD:(i + 1) * HD] for i in range(3))
+    dq_ref, dk_ref, dv_ref = (o_ref.at[:, i * HD:(i + 1) * HD] for i in range(3))
     factor = 1.0 / math.sqrt(HD)
 
     def softmax_grads(qb, ub, keys, values, mask):
@@ -90,19 +91,24 @@
     dv_ref[...] = dv_acc[...].astype(jnp.bfloat16)
 
 
-def attention_grads(queries, key_rows, value_rows, upstream, random_ids):
-    length, width = queries.shape
-    heads = width // HD
+def attention_grads(stacked, upstream, random_ids):
+    length = stacked.shape[0]
+    count = length // BLOCK
     spec = pl.BlockSpec((length, HD), lambda h, rb: (0, h))
-    out = jax.ShapeDtypeStruct((length, width), jnp.bfloat16)
+    whole = pl.BlockSpec((length, 3 * HD), lambda h, rb: (0, 0))
+    out = jax.ShapeDtypeStruct((length, 3 * HD), jnp.bfloat16)
+    pairs = 2 * BLOCK * length + (count - 2) * BLOCK * SLOTS * BLOCK
+    cost = pl.CostEstimate(
+        flops=12 * pairs * HD, transcendentals=pairs, bytes_accessed=14 * length * HD
+    )
     return pl.pallas_call(
         functools.partial(_attention_kernel, length=length),
-        out_shape=(out, out, out),
+        out_shape=out,
         grid_spec=pltpu.PrefetchScalarGridSpec(
             num_scalar_prefetch=1,
-            grid=(heads,),
-            in_specs=[spec, spec, spec, spec],
-            out_specs=[spec, spec, spec],
+            grid=(1,),
+            in_specs=[whole, spec],
+            out_specs=whole,
             scratch_shapes=[
                 pltpu.VMEM((length, HD), jnp.float32),
                 pltpu.VMEM((length, HD), jnp.float32),
@@ -111,40 +117,27 @@
             ],
         ),
         compiler_params=pltpu.CompilerParams(dimension_semantics=("arbitrary",)),
-    )(random_ids.reshape(-1), queries, key_rows, value_rows, upstream)
+        cost_estimate=cost,
+    )(random_ids.reshape(-1), stacked, upstream)
 
 
 def body(queries, key_rows, value_rows, cotangent, out_weight, random_blocks):
     dp = lax.axis_size("dp")
     ctx = lax.axis_size("context")
-    local_queries = queries[0]
-    local_keys = key_rows[0]
-    local_values = value_rows[0]
+    local = (queries[0], key_rows[0], value_rows[0])
     local_cotangent = cotangent[0]
-    tokens, width = local_queries.shape
+    tokens, width = local[0].shape
     total_heads = width // HD
+    local_heads = total_heads // ctx
     rows_per_device = out_weight.shape[0]
-    strided = rows_per_device == HD and total_heads == dp * ctx
+    strided = rows_per_device == HD and local_heads == dp
 
     if strided:
         head_weight = lax.all_gather(out_weight, "dp", axis=0, tiled=True)
         full_cotangent = lax.all_gather(local_cotangent, "context", axis=0, tiled=True)
-        upstream = lax.dot_general(
-            full_cotangent, head_weight, (((1,), (1,)), ((), ())),
-            preferred_element_type=jnp.float32,
-        ).astype(jnp.bfloat16)
 
-        def send(array):
-            split = array.reshape(tokens, dp, ctx, HD)
-            moved = lax.all_to_all(split, "context", split_axis=2, concat_axis=0, tiled=True)
-            return moved.reshape(tokens * ctx, dp * HD)
-
-        def back(array):
-            split = array.reshape(tokens * ctx, dp, 1, HD)
-            moved = lax.all_to_all(split, "context", split_axis=0, concat_axis=2, tiled=True)
-            return moved.reshape(tokens, width)
-
-        head_upstream = upstream
+        def chunk(array, c):
+            return array.reshape(tokens, dp, ctx, HD)[:, c]
     else:
         upstream = lax.dot_general(
             local_cotangent,
@@ -152,20 +145,33 @@
             (((1,), (1,)), ((), ())),
             preferred_element_type=jnp.float32,
         ).astype(jnp.bfloat16)
+        local = local + (upstream,)
 
-        def send(array):
-            return lax.all_to_all(array, "context", split_axis=1, concat_axis=0, tiled=True)
+        def chunk(array, c):
+            return array.reshape(tokens, ctx, local_heads, HD)[:, :, c]
 
-        def back(array):
-            return lax.all_to_all(array, "context", split_axis=0, concat_axis=1, tiled=True)
+    pieces = []
+    for c in range(local_heads):
+        stacked = jnp.stack([chunk(array, c) for array in local], axis=1)
+        moved = lax.all_to_all(stacked, "context", split_axis=2, concat_axis=0, tiled=True)
+        moved = moved.reshape(tokens * ctx, len(local) * HD)
+        if strided:
+            head_upstream = lax.dot_general(
+                full_cotangent, head_weight[c * HD:(c + 1) * HD], (((1,), (1,)), ((), ())),
+                preferred_element_type=jnp.float32,
+            ).astype(jnp.bfloat16)
+        else:
+            head_upstream = moved[:, 3 * HD:]
+        grads = attention_grads(moved[:, :3 * HD], head_upstream, random_blocks[0])
+        grads = grads.reshape(tokens * ctx, 3, 1, HD)
+        pieces.append(lax.all_to_all(grads, "context", split_axis=0, concat_axis=2, tiled=True))
 
-        head_upstream = send(upstream)
-
-    grads = attention_grads(
-        send(local_queries), send(local_keys), send(local_values), head_upstream,
-        random_blocks[0],
-    )
-    return tuple(back(grad)[None] for grad in grads)
+    outs = []
+    for g in range(3):
+        parts = [piece[:, g] for piece in pieces]
+        joined = jnp.stack(parts, axis=1 if strided else 2)
+        outs.append(joined.reshape(1, tokens, width))
+    return tuple(outs)
 
 
 def solution(mesh):

time: 227 us -> 265 us (1.17)
  local copies, waits for them, and re-layouts: 24.3 us -> 49.3 us
  waiting for transfers between devices: 102 us -> 77.2 us
  matrix products: 6.2 us -> 17.1 us
  other arithmetic: 0 us -> 8.86 us
  starting transfers between devices: 23.2 us -> 32 us
  Pallas kernels: 56.5 us -> 65.2 us
    all_to_all x6 -> x8, waiting for transfers between devices: 76.3 us -> 44.7 us  [the longest x4 34.4 us: body(): lax.all_to_all(stacked, 'context', split_axis=2, concat_axis=0, tiled=True)]
    slice x0 -> x6, local copies, waits for them, and re-layouts: none -> 11.4 us  [the longest x4 9.56 us: body(): parts = [piece[:, g] for piece in pieces]]
    dot_general x1 -> x4, matrix products: 6.2 us -> 17.1 us  [body(): lax.dot_general(full_cotangent, head_weight[c * HD:(c + 1) * HD], (((1,),...]
    reshape x3 -> x11, local copies, waits for them, and re-layouts: 4.47 us -> 15.1 us  [the longest x4 6.61 us: body(): grads = grads.reshape(tokens * ctx, 3, 1, HD)]
    another operation x0 -> x7, other arithmetic: none -> 8.86 us  [the longest x3 8.5 us: body(): joined = jnp.stack(parts, axis=1 if strided else 2)]
    all_to_all x6 -> x8, starting transfers between devices: 23.1 us -> 31.9 us  [the longest x4 16.1 us: body(): lax.all_to_all(grads, 'context', split_axis=0, concat_axis=2, tiled=True)]
    pallas_call x1 -> x4, Pallas kernels: 56.5 us -> 65.2 us  [attention_grads(): pl.pallas_call(functools.partial(_attention_kernel, length=length), out_s...]
    all_gather x1, waiting for transfers between devices: 24.5 us -> 31.1 us  [body(): lax.all_gather(local_cotangent, 'context', axis=0, tiled=True)]
  transfers between devices with their start and end apart: 8 -> 10, of which waited for: 7 -> 5; matrix products, arithmetic and copies ran while one was open for 9% -> 22% of each run, Pallas kernels for 0% -> 25%
where the time goes in v1:
time: 265 us; the launch traced here: 264 us
  waiting for transfers between devices  77.2 us (29%)
  Pallas kernels  65.2 us (25%)
  local copies, waits for them, and re-layouts  49.3 us (19%)
  starting transfers between devices  32 us (12%)
  matrix products  17.1 us (6%)
  between operations  14.3 us (5%)
  other arithmetic  8.86 us (3%)
    pallas_call x4, Pallas kernels, attention_grads(): pl.pallas_call(functools.partial(_attention_kernel, length=length), out_s...  65.2 us
    all_to_all x4, waiting for transfers between devices, body(): lax.all_to_all(stacked, 'context', split_axis=2, concat_axis=0, tiled=True)  34.4 us
    all_gather x1, waiting for transfers between devices, body(): lax.all_gather(local_cotangent, 'context', axis=0, tiled=True)  31.1 us
    dot_general x4, matrix products, body(): lax.dot_general(full_cotangent, head_weight[c * HD:(c + 1) * HD], (((1,),...  17.1 us
    all_to_all x4, starting transfers between devices, body(): lax.all_to_all(grads, 'context', split_axis=0, concat_axis=2, tiled=True)  16.1 us
    all_to_all x4, starting transfers between devices, body(): lax.all_to_all(stacked, 'context', split_axis=2, concat_axis=0, tiled=True)  15.8 us
    all_to_all x4, waiting for transfers between devices, body(): lax.all_to_all(grads, 'context', split_axis=0, concat_axis=2, tiled=True)  10.4 us
    slice x4, local copies, waits for them, and re-layouts, body(): parts = [piece[:, g] for piece in pieces]  9.56 us
  transfers between devices with their start and end apart: 10, of which 5 were waited for; matrix products, arithmetic and copies ran while one was open for 22% of the time, Pallas kernels for 25%

profile of v1, /device:TPU:0, one launch (start us, length us, event | category | flops | bytes accessed | tf_op | source)
XLA Modules:
  0.0 264.1 jit_solution(6235429180404658662)
XLA Ops:
  8.7 1.6 copy.71
  11.0 1.6 copy.73
  15.5 5.2 %all-to-all-start = ((bf16[128,3,8,128]{0,3,1,2:T(8,128)(2,1)}), bf16[128,3,8,128]{0,3,1,2:T(8,128)(2,1)S(1)}, u32[]{:S(2)}, u32[]{:S(2)}) async-start(bf16[128,3,8,128]{0,3,1,2:T(8,128)(2,1)} %copy.74), calls=%async_computation | async-start | bytes 1572864 | tf_op jit(solution)/shard_map/all_to_all | solution.py:156
  21.7 11.5 %all-to-all-done = bf16[128,3,8,128]{0,3,1,2:T(8,128)(2,1)S(1)} async-done(((bf16[128,3,8,128]{0,3,1,2:T(8,128)(2,1)}), bf16[128,3,8,128]{0,3,1,2:T(8,128)(2,1)S(1)}, u32[]{:S(2)}, u32[]{:S(2)}) %all-to-all-start) | async-done | bytes 786464 | tf_op jit(solution)/shard_map/all_to_all | solution.py:156
  33.2 3.5 %all-to-all-start.6 = ((bf16[128,3,8,128]{0,3,1,2:T(8,128)(2,1)}), bf16[128,3,8,128]{0,3,1,2:T(8,128)(2,1)S(1)}, u32[]{:S(2)}, u32[]{:S(2)}) async-start(bf16[128,3,8,128]{0,3,1,2:T(8,128)(2,1)} %copy.89), calls=%async_computation.6 | async-start | bytes 1572864 | tf_op jit(solution)/shard_map/all_to_all | solution.py:156
  37.9 11.5 %all-to-all-done.6 = bf16[128,3,8,128]{0,3,1,2:T(8,128)(2,1)S(1)} async-done(((bf16[128,3,8,128]{0,3,1,2:T(8,128)(2,1)}), bf16[128,3,8,128]{0,3,1,2:T(8,128)(2,1)S(1)}, u32[]{:S(2)}, u32[]{:S(2)}) %all-to-all-start.6) | async-done | bytes 786464 | tf_op jit(solution)/shard_map/all_to_all | solution.py:156
  49.3 3.5 %all-to-all-start.4 = ((bf16[128,3,8,128]{0,3,1,2:T(8,128)(2,1)}), bf16[128,3,8,128]{0,3,1,2:T(8,128)(2,1)S(1)}, u32[]{:S(2)}, u32[]{:S(2)}) async-start(bf16[128,3,8,128]{0,3,1,2:T(8,128)(2,1)} %copy.84), calls=%async_computation.4 | async-start | bytes 1572864 | tf_op jit(solution)/shard_map/all_to_all | solution.py:156
  53.0 1.0 copy.79
  54.0 11.4 %all-to-all-done.4 = bf16[128,3,8,128]{0,3,1,2:T(8,128)(2,1)S(1)} async-done(((bf16[128,3,8,128]{0,3,1,2:T(8,128)(2,1)}), bf16[128,3,8,128]{0,3,1,2:T(8,128)(2,1)S(1)}, u32[]{:S(2)}, u32[]{:S(2)}) %all-to-all-start.4) | async-done | bytes 786464 | tf_op jit(solution)/shard_map/all_to_all | solution.py:156
  65.4 3.5 %all-to-all-start.2 = ((bf16[128,3,8,128]{0,3,1,2:T(8,128)(2,1)}), bf16[128,3,8,128]{0,3,1,2:T(8,128)(2,1)S(1)}, u32[]{:S(2)}, u32[]{:S(2)}) async-start(bf16[128,3,8,128]{0,3,1,2:T(8,128)(2,1)} %copy.79), calls=%async_computation.2 | async-start | bytes 1572864 | tf_op jit(solution)/shard_map/all_to_all | solution.py:156
  70.5 1.0 copy.113
  71.5 31.1 %all-gather.6.cloned.1.call-done = bf16[1,1024,2048]{2,1,0:T(8,128)(2,1)} async-done(((bf16[1,128,2048]{2,1,0:T(8,128)(2,1)}), bf16[1,1024,2048]{2,1,0:T(8,128)(2,1)}) %all-gather.6.cloned.1.call-update) | async-done | bytes 4194320 | tf_op jit(solution)/shard_map/all_gather | solution.py:137
  102.6 4.3 %fusion.17.u_ref = bf16[1024,128]{1,0:T(8,128)(2,1)} fusion(bf16[1,1024,2048]{2,1,0:T(8,128)(2,1)} %all-gather.6.cloned.1.call-done, bf16[512,2048]{1,0:T(8,128)(2,1)} %all-gather.4.cloned.1.call-done), kind=kOutput, calls=%fused_computation.11 | convolution fusion | flops 537001984 | bytes 4980736 | tf_op jit(solution)/shard_map/dot_general | solution.py:159
  106.9 16.3 %shard_map.88 = bf16[1024,384]{1,0:T(8,128)(2,1)} custom-call(s32[42]{0:T(128)} %reshape_squeeze.8.rb_ref, bf16[1024,384]{1,0:T(8,128)(2,1)} %bitcast.106, bf16[1024,128]{1,0:T(8,128)(2,1)} %fusion.17.u_ref), custom_call_target="tpu_custom_call" | custom-call | flops 905969664 | bytes 1835008 | tf_op jit(solution)/shard_map/pallas_call | solution.py:104
  123.2 1.4 copy.92
  124.6 1.4 copy.93
  126.1 3.6 %all-to-all-start.7 = ((bf16[1024,3,1,128]{3,1,2,0:T(4,128)(2,1)}), bf16[1024,3,1,128]{3,1,2,0:T(4,128)(2,1)S(1)}, u32[]{:S(2)}, u32[]{:S(2)}) async-start(bf16[1024,3,1,128]{3,1,2,0:T(4,128)(2,1)} %copy.93), calls=%async_computation.7 | async-start | bytes 2097152 | tf_op jit(solution)/shard_map/all_to_all | solution.py:167
  131.4 4.3 %fusion.11.u_ref = bf16[1024,128]{1,0:T(8,128)(2,1)} fusion(bf16[1,1024,2048]{2,1,0:T(8,128)(2,1)} %all-gather.6.cloned.1.call-done, bf16[512,2048]{1,0:T(8,128)(2,1)} %all-gather.4.cloned.1.call-done), kind=kOutput, calls=%fused_computation.9 | convolution fusion | flops 537001984 | bytes 4980736 | tf_op jit(solution)/shard_map/dot_general | solution.py:159
  135.7 16.4 %shard_map.86 = bf16[1024,384]{1,0:T(8,128)(2,1)} custom-call(s32[42]{0:T(128)} %reshape_squeeze.8.rb_ref, bf16[1024,384]{1,0:T(8,128)(2,1)} %bitcast.107, bf16[1024,128]{1,0:T(8,128)(2,1)} %fusion.11.u_ref), custom_call_target="tpu_custom_call" | custom-call | flops 905969664 | bytes 1835008 | tf_op jit(solution)/shard_map/pallas_call | solution.py:104
  152.0 1.4 copy.82
  153.4 1.4 copy.83
  154.9 4.1 %all-to-all-start.3 = ((bf16[1024,3,1,128]{3,1,2,0:T(4,128)(2,1)}), bf16[1024,3,1,128]{3,1,2,0:T(4,128)(2,1)S(1)}, u32[]{:S(2)}, u32[]{:S(2)}) async-start(bf16[1024,3,1,128]{3,1,2,0:T(4,128)(2,1)} %copy.83), calls=%async_computation.3 | async-start | bytes 2097152 | tf_op jit(solution)/shard_map/all_to_all | solution.py:167
  159.0 1.6 copy.97
  161.6 1.6 copy.99
  164.3 4.3 %fusion.14.u_ref = bf16[1024,128]{1,0:T(8,128)(2,1)} fusion(bf16[1,1024,2048]{2,1,0:T(8,128)(2,1)} %all-gather.6.cloned.1.call-done, bf16[512,2048]{1,0:T(8,128)(2,1)} %all-gather.4.cloned.1.call-done), kind=kOutput, calls=%fused_computation.10 | convolution fusion | flops 537001984 | bytes 4980736 | tf_op jit(solution)/shard_map/dot_general | solution.py:159
  168.5 16.3 %shard_map.87 = bf16[1024,384]{1,0:T(8,128)(2,1)} custom-call(s32[42]{0:T(128)} %reshape_squeeze.8.rb_ref, bf16[1024,384]{1,0:T(8,128)(2,1)} %bitcast.108, bf16[1024,128]{1,0:T(8,128)(2,1)} %fusion.14.u_ref), custom_call_target="tpu_custom_call" | custom-call | flops 905969664 | bytes 1835008 | tf_op jit(solution)/shard_map/pallas_call | solution.py:104
  184.8 1.4 copy.87
  186.2 1.4 copy.88
  187.7 4.2 %all-to-all-start.5 = ((bf16[1024,3,1,128]{3,1,2,0:T(4,128)(2,1)}), bf16[1024,3,1,128]{3,1,2,0:T(4,128)(2,1)S(1)}, u32[]{:S(2)}, u32[]{:S(2)}) async-start(bf16[1024,3,1,128]{3,1,2,0:T(4,128)(2,1)} %copy.88), calls=%async_computation.5 | async-start | bytes 2097152 | tf_op jit(solution)/shard_map/all_to_all | solution.py:167
  191.9 4.3 %fusion.8.u_ref = bf16[1024,128]{1,0:T(8,128)(2,1)} fusion(bf16[1,1024,2048]{2,1,0:T(8,128)(2,1)} %all-gather.6.cloned.1.call-done, bf16[512,2048]{1,0:T(8,128)(2,1)} %all-gather.4.cloned.1.call-done), kind=kOutput, calls=%fused_computation.8 | convolution fusion | flops 537001984 | bytes 4980736 | tf_op jit(solution)/shard_map/dot_general | solution.py:159
  196.1 16.3 %shard_map.85 = bf16[1024,384]{1,0:T(8,128)(2,1)} custom-call(s32[42]{0:T(128)} %reshape_squeeze.8.rb_ref, bf16[1024,384]{1,0:T(8,128)(2,1)} %bitcast.105, bf16[1024,128]{1,0:T(8,128)(2,1)} %fusion.8.u_ref), custom_call_target="tpu_custom_call" | custom-call | flops 905969664 | bytes 1835008 | tf_op jit(solution)/shard_map/pallas_call | solution.py:104
  212.4 2.3 copy.77
  214.7 2.3 copy.78
  217.0 2.5 fusion.25
  219.6 4.2 %all-to-all-start.1 = ((bf16[1024,3,1,128]{3,1,2,0:T(4,128)(2,1)}), bf16[1024,3,1,128]{3,1,2,0:T(4,128)(2,1)S(1)}, u32[]{:S(2)}, u32[]{:S(2)}) async-start(bf16[1024,3,1,128]{3,1,2,0:T(4,128)(2,1)} %copy.78), calls=%async_computation.1 | async-start | bytes 2097152 | tf_op jit(solution)/shard_map/all_to_all | solution.py:167
  223.8 2.5 fusion.26
  226.3 2.5 fusion.27
  228.8 10.3 %all-to-all-done.1 = bf16[1024,3,1,128]{3,1,2,0:T(4,128)(2,1)S(1)} async-done(((bf16[1024,3,1,128]{3,1,2,0:T(4,128)(2,1)}), bf16[1024,3,1,128]{3,1,2,0:T(4,128)(2,1)S(1)}, u32[]{:S(2)}, u32[]{:S(2)}) %all-to-all-start.1) | async-done | bytes 786464 | tf_op jit(solution)/shard_map/all_to_all | solution.py:167
  239.2 2.0 fusion.24
  241.2 2.4 pad_maximum_fusion
  243.6 1.2 copy.94
  244.9 1.3 reshape.51
  246.1 3.6 %pad_maximum_fusion.1 = bf16[128,4,8,128]{3,1,0,2:T(4,128)(2,1)S(1)} fusion(bf16[128,1,8,128]{3,1,0,2:T(2,128)(2,1)} %get-tuple-element.13, bf16[128,1,8,128]{3,1,0,2:T(2,128)(2,1)S(1)} %copy-done.6, bf16[128,1,8,128]{3,1,0,2:T(2,128)(2,1)S(1)} %copy-done.3, bf16[128,1,8,128]{3,1,0,2:T(2,128)(2,1)} %get-tuple-element.4), kind=kLoop, calls=%fused_computation.13 | loop fusion | flops 4194304 | bytes 2097152 | tf_op jit(solution)/shard_map/stack | solution.py:172
  249.8 1.2 copy.95
  251.0 1.3 reshape.52
  252.3 2.4 pad_maximum_fusion.2
  254.7 1.2 copy.96
  256.0 1.3 reshape.53
  (56 shorter events, 12.5 us)
Async XLA Ops:
  7.2 3.1 %copy-start.9 = (bf16[1,128,4096]{2,1,0:T(8,128)(2,1)S(1)}, bf16[1,128,4096]{2,1,0:T(8,128)(2,1)}, u32[]{:S(2)}) copy-start(bf16[1,128,4096]{2,1,0:T(8,128)(2,1)} %param.7) | copy-start | bytes 3145732
  7.2 64.3 %all-gather.4.cloned.1.call-start = ((), (), s32[]{:S(2)}) async-start(), calls=%async_computation.8 | async-start | bytes 2621440 | tf_op jit(solution)/shard_map/all_gather | solution.py:136
  7.9 94.7 %all-gather.6.cloned.1.call-start = ((), (), s32[]{:S(2)}) async-start(), calls=%async_computation.9 | async-start | bytes 4718592 | tf_op jit(solution)/shard_map/all_gather | solution.py:137
  14.4 6.2 %copy-start.10 = (bf16[128,1,8,128]{0,3,2,1:T(8,128)(2,1)S(1)}, bf16[128,1,8,128]{0,3,2,1:T(8,128)(2,1)}, u32[]{:S(2)}) copy-start(bf16[128,1,8,128]{0,3,2,1:T(8,128)(2,1)} %get-tuple-element.29) | copy-start | bytes 786436
  14.4 6.2 %copy-start.13 = (bf16[128,1,8,128]{0,3,2,1:T(8,128)(2,1)S(1)}, bf16[128,1,8,128]{0,3,2,1:T(8,128)(2,1)}, u32[]{:S(2)}) copy-start(bf16[128,1,8,128]{0,3,2,1:T(8,128)(2,1)} %get-tuple-element.24) | copy-start | bytes 786436
  15.5 17.8 %all-to-all-start = ((bf16[128,3,8,128]{0,3,1,2:T(8,128)(2,1)}), bf16[128,3,8,128]{0,3,1,2:T(8,128)(2,1)S(1)}, u32[]{:S(2)}, u32[]{:S(2)}) async-start(bf16[128,3,8,128]{0,3,1,2:T(8,128)(2,1)} %copy.74), calls=%async_computation | async-start | bytes 1572864 | tf_op jit(solution)/shard_map/all_to_all | solution.py:156
  20.7 16.1 %copy-start.12 = (bf16[128,1,8,128]{0,3,2,1:T(8,128)(2,1)S(1)}, bf16[128,1,8,128]{0,3,2,1:T(8,128)(2,1)}, u32[]{:S(2)}) copy-start(bf16[128,1,8,128]{0,3,2,1:T(8,128)(2,1)} %get-tuple-element.25) | copy-start | bytes 786436
  33.2 4.6 %copy-start = (bf16[128,3,8,128]{0,3,1,2:T(8,128)(2,1)}, bf16[128,3,8,128]{0,3,1,2:T(8,128)(2,1)S(1)}, u32[]{:S(2)}) copy-start(bf16[128,3,8,128]{0,3,1,2:T(8,128)(2,1)S(1)} %all-to-all-done) | copy-start | bytes 2359300
  33.2 16.1 %all-to-all-start.6 = ((bf16[128,3,8,128]{0,3,1,2:T(8,128)(2,1)}), bf16[128,3,8,128]{0,3,1,2:T(8,128)(2,1)S(1)}, u32[]{:S(2)}, u32[]{:S(2)}) async-start(bf16[128,3,8,128]{0,3,1,2:T(8,128)(2,1)} %copy.89), calls=%async_computation.6 | async-start | bytes 1572864 | tf_op jit(solution)/shard_map/all_to_all | solution.py:156
  36.8 16.1 %copy-start.11 = (bf16[128,1,8,128]{0,3,2,1:T(8,128)(2,1)S(1)}, bf16[128,1,8,128]{0,3,2,1:T(8,128)(2,1)}, u32[]{:S(2)}) copy-start(bf16[128,1,8,128]{0,3,2,1:T(8,128)(2,1)} %get-tuple-element.26) | copy-start | bytes 786436
  49.3 16.1 %all-to-all-start.4 = ((bf16[128,3,8,128]{0,3,1,2:T(8,128)(2,1)}), bf16[128,3,8,128]{0,3,1,2:T(8,128)(2,1)S(1)}, u32[]{:S(2)}, u32[]{:S(2)}) async-start(bf16[128,3,8,128]{0,3,1,2:T(8,128)(2,1)} %copy.84), calls=%async_computation.4 | async-start | bytes 1572864 | tf_op jit(solution)/shard_map/all_to_all | solution.py:156
  52.9 16.1 %copy-start.14 = (s32[1,14,3]{1,0,2:T(1,128)S(1)}, s32[1,14,3]{1,0,2:T(1,128)}, u32[]{:S(2)}) copy-start(s32[1,14,3]{1,0,2:T(1,128)} %param.11) | copy-start | bytes 508
  65.4 4.3 %copy-start.1 = (bf16[128,3,8,128]{0,3,1,2:T(8,128)(2,1)}, bf16[128,3,8,128]{0,3,1,2:T(8,128)(2,1)S(1)}, u32[]{:S(2)}) copy-start(bf16[128,3,8,128]{0,3,1,2:T(8,128)(2,1)S(1)} %all-to-all-done.4) | copy-start | bytes 2359300
  65.4 60.6 %all-to-all-start.2 = ((bf16[128,3,8,128]{0,3,1,2:T(8,128)(2,1)}), bf16[128,3,8,128]{0,3,1,2:T(8,128)(2,1)S(1)}, u32[]{:S(2)}, u32[]{:S(2)}) async-start(bf16[128,3,8,128]{0,3,1,2:T(8,128)(2,1)} %copy.79), calls=%async_computation.2 | async-start | bytes 1572864 | tf_op jit(solution)/shard_map/all_to_all | solution.py:156
  126.1 28.8 %all-to-all-start.7 = ((bf16[1024,3,1,128]{3,1,2,0:T(4,128)(2,1)}), bf16[1024,3,1,128]{3,1,2,0:T(4,128)(2,1)S(1)}, u32[]{:S(2)}, u32[]{:S(2)}) async-start(bf16[1024,3,1,128]{3,1,2,0:T(4,128)(2,1)} %copy.93), calls=%async_computation.7 | async-start | bytes 2097152 | tf_op jit(solution)/shard_map/all_to_all | solution.py:167
  154.9 32.8 %all-to-all-start.3 = ((bf16[1024,3,1,128]{3,1,2,0:T(4,128)(2,1)}), bf16[1024,3,1,128]{3,1,2,0:T(4,128)(2,1)S(1)}, u32[]{:S(2)}, u32[]{:S(2)}) async-start(bf16[1024,3,1,128]{3,1,2,0:T(4,128)(2,1)} %copy.83), calls=%async_computation.3 | async-start | bytes 2097152 | tf_op jit(solution)/shard_map/all_to_all | solution.py:167
  187.7 31.9 %all-to-all-start.5 = ((bf16[1024,3,1,128]{3,1,2,0:T(4,128)(2,1)}), bf16[1024,3,1,128]{3,1,2,0:T(4,128)(2,1)S(1)}, u32[]{:S(2)}, u32[]{:S(2)}) async-start(bf16[1024,3,1,128]{3,1,2,0:T(4,128)(2,1)} %copy.88), calls=%async_computation.5 | async-start | bytes 2097152 | tf_op jit(solution)/shard_map/all_to_all | solution.py:167
  219.6 19.6 %all-to-all-start.1 = ((bf16[1024,3,1,128]{3,1,2,0:T(4,128)(2,1)}), bf16[1024,3,1,128]{3,1,2,0:T(4,128)(2,1)S(1)}, u32[]{:S(2)}, u32[]{:S(2)}) async-start(bf16[1024,3,1,128]{3,1,2,0:T(4,128)(2,1)} %copy.78), calls=%async_computation.1 | async-start | bytes 2097152 | tf_op jit(solution)/shard_map/all_to_all | solution.py:167
  228.8 12.3 %copy-start.5 = (bf16[128,1,8,128]{3,1,0,2:T(2,128)(2,1)S(1)}, bf16[128,1,8,128]{3,1,0,2:T(2,128)(2,1)}, u32[]{:S(2)}) copy-start(bf16[128,1,8,128]{3,1,0,2:T(2,128)(2,1)} %get-tuple-element.8) | copy-start | bytes 786436
  228.8 12.3 %copy-start.7 = (bf16[128,1,8,128]{3,1,0,2:T(2,128)(2,1)S(1)}, bf16[128,1,8,128]{3,1,0,2:T(2,128)(2,1)}, u32[]{:S(2)}) copy-start(bf16[128,1,8,128]{3,1,0,2:T(2,128)(2,1)} %get-tuple-element.11) | copy-start | bytes 786436
  239.2 2.0 copy-start.8
  243.6 2.5 copy-start.3
  243.6 2.5 copy-start.6
  249.8 2.5 copy-start.2
  249.8 2.5 copy-start.4
Sparse Core Ops, SparseCore 0:
  9.6 48.6 all-gather.3
  60.1 42.4 all-gather.5

commit v2 on v1

--- a/solution.py
+++ b/solution.py
@@ -26,11 +26,19 @@
     return lax.dot_general(a, b, (((1,), (0,)), ((), ())), preferred_element_type=jnp.float32)
 
 
-def _attention_kernel(rb_ref, x_ref, u_ref, o_ref, dk_acc, dv_acc, kg_ref, vg_ref, *, length):
+def _attention_kernel(rb_ref, x_ref, u_ref, o_ref, dk_acc, dv_acc, kg_ref, vg_ref):
+    parts, _, tokens, _ = x_ref.shape
+    per_part = tokens // BLOCK
+    length = parts * tokens
     count = length // BLOCK
-    q_ref, k_ref, v_ref = (x_ref.at[:, i * HD:(i + 1) * HD] for i in range(3))
-    dq_ref, dk_ref, dv_ref = (o_ref.at[:, i * HD:(i + 1) * HD] for i in range(3))
     factor = 1.0 / math.sqrt(HD)
+
+    def rows(ref, which, block):
+        if isinstance(block, int):
+            offset = (block % per_part) * BLOCK
+        else:
+            offset = pl.multiple_of((block % per_part) * BLOCK, BLOCK)
+        return ref.at[block // per_part, which, pl.ds(offset, BLOCK), :]
 
     def softmax_grads(qb, ub, keys, values, mask):
         scores = _nt(qb, keys) * factor
@@ -49,13 +57,13 @@
         value_grad = _tn(rounded, ub)
         return query_grad, key_grad, value_grad
 
-    keys_all = k_ref[...]
-    values_all = v_ref[...]
-    for index, start in enumerate((0, length - BLOCK)):
-        qb = q_ref[start:start + BLOCK, :]
-        ub = u_ref[start:start + BLOCK, :]
+    keys_all = x_ref[:, 1, :, :].reshape(length, HD)
+    values_all = x_ref[:, 2, :, :].reshape(length, HD)
+    for index, block in enumerate((0, count - 1)):
+        qb = rows(x_ref, 0, block)[...]
+        ub = u_ref[block * BLOCK:(block + 1) * BLOCK, :]
         query_grad, key_grad, value_grad = softmax_grads(qb, ub, keys_all, values_all, None)
-        dq_ref[start:start + BLOCK, :] = query_grad.astype(jnp.bfloat16)
+        rows(o_ref, 0, block)[...] = query_grad.astype(jnp.bfloat16)
         if index == 0:
             dk_acc[...] = key_grad
             dv_acc[...] = value_grad
@@ -71,15 +79,14 @@
         upper = jnp.where(m + 1 <= count - 2, m + 1, m)
         ids = [0, count - 1, lower, m, upper] + [rb_ref[base + r] for r in range(RAND)]
         for slot, block in enumerate(ids):
-            row = pl.multiple_of(block * BLOCK, BLOCK)
-            kg_ref[slot * BLOCK:(slot + 1) * BLOCK, :] = k_ref[pl.ds(row, BLOCK), :]
-            vg_ref[slot * BLOCK:(slot + 1) * BLOCK, :] = v_ref[pl.ds(row, BLOCK), :]
+            kg_ref[slot * BLOCK:(slot + 1) * BLOCK, :] = rows(x_ref, 1, block)[...]
+            vg_ref[slot * BLOCK:(slot + 1) * BLOCK, :] = rows(x_ref, 2, block)[...]
         start = pl.multiple_of(m * BLOCK, BLOCK)
-        qb = q_ref[pl.ds(start, BLOCK), :]
+        qb = rows(x_ref, 0, m)[...]
         ub = u_ref[pl.ds(start, BLOCK), :]
         mask = ((columns == 2) & (m == 1)) | ((columns == 4) & (m == count - 2))
         query_grad, key_grad, value_grad = softmax_grads(qb, ub, kg_ref[...], vg_ref[...], mask)
-        dq_ref[pl.ds(start, BLOCK), :] = query_grad.astype(jnp.bfloat16)
+        rows(o_ref, 0, m)[...] = query_grad.astype(jnp.bfloat16)
         for slot, block in enumerate(ids):
             row = pl.multiple_of(block * BLOCK, BLOCK)
             dk_acc[pl.ds(row, BLOCK), :] += key_grad[slot * BLOCK:(slot + 1) * BLOCK, :]
@@ -87,22 +94,23 @@
         return carry
 
     lax.fori_loop(1, count - 1, mid_step, 0)
-    dk_ref[...] = dk_acc[...].astype(jnp.bfloat16)
-    dv_ref[...] = dv_acc[...].astype(jnp.bfloat16)
+    o_ref[:, 1, :, :] = dk_acc[...].reshape(parts, tokens, HD).astype(jnp.bfloat16)
+    o_ref[:, 2, :, :] = dv_acc[...].reshape(parts, tokens, HD).astype(jnp.bfloat16)
 
 
-def attention_grads(stacked, upstream, random_ids):
-    length = stacked.shape[0]
+def attention_grads(stacked, upstream, head, random_ids):
+    parts, _, tokens, _ = stacked.shape
+    length = parts * tokens
     count = length // BLOCK
-    spec = pl.BlockSpec((length, HD), lambda h, rb: (0, h))
-    whole = pl.BlockSpec((length, 3 * HD), lambda h, rb: (0, 0))
-    out = jax.ShapeDtypeStruct((length, 3 * HD), jnp.bfloat16)
+    whole = pl.BlockSpec((parts, 3, tokens, HD), lambda h, rb: (0, 0, 0, 0))
+    spec = pl.BlockSpec((length, HD), lambda h, rb: (0, head))
+    out = jax.ShapeDtypeStruct((parts, 3, tokens, HD), jnp.bfloat16)
     pairs = 2 * BLOCK * length + (count - 2) * BLOCK * SLOTS * BLOCK
     cost = pl.CostEstimate(
         flops=12 * pairs * HD, transcendentals=pairs, bytes_accessed=14 * length * HD
     )
     return pl.pallas_call(
-        functools.partial(_attention_kernel, length=length),
+        _attention_kernel,
         out_shape=out,
         grid_spec=pltpu.PrefetchScalarGridSpec(
             num_scalar_prefetch=1,
@@ -135,6 +143,10 @@
     if strided:
         head_weight = lax.all_gather(out_weight, "dp", axis=0, tiled=True)
         full_cotangent = lax.all_gather(local_cotangent, "context", axis=0, tiled=True)
+        upstream = lax.dot_general(
+            full_cotangent, head_weight, (((1,), (1,)), ((), ())),
+            preferred_element_type=jnp.float32,
+        ).astype(jnp.bfloat16)
 
         def chunk(array, c):
             return array.reshape(tokens, dp, ctx, HD)[:, c]
@@ -152,24 +164,19 @@
 
     pieces = []
     for c in range(local_heads):
-        stacked = jnp.stack([chunk(array, c) for array in local], axis=1)
-        moved = lax.all_to_all(stacked, "context", split_axis=2, concat_axis=0, tiled=True)
-        moved = moved.reshape(tokens * ctx, len(local) * HD)
+        stacked = jnp.stack([chunk(array, c).transpose(1, 0, 2) for array in local], axis=1)
+        moved = lax.all_to_all(stacked, "context", split_axis=0, concat_axis=0, tiled=True)
         if strided:
-            head_upstream = lax.dot_general(
-                full_cotangent, head_weight[c * HD:(c + 1) * HD], (((1,), (1,)), ((), ())),
-                preferred_element_type=jnp.float32,
-            ).astype(jnp.bfloat16)
+            grads = attention_grads(moved, upstream, c, random_blocks[0])
         else:
-            head_upstream = moved[:, 3 * HD:]
-        grads = attention_grads(moved[:, :3 * HD], head_upstream, random_blocks[0])
-        grads = grads.reshape(tokens * ctx, 3, 1, HD)
-        pieces.append(lax.all_to_all(grads, "context", split_axis=0, concat_axis=2, tiled=True))
+            head_upstream = moved[:, 3].reshape(tokens * ctx, HD)
+            grads = attention_grads(moved[:, :3], head_upstream, 0, random_blocks[0])
+        back = lax.all_to_all(grads, "context", split_axis=0, concat_axis=0, tiled=True)
+        pieces.append(back.transpose(1, 2, 0, 3))
 
     outs = []
     for g in range(3):
-        parts = [piece[:, g] for piece in pieces]
-        joined = jnp.stack(parts, axis=1 if strided else 2)
+        joined = jnp.stack([piece[g] for piece in pieces], axis=1 if strided else 2)
         outs.append(joined.reshape(1, tokens, width))
     return tuple(outs)
 

time: 265 us -> 221 us (0.83)
  local copies, waits for them, and re-layouts: 49.3 us -> 19.2 us
  matrix products: 17.1 us -> 6.2 us
  other arithmetic: 8.86 us -> 5.37 us
    reshape x11 -> x0, local copies, waits for them, and re-layouts: 15.1 us -> none  [the longest x4 6.61 us: body(): grads = grads.reshape(tokens * ctx, 3, 1, HD)]
    dot_general x4 -> x1, matrix products: 17.1 us -> 6.2 us  [body(): lax.dot_general(full_cotangent, head_weight, (((1,), (1,)), ((), ())), pr...]
    slice x4 -> x0, local copies, waits for them, and re-layouts: 9.56 us -> none  [body(): parts = [piece[:, g] for piece in pieces]]
    pallas_call x4 -> x0, local copies, waits for them, and re-layouts: 6.5 us -> none  [attention_grads(): pl.pallas_call(functools.partial(_attention_kernel, length=length), out_s...]
    another operation x7 -> x6, other arithmetic: 8.86 us -> 5.37 us  [the longest x4 3.87 us: body(): jnp.stack([chunk(array, c).transpose(1, 0, 2) for array in local], axis=1)]
    unnamed x38 -> x53, local copies, waits for them, and re-layouts: 8.09 us -> 10.1 us
  transfers between devices with their start and end apart: 10 -> 10, of which waited for: 5 -> 5; matrix products, arithmetic and copies ran while one was open for 22% -> 10% of each run, Pallas kernels for 25% -> 30%
where the time goes in v2:
time: 221 us; the launch traced here: 220 us
  waiting for transfers between devices  76.2 us (34%)
  Pallas kernels  65.6 us (30%)
  starting transfers between devices  32.8 us (15%)
  local copies, waits for them, and re-layouts  19.2 us (9%)
  between operations  14.4 us (7%)
  matrix products  6.2 us (3%)
  other arithmetic  5.37 us (2%)
    pallas_call x4, Pallas kernels, attention_grads(): pl.pallas_call(_attention_kernel, out_shape=out, grid_spec=pltpu.Prefetch...  65.6 us
    all_gather x1, waiting for transfers between devices, body(): lax.all_gather(local_cotangent, 'context', axis=0, tiled=True)  32.5 us
    all_to_all x4, waiting for transfers between devices, body(): lax.all_to_all(stacked, 'context', split_axis=0, concat_axis=0, tiled=True)  32.3 us
    all_to_all x4, starting transfers between devices, body(): lax.all_to_all(stacked, 'context', split_axis=0, concat_axis=0, tiled=True)  16.5 us
    all_to_all x4, starting transfers between devices, body(): lax.all_to_all(grads, 'context', split_axis=0, concat_axis=0, tiled=True)  16.2 us
    unnamed x53, local copies, waits for them, and re-layouts  10.1 us
    all_to_all x4, waiting for transfers between devices, body(): lax.all_to_all(grads, 'context', split_axis=0, concat_axis=0, tiled=True)  9.99 us
    dot_general x1, matrix products, body(): lax.dot_general(full_cotangent, head_weight, (((1,), (1,)), ((), ())), pr...  6.2 us
  transfers between devices with their start and end apart: 10, of which 5 were waited for; matrix products, arithmetic and copies ran while one was open for 10% of the time, Pallas kernels for 30%

profile of v2, /device:TPU:0, one launch (start us, length us, event | category | flops | bytes accessed | tf_op | source)
XLA Modules:
  0.0 219.8 jit_solution(12582818503415199513)
XLA Ops:
  7.2 0.7 all-gather.4.cloned.1.call-update
  7.9 0.7 all-gather.6.cloned.1.call-update
  8.7 1.7 copy.48
  10.4 1.0 fusion.5
  11.6 0.7 copy.50
  12.2 0.9 fusion.6
  13.3 0.7 copy.52
  14.1 0.2 copy.76
  14.3 1.0 pad_maximum_fusion.3
  15.3 5.2 %all-to-all-start = ((bf16[8,3,128,128]{3,2,1,0:T(8,128)(2,1)}), bf16[8,3,128,128]{3,2,1,0:T(8,128)(2,1)S(1)}, u32[]{:S(2)}, u32[]{:S(2)}) async-start(bf16[8,3,128,128]{3,2,1,0:T(8,128)(2,1)} %pad_maximum_fusion.3), calls=%async_computation | async-start | bytes 1572864 | tf_op jit(solution)/shard_map/all_to_all | solution.py:168
  20.5 0.2 copy.80
  20.7 0.2 copy.81
  20.9 0.2 copy.82
  21.0 1.0 pad_maximum_fusion.5
  22.0 11.0 %all-to-all-done.x_ref = bf16[8,3,128,128]{3,2,1,0:T(8,128)(2,1)S(1)} async-done(((bf16[8,3,128,128]{3,2,1,0:T(8,128)(2,1)}), bf16[8,3,128,128]{3,2,1,0:T(8,128)(2,1)S(1)}, u32[]{:S(2)}, u32[]{:S(2)}) %all-to-all-start) | async-done | bytes 786464 | tf_op jit(solution)/shard_map/all_to_all | solution.py:168
  33.1 4.2 %all-to-all-start.4 = ((bf16[8,3,128,128]{3,2,1,0:T(8,128)(2,1)}), bf16[8,3,128,128]{3,2,1,0:T(8,128)(2,1)}, u32[]{:S(2)}, u32[]{:S(2)}) async-start(bf16[8,3,128,128]{3,2,1,0:T(8,128)(2,1)} %pad_maximum_fusion.5), calls=%async_computation.4 | async-start | bytes 1572864 | tf_op jit(solution)/shard_map/all_to_all | solution.py:168
  37.9 1.0 pad_maximum_fusion.4
  38.9 11.0 %all-to-all-done.4.x_ref = bf16[8,3,128,128]{3,2,1,0:T(8,128)(2,1)} async-done(((bf16[8,3,128,128]{3,2,1,0:T(8,128)(2,1)}), bf16[8,3,128,128]{3,2,1,0:T(8,128)(2,1)}, u32[]{:S(2)}, u32[]{:S(2)}) %all-to-all-start.4) | async-done | bytes 786464 | tf_op jit(solution)/shard_map/all_to_all | solution.py:168
  49.9 3.5 %all-to-all-start.2 = ((bf16[8,3,128,128]{3,2,1,0:T(8,128)(2,1)}), bf16[8,3,128,128]{3,2,1,0:T(8,128)(2,1)S(1)}, u32[]{:S(2)}, u32[]{:S(2)}) async-start(bf16[8,3,128,128]{3,2,1,0:T(8,128)(2,1)} %pad_maximum_fusion.4), calls=%async_computation.2 | async-start | bytes 1572864 | tf_op jit(solution)/shard_map/all_to_all | solution.py:168
  53.5 0.7 reshape_squeeze.8.rb_ref
  54.6 0.2 copy.85
  54.8 1.0 pad_maximum_fusion.6
  55.7 10.2 %all-to-all-done.2.x_ref = bf16[8,3,128,128]{3,2,1,0:T(8,128)(2,1)S(1)} async-done(((bf16[8,3,128,128]{3,2,1,0:T(8,128)(2,1)}), bf16[8,3,128,128]{3,2,1,0:T(8,128)(2,1)S(1)}, u32[]{:S(2)}, u32[]{:S(2)}) %all-to-all-start.2) | async-done | bytes 786464 | tf_op jit(solution)/shard_map/all_to_all | solution.py:168
  66.0 3.5 %all-to-all-start.6 = ((bf16[8,3,128,128]{3,2,1,0:T(8,128)(2,1)}), bf16[8,3,128,128]{3,2,1,0:T(8,128)(2,1)S(1)}, u32[]{:S(2)}, u32[]{:S(2)}) async-start(bf16[8,3,128,128]{3,2,1,0:T(8,128)(2,1)} %pad_maximum_fusion.6), calls=%async_computation.6 | async-start | bytes 1572864 | tf_op jit(solution)/shard_map/all_to_all | solution.py:168
  69.6 32.5 %all-gather.6.cloned.1.call-done = bf16[1,1024,2048]{2,1,0:T(8,128)(2,1)} async-done(((bf16[1,128,2048]{2,1,0:T(8,128)(2,1)}), bf16[1,1024,2048]{2,1,0:T(8,128)(2,1)}) %all-gather.6.cloned.1.call-update) | async-done | bytes 4194320 | tf_op jit(solution)/shard_map/all_gather | solution.py:145
  102.1 6.2 %fusion.2.u_ref = bf16[1024,512]{1,0:T(8,128)(2,1)} fusion(bf16[512,2048]{1,0:T(8,128)(2,1)} %all-gather.4.cloned.1.call-done, bf16[1,1024,2048]{2,1,0:T(8,128)(2,1)} %all-gather.6.cloned.1.call-done), kind=kOutput, calls=%fused_computation.2 | convolution fusion | flops 2148007936 | bytes 7340032 | tf_op jit(solution)/shard_map/dot_general | solution.py:146
  108.3 16.4 %shard_map.85 = bf16[8,3,128,128]{3,2,1,0:T(8,128)(2,1)} custom-call(s32[42]{0:T(128)} %reshape_squeeze.8.rb_ref, bf16[8,3,128,128]{3,2,1,0:T(8,128)(2,1)} %copy-done.13, bf16[1024,512]{1,0:T(8,128)(2,1)} %fusion.2.u_ref), custom_call_target="tpu_custom_call" | custom-call | flops 905969664 | bytes 1835008 | tf_op jit(solution)/shard_map/pallas_call | solution.py:112
  124.7 0.9 copy-done.15
  125.5 3.5 %all-to-all-start.1 = ((bf16[8,3,128,128]{3,2,1,0:T(8,128)(2,1)}), bf16[8,3,128,128]{3,2,1,0:T(8,128)(2,1)S(1)}, u32[]{:S(2)}, u32[]{:S(2)}) async-start(bf16[8,3,128,128]{3,2,1,0:T(8,128)(2,1)} %shard_map.85), calls=%async_computation.1 | async-start | bytes 1572864 | tf_op jit(solution)/shard_map/all_to_all | solution.py:174
  129.1 16.4 %shard_map.87 = bf16[8,3,128,128]{3,2,1,0:T(8,128)(2,1)} custom-call(s32[42]{0:T(128)} %reshape_squeeze.8.rb_ref, bf16[8,3,128,128]{3,2,1,0:T(8,128)(2,1)} %all-to-all-done.4.x_ref, bf16[1024,512]{1,0:T(8,128)(2,1)} %fusion.2.u_ref), custom_call_target="tpu_custom_call" | custom-call | flops 905969664 | bytes 1835008 | tf_op jit(solution)/shard_map/pallas_call | solution.py:112
  145.5 4.1 %all-to-all-start.5 = ((bf16[8,3,128,128]{3,2,1,0:T(8,128)(2,1)}), bf16[8,3,128,128]{3,2,1,0:T(8,128)(2,1)S(1)}, u32[]{:S(2)}, u32[]{:S(2)}) async-start(bf16[8,3,128,128]{3,2,1,0:T(8,128)(2,1)} %shard_map.87), calls=%async_computation.5 | async-start | bytes 1572864 | tf_op jit(solution)/shard_map/all_to_all | solution.py:174
  149.6 16.4 %shard_map.86 = bf16[8,3,128,128]{3,2,1,0:T(8,128)(2,1)} custom-call(s32[42]{0:T(128)} %reshape_squeeze.8.rb_ref, bf16[8,3,128,128]{3,2,1,0:T(8,128)(2,1)} %copy-done.14, bf16[1024,512]{1,0:T(8,128)(2,1)} %fusion.2.u_ref), custom_call_target="tpu_custom_call" | custom-call | flops 905969664 | bytes 1835008 | tf_op jit(solution)/shard_map/pallas_call | solution.py:112
  166.0 4.2 %all-to-all-start.3 = ((bf16[8,3,128,128]{3,2,1,0:T(8,128)(2,1)}), bf16[8,3,128,128]{3,2,1,0:T(8,128)(2,1)S(1)}, u32[]{:S(2)}, u32[]{:S(2)}) async-start(bf16[8,3,128,128]{3,2,1,0:T(8,128)(2,1)} %shard_map.86), calls=%async_computation.3 | async-start | bytes 1572864 | tf_op jit(solution)/shard_map/all_to_all | solution.py:174
  170.2 16.4 %shard_map.88 = bf16[8,3,128,128]{3,2,1,0:T(8,128)(2,1)} custom-call(s32[42]{0:T(128)} %reshape_squeeze.8.rb_ref, bf16[8,3,128,128]{3,2,1,0:T(8,128)(2,1)} %copy-done.15, bf16[1024,512]{1,0:T(8,128)(2,1)} %fusion.2.u_ref), custom_call_target="tpu_custom_call" | custom-call | flops 905969664 | bytes 1835008 | tf_op jit(solution)/shard_map/pallas_call | solution.py:112
  186.6 0.9 copy.93
  187.6 4.3 %all-to-all-start.7 = ((bf16[8,3,128,128]{3,2,1,0:T(8,128)(2,1)}), bf16[8,3,128,128]{3,2,1,0:T(8,128)(2,1)S(1)}, u32[]{:S(2)}, u32[]{:S(2)}) async-start(bf16[8,3,128,128]{3,2,1,0:T(8,128)(2,1)} %shard_map.88), calls=%async_computation.7 | async-start | bytes 1572864 | tf_op jit(solution)/shard_map/all_to_all | solution.py:174
  192.0 0.8 slice_bitcast_fusion.3
  192.8 0.9 slice_bitcast_fusion.1
  193.7 0.9 slice_bitcast_fusion.2
  194.6 10.0 %all-to-all-done.7 = bf16[8,3,128,128]{3,2,1,0:T(8,128)(2,1)S(1)} async-done(((bf16[8,3,128,128]{3,2,1,0:T(8,128)(2,1)}), bf16[8,3,128,128]{3,2,1,0:T(8,128)(2,1)S(1)}, u32[]{:S(2)}, u32[]{:S(2)}) %all-to-all-start.7) | async-done | bytes 786464 | tf_op jit(solution)/shard_map/all_to_all | solution.py:174
  204.6 0.8 slice_bitcast_fusion
  205.6 0.7 copy.70
  206.3 1.3 copy.73
  207.6 1.4 pad_maximum_fusion
  209.0 0.7 copy.67
  209.6 1.3 copy.71
  211.0 0.7 copy.69
  211.6 1.3 copy.72
  (52 shorter events, 1.9 us)
Async XLA Ops:
  7.2 62.4 %all-gather.4.cloned.1.call-start = ((), (), s32[]{:S(2)}) async-start(), calls=%async_computation.8 | async-start | bytes 2621440 | tf_op jit(solution)/shard_map/all_gather | solution.py:144
  7.9 94.2 %all-gather.6.cloned.1.call-start = ((), (), s32[]{:S(2)}) async-start(), calls=%async_computation.9 | async-start | bytes 4718592 | tf_op jit(solution)/shard_map/all_gather | solution.py:145
  8.6 2.9 %copy-start.1 = (bf16[1,128,4096]{2,1,0:T(8,128)(2,1)S(1)}, bf16[1,128,4096]{2,1,0:T(8,128)(2,1)}, u32[]{:S(2)}) copy-start(bf16[1,128,4096]{2,1,0:T(8,128)(2,1)} %param.7) | copy-start | bytes 3145732
  11.5 1.8 copy-start.2
  14.1 6.3 %copy-start.11 = (bf16[128,1,8,128]{0,3,2,1:T(8,128)(2,1)S(1)}, bf16[128,1,8,128]{0,3,2,1:T(8,128)(2,1)}, u32[]{:S(2)}) copy-start(bf16[128,1,8,128]{0,3,2,1:T(8,128)(2,1)} %get-tuple-element.10) | copy-start | bytes 786436
  14.1 6.5 %copy-start.12 = (bf16[128,1,8,128]{0,3,2,1:T(8,128)(2,1)S(1)}, bf16[128,1,8,128]{0,3,2,1:T(8,128)(2,1)}, u32[]{:S(2)}) copy-start(bf16[128,1,8,128]{0,3,2,1:T(8,128)(2,1)} %get-tuple-element.14) | copy-start | bytes 786436
  15.3 17.8 %all-to-all-start = ((bf16[8,3,128,128]{3,2,1,0:T(8,128)(2,1)}), bf16[8,3,128,128]{3,2,1,0:T(8,128)(2,1)S(1)}, u32[]{:S(2)}, u32[]{:S(2)}) async-start(bf16[8,3,128,128]{3,2,1,0:T(8,128)(2,1)} %pad_maximum_fusion.3), calls=%async_computation | async-start | bytes 1572864 | tf_op jit(solution)/shard_map/all_to_all | solution.py:168
  20.7 16.6 %copy-start.9 = (bf16[128,1,8,128]{0,3,2,1:T(8,128)(2,1)S(1)}, bf16[128,1,8,128]{0,3,2,1:T(8,128)(2,1)}, u32[]{:S(2)}) copy-start(bf16[128,1,8,128]{0,3,2,1:T(8,128)(2,1)} %get-tuple-element.11) | copy-start | bytes 786436
  20.9 16.6 %copy-start.10 = (bf16[128,1,8,128]{0,3,2,1:T(8,128)(2,1)S(1)}, bf16[128,1,8,128]{0,3,2,1:T(8,128)(2,1)}, u32[]{:S(2)}) copy-start(bf16[128,1,8,128]{0,3,2,1:T(8,128)(2,1)} %get-tuple-element.15) | copy-start | bytes 786436
  33.1 5.8 %copy-start.13 = (bf16[8,3,128,128]{3,2,1,0:T(8,128)(2,1)}, bf16[8,3,128,128]{3,2,1,0:T(8,128)(2,1)S(1)}, u32[]{:S(2)}) copy-start(bf16[8,3,128,128]{3,2,1,0:T(8,128)(2,1)S(1)} %all-to-all-done.x_ref) | copy-start | bytes 2359300
  33.1 16.8 %all-to-all-start.4 = ((bf16[8,3,128,128]{3,2,1,0:T(8,128)(2,1)}), bf16[8,3,128,128]{3,2,1,0:T(8,128)(2,1)}, u32[]{:S(2)}, u32[]{:S(2)}) async-start(bf16[8,3,128,128]{3,2,1,0:T(8,128)(2,1)} %pad_maximum_fusion.5), calls=%async_computation.4 | async-start | bytes 1572864 | tf_op jit(solution)/shard_map/all_to_all | solution.py:168
  37.5 16.0 %copy-start.16 = (s32[1,14,3]{1,0,2:T(1,128)S(1)}, s32[1,14,3]{1,0,2:T(1,128)}, u32[]{:S(2)}) copy-start(s32[1,14,3]{1,0,2:T(1,128)} %param.11) | copy-start | bytes 508
  37.5 16.7 %copy-start.7 = (bf16[128,1,8,128]{0,3,2,1:T(8,128)(2,1)S(1)}, bf16[128,1,8,128]{0,3,2,1:T(8,128)(2,1)}, u32[]{:S(2)}) copy-start(bf16[128,1,8,128]{0,3,2,1:T(8,128)(2,1)} %get-tuple-element.12) | copy-start | bytes 786436
  37.7 16.7 %copy-start.8 = (bf16[128,1,8,128]{0,3,2,1:T(8,128)(2,1)S(1)}, bf16[128,1,8,128]{0,3,2,1:T(8,128)(2,1)}, u32[]{:S(2)}) copy-start(bf16[128,1,8,128]{0,3,2,1:T(8,128)(2,1)} %get-tuple-element.16) | copy-start | bytes 786436
  49.9 16.1 %all-to-all-start.2 = ((bf16[8,3,128,128]{3,2,1,0:T(8,128)(2,1)}), bf16[8,3,128,128]{3,2,1,0:T(8,128)(2,1)S(1)}, u32[]{:S(2)}, u32[]{:S(2)}) async-start(bf16[8,3,128,128]{3,2,1,0:T(8,128)(2,1)} %pad_maximum_fusion.4), calls=%async_computation.2 | async-start | bytes 1572864 | tf_op jit(solution)/shard_map/all_to_all | solution.py:168
  66.0 42.3 %copy-start.14 = (bf16[8,3,128,128]{3,2,1,0:T(8,128)(2,1)}, bf16[8,3,128,128]{3,2,1,0:T(8,128)(2,1)S(1)}, u32[]{:S(2)}) copy-start(bf16[8,3,128,128]{3,2,1,0:T(8,128)(2,1)S(1)} %all-to-all-done.2.x_ref) | copy-start | bytes 2359300
  66.0 58.7 %all-to-all-start.6 = ((bf16[8,3,128,128]{3,2,1,0:T(8,128)(2,1)}), bf16[8,3,128,128]{3,2,1,0:T(8,128)(2,1)S(1)}, u32[]{:S(2)}, u32[]{:S(2)}) async-start(bf16[8,3,128,128]{3,2,1,0:T(8,128)(2,1)} %pad_maximum_fusion.6), calls=%async_computation.6 | async-start | bytes 1572864 | tf_op jit(solution)/shard_map/all_to_all | solution.py:168
  124.7 0.9 copy-start.15
  125.5 19.9 %all-to-all-start.1 = ((bf16[8,3,128,128]{3,2,1,0:T(8,128)(2,1)}), bf16[8,3,128,128]{3,2,1,0:T(8,128)(2,1)S(1)}, u32[]{:S(2)}, u32[]{:S(2)}) async-start(bf16[8,3,128,128]{3,2,1,0:T(8,128)(2,1)} %shard_map.85), calls=%async_computation.1 | async-start | bytes 1572864 | tf_op jit(solution)/shard_map/all_to_all | solution.py:174
  145.5 20.5 %all-to-all-start.5 = ((bf16[8,3,128,128]{3,2,1,0:T(8,128)(2,1)}), bf16[8,3,128,128]{3,2,1,0:T(8,128)(2,1)S(1)}, u32[]{:S(2)}, u32[]{:S(2)}) async-start(bf16[8,3,128,128]{3,2,1,0:T(8,128)(2,1)} %shard_map.87), calls=%async_computation.5 | async-start | bytes 1572864 | tf_op jit(solution)/shard_map/all_to_all | solution.py:174
  166.0 21.6 %all-to-all-start.3 = ((bf16[8,3,128,128]{3,2,1,0:T(8,128)(2,1)}), bf16[8,3,128,128]{3,2,1,0:T(8,128)(2,1)S(1)}, u32[]{:S(2)}, u32[]{:S(2)}) async-start(bf16[8,3,128,128]{3,2,1,0:T(8,128)(2,1)} %shard_map.86), calls=%async_computation.3 | async-start | bytes 1572864 | tf_op jit(solution)/shard_map/all_to_all | solution.py:174
  187.6 4.4 %copy-start = (bf16[8,3,128,128]{3,2,0,1:T(8,128)(2,1)S(1)}, bf16[8,3,128,128]{3,2,0,1:T(8,128)(2,1)}, u32[]{:S(2)}) copy-start(bf16[8,3,128,128]{3,2,0,1:T(8,128)(2,1)} %copy.93) | copy-start | bytes 2359300
  187.6 16.9 %all-to-all-start.7 = ((bf16[8,3,128,128]{3,2,1,0:T(8,128)(2,1)}), bf16[8,3,128,128]{3,2,1,0:T(8,128)(2,1)S(1)}, u32[]{:S(2)}, u32[]{:S(2)}) async-start(bf16[8,3,128,128]{3,2,1,0:T(8,128)(2,1)} %shard_map.88), calls=%async_computation.7 | async-start | bytes 1572864 | tf_op jit(solution)/shard_map/all_to_all | solution.py:174
  206.2 1.4 copy-start.3
  206.2 1.3 copy-start.4
  206.2 1.3 copy-start.5
  206.3 1.3 copy-start.6
Sparse Core Ops, SparseCore 0:
  9.6 48.6 all-gather.3
  60.1 41.8 all-gather.5

commit v3 on v2

--- a/solution.py
+++ b/solution.py
@@ -93,7 +93,7 @@
             dv_acc[pl.ds(row, BLOCK), :] += value_grad[slot * BLOCK:(slot + 1) * BLOCK, :]
         return carry
 
-    lax.fori_loop(1, count - 1, mid_step, 0)
+    lax.fori_loop(1, count - 1, mid_step, 0, unroll=2)
     o_ref[:, 1, :, :] = dk_acc[...].reshape(parts, tokens, HD).astype(jnp.bfloat16)
     o_ref[:, 2, :, :] = dv_acc[...].reshape(parts, tokens, HD).astype(jnp.bfloat16)
 
@@ -138,15 +138,35 @@
     total_heads = width // HD
     local_heads = total_heads // ctx
     rows_per_device = out_weight.shape[0]
-    strided = rows_per_device == HD and local_heads == dp
+    strided = rows_per_device == HD and local_heads == dp and ctx % 2 == 0
 
     if strided:
-        head_weight = lax.all_gather(out_weight, "dp", axis=0, tiled=True)
-        full_cotangent = lax.all_gather(local_cotangent, "context", axis=0, tiled=True)
+        me = lax.axis_index("dp")
+        got = [out_weight] + [
+            lax.ppermute(out_weight, "dp", [(a, (a + s) % dp) for a in range(dp)])
+            for s in range(1, dp)
+        ]
+        order = (me - jnp.arange(dp)) % dp
+        head_weight = jnp.take(jnp.stack(got), order, axis=0).reshape(dp * HD, -1)
+        j = lax.axis_index("context")
+        shifts = list(range(0, ctx, 2))
+        mine = jnp.stack([local_cotangent] + [
+            lax.ppermute(local_cotangent, "context", [(a, (a + s) % ctx) for a in range(ctx)])
+            for s in shifts[1:]
+        ])
+        other = lax.ppermute(mine, "context", [(a, a ^ 1) for a in range(ctx)])
+        gathered = jnp.concatenate([mine, other]).reshape(ctx * tokens, -1)
         upstream = lax.dot_general(
-            full_cotangent, head_weight, (((1,), (1,)), ((), ())),
+            gathered, head_weight, (((1,), (1,)), ((), ())),
             preferred_element_type=jnp.float32,
         ).astype(jnp.bfloat16)
+        source = jnp.arange(ctx)
+        same = source % 2 == j % 2
+        position = jnp.where(
+            same, ((j - source) % ctx) // 2, ctx // 2 + (((j ^ 1) - source) % ctx) // 2
+        )
+        upstream = jnp.take(upstream.reshape(ctx, tokens, -1), position, axis=0)
+        upstream = upstream.reshape(ctx * tokens, -1)
 
         def chunk(array, c):
             return array.reshape(tokens, dp, ctx, HD)[:, c]

time: 221 us -> 190 us (0.86)
  waiting for transfers between devices: 76.2 us -> 27.9 us
  local copies, waits for them, and re-layouts: 19.2 us -> 37.3 us
  between operations: 14.4 us -> 1.03 us
  starting transfers between devices: 32.8 us -> 45.3 us
  other arithmetic: 5.37 us -> 11.9 us
  Pallas kernels: 65.6 us -> 61.1 us
    all_gather x2 -> x0, waiting for transfers between devices: 32.5 us -> none  [the longest x1 32.5 us: body(): lax.all_gather(local_cotangent, 'context', axis=0, tiled=True)]
    all_to_all x4, waiting for transfers between devices: 32.3 us -> 8.59 us  [body(): lax.all_to_all(stacked, 'context', split_axis=0, concat_axis=0, tiled=True)]
    ppermute x0 -> x7, starting transfers between devices: none -> 11.5 us  [the longest x3 5.94 us: body(): lax.ppermute(local_cotangent, 'context', [(a, (a + s) % ctx) for a in ran...]
    unnamed x53 -> x57, local copies, waits for them, and re-layouts: 10.1 us -> 21.4 us
    ppermute x0 -> x7, waiting for transfers between devices: none -> 9.29 us  [the longest x3 9.28 us: body(): lax.ppermute(out_weight, 'dp', [(a, (a + s) % dp) for a in range(dp)])]
    pallas_call x4, Pallas kernels: 65.6 us -> 61.1 us  [attention_grads(): pl.pallas_call(_attention_kernel, out_shape=out, grid_spec=pltpu.Prefetch...]
    another operation x0 -> x2, other arithmetic: none -> 3.44 us  [the longest x1 1.78 us: body(): head_weight = jnp.take(jnp.stack(got), order, axis=0).reshape(dp * HD, -1)]
    concatenate x0 -> x1, local copies, waits for them, and re-layouts: none -> 3.18 us  [body(): gathered = jnp.concatenate([mine, other]).reshape(ctx * tokens, -1)]
  transfers between devices with their start and end apart: 10 -> 15, of which waited for: 5 -> 3; matrix products, arithmetic and copies ran while one was open for 10% -> 24% of each run, Pallas kernels for 30% -> 32%
where the time goes in v3:
time: 190 us; the launch traced here: 189 us
  Pallas kernels  61.1 us (32%)
  starting transfers between devices  45.3 us (24%)
  local copies, waits for them, and re-layouts  37.3 us (20%)
  waiting for transfers between devices  27.9 us (15%)
  other arithmetic  11.9 us (6%)
  matrix products  4.55 us (2%)
    pallas_call x4, Pallas kernels, attention_grads(): pl.pallas_call(_attention_kernel, out_shape=out, grid_spec=pltpu.Prefetch...  61.1 us
    unnamed x57, local copies, waits for them, and re-layouts  21.4 us
    all_to_all x4, starting transfers between devices, body(): lax.all_to_all(stacked, 'context', split_axis=0, concat_axis=0, tiled=True)  16.9 us
    all_to_all x4, starting transfers between devices, body(): lax.all_to_all(grads, 'context', split_axis=0, concat_axis=0, tiled=True)  16.8 us
    all_to_all x4, waiting for transfers between devices, body(): lax.all_to_all(grads, 'context', split_axis=0, concat_axis=0, tiled=True)  10 us
    ppermute x3, waiting for transfers between devices, body(): lax.ppermute(out_weight, 'dp', [(a, (a + s) % dp) for a in range(dp)])  9.28 us
    all_to_all x4, waiting for transfers between devices, body(): lax.all_to_all(stacked, 'context', split_axis=0, concat_axis=0, tiled=True)  8.59 us
    ppermute x3, starting transfers between devices, body(): lax.ppermute(local_cotangent, 'context', [(a, (a + s) % ctx) for a in ran...  5.94 us
  transfers between devices with their start and end apart: 15, of which 3 were waited for; matrix products, arithmetic and copies ran while one was open for 24% of the time, Pallas kernels for 32%

profile of v3, /device:TPU:0, one launch (start us, length us, event | category | flops | bytes accessed | tf_op | source)
XLA Modules:
  0.0 189.0 jit_solution(11157056746898387572)
XLA Ops:
  0.6 3.0 %collective-permute-start = (bf16[128,2048]{1,0:T(8,128)(2,1)}, bf16[128,2048]{1,0:T(8,128)(2,1)S(1)}, u32[]{:S(2)}, u32[]{:S(2)}) collective-permute-start(bf16[128,2048]{1,0:T(8,128)(2,1)} %bitcast.139), channel_id=1, source_target_pairs={{0,2},{1,3},{2,4},{3,5},{4,6},{5,7},{6,0},{7,1},{8,10},{9,11},{10,... | collective-permute-start | bytes 1572872 | tf_op jit(solution)/shard_map/ppermute | solution.py:154
  3.6 1.5 collective-permute-start.1
  5.1 1.4 collective-permute-start.2
  6.6 1.6 collective-permute-start.4
  8.2 2.6 %collective-permute-start.5 = (bf16[128,2048]{1,0:T(8,128)(2,1)}, bf16[128,2048]{1,0:T(8,128)(2,1)}, u32[]{:S(2)}, u32[]{:S(2)}) collective-permute-start(bf16[128,2048]{1,0:T(8,128)(2,1)} %param.10), channel_id=1, source_target_pairs={{0,16},{8,24},{16,0},{24,8},{1,17},{9,25},{17,1},{25,9},{2,18},{10... | collective-permute-start | bytes 1572872 | tf_op jit(solution)/shard_map/ppermute | solution.py:146
  10.7 1.6 copy.52
  13.4 1.6 copy.48
  15.1 1.0 fusion.8
  16.0 1.1 copy.74
  17.2 1.6 copy.50
  18.8 1.0 fusion.9
  19.8 1.2 copy.75
  21.0 1.0 pad_maximum_fusion.5
  22.0 4.3 %all-to-all-start = ((bf16[8,3,128,128]{3,2,1,0:T(8,128)(2,1)}), bf16[8,3,128,128]{3,2,1,0:T(8,128)(2,1)}, u32[]{:S(2)}, u32[]{:S(2)}) async-start(bf16[8,3,128,128]{3,2,1,0:T(8,128)(2,1)} %pad_maximum_fusion.5), calls=%async_computation | async-start | bytes 1572864 | tf_op jit(solution)/shard_map/all_to_all | solution.py:188
  28.4 1.1 copy.83
  29.5 1.8 copy.84
  31.3 1.8 copy.85
  33.1 1.0 pad_maximum_fusion.6
  34.1 1.0 pad_maximum_fusion.7
  35.0 1.0 pad_maximum_fusion.8
  36.9 1.4 collective-permute-start.6
  38.3 1.7 pad_maximum_fusion
  41.8 4.1 %all-to-all-start.2 = ((bf16[8,3,128,128]{3,2,1,0:T(8,128)(2,1)}), bf16[8,3,128,128]{3,2,1,0:T(8,128)(2,1)S(1)}, u32[]{:S(2)}, u32[]{:S(2)}) async-start(bf16[8,3,128,128]{3,2,1,0:T(8,128)(2,1)} %pad_maximum_fusion.6), calls=%async_computation.2 | async-start | bytes 1572864 | tf_op jit(solution)/shard_map/all_to_all | solution.py:188
  45.9 9.3 %collective-permute-done.6 = bf16[128,2048]{1,0:T(8,128)(2,1)S(1)} collective-permute-done((bf16[128,2048]{1,0:T(8,128)(2,1)S(1)}, bf16[128,2048]{1,0:T(8,128)(2,1)S(1)}, u32[]{:S(2)}, u32[]{:S(2)}) %collective-permute-start.6) | collective-permute-done | bytes 524320 | tf_op jit(solution)/shard_map/ppermute | solution.py:146
  56.0 1.8 pad_maximum_fusion.1
  57.8 2.0 %gather_fusion = bf16[4,128,2048]{2,1,0:T(8,128)(2,1)} fusion(bf16[4,128,2048]{2,1,0:T(8,128)(2,1)S(1)} %pad_maximum_fusion.1, s32[1024]{0:T(1024)S(1)} %pad_clamp_fusion.1), kind=kCustom, calls=%fused_computation | custom fusion | bytes 4194320 | tf_op jit(solution)/shard_map/jit(_take)/gather | solution.py:150
  59.8 1.9 broadcast_select_fusion
  61.6 4.2 %all-to-all-start.4 = ((bf16[8,3,128,128]{3,2,1,0:T(8,128)(2,1)}), bf16[8,3,128,128]{3,2,1,0:T(8,128)(2,1)}, u32[]{:S(2)}, u32[]{:S(2)}) async-start(bf16[8,3,128,128]{3,2,1,0:T(8,128)(2,1)} %pad_maximum_fusion.7), calls=%async_computation.4 | async-start | bytes 1572864 | tf_op jit(solution)/shard_map/all_to_all | solution.py:188
  66.7 3.2 %constant_dynamic-update-slice_fusion = bf16[8,128,2048]{2,1,0:T(8,128)(2,1)} fusion(bf16[8,128,2048]{2,1,0:T(8,128)(2,1)} %constant_dynamic-update-slice_fusion.1, bf16[4,128,2048]{2,1,0:T(8,128)(2,1)} %collective-permute-done.3), kind=kLoop, calls=%fused_computation.29 | loop fusion | bytes 4194304 | tf_op jit(solution)/shard_map/concatenate | solution.py:158
  69.9 8.6 %all-to-all-done.4.x_ref = bf16[8,3,128,128]{3,2,1,0:T(8,128)(2,1)} async-done(((bf16[8,3,128,128]{3,2,1,0:T(8,128)(2,1)}), bf16[8,3,128,128]{3,2,1,0:T(8,128)(2,1)}, u32[]{:S(2)}, u32[]{:S(2)}) %all-to-all-start.4) | async-done | bytes 786464 | tf_op jit(solution)/shard_map/all_to_all | solution.py:188
  78.5 4.2 %all-to-all-start.6 = ((bf16[8,3,128,128]{3,2,1,0:T(8,128)(2,1)}), bf16[8,3,128,128]{3,2,1,0:T(8,128)(2,1)}, u32[]{:S(2)}, u32[]{:S(2)}) async-start(bf16[8,3,128,128]{3,2,1,0:T(8,128)(2,1)} %pad_maximum_fusion.8), calls=%async_computation.6 | async-start | bytes 1572864 | tf_op jit(solution)/shard_map/all_to_all | solution.py:188
  82.7 4.5 %convolution_convert_fusion = bf16[1024,512]{1,0:T(8,128)(2,1)S(1)} fusion(bf16[1024,2048]{1,0:T(8,128)(2,1)} %bitcast.17, bf16[512,2048]{1,0:T(8,128)(2,1)S(1)} %bitcast.138), kind=kOutput, calls=%fused_computation.5 | convolution fusion | flops 2148007936 | bytes 7340032 | tf_op jit(solution)/shard_map/dot_general | solution.py:159
  87.9 1.2 bitcast_select_fusion.u_ref
  89.1 15.3 %shard_map.85 = bf16[8,3,128,128]{3,2,1,0:T(8,128)(2,1)} custom-call(s32[42]{0:T(128)} %reshape_squeeze.8.rb_ref, bf16[8,3,128,128]{3,2,1,0:T(8,128)(2,1)} %all-to-all-done.x_ref, bf16[1024,512]{1,0:T(8,128)(2,1)} %bitcast_select_fusion.u_ref), custom_call_target="tpu_custom_call" | custom-call | flops 905969664 | bytes 1835008 | tf_op jit(solution)/shard_map/pallas_call | solution.py:112
  104.4 4.1 %all-to-all-start.1 = ((bf16[8,3,128,128]{3,2,1,0:T(8,128)(2,1)}), bf16[8,3,128,128]{3,2,1,0:T(8,128)(2,1)S(1)}, u32[]{:S(2)}, u32[]{:S(2)}) async-start(bf16[8,3,128,128]{3,2,1,0:T(8,128)(2,1)} %shard_map.85), calls=%async_computation.1 | async-start | bytes 1572864 | tf_op jit(solution)/shard_map/all_to_all | solution.py:194
  108.5 15.3 %shard_map.86 = bf16[8,3,128,128]{3,2,1,0:T(8,128)(2,1)} custom-call(s32[42]{0:T(128)} %reshape_squeeze.8.rb_ref, bf16[8,3,128,128]{3,2,1,0:T(8,128)(2,1)} %copy-done.13, bf16[1024,512]{1,0:T(8,128)(2,1)} %bitcast_select_fusion.u_ref), custom_call_target="tpu_custom_call" | custom-call | flops 905969664 | bytes 1835008 | tf_op jit(solution)/shard_map/pallas_call | solution.py:112
  123.7 4.2 %all-to-all-start.3 = ((bf16[8,3,128,128]{3,2,1,0:T(8,128)(2,1)}), bf16[8,3,128,128]{3,2,1,0:T(8,128)(2,1)S(1)}, u32[]{:S(2)}, u32[]{:S(2)}) async-start(bf16[8,3,128,128]{3,2,1,0:T(8,128)(2,1)} %shard_map.86), calls=%async_computation.3 | async-start | bytes 1572864 | tf_op jit(solution)/shard_map/all_to_all | solution.py:194
  127.9 15.3 %shard_map.87 = bf16[8,3,128,128]{3,2,1,0:T(8,128)(2,1)} custom-call(s32[42]{0:T(128)} %reshape_squeeze.8.rb_ref, bf16[8,3,128,128]{3,2,1,0:T(8,128)(2,1)} %all-to-all-done.4.x_ref, bf16[1024,512]{1,0:T(8,128)(2,1)} %bitcast_select_fusion.u_ref), custom_call_target="tpu_custom_call" | custom-call | flops 905969664 | bytes 1835008 | tf_op jit(solution)/shard_map/pallas_call | solution.py:112
  143.2 4.2 %all-to-all-start.5 = ((bf16[8,3,128,128]{3,2,1,0:T(8,128)(2,1)}), bf16[8,3,128,128]{3,2,1,0:T(8,128)(2,1)S(1)}, u32[]{:S(2)}, u32[]{:S(2)}) async-start(bf16[8,3,128,128]{3,2,1,0:T(8,128)(2,1)} %shard_map.87), calls=%async_computation.5 | async-start | bytes 1572864 | tf_op jit(solution)/shard_map/all_to_all | solution.py:194
  147.4 15.3 %shard_map.88 = bf16[8,3,128,128]{3,2,1,0:T(8,128)(2,1)} custom-call(s32[42]{0:T(128)} %reshape_squeeze.8.rb_ref, bf16[8,3,128,128]{3,2,1,0:T(8,128)(2,1)} %all-to-all-done.6.x_ref, bf16[1024,512]{1,0:T(8,128)(2,1)} %bitcast_select_fusion.u_ref), custom_call_target="tpu_custom_call" | custom-call | flops 905969664 | bytes 1835008 | tf_op jit(solution)/shard_map/pallas_call | solution.py:112
  162.7 0.9 copy.93
  163.7 4.3 %all-to-all-start.7 = ((bf16[8,3,128,128]{3,2,1,0:T(8,128)(2,1)}), bf16[8,3,128,128]{3,2,1,0:T(8,128)(2,1)S(1)}, u32[]{:S(2)}, u32[]{:S(2)}) async-start(bf16[8,3,128,128]{3,2,1,0:T(8,128)(2,1)} %shard_map.88), calls=%async_computation.7 | async-start | bytes 1572864 | tf_op jit(solution)/shard_map/all_to_all | solution.py:194
  168.9 0.9 slice_bitcast_fusion.2
  170.6 10.0 %all-to-all-done.7 = bf16[8,3,128,128]{3,2,1,0:T(8,128)(2,1)S(1)} async-done(((bf16[8,3,128,128]{3,2,1,0:T(8,128)(2,1)}), bf16[8,3,128,128]{3,2,1,0:T(8,128)(2,1)S(1)}, u32[]{:S(2)}, u32[]{:S(2)}) %all-to-all-start.7) | async-done | bytes 786464 | tf_op jit(solution)/shard_map/all_to_all | solution.py:194
  182.3 1.3 copy.73
  183.7 1.4 pad_maximum_fusion.2
  185.7 1.3 copy.71
  187.7 1.3 copy.72
  (78 shorter events, 12.8 us)
Async XLA Ops:
  0.6 36.3 %collective-permute-start = (bf16[128,2048]{1,0:T(8,128)(2,1)}, bf16[128,2048]{1,0:T(8,128)(2,1)S(1)}, u32[]{:S(2)}, u32[]{:S(2)}) collective-permute-start(bf16[128,2048]{1,0:T(8,128)(2,1)} %bitcast.139), channel_id=1, source_target_pairs={{0,2},{1,3},{2,4},{3,5},{4,6},{5,7},{6,0},{7,1},{8,10},{9,11},{10,... | collective-permute-start | bytes 1572872 | tf_op jit(solution)/shard_map/ppermute | solution.py:154
  3.6 34.7 %collective-permute-start.1 = (bf16[128,2048]{1,0:T(8,128)(2,1)}, bf16[128,2048]{1,0:T(8,128)(2,1)S(1)}, u32[]{:S(2)}, u32[]{:S(2)}) collective-permute-start(bf16[128,2048]{1,0:T(8,128)(2,1)} %bitcast.140), channel_id=1, source_target_pairs={{0,4},{1,5},{2,6},{3,7},{4,0},{5,1},{6,2},{7,3},{8,12},{9,13},{10,... | collective-permute-start | bytes 1572872 | tf_op jit(solution)/shard_map/ppermute | solution.py:154
  5.1 33.2 %collective-permute-start.2 = (bf16[128,2048]{1,0:T(8,128)(2,1)}, bf16[128,2048]{1,0:T(8,128)(2,1)S(1)}, u32[]{:S(2)}, u32[]{:S(2)}) collective-permute-start(bf16[128,2048]{1,0:T(8,128)(2,1)} %bitcast.141), channel_id=1, source_target_pairs={{0,6},{1,7},{2,0},{3,1},{4,2},{5,3},{6,4},{7,5},{8,14},{9,15},{10,... | collective-permute-start | bytes 1572872 | tf_op jit(solution)/shard_map/ppermute | solution.py:154
  6.6 39.3 %collective-permute-start.4 = (bf16[128,2048]{1,0:T(8,128)(2,1)}, bf16[128,2048]{1,0:T(8,128)(2,1)}, u32[]{:S(2)}, u32[]{:S(2)}) collective-permute-start(bf16[128,2048]{1,0:T(8,128)(2,1)} %param.10), channel_id=1, source_target_pairs={{0,8},{8,16},{16,24},{24,0},{1,9},{9,17},{17,25},{25,1},{2,10},{10... | collective-permute-start | bytes 1572872 | tf_op jit(solution)/shard_map/ppermute | solution.py:146
  8.2 37.7 %collective-permute-start.5 = (bf16[128,2048]{1,0:T(8,128)(2,1)}, bf16[128,2048]{1,0:T(8,128)(2,1)}, u32[]{:S(2)}, u32[]{:S(2)}) collective-permute-start(bf16[128,2048]{1,0:T(8,128)(2,1)} %param.10), channel_id=1, source_target_pairs={{0,16},{8,24},{16,0},{24,8},{1,17},{9,25},{17,1},{25,9},{2,18},{10... | collective-permute-start | bytes 1572872 | tf_op jit(solution)/shard_map/ppermute | solution.py:146
  19.8 6.6 %copy-start.16 = (s32[1,14,3]{1,0,2:T(1,128)S(1)}, s32[1,14,3]{1,0,2:T(1,128)}, u32[]{:S(2)}) copy-start(s32[1,14,3]{1,0,2:T(1,128)} %param.11) | copy-start | bytes 508
  19.8 7.4 %copy-start.10 = (bf16[128,1,8,128]{0,3,2,1:T(8,128)(2,1)S(1)}, bf16[128,1,8,128]{0,3,2,1:T(8,128)(2,1)}, u32[]{:S(2)}) copy-start(bf16[128,1,8,128]{0,3,2,1:T(8,128)(2,1)} %get-tuple-element.11) | copy-start | bytes 786436
  19.8 7.6 %copy-start.12 = (bf16[128,1,8,128]{0,3,2,1:T(8,128)(2,1)S(1)}, bf16[128,1,8,128]{0,3,2,1:T(8,128)(2,1)}, u32[]{:S(2)}) copy-start(bf16[128,1,8,128]{0,3,2,1:T(8,128)(2,1)} %get-tuple-element.15) | copy-start | bytes 786436
  21.0 6.6 %copy-start.8 = (bf16[128,1,8,128]{0,3,2,1:T(8,128)(2,1)S(1)}, bf16[128,1,8,128]{0,3,2,1:T(8,128)(2,1)}, u32[]{:S(2)}) copy-start(bf16[128,1,8,128]{0,3,2,1:T(8,128)(2,1)} %get-tuple-element.19) | copy-start | bytes 786436
  22.0 5.8 %copy-start.9 = (bf16[128,1,8,128]{0,3,2,1:T(8,128)(2,1)S(1)}, bf16[128,1,8,128]{0,3,2,1:T(8,128)(2,1)}, u32[]{:S(2)}) copy-start(bf16[128,1,8,128]{0,3,2,1:T(8,128)(2,1)} %get-tuple-element.10) | copy-start | bytes 786436
  22.0 6.0 %copy-start.11 = (bf16[128,1,8,128]{0,3,2,1:T(8,128)(2,1)S(1)}, bf16[128,1,8,128]{0,3,2,1:T(8,128)(2,1)}, u32[]{:S(2)}) copy-start(bf16[128,1,8,128]{0,3,2,1:T(8,128)(2,1)} %get-tuple-element.14) | copy-start | bytes 786436
  22.0 19.8 %all-to-all-start = ((bf16[8,3,128,128]{3,2,1,0:T(8,128)(2,1)}), bf16[8,3,128,128]{3,2,1,0:T(8,128)(2,1)}, u32[]{:S(2)}, u32[]{:S(2)}) async-start(bf16[8,3,128,128]{3,2,1,0:T(8,128)(2,1)} %pad_maximum_fusion.5), calls=%async_computation | async-start | bytes 1572864 | tf_op jit(solution)/shard_map/all_to_all | solution.py:188
  33.1 1.9 %copy-start.6 = (bf16[128,1,8,128]{3,0,2,1:T(8,128)(2,1)S(1)}, bf16[128,1,8,128]{3,0,2,1:T(8,128)(2,1)}, u32[]{:S(2)}) copy-start(bf16[128,1,8,128]{3,0,2,1:T(8,128)(2,1)} %copy.84) | copy-start | bytes 786436
  33.1 1.9 %copy-start.7 = (bf16[128,1,8,128]{3,0,2,1:T(8,128)(2,1)S(1)}, bf16[128,1,8,128]{3,0,2,1:T(8,128)(2,1)}, u32[]{:S(2)}) copy-start(bf16[128,1,8,128]{3,0,2,1:T(8,128)(2,1)} %copy.85) | copy-start | bytes 786436
  33.1 3.0 %copy-start.1 = (bf16[1,128,2048]{2,1,0:T(8,128)(2,1)S(1)}, bf16[1,128,2048]{2,1,0:T(8,128)(2,1)}, u32[]{:S(2)}) copy-start(bf16[1,128,2048]{2,1,0:T(8,128)(2,1)} %param.9) | copy-start | bytes 1572868
  34.1 2.9 %copy-start.14 = (bf16[128,2048]{1,0:T(8,128)(2,1)S(1)}, bf16[128,2048]{1,0:T(8,128)(2,1)}, u32[]{:S(2)}) copy-start(bf16[128,2048]{1,0:T(8,128)(2,1)} %param.10) | copy-start | bytes 1572868
  36.9 18.2 %collective-permute-start.6 = (bf16[128,2048]{1,0:T(8,128)(2,1)S(1)}, bf16[128,2048]{1,0:T(8,128)(2,1)S(1)}, u32[]{:S(2)}, u32[]{:S(2)}) collective-permute-start(bf16[128,2048]{1,0:T(8,128)(2,1)S(1)} %copy-done.14), channel_id=1, source_target_pairs={{0,24},{8,0},{16,8},{24,16},{1,25},{9,1},{17,9},{25,17},{2,26},{10... | collective-permute-start | bytes 1572872 | tf_op jit(solution)/shard_map/ppermute | solution.py:146
  40.0 26.8 %collective-permute-start.3 = (bf16[4,128,2048]{2,1,0:T(8,128)(2,1)}, bf16[4,128,2048]{2,1,0:T(8,128)(2,1)}, u32[]{:S(2)}, u32[]{:S(2)}) collective-permute-start(bf16[4,128,2048]{2,1,0:T(8,128)(2,1)} %pad_maximum_fusion), channel_id=1, source_target_pairs={{0,1},{1,0},{2,3},{3,2},{4,5},{5,4},{6,7},{7,6},{8,9},{9,8},{10,11... | collective-permute-start | bytes 6291464 | tf_op jit(solution)/shard_map/ppermute | solution.py:157
  41.8 19.9 %all-to-all-start.2 = ((bf16[8,3,128,128]{3,2,1,0:T(8,128)(2,1)}), bf16[8,3,128,128]{3,2,1,0:T(8,128)(2,1)S(1)}, u32[]{:S(2)}, u32[]{:S(2)}) async-start(bf16[8,3,128,128]{3,2,1,0:T(8,128)(2,1)} %pad_maximum_fusion.6), calls=%async_computation.2 | async-start | bytes 1572864 | tf_op jit(solution)/shard_map/all_to_all | solution.py:188
  55.2 0.8 copy-start.15
  61.6 8.3 %copy-start.13 = (bf16[8,3,128,128]{3,2,1,0:T(8,128)(2,1)}, bf16[8,3,128,128]{3,2,1,0:T(8,128)(2,1)S(1)}, u32[]{:S(2)}) copy-start(bf16[8,3,128,128]{3,2,1,0:T(8,128)(2,1)S(1)} %all-to-all-done.2.x_ref) | copy-start | bytes 2359300
  61.6 16.8 %all-to-all-start.4 = ((bf16[8,3,128,128]{3,2,1,0:T(8,128)(2,1)}), bf16[8,3,128,128]{3,2,1,0:T(8,128)(2,1)}, u32[]{:S(2)}, u32[]{:S(2)}) async-start(bf16[8,3,128,128]{3,2,1,0:T(8,128)(2,1)} %pad_maximum_fusion.7), calls=%async_computation.4 | async-start | bytes 1572864 | tf_op jit(solution)/shard_map/all_to_all | solution.py:188
  78.5 25.9 %all-to-all-start.6 = ((bf16[8,3,128,128]{3,2,1,0:T(8,128)(2,1)}), bf16[8,3,128,128]{3,2,1,0:T(8,128)(2,1)}, u32[]{:S(2)}, u32[]{:S(2)}) async-start(bf16[8,3,128,128]{3,2,1,0:T(8,128)(2,1)} %pad_maximum_fusion.8), calls=%async_computation.6 | async-start | bytes 1572864 | tf_op jit(solution)/shard_map/all_to_all | solution.py:188
  104.4 19.4 %all-to-all-start.1 = ((bf16[8,3,128,128]{3,2,1,0:T(8,128)(2,1)}), bf16[8,3,128,128]{3,2,1,0:T(8,128)(2,1)S(1)}, u32[]{:S(2)}, u32[]{:S(2)}) async-start(bf16[8,3,128,128]{3,2,1,0:T(8,128)(2,1)} %shard_map.85), calls=%async_computation.1 | async-start | bytes 1572864 | tf_op jit(solution)/shard_map/all_to_all | solution.py:194
  123.7 19.5 %all-to-all-start.3 = ((bf16[8,3,128,128]{3,2,1,0:T(8,128)(2,1)}), bf16[8,3,128,128]{3,2,1,0:T(8,128)(2,1)S(1)}, u32[]{:S(2)}, u32[]{:S(2)}) async-start(bf16[8,3,128,128]{3,2,1,0:T(8,128)(2,1)} %shard_map.86), calls=%async_computation.3 | async-start | bytes 1572864 | tf_op jit(solution)/shard_map/all_to_all | solution.py:194
  143.2 20.5 %all-to-all-start.5 = ((bf16[8,3,128,128]{3,2,1,0:T(8,128)(2,1)}), bf16[8,3,128,128]{3,2,1,0:T(8,128)(2,1)S(1)}, u32[]{:S(2)}, u32[]{:S(2)}) async-start(bf16[8,3,128,128]{3,2,1,0:T(8,128)(2,1)} %shard_map.87), calls=%async_computation.5 | async-start | bytes 1572864 | tf_op jit(solution)/shard_map/all_to_all | solution.py:194
  163.7 4.4 %copy-start = (bf16[8,3,128,128]{3,2,0,1:T(8,128)(2,1)S(1)}, bf16[8,3,128,128]{3,2,0,1:T(8,128)(2,1)}, u32[]{:S(2)}) copy-start(bf16[8,3,128,128]{3,2,0,1:T(8,128)(2,1)} %copy.93) | copy-start | bytes 2359300
  163.7 16.9 %all-to-all-start.7 = ((bf16[8,3,128,128]{3,2,1,0:T(8,128)(2,1)}), bf16[8,3,128,128]{3,2,1,0:T(8,128)(2,1)S(1)}, u32[]{:S(2)}, u32[]{:S(2)}) async-start(bf16[8,3,128,128]{3,2,1,0:T(8,128)(2,1)} %shard_map.88), calls=%async_computation.7 | async-start | bytes 1572864 | tf_op jit(solution)/shard_map/all_to_all | solution.py:194
  182.3 1.4 copy-start.2
  182.3 1.3 copy-start.3
  182.3 1.3 copy-start.4
  182.3 1.3 copy-start.5

commit v4 on v3

--- a/solution.py
+++ b/solution.py
@@ -99,9 +99,10 @@
 
 
 def attention_grads(stacked, upstream, head, random_ids):
-    parts, _, tokens, _ = stacked.shape
+    parts, _, _, tokens, _ = stacked.shape
     length = parts * tokens
     count = length // BLOCK
+    source = pl.BlockSpec((parts, 3, None, tokens, HD), lambda h, rb: (0, 0, head, 0, 0))
     whole = pl.BlockSpec((parts, 3, tokens, HD), lambda h, rb: (0, 0, 0, 0))
     spec = pl.BlockSpec((length, HD), lambda h, rb: (0, head))
     out = jax.ShapeDtypeStruct((parts, 3, tokens, HD), jnp.bfloat16)
@@ -115,7 +116,7 @@
         grid_spec=pltpu.PrefetchScalarGridSpec(
             num_scalar_prefetch=1,
             grid=(1,),
-            in_specs=[whole, spec],
+            in_specs=[source, spec],
             out_specs=whole,
             scratch_shapes=[
                 pltpu.VMEM((length, HD), jnp.float32),
@@ -168,8 +169,8 @@
         upstream = jnp.take(upstream.reshape(ctx, tokens, -1), position, axis=0)
         upstream = upstream.reshape(ctx * tokens, -1)
 
-        def chunk(array, c):
-            return array.reshape(tokens, dp, ctx, HD)[:, c]
+        def chunk(array):
+            return array.reshape(tokens, dp, ctx, HD).transpose(2, 1, 0, 3)
     else:
         upstream = lax.dot_general(
             local_cotangent,
@@ -179,18 +180,20 @@
         ).astype(jnp.bfloat16)
         local = local + (upstream,)
 
-        def chunk(array, c):
-            return array.reshape(tokens, ctx, local_heads, HD)[:, :, c]
-
+        def chunk(array):
+            return array.reshape(tokens, ctx, local_heads, HD).transpose(1, 2, 0, 3)
+
+    stacked = jnp.stack([chunk(array) for array in local], axis=1)
+    moved = lax.all_to_all(stacked, "context", split_axis=0, concat_axis=0, tiled=True)
+    if not strided:
+        head_upstream = moved[:, 3].transpose(1, 0, 2, 3).reshape(local_heads, tokens * ctx, HD)
+        moved = moved[:, :3]
     pieces = []
     for c in range(local_heads):
-        stacked = jnp.stack([chunk(array, c).transpose(1, 0, 2) for array in local], axis=1)
-        moved = lax.all_to_all(stacked, "context", split_axis=0, concat_axis=0, tiled=True)
         if strided:
             grads = attention_grads(moved, upstream, c, random_blocks[0])
         else:
-            head_upstream = moved[:, 3].reshape(tokens * ctx, HD)
-            grads = attention_grads(moved[:, :3], head_upstream, 0, random_blocks[0])
+            grads = attention_grads(moved, head_upstream[c], 0, random_blocks[0])
         back = lax.all_to_all(grads, "context", split_axis=0, concat_axis=0, tiled=True)
         pieces.append(back.transpose(1, 2, 0, 3))
 

time: 190 us -> 179 us (0.942)
  starting transfers between devices: 45.3 us -> 31.9 us
  other arithmetic: 11.9 us -> 15.2 us
    all_to_all x4 -> x1, starting transfers between devices: 16.9 us -> 3.78 us  [body(): lax.all_to_all(stacked, 'context', split_axis=0, concat_axis=0, tiled=True)]
    ppermute x3, waiting for transfers between devices: 9.28 us -> 18.6 us  [body(): lax.ppermute(out_weight, 'dp', [(a, (a + s) % dp) for a in range(dp)])]
    all_to_all x4 -> x1, waiting for transfers between devices: 8.59 us -> 0.01 us  [body(): lax.all_to_all(stacked, 'context', split_axis=0, concat_axis=0, tiled=True)]
    unnamed x57 -> x31, local copies, waits for them, and re-layouts: 21.4 us -> 18 us
    slice x3 -> x0, local copies, waits for them, and re-layouts: 2.87 us -> none  [chunk(): return array.reshape(tokens, dp, ctx, HD)[:, c]]
    another operation x0 -> x3, local copies, waits for them, and re-layouts: none -> 2.64 us  [chunk(): return array.reshape(tokens, dp, ctx, HD).transpose(2, 1, 0, 3)]
    gather x1, local copies, waits for them, and re-layouts: 0.61 us -> 2.81 us  [body(): upstream = jnp.take(upstream.reshape(ctx, tokens, -1), position, axis=0)]
    another operation x4 -> x1, other arithmetic: 3.86 us -> 3.22 us  [body(): stacked = jnp.stack([chunk(array) for array in local], axis=1)]
  transfers between devices with their start and end apart: 15 -> 12, of which waited for: 3 -> 4; matrix products, arithmetic and copies ran while one was open for 24% -> 25% of each run, Pallas kernels for 32% -> 26%
where the time goes in v4:
time: 179 us; the launch traced here: 178 us
  Pallas kernels  61.1 us (34%)
  local copies, waits for them, and re-layouts  36 us (20%)
  starting transfers between devices  31.9 us (18%)
  waiting for transfers between devices  29.1 us (16%)
  other arithmetic  15.2 us (8%)
  matrix products  3.34 us (2%)
    pallas_call x4, Pallas kernels, attention_grads(): pl.pallas_call(_attention_kernel, out_shape=out, grid_spec=pltpu.Prefetch...  61.1 us
    ppermute x3, waiting for transfers between devices, body(): lax.ppermute(out_weight, 'dp', [(a, (a + s) % dp) for a in range(dp)])  18.6 us
    unnamed x31, local copies, waits for them, and re-layouts  18 us
    all_to_all x4, starting transfers between devices, body(): lax.all_to_all(grads, 'context', split_axis=0, concat_axis=0, tiled=True)  16.6 us
    all_to_all x4, waiting for transfers between devices, body(): lax.all_to_all(grads, 'context', split_axis=0, concat_axis=0, tiled=True)  9.98 us
    ppermute x3, starting transfers between devices, body(): lax.ppermute(local_cotangent, 'context', [(a, (a + s) % ctx) for a in ran...  5.94 us
    ppermute x3, starting transfers between devices, body(): lax.ppermute(out_weight, 'dp', [(a, (a + s) % dp) for a in range(dp)])  5.54 us
    another operation x7, local copies, waits for them, and re-layouts, body(): joined = jnp.stack([piece[g] for piece in pieces], axis=1 if strided else 2)  5.39 us
  transfers between devices with their start and end apart: 12, of which 4 were waited for; matrix products, arithmetic and copies ran while one was open for 25% of the time, Pallas kernels for 26%

profile of v4, /device:TPU:0, one launch (start us, length us, event | category | flops | bytes accessed | tf_op | source)
XLA Modules:
  0.0 177.5 jit_solution(10171668169071157768)
XLA Ops:
  0.6 3.0 %collective-permute-start = (bf16[128,2048]{1,0:T(8,128)(2,1)}, bf16[128,2048]{1,0:T(8,128)(2,1)}, u32[]{:S(2)}, u32[]{:S(2)}) collective-permute-start(bf16[128,2048]{1,0:T(8,128)(2,1)} %bitcast.91), channel_id=1, source_target_pairs={{0,2},{1,3},{2,4},{3,5},{4,6},{5,7},{6,0},{7,1},{8,10},{9,11},{10,... | collective-permute-start | bytes 1572872 | tf_op jit(solution)/shard_map/ppermute | solution.py:155
  3.6 1.5 collective-permute-start.1
  5.2 1.4 collective-permute-start.2
  6.6 1.6 collective-permute-start.4
  8.2 2.6 %collective-permute-start.5 = (bf16[128,2048]{1,0:T(8,128)(2,1)}, bf16[128,2048]{1,0:T(8,128)(2,1)}, u32[]{:S(2)}, u32[]{:S(2)}) collective-permute-start(bf16[128,2048]{1,0:T(8,128)(2,1)} %param.10), channel_id=1, source_target_pairs={{0,16},{8,24},{16,0},{24,8},{1,17},{9,25},{17,1},{25,9},{2,18},{10... | collective-permute-start | bytes 1572872 | tf_op jit(solution)/shard_map/ppermute | solution.py:147
  10.8 1.6 copy.34
  12.4 0.7 copy.35
  13.7 0.7 copy.37
  14.4 1.6 copy.38
  16.0 1.3 copy.39
  17.3 3.2 %pad_maximum_fusion = bf16[8,3,4,128,128]{4,3,2,1,0:T(8,128)(2,1)} fusion(bf16[8,1,4,128,128]{4,3,2,1,0:T(8,128)(2,1)} %bitcast.85, bf16[8,1,4,128,128]{4,3,2,1,0:T(8,128)(2,1)S(1)} %bitcast.84, bf16[8,1,4,128,128]{4,3,2,1,0:T(8,128)(2,1)S(1)} %bitcast.83), kind=kLoop, calls=%fused_computation.2 | loop fusion | flops 3145728 | bytes 6291456 | tf_op jit(solution)/shard_map/stack | solution.py:186
  20.6 3.8 %all-to-all-start = ((bf16[8,3,4,128,128]{4,3,2,1,0:T(8,128)(2,1)}), bf16[8,3,4,128,128]{4,3,2,1,0:T(8,128)(2,1)S(1)}, u32[]{:S(2)}, u32[]{:S(2)}) async-start(bf16[8,3,4,128,128]{4,3,2,1,0:T(8,128)(2,1)} %pad_maximum_fusion), calls=%async_computation | async-start | bytes 6291456 | tf_op jit(solution)/shard_map/all_to_all | solution.py:187
  25.3 1.9 %constant_dynamic-update-slice_fusion.4 = bf16[8,128,2048]{2,1,0:T(8,128)(2,1)} fusion(bf16[1,128,2048]{2,1,0:T(8,128)(2,1)} %param.9), kind=kLoop, calls=%fused_computation.30 | loop fusion | bytes 1048576
  27.2 1.4 collective-permute-start.6
  29.1 3.1 %pad_maximum_fusion.1 = bf16[4,128,2048]{2,1,0:T(8,128)(2,1)} fusion(bf16[1,128,2048]{2,1,0:T(8,128)(2,1)} %bitcast.13, bf16[1,128,2048]{2,1,0:T(8,128)(2,1)} %bitcast.12, bf16[1,128,2048]{2,1,0:T(8,128)(2,1)} %bitcast.11, bf16[1,128,2048]{2,1,0:T(8,128)(2,1)} %param.9), kind=kLoop, calls=%fused_computation.3 | loop fusion | flops 3145728 | bytes 4194304 | tf_op jit(solution)/shard_map/stack | solution.py:154
  32.2 1.9 %constant_dynamic-update-slice_fusion.3 = bf16[8,128,2048]{2,1,0:T(8,128)(2,1)} fusion(bf16[8,128,2048]{2,1,0:T(8,128)(2,1)} %constant_dynamic-update-slice_fusion.4, bf16[128,2048]{1,0:T(8,128)(2,1)} %collective-permute-done), kind=kLoop, calls=%fused_computation.29 | loop fusion | bytes 1048576
  34.1 10.1 %collective-permute-done.5 = bf16[128,2048]{1,0:T(8,128)(2,1)} collective-permute-done((bf16[128,2048]{1,0:T(8,128)(2,1)}, bf16[128,2048]{1,0:T(8,128)(2,1)}, u32[]{:S(2)}, u32[]{:S(2)}) %collective-permute-start.5) | collective-permute-done | bytes 524320 | tf_op jit(solution)/shard_map/ppermute | solution.py:147
  44.2 8.5 %collective-permute-done.6 = bf16[128,2048]{1,0:T(8,128)(2,1)S(1)} collective-permute-done((bf16[128,2048]{1,0:T(8,128)(2,1)}, bf16[128,2048]{1,0:T(8,128)(2,1)S(1)}, u32[]{:S(2)}, u32[]{:S(2)}) %collective-permute-start.6) | collective-permute-done | bytes 524320 | tf_op jit(solution)/shard_map/ppermute | solution.py:147
  52.7 2.8 %pad_maximum_fusion.2 = bf16[4,128,2048]{2,1,0:T(8,128)(2,1)} fusion(bf16[1,128,2048]{2,1,0:T(8,128)(2,1)S(1)} %bitcast.96, bf16[1,128,2048]{2,1,0:T(8,128)(2,1)} %bitcast.17, bf16[1,128,2048]{2,1,0:T(8,128)(2,1)} %bitcast.16, bf16[1,128,2048]{2,1,0:T(8,128)(2,1)S(1)} %bitcast.95), kind=kLoop, calls=%fused_computation.4 | loop fusion | flops 3145728 | bytes 4194304 | tf_op jit(solution)/shard_map/stack | solution.py:151
  55.5 3.7 %gather_fusion = bf16[4,128,2048]{2,1,0:T(8,128)(2,1)} fusion(bf16[4,128,2048]{2,1,0:T(8,128)(2,1)} %pad_maximum_fusion.2, s32[1024]{0:T(1024)S(1)} %pad_clamp_fusion.1), kind=kCustom, calls=%fused_computation | custom fusion | bytes 4194320 | tf_op jit(solution)/shard_map/jit(_take)/gather | solution.py:151
  59.2 1.9 %constant_dynamic-update-slice_fusion.2 = bf16[8,128,2048]{2,1,0:T(8,128)(2,1)} fusion(bf16[8,128,2048]{2,1,0:T(8,128)(2,1)} %constant_dynamic-update-slice_fusion.3, bf16[128,2048]{1,0:T(8,128)(2,1)} %collective-permute-done.1), kind=kLoop, calls=%fused_computation.28 | loop fusion | bytes 1048576
  61.1 1.9 %constant_dynamic-update-slice_fusion.1 = bf16[8,128,2048]{2,1,0:T(8,128)(2,1)} fusion(bf16[8,128,2048]{2,1,0:T(8,128)(2,1)} %constant_dynamic-update-slice_fusion.2, bf16[128,2048]{1,0:T(8,128)(2,1)} %collective-permute-done.2), kind=kLoop, calls=%fused_computation.27 | loop fusion | bytes 1048576
  63.0 2.0 %broadcast_select_fusion = bf16[4,128,2048]{2,1,0:T(8,128)(2,1)S(1)} fusion(bf16[4,128,2048]{2,1,0:T(8,128)(2,1)} %gather_fusion, pred[4]{0:T(512)(128)(4,1)S(1)} %compare_and_fusion), kind=kLoop, calls=%fused_computation.5 | loop fusion | flops 1048576 | bytes 4194308 | tf_op jit(solution)/shard_map/jit(_take)/select_n | solution.py:151
  65.0 0.8 copy-done.8
  65.8 1.8 %constant_dynamic-update-slice_fusion = bf16[8,128,2048]{2,1,0:T(8,128)(2,1)S(1)} fusion(bf16[8,128,2048]{2,1,0:T(8,128)(2,1)S(1)} %copy-done.8, bf16[4,128,2048]{2,1,0:T(8,128)(2,1)} %collective-permute-done.3), kind=kLoop, calls=%fused_computation.26 | loop fusion | bytes 4194304 | tf_op jit(solution)/shard_map/concatenate | solution.py:159
  67.6 3.3 %convolution_convert_fusion = bf16[1024,512]{1,0:T(8,128)(2,1)} fusion(bf16[1024,2048]{1,0:T(8,128)(2,1)S(1)} %bitcast.97, bf16[512,2048]{1,0:T(8,128)(2,1)S(1)} %bitcast.90), kind=kOutput, calls=%fused_computation.6 | convolution fusion | flops 2148007936 | bytes 7340032 | tf_op jit(solution)/shard_map/dot_general | solution.py:160
  71.0 2.8 %gather_fusion.1 = bf16[8,128,512]{2,1,0:T(8,128)(2,1)} fusion(bf16[8,128,512]{2,1,0:T(8,128)(2,1)} %bitcast.94, s32[1024]{0:T(1024)S(1)} %pad_clamp_fusion), kind=kCustom, calls=%fused_computation.1 | custom fusion | bytes 2097184 | tf_op jit(solution)/shard_map/jit(_take)/gather | solution.py:169
  73.8 2.4 %bitcast_select_fusion.u_ref = bf16[1024,512]{1,0:T(8,128)(2,1)} fusion(bf16[8,128,512]{2,1,0:T(8,128)(2,1)} %gather_fusion.1, pred[1024]{0:T(1024)(128)(4,1)S(1)} %broadcast_bitcast_fusion), kind=kLoop, calls=%fused_computation.10 | loop fusion | flops 524288 | bytes 2098176 | tf_op jit(solution)/shard_map/jit(_take)/select_n | solution.py:169
  76.2 1.6 copy-done
  77.8 15.3 %shard_map.86 = bf16[8,3,128,128]{3,2,1,0:T(8,128)(2,1)} custom-call(s32[42]{0:T(128)} %reshape_squeeze.15.rb_ref, bf16[8,3,4,128,128]{4,3,2,1,0:T(8,128)(2,1)} %copy-done, bf16[1024,512]{1,0:T(8,128)(2,1)} %bitcast_select_fusion.u_ref), custom_call_target="tpu_custom_call" | custom-call | flops 905969664 | bytes 1835008 | tf_op jit(solution)/shard_map/pallas_call | solution.py:113
  93.1 3.8 %all-to-all-start.2 = ((bf16[8,3,128,128]{3,2,1,0:T(8,128)(2,1)}), bf16[8,3,128,128]{3,2,1,0:T(8,128)(2,1)S(1)}, u32[]{:S(2)}, u32[]{:S(2)}) async-start(bf16[8,3,128,128]{3,2,1,0:T(8,128)(2,1)} %shard_map.86), calls=%async_computation.2 | async-start | bytes 1572864 | tf_op jit(solution)/shard_map/all_to_all | solution.py:197
  96.9 15.3 %shard_map.85 = bf16[8,3,128,128]{3,2,1,0:T(8,128)(2,1)} custom-call(s32[42]{0:T(128)} %reshape_squeeze.15.rb_ref, bf16[8,3,4,128,128]{4,3,2,1,0:T(8,128)(2,1)} %copy-done, bf16[1024,512]{1,0:T(8,128)(2,1)} %bitcast_select_fusion.u_ref), custom_call_target="tpu_custom_call" | custom-call | flops 905969664 | bytes 1835008 | tf_op jit(solution)/shard_map/pallas_call | solution.py:113
  112.2 4.2 %all-to-all-start.1 = ((bf16[8,3,128,128]{3,2,1,0:T(8,128)(2,1)}), bf16[8,3,128,128]{3,2,1,0:T(8,128)(2,1)S(1)}, u32[]{:S(2)}, u32[]{:S(2)}) async-start(bf16[8,3,128,128]{3,2,1,0:T(8,128)(2,1)} %shard_map.85), calls=%async_computation.1 | async-start | bytes 1572864 | tf_op jit(solution)/shard_map/all_to_all | solution.py:197
  116.4 15.3 %shard_map.87 = bf16[8,3,128,128]{3,2,1,0:T(8,128)(2,1)} custom-call(s32[42]{0:T(128)} %reshape_squeeze.15.rb_ref, bf16[8,3,4,128,128]{4,3,2,1,0:T(8,128)(2,1)} %copy-done, bf16[1024,512]{1,0:T(8,128)(2,1)} %bitcast_select_fusion.u_ref), custom_call_target="tpu_custom_call" | custom-call | flops 905969664 | bytes 1835008 | tf_op jit(solution)/shard_map/pallas_call | solution.py:113
  131.7 4.2 %all-to-all-start.3 = ((bf16[8,3,128,128]{3,2,1,0:T(8,128)(2,1)}), bf16[8,3,128,128]{3,2,1,0:T(8,128)(2,1)S(1)}, u32[]{:S(2)}, u32[]{:S(2)}) async-start(bf16[8,3,128,128]{3,2,1,0:T(8,128)(2,1)} %shard_map.87), calls=%async_computation.3 | async-start | bytes 1572864 | tf_op jit(solution)/shard_map/all_to_all | solution.py:197
  135.9 15.3 %shard_map.88 = bf16[8,3,128,128]{3,2,1,0:T(8,128)(2,1)} custom-call(s32[42]{0:T(128)} %reshape_squeeze.15.rb_ref, bf16[8,3,4,128,128]{4,3,2,1,0:T(8,128)(2,1)} %copy-done, bf16[1024,512]{1,0:T(8,128)(2,1)} %bitcast_select_fusion.u_ref), custom_call_target="tpu_custom_call" | custom-call | flops 905969664 | bytes 1835008 | tf_op jit(solution)/shard_map/pallas_call | solution.py:113
  151.2 0.9 copy.57
  152.2 4.3 %all-to-all-start.4 = ((bf16[8,3,128,128]{3,2,1,0:T(8,128)(2,1)}), bf16[8,3,128,128]{3,2,1,0:T(8,128)(2,1)S(1)}, u32[]{:S(2)}, u32[]{:S(2)}) async-start(bf16[8,3,128,128]{3,2,1,0:T(8,128)(2,1)} %shard_map.88), calls=%async_computation.4 | async-start | bytes 1572864 | tf_op jit(solution)/shard_map/all_to_all | solution.py:197
  156.6 0.8 slice_bitcast_fusion.2
  157.4 0.9 slice_bitcast_fusion.3
  158.3 0.9 slice_bitcast_fusion.1
  159.2 10.0 %all-to-all-done.4 = bf16[8,3,128,128]{3,2,1,0:T(8,128)(2,1)S(1)} async-done(((bf16[8,3,128,128]{3,2,1,0:T(8,128)(2,1)}), bf16[8,3,128,128]{3,2,1,0:T(8,128)(2,1)S(1)}, u32[]{:S(2)}, u32[]{:S(2)}) %all-to-all-start.4) | async-done | bytes 786464 | tf_op jit(solution)/shard_map/all_to_all | solution.py:197
  169.1 0.8 slice_bitcast_fusion
  170.1 0.7 copy.47
  170.8 1.3 copy.50
  172.2 1.4 pad_maximum_fusion.3
  174.2 1.3 copy.48
  176.2 1.3 copy.49
  (43 shorter events, 3.7 us)
Async XLA Ops:
  0.6 12.4 %copy-start.2 = (bf16[1,128,4096]{2,1,0:T(8,128)(2,1)S(1)}, bf16[1,128,4096]{2,1,0:T(8,128)(2,1)}, u32[]{:S(2)}) copy-start(bf16[1,128,4096]{2,1,0:T(8,128)(2,1)} %param.7) | copy-start | bytes 3145732
  0.6 26.5 %collective-permute-start = (bf16[128,2048]{1,0:T(8,128)(2,1)}, bf16[128,2048]{1,0:T(8,128)(2,1)}, u32[]{:S(2)}, u32[]{:S(2)}) collective-permute-start(bf16[128,2048]{1,0:T(8,128)(2,1)} %bitcast.91), channel_id=1, source_target_pairs={{0,2},{1,3},{2,4},{3,5},{4,6},{5,7},{6,0},{7,1},{8,10},{9,11},{10,... | collective-permute-start | bytes 1572872 | tf_op jit(solution)/shard_map/ppermute | solution.py:155
  3.6 24.9 %collective-permute-start.1 = (bf16[128,2048]{1,0:T(8,128)(2,1)}, bf16[128,2048]{1,0:T(8,128)(2,1)}, u32[]{:S(2)}, u32[]{:S(2)}) collective-permute-start(bf16[128,2048]{1,0:T(8,128)(2,1)} %bitcast.92), channel_id=1, source_target_pairs={{0,4},{1,5},{2,6},{3,7},{4,0},{5,1},{6,2},{7,3},{8,12},{9,13},{10,... | collective-permute-start | bytes 1572872 | tf_op jit(solution)/shard_map/ppermute | solution.py:155
  5.2 23.9 %collective-permute-start.2 = (bf16[128,2048]{1,0:T(8,128)(2,1)}, bf16[128,2048]{1,0:T(8,128)(2,1)}, u32[]{:S(2)}, u32[]{:S(2)}) collective-permute-start(bf16[128,2048]{1,0:T(8,128)(2,1)} %bitcast.93), channel_id=1, source_target_pairs={{0,6},{1,7},{2,0},{3,1},{4,2},{5,3},{6,4},{7,5},{8,14},{9,15},{10,... | collective-permute-start | bytes 1572872 | tf_op jit(solution)/shard_map/ppermute | solution.py:155
  6.6 27.5 %collective-permute-start.4 = (bf16[128,2048]{1,0:T(8,128)(2,1)}, bf16[128,2048]{1,0:T(8,128)(2,1)}, u32[]{:S(2)}, u32[]{:S(2)}) collective-permute-start(bf16[128,2048]{1,0:T(8,128)(2,1)} %param.10), channel_id=1, source_target_pairs={{0,8},{8,16},{16,24},{24,0},{1,9},{9,17},{17,25},{25,1},{2,10},{10... | collective-permute-start | bytes 1572872 | tf_op jit(solution)/shard_map/ppermute | solution.py:147
  8.2 36.0 %collective-permute-start.5 = (bf16[128,2048]{1,0:T(8,128)(2,1)}, bf16[128,2048]{1,0:T(8,128)(2,1)}, u32[]{:S(2)}, u32[]{:S(2)}) collective-permute-start(bf16[128,2048]{1,0:T(8,128)(2,1)} %param.10), channel_id=1, source_target_pairs={{0,16},{8,24},{16,0},{24,8},{1,17},{9,25},{17,1},{25,9},{2,18},{10... | collective-permute-start | bytes 1572872 | tf_op jit(solution)/shard_map/ppermute | solution.py:147
  20.6 3.9 %copy-start.9 = (s32[1,14,3]{1,0,2:T(1,128)S(1)}, s32[1,14,3]{1,0,2:T(1,128)}, u32[]{:S(2)}) copy-start(s32[1,14,3]{1,0,2:T(1,128)} %param.11) | copy-start | bytes 508
  20.6 55.6 %all-to-all-start = ((bf16[8,3,4,128,128]{4,3,2,1,0:T(8,128)(2,1)}), bf16[8,3,4,128,128]{4,3,2,1,0:T(8,128)(2,1)S(1)}, u32[]{:S(2)}, u32[]{:S(2)}) async-start(bf16[8,3,4,128,128]{4,3,2,1,0:T(8,128)(2,1)} %pad_maximum_fusion), calls=%async_computation | async-start | bytes 6291456 | tf_op jit(solution)/shard_map/all_to_all | solution.py:187
  27.2 25.6 %collective-permute-start.6 = (bf16[128,2048]{1,0:T(8,128)(2,1)}, bf16[128,2048]{1,0:T(8,128)(2,1)S(1)}, u32[]{:S(2)}, u32[]{:S(2)}) collective-permute-start(bf16[128,2048]{1,0:T(8,128)(2,1)} %param.10), channel_id=1, source_target_pairs={{0,24},{8,0},{16,8},{24,16},{1,25},{9,1},{17,9},{25,17},{2,26},{10... | collective-permute-start | bytes 1572872 | tf_op jit(solution)/shard_map/ppermute | solution.py:147
  29.1 23.7 %copy-start.7 = (bf16[128,2048]{1,0:T(8,128)(2,1)S(1)}, bf16[128,2048]{1,0:T(8,128)(2,1)}, u32[]{:S(2)}) copy-start(bf16[128,2048]{1,0:T(8,128)(2,1)} %param.10) | copy-start | bytes 1572868
  32.2 32.8 %collective-permute-start.3 = (bf16[4,128,2048]{2,1,0:T(8,128)(2,1)}, bf16[4,128,2048]{2,1,0:T(8,128)(2,1)}, u32[]{:S(2)}, u32[]{:S(2)}) collective-permute-start(bf16[4,128,2048]{2,1,0:T(8,128)(2,1)} %pad_maximum_fusion.1), channel_id=1, source_target_pairs={{0,1},{1,0},{2,3},{3,2},{4,5},{5,4},{6,7},{7,6},{8,9},{9,8},{10,11... | collective-permute-start | bytes 6291464 | tf_op jit(solution)/shard_map/ppermute | solution.py:158
  63.0 2.8 %copy-start.8 = (bf16[8,128,2048]{2,1,0:T(8,128)(2,1)S(1)}, bf16[8,128,2048]{2,1,0:T(8,128)(2,1)}, u32[]{:S(2)}) copy-start(bf16[8,128,2048]{2,1,0:T(8,128)(2,1)} %constant_dynamic-update-slice_fusion.1) | copy-start | bytes 12582916
  76.2 1.6 copy-start
  93.1 19.1 %all-to-all-start.2 = ((bf16[8,3,128,128]{3,2,1,0:T(8,128)(2,1)}), bf16[8,3,128,128]{3,2,1,0:T(8,128)(2,1)S(1)}, u32[]{:S(2)}, u32[]{:S(2)}) async-start(bf16[8,3,128,128]{3,2,1,0:T(8,128)(2,1)} %shard_map.86), calls=%async_computation.2 | async-start | bytes 1572864 | tf_op jit(solution)/shard_map/all_to_all | solution.py:197
  112.2 19.5 %all-to-all-start.1 = ((bf16[8,3,128,128]{3,2,1,0:T(8,128)(2,1)}), bf16[8,3,128,128]{3,2,1,0:T(8,128)(2,1)S(1)}, u32[]{:S(2)}, u32[]{:S(2)}) async-start(bf16[8,3,128,128]{3,2,1,0:T(8,128)(2,1)} %shard_map.85), calls=%async_computation.1 | async-start | bytes 1572864 | tf_op jit(solution)/shard_map/all_to_all | solution.py:197
  131.7 20.5 %all-to-all-start.3 = ((bf16[8,3,128,128]{3,2,1,0:T(8,128)(2,1)}), bf16[8,3,128,128]{3,2,1,0:T(8,128)(2,1)S(1)}, u32[]{:S(2)}, u32[]{:S(2)}) async-start(bf16[8,3,128,128]{3,2,1,0:T(8,128)(2,1)} %shard_map.87), calls=%async_computation.3 | async-start | bytes 1572864 | tf_op jit(solution)/shard_map/all_to_all | solution.py:197
  152.2 4.4 %copy-start.1 = (bf16[8,3,128,128]{3,2,0,1:T(8,128)(2,1)S(1)}, bf16[8,3,128,128]{3,2,0,1:T(8,128)(2,1)}, u32[]{:S(2)}) copy-start(bf16[8,3,128,128]{3,2,0,1:T(8,128)(2,1)} %copy.57) | copy-start | bytes 2359300
  152.2 16.9 %all-to-all-start.4 = ((bf16[8,3,128,128]{3,2,1,0:T(8,128)(2,1)}), bf16[8,3,128,128]{3,2,1,0:T(8,128)(2,1)S(1)}, u32[]{:S(2)}, u32[]{:S(2)}) async-start(bf16[8,3,128,128]{3,2,1,0:T(8,128)(2,1)} %shard_map.88), calls=%async_computation.4 | async-start | bytes 1572864 | tf_op jit(solution)/shard_map/all_to_all | solution.py:197
  170.8 1.4 copy-start.3
  170.8 1.3 copy-start.4
  170.8 1.3 copy-start.5
  170.8 1.3 copy-start.6

commit v5 on v4

--- a/solution.py
+++ b/solution.py
@@ -26,7 +26,7 @@
     return lax.dot_general(a, b, (((1,), (0,)), ((), ())), preferred_element_type=jnp.float32)
 
 
-def _attention_kernel(rb_ref, x_ref, u_ref, o_ref, dk_acc, dv_acc, kg_ref, vg_ref):
+def _attention_kernel(rb_ref, pos_ref, col_ref, x_ref, u_ref, o_ref, dk_acc, dv_acc, kg_ref, vg_ref):
     parts, _, tokens, _ = x_ref.shape
     per_part = tokens // BLOCK
     length = parts * tokens
@@ -39,6 +39,10 @@
         else:
             offset = pl.multiple_of((block % per_part) * BLOCK, BLOCK)
         return ref.at[block // per_part, which, pl.ds(offset, BLOCK), :]
+
+    def upstream_rows(block):
+        offset = pos_ref[block // per_part] * tokens + (block % per_part) * BLOCK
+        return u_ref[pl.ds(pl.multiple_of(offset, BLOCK), BLOCK), :]
 
     def softmax_grads(qb, ub, keys, values, mask):
         scores = _nt(qb, keys) * factor
@@ -61,7 +65,7 @@
     values_all = x_ref[:, 2, :, :].reshape(length, HD)
     for index, block in enumerate((0, count - 1)):
         qb = rows(x_ref, 0, block)[...]
-        ub = u_ref[block * BLOCK:(block + 1) * BLOCK, :]
+        ub = upstream_rows(block)
         query_grad, key_grad, value_grad = softmax_grads(qb, ub, keys_all, values_all, None)
         rows(o_ref, 0, block)[...] = query_grad.astype(jnp.bfloat16)
         if index == 0:
@@ -83,7 +87,7 @@
             vg_ref[slot * BLOCK:(slot + 1) * BLOCK, :] = rows(x_ref, 2, block)[...]
         start = pl.multiple_of(m * BLOCK, BLOCK)
         qb = rows(x_ref, 0, m)[...]
-        ub = u_ref[pl.ds(start, BLOCK), :]
+        ub = upstream_rows(m)
         mask = ((columns == 2) & (m == 1)) | ((columns == 4) & (m == count - 2))
         query_grad, key_grad, value_grad = softmax_grads(qb, ub, kg_ref[...], vg_ref[...], mask)
         rows(o_ref, 0, m)[...] = query_grad.astype(jnp.bfloat16)
@@ -98,13 +102,13 @@
     o_ref[:, 2, :, :] = dv_acc[...].reshape(parts, tokens, HD).astype(jnp.bfloat16)
 
 
-def attention_grads(stacked, upstream, head, random_ids):
+def attention_grads(stacked, upstream, head, column, positions, random_ids):
     parts, _, _, tokens, _ = stacked.shape
     length = parts * tokens
     count = length // BLOCK
-    source = pl.BlockSpec((parts, 3, None, tokens, HD), lambda h, rb: (0, 0, head, 0, 0))
-    whole = pl.BlockSpec((parts, 3, tokens, HD), lambda h, rb: (0, 0, 0, 0))
-    spec = pl.BlockSpec((length, HD), lambda h, rb: (0, head))
+    source = pl.BlockSpec((parts, 3, None, tokens, HD), lambda h, rb, ps, cl: (0, 0, head, 0, 0))
+    whole = pl.BlockSpec((parts, 3, tokens, HD), lambda h, rb, ps, cl: (0, 0, 0, 0))
+    spec = pl.BlockSpec((length, HD), lambda h, rb, ps, cl: (0, cl[0]))
     out = jax.ShapeDtypeStruct((parts, 3, tokens, HD), jnp.bfloat16)
     pairs = 2 * BLOCK * length + (count - 2) * BLOCK * SLOTS * BLOCK
     cost = pl.CostEstimate(
@@ -114,7 +118,7 @@
         _attention_kernel,
         out_shape=out,
         grid_spec=pltpu.PrefetchScalarGridSpec(
-            num_scalar_prefetch=1,
+            num_scalar_prefetch=3,
             grid=(1,),
             in_specs=[source, spec],
             out_specs=whole,
@@ -127,7 +131,7 @@
         ),
         compiler_params=pltpu.CompilerParams(dimension_semantics=("arbitrary",)),
         cost_estimate=cost,
-    )(random_ids.reshape(-1), stacked, upstream)
+    )(random_ids.reshape(-1), positions, column.reshape(1), stacked, upstream)
 
 
 def body(queries, key_rows, value_rows, cotangent, out_weight, random_blocks):
@@ -147,8 +151,8 @@
             lax.ppermute(out_weight, "dp", [(a, (a + s) % dp) for a in range(dp)])
             for s in range(1, dp)
         ]
-        order = (me - jnp.arange(dp)) % dp
-        head_weight = jnp.take(jnp.stack(got), order, axis=0).reshape(dp * HD, -1)
+        head_weight = jnp.concatenate(got, axis=0)
+        columns = [(me - c) % dp for c in range(local_heads)]
         j = lax.axis_index("context")
         shifts = list(range(0, ctx, 2))
         mine = jnp.stack([local_cotangent] + [
@@ -156,18 +160,19 @@
             for s in shifts[1:]
         ])
         other = lax.ppermute(mine, "context", [(a, a ^ 1) for a in range(ctx)])
-        gathered = jnp.concatenate([mine, other]).reshape(ctx * tokens, -1)
-        upstream = lax.dot_general(
-            gathered, head_weight, (((1,), (1,)), ((), ())),
-            preferred_element_type=jnp.float32,
-        ).astype(jnp.bfloat16)
+
+        def project(piece):
+            return lax.dot_general(
+                piece.reshape(-1, piece.shape[-1]), head_weight, (((1,), (1,)), ((), ())),
+                preferred_element_type=jnp.float32,
+            ).astype(jnp.bfloat16)
+
+        upstream = jnp.concatenate([project(mine), project(other)], axis=0)
         source = jnp.arange(ctx)
         same = source % 2 == j % 2
-        position = jnp.where(
+        positions = jnp.where(
             same, ((j - source) % ctx) // 2, ctx // 2 + (((j ^ 1) - source) % ctx) // 2
-        )
-        upstream = jnp.take(upstream.reshape(ctx, tokens, -1), position, axis=0)
-        upstream = upstream.reshape(ctx * tokens, -1)
+        ).astype(jnp.int32)
 
         def chunk(array):
             return array.reshape(tokens, dp, ctx, HD).transpose(2, 1, 0, 3)
@@ -179,6 +184,7 @@
             preferred_element_type=jnp.float32,
         ).astype(jnp.bfloat16)
         local = local + (upstream,)
+        positions = jnp.arange(ctx, dtype=jnp.int32)
 
         def chunk(array):
             return array.reshape(tokens, ctx, local_heads, HD).transpose(1, 2, 0, 3)
@@ -191,9 +197,13 @@
     pieces = []
     for c in range(local_heads):
         if strided:
-            grads = attention_grads(moved, upstream, c, random_blocks[0])
+            grads = attention_grads(
+                moved, upstream, c, columns[c].astype(jnp.int32), positions, random_blocks[0]
+            )
         else:
-            grads = attention_grads(moved, head_upstream[c], 0, random_blocks[0])
+            grads = attention_grads(
+                moved, head_upstream[c], 0, jnp.zeros((), jnp.int32), positions, random_blocks[0]
+            )
         back = lax.all_to_all(grads, "context", split_axis=0, concat_axis=0, tiled=True)
         pieces.append(back.transpose(1, 2, 0, 3))
 

time: 179 us -> 199 us (1.11)
  the two profiles are of different devices: /device:TPU:0 before, /device:TPU:24 now
where the time goes in v5:
time: 199 us; the launch traced here: 198 us
  Pallas kernels  61.2 us (31%)
  waiting for transfers between devices  59.3 us (30%)
  starting transfers between devices  32.7 us (16%)
  local copies, waits for them, and re-layouts  27.9 us (14%)
  other arithmetic  9.4 us (5%)
  matrix products  6.53 us (3%)
    pallas_call x4, Pallas kernels, attention_grads(): pl.pallas_call(_attention_kernel, out_shape=out, grid_spec=pltpu.Prefetch...  61.2 us
    ppermute x3, waiting for transfers between devices, body(): lax.ppermute(out_weight, 'dp', [(a, (a + s) % dp) for a in range(dp)])  40.8 us
    all_to_all x4, starting transfers between devices, body(): lax.all_to_all(grads, 'context', split_axis=0, concat_axis=0, tiled=True)  22.2 us
    unnamed x26, local copies, waits for them, and re-layouts  16.4 us
    all_to_all x4, waiting for transfers between devices, body(): lax.all_to_all(grads, 'context', split_axis=0, concat_axis=0, tiled=True)  10 us
    ppermute x3, waiting for transfers between devices, body(): lax.ppermute(local_cotangent, 'context', [(a, (a + s) % ctx) for a in ran...  8.53 us
    dot_general x2, matrix products, project(): lax.dot_general(piece.reshape(-1, piece.shape[-1]), head_weight, (((1,),...  6.53 us
    another operation x7, local copies, waits for them, and re-layouts, body(): joined = jnp.stack([piece[g] for piece in pieces], axis=1 if strided else 2)  5.35 us
  transfers between devices with their start and end apart: 12, of which 5 were waited for; matrix products, arithmetic and copies ran while one was open for 17% of the time, Pallas kernels for 23%

profile of v5, /device:TPU:24, one launch (start us, length us, event | category | flops | bytes accessed | tf_op | source)
XLA Modules:
  0.0 198.0 jit_solution(8219527631128847904)
XLA Ops:
  0.6 1.5 collective-permute-start
  2.2 1.5 collective-permute-start.1
  3.7 1.4 collective-permute-start.2
  5.1 1.6 copy.34
  6.7 0.7 copy.35
  7.4 1.6 copy.36
  9.0 0.7 copy.37
  9.7 1.6 copy.38
  11.3 1.3 copy.39
  12.7 3.2 %pad_maximum_fusion = bf16[8,3,4,128,128]{4,3,2,1,0:T(8,128)(2,1)} fusion(bf16[8,1,4,128,128]{4,3,2,1,0:T(8,128)(2,1)} %bitcast.75, bf16[8,1,4,128,128]{4,3,2,1,0:T(8,128)(2,1)S(1)} %bitcast.74, bf16[8,1,4,128,128]{4,3,2,1,0:T(8,128)(2,1)S(1)} %bitcast.73), kind=kLoop, calls=%fused_computation | loop fusion | flops 3145728 | bytes 6291456 | tf_op jit(solution)/shard_map/stack | solution.py:192
  15.8 3.6 %all-to-all-start = ((bf16[8,3,4,128,128]{4,3,2,1,0:T(8,128)(2,1)}), bf16[8,3,4,128,128]{4,3,2,1,0:T(8,128)(2,1)S(1)}, u32[]{:S(2)}, u32[]{:S(2)}) async-start(bf16[8,3,4,128,128]{4,3,2,1,0:T(8,128)(2,1)} %pad_maximum_fusion), calls=%async_computation | async-start | bytes 6291456 | tf_op jit(solution)/shard_map/all_to_all | solution.py:193
  19.5 7.4 %collective-permute-done.1 = bf16[128,2048]{1,0:T(8,128)(2,1)} collective-permute-done((bf16[128,2048]{1,0:T(8,128)(2,1)}, bf16[128,2048]{1,0:T(8,128)(2,1)}, u32[]{:S(2)}, u32[]{:S(2)}) %collective-permute-start.1) | collective-permute-done | bytes 524320 | tf_op jit(solution)/shard_map/ppermute | solution.py:159
  26.9 1.2 collective-permute-done.2
  28.0 3.1 %pad_maximum_fusion.1 = bf16[4,128,2048]{2,1,0:T(8,128)(2,1)} fusion(bf16[1,128,2048]{2,1,0:T(8,128)(2,1)} %bitcast.13, bf16[1,128,2048]{2,1,0:T(8,128)(2,1)} %bitcast.12, bf16[1,128,2048]{2,1,0:T(8,128)(2,1)} %bitcast.11, bf16[1,128,2048]{2,1,0:T(8,128)(2,1)} %param.9), kind=kLoop, calls=%fused_computation.1 | loop fusion | flops 3145728 | bytes 4194304 | tf_op jit(solution)/shard_map/stack | solution.py:158
  31.4 1.7 collective-permute-start.4
  33.6 1.9 constant_dynamic-update-slice_fusion.3
  35.5 0.5 compare_select_fusion.4.pos_ref
  36.1 0.6 reshape_squeeze.15.rb_ref
  36.7 9.3 %collective-permute-done.3 = bf16[128,2048]{1,0:T(8,128)(2,1)} collective-permute-done((bf16[128,2048]{1,0:T(8,128)(2,1)}, bf16[128,2048]{1,0:T(8,128)(2,1)}, u32[]{:S(2)}, u32[]{:S(2)}) %collective-permute-start.3) | collective-permute-done | bytes 524320 | tf_op jit(solution)/shard_map/ppermute | solution.py:151
  46.0 1.9 constant_dynamic-update-slice_fusion.2
  47.9 31.5 %collective-permute-done.4 = bf16[128,2048]{1,0:T(8,128)(2,1)} collective-permute-done((bf16[128,2048]{1,0:T(8,128)(2,1)}, bf16[128,2048]{1,0:T(8,128)(2,1)}, u32[]{:S(2)}, u32[]{:S(2)}) %collective-permute-start.4) | collective-permute-done | bytes 524320 | tf_op jit(solution)/shard_map/ppermute | solution.py:151
  79.4 2.0 constant_dynamic-update-slice_fusion.1
  81.4 1.9 constant_dynamic-update-slice_fusion
  83.3 3.6 %convolution_convert_fusion.1 = bf16[512,512]{1,0:T(8,128)(2,1)S(1)} fusion(bf16[512,2048]{1,0:T(8,128)(2,1)} %bitcast.14, bf16[512,2048]{1,0:T(8,128)(2,1)} %constant_dynamic-update-slice_fusion), kind=kOutput, calls=%fused_computation.3 | convolution fusion | flops 1074003968 | bytes 4718592 | tf_op jit(solution)/shard_map/dot_general | solution.py:165
  87.0 2.9 %convolution_convert_fusion = bf16[512,512]{1,0:T(8,128)(2,1)S(1)} fusion(bf16[512,2048]{1,0:T(8,128)(2,1)} %bitcast.15, bf16[512,2048]{1,0:T(8,128)(2,1)S(1)} %copy-done.6), kind=kOutput, calls=%fused_computation.2 | convolution fusion | flops 1074003968 | bytes 4718592 | tf_op jit(solution)/shard_map/dot_general | solution.py:165
  89.8 1.0 pad_maximum_fusion.2.u_ref
  90.9 1.6 copy-done
  92.5 15.3 %shard_map.85 = bf16[8,3,128,128]{3,2,1,0:T(8,128)(2,1)} custom-call(s32[42]{0:T(128)} %reshape_squeeze.15.rb_ref, s32[8]{0:T(128)} %compare_select_fusion.4.pos_ref, s32[1]{0:T(128)} %bitcast.col_ref, bf16[8,3,4,128,128]{4,3,2,1,0:T(8,128)(2,1)} %copy-done, bf16[1024,512]{1,0:T(8,128)(2,1)} %pad_maximum_fusion.2.u_ref), custom_call_target="tpu_custom_call" | custom-call | flops 905969664 | bytes 1835008 | tf_op jit(solution)/shard_map/pallas_call | solution.py:117
  107.8 9.5 %all-to-all-start.1 = ((bf16[8,3,128,128]{3,2,1,0:T(8,128)(2,1)}), bf16[8,3,128,128]{3,2,1,0:T(8,128)(2,1)S(1)}, u32[]{:S(2)}, u32[]{:S(2)}) async-start(bf16[8,3,128,128]{3,2,1,0:T(8,128)(2,1)} %shard_map.85), calls=%async_computation.1 | async-start | bytes 1572864 | tf_op jit(solution)/shard_map/all_to_all | solution.py:207
  117.3 15.3 %shard_map.86 = bf16[8,3,128,128]{3,2,1,0:T(8,128)(2,1)} custom-call(s32[42]{0:T(128)} %reshape_squeeze.15.rb_ref, s32[8]{0:T(128)} %compare_select_fusion.4.pos_ref, s32[1]{0:T(128)} %bitcast.18.col_ref, bf16[8,3,4,128,128]{4,3,2,1,0:T(8,128)(2,1)} %copy-done, bf16[1024,512]{1,0:T(8,128)(2,1)} %pad_maximum_fusion.2.u_ref), custom_call_target="tpu_custom_call" | custom-call | flops 905969664 | bytes 1835008 | tf_op jit(solution)/shard_map/pallas_call | solution.py:117
  132.6 4.2 %all-to-all-start.2 = ((bf16[8,3,128,128]{3,2,1,0:T(8,128)(2,1)}), bf16[8,3,128,128]{3,2,1,0:T(8,128)(2,1)S(1)}, u32[]{:S(2)}, u32[]{:S(2)}) async-start(bf16[8,3,128,128]{3,2,1,0:T(8,128)(2,1)} %shard_map.86), calls=%async_computation.2 | async-start | bytes 1572864 | tf_op jit(solution)/shard_map/all_to_all | solution.py:207
  136.8 15.3 %shard_map.87 = bf16[8,3,128,128]{3,2,1,0:T(8,128)(2,1)} custom-call(s32[42]{0:T(128)} %reshape_squeeze.15.rb_ref, s32[8]{0:T(128)} %compare_select_fusion.4.pos_ref, s32[1]{0:T(128)} %bitcast.21.col_ref, bf16[8,3,4,128,128]{4,3,2,1,0:T(8,128)(2,1)} %copy-done, bf16[1024,512]{1,0:T(8,128)(2,1)} %pad_maximum_fusion.2.u_ref), custom_call_target="tpu_custom_call" | custom-call | flops 905969664 | bytes 1835008 | tf_op jit(solution)/shard_map/pallas_call | solution.py:117
  152.1 4.2 %all-to-all-start.3 = ((bf16[8,3,128,128]{3,2,1,0:T(8,128)(2,1)}), bf16[8,3,128,128]{3,2,1,0:T(8,128)(2,1)S(1)}, u32[]{:S(2)}, u32[]{:S(2)}) async-start(bf16[8,3,128,128]{3,2,1,0:T(8,128)(2,1)} %shard_map.87), calls=%async_computation.3 | async-start | bytes 1572864 | tf_op jit(solution)/shard_map/all_to_all | solution.py:207
  156.3 15.3 %shard_map.88 = bf16[8,3,128,128]{3,2,1,0:T(8,128)(2,1)} custom-call(s32[42]{0:T(128)} %reshape_squeeze.15.rb_ref, s32[8]{0:T(128)} %compare_select_fusion.4.pos_ref, s32[1]{0:T(128)} %bitcast.24.col_ref, bf16[8,3,4,128,128]{4,3,2,1,0:T(8,128)(2,1)} %copy-done, bf16[1024,512]{1,0:T(8,128)(2,1)} %pad_maximum_fusion.2.u_ref), custom_call_target="tpu_custom_call" | custom-call | flops 905969664 | bytes 1835008 | tf_op jit(solution)/shard_map/pallas_call | solution.py:117
  171.7 0.9 copy.58
  172.7 4.3 %all-to-all-start.4 = ((bf16[8,3,128,128]{3,2,1,0:T(8,128)(2,1)}), bf16[8,3,128,128]{3,2,1,0:T(8,128)(2,1)S(1)}, u32[]{:S(2)}, u32[]{:S(2)}) async-start(bf16[8,3,128,128]{3,2,1,0:T(8,128)(2,1)} %shard_map.88), calls=%async_computation.4 | async-start | bytes 1572864 | tf_op jit(solution)/shard_map/all_to_all | solution.py:207
  177.1 0.8 slice_bitcast_fusion.3
  177.9 0.9 slice_bitcast_fusion.2
  178.7 0.9 slice_bitcast_fusion.1
  179.6 10.0 %all-to-all-done.4 = bf16[8,3,128,128]{3,2,1,0:T(8,128)(2,1)S(1)} async-done(((bf16[8,3,128,128]{3,2,1,0:T(8,128)(2,1)}), bf16[8,3,128,128]{3,2,1,0:T(8,128)(2,1)S(1)}, u32[]{:S(2)}, u32[]{:S(2)}) %all-to-all-start.4) | async-done | bytes 786464 | tf_op jit(solution)/shard_map/all_to_all | solution.py:207
  189.6 0.8 slice_bitcast_fusion
  190.6 0.7 copy.47
  191.3 1.3 copy.50
  192.7 1.4 pad_maximum_fusion.3
  194.0 0.7 copy.44
  194.7 1.3 copy.48
  196.0 0.7 copy.46
  196.7 1.3 copy.49
  (29 shorter events, 1.1 us)
Async XLA Ops:
  0.6 18.9 %collective-permute-start = (bf16[128,2048]{1,0:T(8,128)(2,1)}, bf16[128,2048]{1,0:T(8,128)(2,1)}, u32[]{:S(2)}, u32[]{:S(2)}) collective-permute-start(bf16[128,2048]{1,0:T(8,128)(2,1)} %bitcast.80), channel_id=1, source_target_pairs={{0,2},{1,3},{2,4},{3,5},{4,6},{5,7},{6,0},{7,1},{8,10},{9,11},{10,... | collective-permute-start | bytes 1572872 | tf_op jit(solution)/shard_map/ppermute | solution.py:159
  2.2 24.7 %collective-permute-start.1 = (bf16[128,2048]{1,0:T(8,128)(2,1)}, bf16[128,2048]{1,0:T(8,128)(2,1)}, u32[]{:S(2)}, u32[]{:S(2)}) collective-permute-start(bf16[128,2048]{1,0:T(8,128)(2,1)} %bitcast.81), channel_id=1, source_target_pairs={{0,4},{1,5},{2,6},{3,7},{4,0},{5,1},{6,2},{7,3},{8,12},{9,13},{10,... | collective-permute-start | bytes 1572872 | tf_op jit(solution)/shard_map/ppermute | solution.py:159
  3.7 24.3 %collective-permute-start.2 = (bf16[128,2048]{1,0:T(8,128)(2,1)}, bf16[128,2048]{1,0:T(8,128)(2,1)}, u32[]{:S(2)}, u32[]{:S(2)}) collective-permute-start(bf16[128,2048]{1,0:T(8,128)(2,1)} %bitcast.82), channel_id=1, source_target_pairs={{0,6},{1,7},{2,0},{3,1},{4,2},{5,3},{6,4},{7,5},{8,14},{9,15},{10,... | collective-permute-start | bytes 1572872 | tf_op jit(solution)/shard_map/ppermute | solution.py:159
  15.8 75.0 %all-to-all-start = ((bf16[8,3,4,128,128]{4,3,2,1,0:T(8,128)(2,1)}), bf16[8,3,4,128,128]{4,3,2,1,0:T(8,128)(2,1)S(1)}, u32[]{:S(2)}, u32[]{:S(2)}) async-start(bf16[8,3,4,128,128]{4,3,2,1,0:T(8,128)(2,1)} %pad_maximum_fusion), calls=%async_computation | async-start | bytes 6291456 | tf_op jit(solution)/shard_map/all_to_all | solution.py:193
  28.0 8.0 %copy-start.7 = (s32[1,14,3]{1,0,2:T(1,128)S(1)}, s32[1,14,3]{1,0,2:T(1,128)}, u32[]{:S(2)}) copy-start(s32[1,14,3]{1,0,2:T(1,128)} %param.11) | copy-start | bytes 508
  31.2 55.7 %collective-permute-start.6 = (bf16[4,128,2048]{2,1,0:T(8,128)(2,1)}, bf16[4,128,2048]{2,1,0:T(8,128)(2,1)}, u32[]{:S(2)}, u32[]{:S(2)}) collective-permute-start(bf16[4,128,2048]{2,1,0:T(8,128)(2,1)} %pad_maximum_fusion.1), channel_id=1, source_target_pairs={{0,1},{1,0},{2,3},{3,2},{4,5},{5,4},{6,7},{7,6},{8,9},{9,8},{10,11... | collective-permute-start | bytes 6291464 | tf_op jit(solution)/shard_map/ppermute | solution.py:162
  31.2 14.8 %collective-permute-start.3 = (bf16[128,2048]{1,0:T(8,128)(2,1)}, bf16[128,2048]{1,0:T(8,128)(2,1)}, u32[]{:S(2)}, u32[]{:S(2)}) collective-permute-start(bf16[128,2048]{1,0:T(8,128)(2,1)} %param.10), channel_id=1, source_target_pairs={{0,8},{8,16},{16,24},{24,0},{1,9},{9,17},{17,25},{25,1},{2,10},{10... | collective-permute-start | bytes 1572872 | tf_op jit(solution)/shard_map/ppermute | solution.py:151
  31.4 48.0 %collective-permute-start.4 = (bf16[128,2048]{1,0:T(8,128)(2,1)}, bf16[128,2048]{1,0:T(8,128)(2,1)}, u32[]{:S(2)}, u32[]{:S(2)}) collective-permute-start(bf16[128,2048]{1,0:T(8,128)(2,1)} %param.10), channel_id=1, source_target_pairs={{0,16},{8,24},{16,0},{24,8},{1,17},{9,25},{17,1},{25,9},{2,18},{10... | collective-permute-start | bytes 1572872 | tf_op jit(solution)/shard_map/ppermute | solution.py:151
  33.1 48.3 %collective-permute-start.5 = (bf16[128,2048]{1,0:T(8,128)(2,1)}, bf16[128,2048]{1,0:T(8,128)(2,1)}, u32[]{:S(2)}, u32[]{:S(2)}) collective-permute-start(bf16[128,2048]{1,0:T(8,128)(2,1)} %param.10), channel_id=1, source_target_pairs={{0,24},{8,0},{16,8},{24,16},{1,25},{9,1},{17,9},{25,17},{2,26},{10... | collective-permute-start | bytes 1572872 | tf_op jit(solution)/shard_map/ppermute | solution.py:151
  83.3 3.7 %copy-start.6 = (bf16[512,2048]{1,0:T(8,128)(2,1)S(1)}, bf16[512,2048]{1,0:T(8,128)(2,1)}, u32[]{:S(2)}) copy-start(bf16[512,2048]{1,0:T(8,128)(2,1)} %constant_dynamic-update-slice_fusion) | copy-start | bytes 6291460
  90.9 1.6 copy-start
  107.8 24.8 %all-to-all-start.1 = ((bf16[8,3,128,128]{3,2,1,0:T(8,128)(2,1)}), bf16[8,3,128,128]{3,2,1,0:T(8,128)(2,1)S(1)}, u32[]{:S(2)}, u32[]{:S(2)}) async-start(bf16[8,3,128,128]{3,2,1,0:T(8,128)(2,1)} %shard_map.85), calls=%async_computation.1 | async-start | bytes 1572864 | tf_op jit(solution)/shard_map/all_to_all | solution.py:207
  132.6 19.5 %all-to-all-start.2 = ((bf16[8,3,128,128]{3,2,1,0:T(8,128)(2,1)}), bf16[8,3,128,128]{3,2,1,0:T(8,128)(2,1)S(1)}, u32[]{:S(2)}, u32[]{:S(2)}) async-start(bf16[8,3,128,128]{3,2,1,0:T(8,128)(2,1)} %shard_map.86), calls=%async_computation.2 | async-start | bytes 1572864 | tf_op jit(solution)/shard_map/all_to_all | solution.py:207
  152.1 20.5 %all-to-all-start.3 = ((bf16[8,3,128,128]{3,2,1,0:T(8,128)(2,1)}), bf16[8,3,128,128]{3,2,1,0:T(8,128)(2,1)S(1)}, u32[]{:S(2)}, u32[]{:S(2)}) async-start(bf16[8,3,128,128]{3,2,1,0:T(8,128)(2,1)} %shard_map.87), calls=%async_computation.3 | async-start | bytes 1572864 | tf_op jit(solution)/shard_map/all_to_all | solution.py:207
  172.7 4.4 %copy-start.1 = (bf16[8,3,128,128]{3,2,0,1:T(8,128)(2,1)S(1)}, bf16[8,3,128,128]{3,2,0,1:T(8,128)(2,1)}, u32[]{:S(2)}) copy-start(bf16[8,3,128,128]{3,2,0,1:T(8,128)(2,1)} %copy.58) | copy-start | bytes 2359300
  172.7 16.9 %all-to-all-start.4 = ((bf16[8,3,128,128]{3,2,1,0:T(8,128)(2,1)}), bf16[8,3,128,128]{3,2,1,0:T(8,128)(2,1)S(1)}, u32[]{:S(2)}, u32[]{:S(2)}) async-start(bf16[8,3,128,128]{3,2,1,0:T(8,128)(2,1)} %shard_map.88), calls=%async_computation.4 | async-start | bytes 1572864 | tf_op jit(solution)/shard_map/all_to_all | solution.py:207
  191.3 1.4 copy-start.2
  191.3 1.3 copy-start.3
  191.3 1.3 copy-start.4
  191.3 1.3 copy-start.5

commit v6 on v5

--- a/solution.py
+++ b/solution.py
@@ -146,13 +146,10 @@
     strided = rows_per_device == HD and local_heads == dp and ctx % 2 == 0
 
     if strided:
-        me = lax.axis_index("dp")
-        got = [out_weight] + [
-            lax.ppermute(out_weight, "dp", [(a, (a + s) % dp) for a in range(dp)])
-            for s in range(1, dp)
-        ]
-        head_weight = jnp.concatenate(got, axis=0)
-        columns = [(me - c) % dp for c in range(local_heads)]
+        spread = jnp.broadcast_to(out_weight[None], (dp,) + out_weight.shape)
+        head_weight = lax.all_to_all(spread, "dp", split_axis=0, concat_axis=0, tiled=True)
+        head_weight = head_weight.reshape(dp * HD, -1)
+        columns = [jnp.array(c, jnp.int32) for c in range(local_heads)]
         j = lax.axis_index("context")
         shifts = list(range(0, ctx, 2))
         mine = jnp.stack([local_cotangent] + [

time: 199 us -> 202 us (1.015)
  the two profiles are of different devices: /device:TPU:24 before, /device:TPU:0 now
where the time goes in v6:
time: 202 us; the launch traced here: 201 us
  waiting for transfers between devices  71 us (35%)
  Pallas kernels  61.2 us (30%)
  starting transfers between devices  30.8 us (15%)
  local copies, waits for them, and re-layouts  21.9 us (11%)
  other arithmetic  7.89 us (4%)
  matrix products  7 us (3%)
    pallas_call x4, Pallas kernels, attention_grads(): pl.pallas_call(_attention_kernel, out_shape=out, grid_spec=pltpu.Prefetch...  61.2 us
    all_to_all x1, waiting for transfers between devices, body(): lax.all_to_all(stacked, 'context', split_axis=0, concat_axis=0, tiled=True)  28.5 us
    ppermute x3, waiting for transfers between devices, body(): lax.ppermute(local_cotangent, 'context', [(a, (a + s) % ctx) for a in ran...  21.2 us
    all_to_all x4, starting transfers between devices, body(): lax.all_to_all(grads, 'context', split_axis=0, concat_axis=0, tiled=True)  16.2 us
    all_to_all x1, waiting for transfers between devices, body(): lax.all_to_all(spread, 'dp', split_axis=0, concat_axis=0, tiled=True)  11.3 us
    all_to_all x4, waiting for transfers between devices, body(): lax.all_to_all(grads, 'context', split_axis=0, concat_axis=0, tiled=True)  10 us
    unnamed x25, local copies, waits for them, and re-layouts  9.59 us
    dot_general x2, matrix products, project(): lax.dot_general(piece.reshape(-1, piece.shape[-1]), head_weight, (((1,),...  7 us
  transfers between devices with their start and end apart: 10, of which 6 were waited for; matrix products, arithmetic and copies ran while one was open for 12% of the time, Pallas kernels for 23%

profile of v6, /device:TPU:0, one launch (start us, length us, event | category | flops | bytes accessed | tf_op | source)
XLA Modules:
  0.0 200.7 jit_solution(13401089355291339717)
XLA Ops:
  0.6 2.6 %broadcast_in_dim.2 = bf16[4,128,2048]{2,1,0:T(8,128)(2,1)} broadcast(bf16[128,2048]{1,0:T(8,128)(2,1)} %param.10), dimensions={1,2} | broadcast | bytes 2621440 | tf_op jit(solution)/shard_map/broadcast_in_dim | solution.py:149
  3.2 6.4 %all-to-all-start.1 = ((bf16[4,128,2048]{2,1,0:T(8,128)(2,1)}), bf16[4,128,2048]{2,1,0:T(8,128)(2,1)}, u32[]{:S(2)}, u32[]{:S(2)}) async-start(bf16[4,128,2048]{2,1,0:T(8,128)(2,1)} %broadcast_in_dim.2), calls=%async_computation.1 | async-start | bytes 4194304 | tf_op jit(solution)/shard_map/all_to_all | solution.py:150
  9.7 1.5 collective-permute-start
  11.2 1.5 collective-permute-start.1
  12.7 1.4 collective-permute-start.2
  14.1 11.3 %collective-permute-done = bf16[128,2048]{1,0:T(8,128)(2,1)S(1)} collective-permute-done((bf16[128,2048]{1,0:T(8,128)(2,1)S(1)}, bf16[128,2048]{1,0:T(8,128)(2,1)S(1)}, u32[]{:S(2)}, u32[]{:S(2)}) %collective-permute-start) | collective-permute-done | bytes 524320 | tf_op jit(solution)/shard_map/ppermute | solution.py:156
  25.5 9.7 %collective-permute-done.1 = bf16[128,2048]{1,0:T(8,128)(2,1)S(1)} collective-permute-done((bf16[128,2048]{1,0:T(8,128)(2,1)S(1)}, bf16[128,2048]{1,0:T(8,128)(2,1)S(1)}, u32[]{:S(2)}, u32[]{:S(2)}) %collective-permute-start.1) | collective-permute-done | bytes 524320 | tf_op jit(solution)/shard_map/ppermute | solution.py:156
  35.2 0.1 collective-permute-done.2
  35.3 1.6 pad_maximum_fusion.1
  36.9 0.7 copy.34
  37.6 0.7 copy.35
  38.2 1.6 copy.36
  39.9 0.7 copy.37
  40.5 1.6 copy.38
  42.2 1.3 copy.39
  43.5 3.2 %pad_maximum_fusion = bf16[8,3,4,128,128]{4,3,2,1,0:T(8,128)(2,1)} fusion(bf16[8,1,4,128,128]{4,3,2,1,0:T(8,128)(2,1)} %bitcast.72, bf16[8,1,4,128,128]{4,3,2,1,0:T(8,128)(2,1)S(1)} %bitcast.71, bf16[8,1,4,128,128]{4,3,2,1,0:T(8,128)(2,1)S(1)} %bitcast.70), kind=kLoop, calls=%fused_computation | loop fusion | flops 3145728 | bytes 6291456 | tf_op jit(solution)/shard_map/stack | solution.py:189
  46.7 11.3 %all-to-all-done.1 = bf16[4,128,2048]{2,1,0:T(8,128)(2,1)} async-done(((bf16[4,128,2048]{2,1,0:T(8,128)(2,1)}), bf16[4,128,2048]{2,1,0:T(8,128)(2,1)}, u32[]{:S(2)}, u32[]{:S(2)}) %all-to-all-start.1) | async-done | bytes 2097184 | tf_op jit(solution)/shard_map/all_to_all | solution.py:150
  58.0 3.7 %all-to-all-start = ((bf16[8,3,4,128,128]{4,3,2,1,0:T(8,128)(2,1)}), bf16[8,3,4,128,128]{4,3,2,1,0:T(8,128)(2,1)S(1)}, u32[]{:S(2)}, u32[]{:S(2)}) async-start(bf16[8,3,4,128,128]{4,3,2,1,0:T(8,128)(2,1)} %pad_maximum_fusion), calls=%async_computation | async-start | bytes 6291456 | tf_op jit(solution)/shard_map/all_to_all | solution.py:190
  61.7 0.1 copy.33
  61.8 0.7 reshape_squeeze.15.rb_ref
  62.5 0.6 compare_select_fusion.4.pos_ref
  63.0 3.5 %convolution_convert_fusion = bf16[512,512]{1,0:T(8,128)(2,1)S(1)} fusion(bf16[512,2048]{1,0:T(8,128)(2,1)} %bitcast.15, bf16[512,2048]{1,0:T(8,128)(2,1)} %bitcast.14), kind=kOutput, calls=%fused_computation.2 | convolution fusion | flops 1074003968 | bytes 4718592 | tf_op jit(solution)/shard_map/dot_general | solution.py:162
  66.5 3.5 %convolution_convert_fusion.1 = bf16[512,512]{1,0:T(8,128)(2,1)S(1)} fusion(bf16[512,2048]{1,0:T(8,128)(2,1)} %bitcast.13, bf16[512,2048]{1,0:T(8,128)(2,1)} %bitcast.14), kind=kOutput, calls=%fused_computation.3 | convolution fusion | flops 1074003968 | bytes 4718592 | tf_op jit(solution)/shard_map/dot_general | solution.py:162
  70.1 1.0 pad_maximum_fusion.2.u_ref
  71.1 28.5 %all-to-all-done.x_ref = bf16[8,3,4,128,128]{4,3,2,1,0:T(8,128)(2,1)S(1)} async-done(((bf16[8,3,4,128,128]{4,3,2,1,0:T(8,128)(2,1)}), bf16[8,3,4,128,128]{4,3,2,1,0:T(8,128)(2,1)S(1)}, u32[]{:S(2)}, u32[]{:S(2)}) %all-to-all-start) | async-done | bytes 3145760 | tf_op jit(solution)/shard_map/all_to_all | solution.py:190
  99.6 1.6 copy-done
  101.2 15.3 %shard_map.85 = bf16[8,3,128,128]{3,2,1,0:T(8,128)(2,1)} custom-call(s32[42]{0:T(128)} %reshape_squeeze.15.rb_ref, s32[8]{0:T(128)} %compare_select_fusion.4.pos_ref, s32[1]{0:T(128)} %constant.67.clone.1.col_ref, bf16[8,3,4,128,128]{4,3,2,1,0:T(8,128)(2,1)} %copy-done, bf16[1024,512]{1,0:T(8,128)(2,1)} %pad_maximum_fusion.2.u_ref), custom_call_target="tpu_custom_call" | custom-call | flops 905969664 | bytes 1835008 | tf_op jit(solution)/shard_map/pallas_call | solution.py:117
  116.5 3.5 %all-to-all-start.2 = ((bf16[8,3,128,128]{3,2,1,0:T(8,128)(2,1)}), bf16[8,3,128,128]{3,2,1,0:T(8,128)(2,1)S(1)}, u32[]{:S(2)}, u32[]{:S(2)}) async-start(bf16[8,3,128,128]{3,2,1,0:T(8,128)(2,1)} %shard_map.85), calls=%async_computation.2 | async-start | bytes 1572864 | tf_op jit(solution)/shard_map/all_to_all | solution.py:204
  120.1 15.3 %shard_map.86 = bf16[8,3,128,128]{3,2,1,0:T(8,128)(2,1)} custom-call(s32[42]{0:T(128)} %reshape_squeeze.15.rb_ref, s32[8]{0:T(128)} %compare_select_fusion.4.pos_ref, s32[1]{0:T(128)} %constant.68.clone.1.col_ref, bf16[8,3,4,128,128]{4,3,2,1,0:T(8,128)(2,1)} %copy-done, bf16[1024,512]{1,0:T(8,128)(2,1)} %pad_maximum_fusion.2.u_ref), custom_call_target="tpu_custom_call" | custom-call | flops 905969664 | bytes 1835008 | tf_op jit(solution)/shard_map/pallas_call | solution.py:117
  135.4 4.1 %all-to-all-start.3 = ((bf16[8,3,128,128]{3,2,1,0:T(8,128)(2,1)}), bf16[8,3,128,128]{3,2,1,0:T(8,128)(2,1)S(1)}, u32[]{:S(2)}, u32[]{:S(2)}) async-start(bf16[8,3,128,128]{3,2,1,0:T(8,128)(2,1)} %shard_map.86), calls=%async_computation.3 | async-start | bytes 1572864 | tf_op jit(solution)/shard_map/all_to_all | solution.py:204
  139.5 15.3 %shard_map.87 = bf16[8,3,128,128]{3,2,1,0:T(8,128)(2,1)} custom-call(s32[42]{0:T(128)} %reshape_squeeze.15.rb_ref, s32[8]{0:T(128)} %compare_select_fusion.4.pos_ref, s32[1]{0:T(128)} %constant.69.clone.1.col_ref, bf16[8,3,4,128,128]{4,3,2,1,0:T(8,128)(2,1)} %copy-done, bf16[1024,512]{1,0:T(8,128)(2,1)} %pad_maximum_fusion.2.u_ref), custom_call_target="tpu_custom_call" | custom-call | flops 905969664 | bytes 1835008 | tf_op jit(solution)/shard_map/pallas_call | solution.py:117
  154.8 4.2 %all-to-all-start.4 = ((bf16[8,3,128,128]{3,2,1,0:T(8,128)(2,1)}), bf16[8,3,128,128]{3,2,1,0:T(8,128)(2,1)S(1)}, u32[]{:S(2)}, u32[]{:S(2)}) async-start(bf16[8,3,128,128]{3,2,1,0:T(8,128)(2,1)} %shard_map.87), calls=%async_computation.4 | async-start | bytes 1572864 | tf_op jit(solution)/shard_map/all_to_all | solution.py:204
  159.0 15.3 %shard_map.88 = bf16[8,3,128,128]{3,2,1,0:T(8,128)(2,1)} custom-call(s32[42]{0:T(128)} %reshape_squeeze.15.rb_ref, s32[8]{0:T(128)} %compare_select_fusion.4.pos_ref, s32[1]{0:T(128)} %constant.70.clone.1.col_ref, bf16[8,3,4,128,128]{4,3,2,1,0:T(8,128)(2,1)} %copy-done, bf16[1024,512]{1,0:T(8,128)(2,1)} %pad_maximum_fusion.2.u_ref), custom_call_target="tpu_custom_call" | custom-call | flops 905969664 | bytes 1835008 | tf_op jit(solution)/shard_map/pallas_call | solution.py:117
  174.3 0.9 copy.58
  175.4 4.3 %all-to-all-start.5 = ((bf16[8,3,128,128]{3,2,1,0:T(8,128)(2,1)}), bf16[8,3,128,128]{3,2,1,0:T(8,128)(2,1)S(1)}, u32[]{:S(2)}, u32[]{:S(2)}) async-start(bf16[8,3,128,128]{3,2,1,0:T(8,128)(2,1)} %shard_map.88), calls=%async_computation.5 | async-start | bytes 1572864 | tf_op jit(solution)/shard_map/all_to_all | solution.py:204
  179.8 0.8 slice_bitcast_fusion.3
  180.6 0.9 slice_bitcast_fusion.2
  181.4 0.9 slice_bitcast_fusion.1
  182.3 10.0 %all-to-all-done.5 = bf16[8,3,128,128]{3,2,1,0:T(8,128)(2,1)S(1)} async-done(((bf16[8,3,128,128]{3,2,1,0:T(8,128)(2,1)}), bf16[8,3,128,128]{3,2,1,0:T(8,128)(2,1)S(1)}, u32[]{:S(2)}, u32[]{:S(2)}) %all-to-all-start.5) | async-done | bytes 786464 | tf_op jit(solution)/shard_map/all_to_all | solution.py:204
  192.3 0.8 slice_bitcast_fusion
  193.2 0.1 pad_maximum_fusion.5
  193.3 0.7 copy.47
  194.0 1.3 copy.50
  195.4 1.4 pad_maximum_fusion.3
  196.7 0.7 copy.44
  197.4 1.3 copy.48
  198.7 0.7 copy.46
  199.4 1.3 copy.49
  (24 shorter events, 0.2 us)
Async XLA Ops:
  3.2 6.5 %copy-start.7 = (bf16[1,128,2048]{2,1,0:T(8,128)(2,1)S(1)}, bf16[1,128,2048]{2,1,0:T(8,128)(2,1)}, u32[]{:S(2)}) copy-start(bf16[1,128,2048]{2,1,0:T(8,128)(2,1)} %param.9) | copy-start | bytes 1572868
  3.2 54.8 %all-to-all-start.1 = ((bf16[4,128,2048]{2,1,0:T(8,128)(2,1)}), bf16[4,128,2048]{2,1,0:T(8,128)(2,1)}, u32[]{:S(2)}, u32[]{:S(2)}) async-start(bf16[4,128,2048]{2,1,0:T(8,128)(2,1)} %broadcast_in_dim.2), calls=%async_computation.1 | async-start | bytes 4194304 | tf_op jit(solution)/shard_map/all_to_all | solution.py:150
  9.7 15.8 %collective-permute-start = (bf16[128,2048]{1,0:T(8,128)(2,1)S(1)}, bf16[128,2048]{1,0:T(8,128)(2,1)S(1)}, u32[]{:S(2)}, u32[]{:S(2)}) collective-permute-start(bf16[128,2048]{1,0:T(8,128)(2,1)S(1)} %bitcast.77), channel_id=1, source_target_pairs={{0,2},{1,3},{2,4},{3,5},{4,6},{5,7},{6,0},{7,1},{8,10},{9,11},{10,... | collective-permute-start | bytes 1572872 | tf_op jit(solution)/shard_map/ppermute | solution.py:156
  11.2 24.0 %collective-permute-start.1 = (bf16[128,2048]{1,0:T(8,128)(2,1)S(1)}, bf16[128,2048]{1,0:T(8,128)(2,1)S(1)}, u32[]{:S(2)}, u32[]{:S(2)}) collective-permute-start(bf16[128,2048]{1,0:T(8,128)(2,1)S(1)} %bitcast.78), channel_id=1, source_target_pairs={{0,4},{1,5},{2,6},{3,7},{4,0},{5,1},{6,2},{7,3},{8,12},{9,13},{10,... | collective-permute-start | bytes 1572872 | tf_op jit(solution)/shard_map/ppermute | solution.py:156
  12.7 22.6 %collective-permute-start.2 = (bf16[128,2048]{1,0:T(8,128)(2,1)S(1)}, bf16[128,2048]{1,0:T(8,128)(2,1)S(1)}, u32[]{:S(2)}, u32[]{:S(2)}) collective-permute-start(bf16[128,2048]{1,0:T(8,128)(2,1)S(1)} %bitcast.79), channel_id=1, source_target_pairs={{0,6},{1,7},{2,0},{3,1},{4,2},{5,3},{6,4},{7,5},{8,14},{9,15},{10,... | collective-permute-start | bytes 1572872 | tf_op jit(solution)/shard_map/ppermute | solution.py:156
  35.3 1.6 copy-start.2
  36.9 26.1 %collective-permute-start.3 = (bf16[4,128,2048]{2,1,0:T(8,128)(2,1)}, bf16[4,128,2048]{2,1,0:T(8,128)(2,1)}, u32[]{:S(2)}, u32[]{:S(2)}) collective-permute-start(bf16[4,128,2048]{2,1,0:T(8,128)(2,1)} %pad_maximum_fusion.1), channel_id=1, source_target_pairs={{0,1},{1,0},{2,3},{3,2},{4,5},{5,4},{6,7},{7,6},{8,9},{9,8},{10,11... | collective-permute-start | bytes 6291464 | tf_op jit(solution)/shard_map/ppermute | solution.py:159
  46.7 15.0 %copy-start.8 = (s32[1,14,3]{1,0,2:T(1,128)S(1)}, s32[1,14,3]{1,0,2:T(1,128)}, u32[]{:S(2)}) copy-start(s32[1,14,3]{1,0,2:T(1,128)} %param.11) | copy-start | bytes 508
  58.0 41.6 %all-to-all-start = ((bf16[8,3,4,128,128]{4,3,2,1,0:T(8,128)(2,1)}), bf16[8,3,4,128,128]{4,3,2,1,0:T(8,128)(2,1)S(1)}, u32[]{:S(2)}, u32[]{:S(2)}) async-start(bf16[8,3,4,128,128]{4,3,2,1,0:T(8,128)(2,1)} %pad_maximum_fusion), calls=%async_computation | async-start | bytes 6291456 | tf_op jit(solution)/shard_map/all_to_all | solution.py:190
  99.6 1.6 copy-start
  116.5 18.9 %all-to-all-start.2 = ((bf16[8,3,128,128]{3,2,1,0:T(8,128)(2,1)}), bf16[8,3,128,128]{3,2,1,0:T(8,128)(2,1)S(1)}, u32[]{:S(2)}, u32[]{:S(2)}) async-start(bf16[8,3,128,128]{3,2,1,0:T(8,128)(2,1)} %shard_map.85), calls=%async_computation.2 | async-start | bytes 1572864 | tf_op jit(solution)/shard_map/all_to_all | solution.py:204
  135.4 19.4 %all-to-all-start.3 = ((bf16[8,3,128,128]{3,2,1,0:T(8,128)(2,1)}), bf16[8,3,128,128]{3,2,1,0:T(8,128)(2,1)S(1)}, u32[]{:S(2)}, u32[]{:S(2)}) async-start(bf16[8,3,128,128]{3,2,1,0:T(8,128)(2,1)} %shard_map.86), calls=%async_computation.3 | async-start | bytes 1572864 | tf_op jit(solution)/shard_map/all_to_all | solution.py:204
  154.8 20.5 %all-to-all-start.4 = ((bf16[8,3,128,128]{3,2,1,0:T(8,128)(2,1)}), bf16[8,3,128,128]{3,2,1,0:T(8,128)(2,1)S(1)}, u32[]{:S(2)}, u32[]{:S(2)}) async-start(bf16[8,3,128,128]{3,2,1,0:T(8,128)(2,1)} %shard_map.87), calls=%async_computation.4 | async-start | bytes 1572864 | tf_op jit(solution)/shard_map/all_to_all | solution.py:204
  175.4 4.4 %copy-start.1 = (bf16[8,3,128,128]{3,2,0,1:T(8,128)(2,1)S(1)}, bf16[8,3,128,128]{3,2,0,1:T(8,128)(2,1)}, u32[]{:S(2)}) copy-start(bf16[8,3,128,128]{3,2,0,1:T(8,128)(2,1)} %copy.58) | copy-start | bytes 2359300
  175.4 16.9 %all-to-all-start.5 = ((bf16[8,3,128,128]{3,2,1,0:T(8,128)(2,1)}), bf16[8,3,128,128]{3,2,1,0:T(8,128)(2,1)S(1)}, u32[]{:S(2)}, u32[]{:S(2)}) async-start(bf16[8,3,128,128]{3,2,1,0:T(8,128)(2,1)} %shard_map.88), calls=%async_computation.5 | async-start | bytes 1572864 | tf_op jit(solution)/shard_map/all_to_all | solution.py:204
  194.0 1.4 copy-start.3
  194.0 1.3 copy-start.4
  194.0 1.3 copy-start.5
  194.0 1.3 copy-start.6

commit v7 on v5

--- a/solution.py
+++ b/solution.py
@@ -151,14 +151,16 @@
             lax.ppermute(out_weight, "dp", [(a, (a + s) % dp) for a in range(dp)])
             for s in range(1, dp)
         ]
-        head_weight = jnp.concatenate(got, axis=0)
-        columns = [(me - c) % dp for c in range(local_heads)]
+        order = (me - jnp.arange(dp)) % dp
+        head_weight = jnp.take(jnp.stack(got), order, axis=0).reshape(dp * HD, -1)
+        columns = [jnp.array(c, jnp.int32) for c in range(local_heads)]
         j = lax.axis_index("context")
         shifts = list(range(0, ctx, 2))
         mine = jnp.stack([local_cotangent] + [
             lax.ppermute(local_cotangent, "context", [(a, (a + s) % ctx) for a in range(ctx)])
             for s in shifts[1:]
         ])
+        head_weight, mine = lax.optimization_barrier((head_weight, mine))
         other = lax.ppermute(mine, "context", [(a, a ^ 1) for a in range(ctx)])
 
         def project(piece):

time: 199 us -> 187 us (0.940)
  the two profiles are of different devices: /device:TPU:24 before, /device:TPU:0 now
where the time goes in v7:
time: 187 us; the launch traced here: 186 us
  Pallas kernels  61.2 us (33%)
  waiting for transfers between devices  45.3 us (24%)
  starting transfers between devices  32.7 us (17%)
  local copies, waits for them, and re-layouts  23.9 us (13%)
  other arithmetic  15.6 us (8%)
  matrix products  6.53 us (3%)
    pallas_call x4, Pallas kernels, attention_grads(): pl.pallas_call(_attention_kernel, out_shape=out, grid_spec=pltpu.Prefetch...  61.2 us
    ppermute x3, waiting for transfers between devices, body(): lax.ppermute(local_cotangent, 'context', [(a, (a + s) % ctx) for a in ran...  20.2 us
    all_to_all x4, starting transfers between devices, body(): lax.all_to_all(grads, 'context', split_axis=0, concat_axis=0, tiled=True)  16.2 us
    ppermute x3, waiting for transfers between devices, body(): lax.ppermute(out_weight, 'dp', [(a, (a + s) % dp) for a in range(dp)])  15 us
    unnamed x25, local copies, waits for them, and re-layouts  10.5 us
    all_to_all x4, waiting for transfers between devices, body(): lax.all_to_all(grads, 'context', split_axis=0, concat_axis=0, tiled=True)  10 us
    ppermute x3, starting transfers between devices, body(): lax.ppermute(local_cotangent, 'context', [(a, (a + s) % ctx) for a in ran...  7.35 us
    dot_general x2, matrix products, project(): lax.dot_general(piece.reshape(-1, piece.shape[-1]), head_weight, (((1,),...  6.53 us
  transfers between devices with their start and end apart: 12, of which 3 were waited for; matrix products, arithmetic and copies ran while one was open for 19% of the time, Pallas kernels for 25%

profile of v7, /device:TPU:0, one launch (start us, length us, event | category | flops | bytes accessed | tf_op | source)
XLA Modules:
  0.0 186.2 jit_solution(2129892796902117126)
XLA Ops:
  0.6 3.0 %collective-permute-start.3 = (bf16[128,2048]{1,0:T(8,128)(2,1)}, bf16[128,2048]{1,0:T(8,128)(2,1)}, u32[]{:S(2)}, u32[]{:S(2)}) collective-permute-start(bf16[128,2048]{1,0:T(8,128)(2,1)} %bitcast.87), channel_id=1, source_target_pairs={{0,2},{1,3},{2,4},{3,5},{4,6},{5,7},{6,0},{7,1},{8,10},{9,11},{10,... | collective-permute-start | bytes 1572872 | tf_op jit(solution)/shard_map/ppermute | solution.py:160
  3.6 1.5 collective-permute-start.4
  5.1 1.6 collective-permute-start
  6.7 2.6 %collective-permute-start.1 = (bf16[128,2048]{1,0:T(8,128)(2,1)}, bf16[128,2048]{1,0:T(8,128)(2,1)}, u32[]{:S(2)}, u32[]{:S(2)}) collective-permute-start(bf16[128,2048]{1,0:T(8,128)(2,1)} %param.10), channel_id=1, source_target_pairs={{0,16},{8,24},{16,0},{24,8},{1,17},{9,25},{17,1},{25,9},{2,18},{10... | collective-permute-start | bytes 1572872 | tf_op jit(solution)/shard_map/ppermute | solution.py:151
  9.3 1.3 collective-permute-start.2
  10.7 1.6 copy.34
  12.3 0.7 copy.35
  12.9 1.6 copy.36
  14.6 0.7 copy.37
  15.2 1.6 copy.38
  16.9 1.3 copy.39
  18.2 3.2 %pad_maximum_fusion = bf16[8,3,4,128,128]{4,3,2,1,0:T(8,128)(2,1)} fusion(bf16[8,1,4,128,128]{4,3,2,1,0:T(8,128)(2,1)} %bitcast.81, bf16[8,1,4,128,128]{4,3,2,1,0:T(8,128)(2,1)S(1)} %bitcast.80, bf16[8,1,4,128,128]{4,3,2,1,0:T(8,128)(2,1)S(1)} %bitcast.79), kind=kLoop, calls=%fused_computation.1 | loop fusion | flops 3145728 | bytes 6291456 | tf_op jit(solution)/shard_map/stack | solution.py:194
  21.4 3.6 %all-to-all-start = ((bf16[8,3,4,128,128]{4,3,2,1,0:T(8,128)(2,1)}), bf16[8,3,4,128,128]{4,3,2,1,0:T(8,128)(2,1)S(1)}, u32[]{:S(2)}, u32[]{:S(2)}) async-start(bf16[8,3,4,128,128]{4,3,2,1,0:T(8,128)(2,1)} %pad_maximum_fusion), calls=%async_computation | async-start | bytes 6291456 | tf_op jit(solution)/shard_map/all_to_all | solution.py:195
  25.2 2.8 %collective-permute-start.5 = (bf16[128,2048]{1,0:T(8,128)(2,1)}, bf16[128,2048]{1,0:T(8,128)(2,1)}, u32[]{:S(2)}, u32[]{:S(2)}) collective-permute-start(bf16[128,2048]{1,0:T(8,128)(2,1)} %bitcast.89), channel_id=1, source_target_pairs={{0,6},{1,7},{2,0},{3,1},{4,2},{5,3},{6,4},{7,5},{8,14},{9,15},{10,... | collective-permute-start | bytes 1572872 | tf_op jit(solution)/shard_map/ppermute | solution.py:160
  28.0 15.0 %collective-permute-done.1 = bf16[128,2048]{1,0:T(8,128)(2,1)} collective-permute-done((bf16[128,2048]{1,0:T(8,128)(2,1)}, bf16[128,2048]{1,0:T(8,128)(2,1)}, u32[]{:S(2)}, u32[]{:S(2)}) %collective-permute-start.1) | collective-permute-done | bytes 524320 | tf_op jit(solution)/shard_map/ppermute | solution.py:151
  43.0 3.1 %pad_maximum_fusion.1 = bf16[4,128,2048]{2,1,0:T(8,128)(2,1)} fusion(bf16[1,128,2048]{2,1,0:T(8,128)(2,1)} %bitcast.13, bf16[1,128,2048]{2,1,0:T(8,128)(2,1)} %bitcast.12, bf16[1,128,2048]{2,1,0:T(8,128)(2,1)} %bitcast.11, bf16[1,128,2048]{2,1,0:T(8,128)(2,1)} %bitcast.86), kind=kLoop, calls=%fused_computation.2 | loop fusion | flops 3145728 | bytes 4194304 | tf_op jit(solution)/shard_map/stack | solution.py:155
  46.2 3.6 %gather_fusion = bf16[4,128,2048]{2,1,0:T(8,128)(2,1)} fusion(bf16[4,128,2048]{2,1,0:T(8,128)(2,1)} %pad_maximum_fusion.1, s32[1024]{0:T(1024)S(1)} %pad_clamp_fusion), kind=kCustom, calls=%fused_computation | custom fusion | bytes 4194320 | tf_op jit(solution)/shard_map/jit(_take)/gather | solution.py:155
  49.8 3.3 %bitcast_select_fusion = bf16[512,2048]{1,0:T(8,128)(2,1)} fusion(bf16[4,128,2048]{2,1,0:T(8,128)(2,1)} %gather_fusion, pred[512]{0:T(512)(128)(4,1)S(1)} %broadcast_bitcast_fusion), kind=kLoop, calls=%fused_computation.4 | loop fusion | flops 1048576 | bytes 4194816 | tf_op jit(solution)/shard_map/jit(_take)/select_n | solution.py:155
  53.0 20.2 %collective-permute-done.5 = bf16[128,2048]{1,0:T(8,128)(2,1)} collective-permute-done((bf16[128,2048]{1,0:T(8,128)(2,1)}, bf16[128,2048]{1,0:T(8,128)(2,1)}, u32[]{:S(2)}, u32[]{:S(2)}) %collective-permute-start.5) | collective-permute-done | bytes 524320 | tf_op jit(solution)/shard_map/ppermute | solution.py:160
  73.3 3.0 %pad_maximum_fusion.2 = bf16[4,128,2048]{2,1,0:T(8,128)(2,1)} fusion(bf16[1,128,2048]{2,1,0:T(8,128)(2,1)} %bitcast.19, bf16[1,128,2048]{2,1,0:T(8,128)(2,1)} %bitcast.18, bf16[1,128,2048]{2,1,0:T(8,128)(2,1)} %bitcast.17, bf16[1,128,2048]{2,1,0:T(8,128)(2,1)S(1)} %copy-done.7), kind=kLoop, calls=%fused_computation.3 | loop fusion | flops 3145728 | bytes 4194304 | tf_op jit(solution)/shard_map/stack | solution.py:159
  76.3 0.6 reshape_squeeze.15.rb_ref
  76.9 0.5 compare_select_fusion.10.pos_ref
  77.4 3.6 %convolution_convert_fusion.1 = bf16[512,512]{1,0:T(8,128)(2,1)S(1)} fusion(bf16[512,2048]{1,0:T(8,128)(2,1)} %bitcast.20, bf16[512,2048]{1,0:T(8,128)(2,1)} %bitcast_select_fusion), kind=kOutput, calls=%fused_computation.6 | convolution fusion | flops 1074003968 | bytes 4718592 | tf_op jit(solution)/shard_map/dot_general | solution.py:167
  81.1 2.9 %convolution_convert_fusion = bf16[512,512]{1,0:T(8,128)(2,1)S(1)} fusion(bf16[512,2048]{1,0:T(8,128)(2,1)} %bitcast.21, bf16[512,2048]{1,0:T(8,128)(2,1)S(1)} %copy-done.2), kind=kOutput, calls=%fused_computation.5 | convolution fusion | flops 1074003968 | bytes 4718592 | tf_op jit(solution)/shard_map/dot_general | solution.py:167
  84.0 1.0 pad_maximum_fusion.3.u_ref
  85.1 1.6 copy-done
  86.7 15.3 %shard_map.85 = bf16[8,3,128,128]{3,2,1,0:T(8,128)(2,1)} custom-call(s32[42]{0:T(128)} %reshape_squeeze.15.rb_ref, s32[8]{0:T(128)} %compare_select_fusion.10.pos_ref, s32[1]{0:T(128)} %constant.96.clone.1.col_ref, bf16[8,3,4,128,128]{4,3,2,1,0:T(8,128)(2,1)} %copy-done, bf16[1024,512]{1,0:T(8,128)(2,1)} %pad_maximum_fusion.3.u_ref), custom_call_target="tpu_custom_call" | custom-call | flops 905969664 | bytes 1835008 | tf_op jit(solution)/shard_map/pallas_call | solution.py:117
  102.0 3.5 %all-to-all-start.1 = ((bf16[8,3,128,128]{3,2,1,0:T(8,128)(2,1)}), bf16[8,3,128,128]{3,2,1,0:T(8,128)(2,1)S(1)}, u32[]{:S(2)}, u32[]{:S(2)}) async-start(bf16[8,3,128,128]{3,2,1,0:T(8,128)(2,1)} %shard_map.85), calls=%async_computation.1 | async-start | bytes 1572864 | tf_op jit(solution)/shard_map/all_to_all | solution.py:209
  105.5 15.3 %shard_map.86 = bf16[8,3,128,128]{3,2,1,0:T(8,128)(2,1)} custom-call(s32[42]{0:T(128)} %reshape_squeeze.15.rb_ref, s32[8]{0:T(128)} %compare_select_fusion.10.pos_ref, s32[1]{0:T(128)} %constant.100.clone.1.col_ref, bf16[8,3,4,128,128]{4,3,2,1,0:T(8,128)(2,1)} %copy-done, bf16[1024,512]{1,0:T(8,128)(2,1)} %pad_maximum_fusion.3.u_ref), custom_call_target="tpu_custom_call" | custom-call | flops 905969664 | bytes 1835008 | tf_op jit(solution)/shard_map/pallas_call | solution.py:117
  120.9 4.1 %all-to-all-start.2 = ((bf16[8,3,128,128]{3,2,1,0:T(8,128)(2,1)}), bf16[8,3,128,128]{3,2,1,0:T(8,128)(2,1)S(1)}, u32[]{:S(2)}, u32[]{:S(2)}) async-start(bf16[8,3,128,128]{3,2,1,0:T(8,128)(2,1)} %shard_map.86), calls=%async_computation.2 | async-start | bytes 1572864 | tf_op jit(solution)/shard_map/all_to_all | solution.py:209
  125.0 15.3 %shard_map.87 = bf16[8,3,128,128]{3,2,1,0:T(8,128)(2,1)} custom-call(s32[42]{0:T(128)} %reshape_squeeze.15.rb_ref, s32[8]{0:T(128)} %compare_select_fusion.10.pos_ref, s32[1]{0:T(128)} %constant.101.clone.1.col_ref, bf16[8,3,4,128,128]{4,3,2,1,0:T(8,128)(2,1)} %copy-done, bf16[1024,512]{1,0:T(8,128)(2,1)} %pad_maximum_fusion.3.u_ref), custom_call_target="tpu_custom_call" | custom-call | flops 905969664 | bytes 1835008 | tf_op jit(solution)/shard_map/pallas_call | solution.py:117
  140.3 4.2 %all-to-all-start.3 = ((bf16[8,3,128,128]{3,2,1,0:T(8,128)(2,1)}), bf16[8,3,128,128]{3,2,1,0:T(8,128)(2,1)S(1)}, u32[]{:S(2)}, u32[]{:S(2)}) async-start(bf16[8,3,128,128]{3,2,1,0:T(8,128)(2,1)} %shard_map.87), calls=%async_computation.3 | async-start | bytes 1572864 | tf_op jit(solution)/shard_map/all_to_all | solution.py:209
  144.5 15.3 %shard_map.88 = bf16[8,3,128,128]{3,2,1,0:T(8,128)(2,1)} custom-call(s32[42]{0:T(128)} %reshape_squeeze.15.rb_ref, s32[8]{0:T(128)} %compare_select_fusion.10.pos_ref, s32[1]{0:T(128)} %constant.102.clone.1.col_ref, bf16[8,3,4,128,128]{4,3,2,1,0:T(8,128)(2,1)} %copy-done, bf16[1024,512]{1,0:T(8,128)(2,1)} %pad_maximum_fusion.3.u_ref), custom_call_target="tpu_custom_call" | custom-call | flops 905969664 | bytes 1835008 | tf_op jit(solution)/shard_map/pallas_call | solution.py:117
  159.8 0.9 copy.58
  160.8 4.3 %all-to-all-start.4 = ((bf16[8,3,128,128]{3,2,1,0:T(8,128)(2,1)}), bf16[8,3,128,128]{3,2,1,0:T(8,128)(2,1)S(1)}, u32[]{:S(2)}, u32[]{:S(2)}) async-start(bf16[8,3,128,128]{3,2,1,0:T(8,128)(2,1)} %shard_map.88), calls=%async_computation.4 | async-start | bytes 1572864 | tf_op jit(solution)/shard_map/all_to_all | solution.py:209
  165.2 0.8 slice_bitcast_fusion.3
  166.0 0.9 slice_bitcast_fusion.2
  166.9 0.9 slice_bitcast_fusion.1
  167.8 10.0 %all-to-all-done.4 = bf16[8,3,128,128]{3,2,1,0:T(8,128)(2,1)S(1)} async-done(((bf16[8,3,128,128]{3,2,1,0:T(8,128)(2,1)}), bf16[8,3,128,128]{3,2,1,0:T(8,128)(2,1)S(1)}, u32[]{:S(2)}, u32[]{:S(2)}) %all-to-all-start.4) | async-done | bytes 786464 | tf_op jit(solution)/shard_map/all_to_all | solution.py:209
  177.8 0.8 slice_bitcast_fusion
  178.6 0.1 pad_maximum_fusion.6
  178.8 0.7 copy.47
  179.5 1.3 copy.50
  180.8 1.4 pad_maximum_fusion.4
  182.2 0.7 copy.44
  182.9 1.3 copy.48
  184.2 0.7 copy.46
  184.8 1.3 copy.49
  (34 shorter events, 0.4 us)
Async XLA Ops:
  0.6 52.4 %collective-permute-start.3 = (bf16[128,2048]{1,0:T(8,128)(2,1)}, bf16[128,2048]{1,0:T(8,128)(2,1)}, u32[]{:S(2)}, u32[]{:S(2)}) collective-permute-start(bf16[128,2048]{1,0:T(8,128)(2,1)} %bitcast.87), channel_id=1, source_target_pairs={{0,2},{1,3},{2,4},{3,5},{4,6},{5,7},{6,0},{7,1},{8,10},{9,11},{10,... | collective-permute-start | bytes 1572872 | tf_op jit(solution)/shard_map/ppermute | solution.py:160
  3.6 49.4 %collective-permute-start.4 = (bf16[128,2048]{1,0:T(8,128)(2,1)}, bf16[128,2048]{1,0:T(8,128)(2,1)}, u32[]{:S(2)}, u32[]{:S(2)}) collective-permute-start(bf16[128,2048]{1,0:T(8,128)(2,1)} %bitcast.88), channel_id=1, source_target_pairs={{0,4},{1,5},{2,6},{3,7},{4,0},{5,1},{6,2},{7,3},{8,12},{9,13},{10,... | collective-permute-start | bytes 1572872 | tf_op jit(solution)/shard_map/ppermute | solution.py:160
  5.1 20.0 %collective-permute-start = (bf16[128,2048]{1,0:T(8,128)(2,1)}, bf16[128,2048]{1,0:T(8,128)(2,1)}, u32[]{:S(2)}, u32[]{:S(2)}) collective-permute-start(bf16[128,2048]{1,0:T(8,128)(2,1)} %param.10), channel_id=1, source_target_pairs={{0,8},{8,16},{16,24},{24,0},{1,9},{9,17},{17,25},{25,1},{2,10},{10... | collective-permute-start | bytes 1572872 | tf_op jit(solution)/shard_map/ppermute | solution.py:151
  6.7 36.3 %collective-permute-start.1 = (bf16[128,2048]{1,0:T(8,128)(2,1)}, bf16[128,2048]{1,0:T(8,128)(2,1)}, u32[]{:S(2)}, u32[]{:S(2)}) collective-permute-start(bf16[128,2048]{1,0:T(8,128)(2,1)} %param.10), channel_id=1, source_target_pairs={{0,16},{8,24},{16,0},{24,8},{1,17},{9,25},{17,1},{25,9},{2,18},{10... | collective-permute-start | bytes 1572872 | tf_op jit(solution)/shard_map/ppermute | solution.py:151
  9.3 33.7 %collective-permute-start.2 = (bf16[128,2048]{1,0:T(8,128)(2,1)}, bf16[128,2048]{1,0:T(8,128)(2,1)}, u32[]{:S(2)}, u32[]{:S(2)}) collective-permute-start(bf16[128,2048]{1,0:T(8,128)(2,1)} %param.10), channel_id=1, source_target_pairs={{0,24},{8,0},{16,8},{24,16},{1,25},{9,1},{17,9},{25,17},{2,26},{10... | collective-permute-start | bytes 1572872 | tf_op jit(solution)/shard_map/ppermute | solution.py:151
  21.4 63.7 %all-to-all-start = ((bf16[8,3,4,128,128]{4,3,2,1,0:T(8,128)(2,1)}), bf16[8,3,4,128,128]{4,3,2,1,0:T(8,128)(2,1)S(1)}, u32[]{:S(2)}, u32[]{:S(2)}) async-start(bf16[8,3,4,128,128]{4,3,2,1,0:T(8,128)(2,1)} %pad_maximum_fusion), calls=%async_computation | async-start | bytes 6291456 | tf_op jit(solution)/shard_map/all_to_all | solution.py:195
  25.2 48.1 %collective-permute-start.5 = (bf16[128,2048]{1,0:T(8,128)(2,1)}, bf16[128,2048]{1,0:T(8,128)(2,1)}, u32[]{:S(2)}, u32[]{:S(2)}) collective-permute-start(bf16[128,2048]{1,0:T(8,128)(2,1)} %bitcast.89), channel_id=1, source_target_pairs={{0,6},{1,7},{2,0},{3,1},{4,2},{5,3},{6,4},{7,5},{8,14},{9,15},{10,... | collective-permute-start | bytes 1572872 | tf_op jit(solution)/shard_map/ppermute | solution.py:160
  49.8 23.5 %copy-start.7 = (bf16[1,128,2048]{2,1,0:T(8,128)(2,1)S(1)}, bf16[1,128,2048]{2,1,0:T(8,128)(2,1)}, u32[]{:S(2)}) copy-start(bf16[1,128,2048]{2,1,0:T(8,128)(2,1)} %param.9) | copy-start | bytes 1572868
  73.3 3.0 %copy-start.8 = (s32[1,14,3]{1,0,2:T(1,128)S(1)}, s32[1,14,3]{1,0,2:T(1,128)}, u32[]{:S(2)}) copy-start(s32[1,14,3]{1,0,2:T(1,128)} %param.11) | copy-start | bytes 508
  76.2 4.9 %collective-permute-start.6 = (bf16[4,128,2048]{2,1,0:T(8,128)(2,1)}, bf16[4,128,2048]{2,1,0:T(8,128)(2,1)}, u32[]{:S(2)}, u32[]{:S(2)}) collective-permute-start(bf16[4,128,2048]{2,1,0:T(8,128)(2,1)} %pad_maximum_fusion.2), channel_id=1, source_target_pairs={{0,1},{1,0},{2,3},{3,2},{4,5},{5,4},{6,7},{7,6},{8,9},{9,8},{10,11... | collective-permute-start | bytes 6291464 | tf_op jit(solution)/shard_map/ppermute | solution.py:164
  77.4 3.7 %copy-start.2 = (bf16[512,2048]{1,0:T(8,128)(2,1)S(1)}, bf16[512,2048]{1,0:T(8,128)(2,1)}, u32[]{:S(2)}) copy-start(bf16[512,2048]{1,0:T(8,128)(2,1)} %bitcast_select_fusion) | copy-start | bytes 6291460
  85.1 1.6 copy-start
  102.0 18.9 %all-to-all-start.1 = ((bf16[8,3,128,128]{3,2,1,0:T(8,128)(2,1)}), bf16[8,3,128,128]{3,2,1,0:T(8,128)(2,1)S(1)}, u32[]{:S(2)}, u32[]{:S(2)}) async-start(bf16[8,3,128,128]{3,2,1,0:T(8,128)(2,1)} %shard_map.85), calls=%async_computation.1 | async-start | bytes 1572864 | tf_op jit(solution)/shard_map/all_to_all | solution.py:209
  120.9 19.4 %all-to-all-start.2 = ((bf16[8,3,128,128]{3,2,1,0:T(8,128)(2,1)}), bf16[8,3,128,128]{3,2,1,0:T(8,128)(2,1)S(1)}, u32[]{:S(2)}, u32[]{:S(2)}) async-start(bf16[8,3,128,128]{3,2,1,0:T(8,128)(2,1)} %shard_map.86), calls=%async_computation.2 | async-start | bytes 1572864 | tf_op jit(solution)/shard_map/all_to_all | solution.py:209
  140.3 20.5 %all-to-all-start.3 = ((bf16[8,3,128,128]{3,2,1,0:T(8,128)(2,1)}), bf16[8,3,128,128]{3,2,1,0:T(8,128)(2,1)S(1)}, u32[]{:S(2)}, u32[]{:S(2)}) async-start(bf16[8,3,128,128]{3,2,1,0:T(8,128)(2,1)} %shard_map.87), calls=%async_computation.3 | async-start | bytes 1572864 | tf_op jit(solution)/shard_map/all_to_all | solution.py:209
  160.8 4.4 %copy-start.1 = (bf16[8,3,128,128]{3,2,0,1:T(8,128)(2,1)S(1)}, bf16[8,3,128,128]{3,2,0,1:T(8,128)(2,1)}, u32[]{:S(2)}) copy-start(bf16[8,3,128,128]{3,2,0,1:T(8,128)(2,1)} %copy.58) | copy-start | bytes 2359300
  160.8 16.9 %all-to-all-start.4 = ((bf16[8,3,128,128]{3,2,1,0:T(8,128)(2,1)}), bf16[8,3,128,128]{3,2,1,0:T(8,128)(2,1)S(1)}, u32[]{:S(2)}, u32[]{:S(2)}) async-start(bf16[8,3,128,128]{3,2,1,0:T(8,128)(2,1)} %shard_map.88), calls=%async_computation.4 | async-start | bytes 1572864 | tf_op jit(solution)/shard_map/all_to_all | solution.py:209
  179.4 1.4 copy-start.3
  179.5 1.3 copy-start.4
  179.5 1.3 copy-start.5
  179.5 1.3 copy-start.6

commit v8 on v4

--- a/solution.py
+++ b/solution.py
@@ -130,6 +130,21 @@
     )(random_ids.reshape(-1), stacked, upstream)
 
 
+def _assemble_kernel(*refs):
+    pieces, outs = refs[:-3], refs[-3:]
+    parts = pieces[0].shape[0]
+    for c, piece in enumerate(pieces):
+        for source in range(parts):
+            start = (c * parts + source) * HD
+            for g, out in enumerate(outs):
+                out[0, :, start:start + HD] = piece[source, g]
+
+
+def assemble(pieces, tokens, width):
+    out = jax.ShapeDtypeStruct((1, tokens, width), jnp.bfloat16)
+    return pl.pallas_call(_assemble_kernel, out_shape=(out, out, out))(*pieces)
+
+
 def body(queries, key_rows, value_rows, cotangent, out_weight, random_blocks):
     dp = lax.axis_size("dp")
     ctx = lax.axis_size("context")
@@ -195,8 +210,10 @@
         else:
             grads = attention_grads(moved, head_upstream[c], 0, random_blocks[0])
         back = lax.all_to_all(grads, "context", split_axis=0, concat_axis=0, tiled=True)
-        pieces.append(back.transpose(1, 2, 0, 3))
-
+        pieces.append(back if strided else back.transpose(1, 2, 0, 3))
+
+    if strided:
+        return assemble(pieces, tokens, width)
     outs = []
     for g in range(3):
         joined = jnp.stack([piece[g] for piece in pieces], axis=1 if strided else 2)

time: 179 us -> 174 us (0.972)
  blocking collectives: 0 us -> 16.9 us
  local copies, waits for them, and re-layouts: 36 us -> 25.7 us
  waiting for transfers between devices: 29.1 us -> 19.2 us
  starting transfers between devices: 31.9 us -> 27.5 us
  Pallas kernels: 61.1 us -> 65.4 us
    all_to_all x0 -> x1, blocking collectives: none -> 16.9 us  [body(): lax.all_to_all(grads, 'context', split_axis=0, concat_axis=0, tiled=True)]
    all_to_all x4 -> x3, waiting for transfers between devices: 9.98 us -> 0.01 us  [body(): lax.all_to_all(grads, 'context', split_axis=0, concat_axis=0, tiled=True)]
    another operation x7 -> x0, local copies, waits for them, and re-layouts: 5.39 us -> none  [body(): joined = jnp.stack([piece[g] for piece in pieces], axis=1 if strided else 2)]
    pallas_call x0 -> x1, Pallas kernels: none -> 4.36 us  [assemble(): return pl.pallas_call(_assemble_kernel, out_shape=(out, out, out))(*pieces)]
    all_to_all x4 -> x3, starting transfers between devices: 16.6 us -> 12.3 us  [body(): lax.all_to_all(grads, 'context', split_axis=0, concat_axis=0, tiled=True)]
    unnamed x31 -> x24, local copies, waits for them, and re-layouts: 18 us -> 14 us
  transfers between devices with their start and end apart: 12 -> 11, of which waited for: 4 -> 3; matrix products, arithmetic and copies ran while one was open for 25% -> 23% of each run, Pallas kernels for 26% -> 27%
where the time goes in v8:
time: 174 us; the launch traced here: 172 us
  Pallas kernels  65.4 us (38%)
  starting transfers between devices  27.5 us (16%)
  local copies, waits for them, and re-layouts  25.7 us (15%)
  waiting for transfers between devices  19.2 us (11%)
  blocking collectives  16.9 us (10%)
  other arithmetic  13.6 us (8%)
  matrix products  3.34 us (2%)
    pallas_call x4, Pallas kernels, attention_grads(): pl.pallas_call(_attention_kernel, out_shape=out, grid_spec=pltpu.Prefetch...  61.1 us
    ppermute x3, waiting for transfers between devices, body(): lax.ppermute(out_weight, 'dp', [(a, (a + s) % dp) for a in range(dp)])  18.7 us
    all_to_all x1, blocking collectives, body(): lax.all_to_all(grads, 'context', split_axis=0, concat_axis=0, tiled=True)  16.9 us
    unnamed x24, local copies, waits for them, and re-layouts  14 us
    all_to_all x3, starting transfers between devices, body(): lax.all_to_all(grads, 'context', split_axis=0, concat_axis=0, tiled=True)  12.3 us
    ppermute x3, starting transfers between devices, body(): lax.ppermute(local_cotangent, 'context', [(a, (a + s) % ctx) for a in ran...  5.94 us
    ppermute x3, starting transfers between devices, body(): lax.ppermute(out_weight, 'dp', [(a, (a + s) % dp) for a in range(dp)])  5.54 us
    pallas_call x1, Pallas kernels, assemble(): return pl.pallas_call(_assemble_kernel, out_shape=(out, out, out))(*pieces)  4.36 us
  transfers between devices with their start and end apart: 11, of which 3 were waited for; matrix products, arithmetic and copies ran while one was open for 23% of the time, Pallas kernels for 27%

profile of v8, /device:TPU:0, one launch (start us, length us, event | category | flops | bytes accessed | tf_op | source)
XLA Modules:
  0.0 172.5 jit_solution(9083860579437782589)
XLA Ops:
  0.6 3.0 %collective-permute-start = (bf16[128,2048]{1,0:T(8,128)(2,1)}, bf16[128,2048]{1,0:T(8,128)(2,1)}, u32[]{:S(2)}, u32[]{:S(2)}) collective-permute-start(bf16[128,2048]{1,0:T(8,128)(2,1)} %bitcast.43), channel_id=1, source_target_pairs={{0,2},{1,3},{2,4},{3,5},{4,6},{5,7},{6,0},{7,1},{8,10},{9,11},{10,... | collective-permute-start | bytes 1572872 | tf_op jit(solution)/shard_map/ppermute | solution.py:170
  3.6 1.5 collective-permute-start.1
  5.2 1.4 collective-permute-start.2
  6.6 1.6 collective-permute-start.4
  8.2 2.6 %collective-permute-start.5 = (bf16[128,2048]{1,0:T(8,128)(2,1)}, bf16[128,2048]{1,0:T(8,128)(2,1)}, u32[]{:S(2)}, u32[]{:S(2)}) collective-permute-start(bf16[128,2048]{1,0:T(8,128)(2,1)} %param.10), channel_id=1, source_target_pairs={{0,16},{8,24},{16,0},{24,8},{1,17},{9,25},{17,1},{25,9},{2,18},{10... | collective-permute-start | bytes 1572872 | tf_op jit(solution)/shard_map/ppermute | solution.py:162
  10.8 1.6 copy.11
  12.4 0.7 copy.12
  13.1 0.7 copy.13
  13.7 0.7 copy.14
  14.4 1.6 copy.15
  16.0 1.3 copy.16
  17.3 3.2 %pad_maximum_fusion = bf16[8,3,4,128,128]{4,3,2,1,0:T(8,128)(2,1)} fusion(bf16[8,1,4,128,128]{4,3,2,1,0:T(8,128)(2,1)} %bitcast.41, bf16[8,1,4,128,128]{4,3,2,1,0:T(8,128)(2,1)S(1)} %bitcast.40, bf16[8,1,4,128,128]{4,3,2,1,0:T(8,128)(2,1)S(1)} %bitcast.39), kind=kLoop, calls=%fused_computation.2 | loop fusion | flops 3145728 | bytes 6291456 | tf_op jit(solution)/shard_map/stack | solution.py:201
  20.6 3.8 %all-to-all-start = ((bf16[8,3,4,128,128]{4,3,2,1,0:T(8,128)(2,1)}), bf16[8,3,4,128,128]{4,3,2,1,0:T(8,128)(2,1)S(1)}, u32[]{:S(2)}, u32[]{:S(2)}) async-start(bf16[8,3,4,128,128]{4,3,2,1,0:T(8,128)(2,1)} %pad_maximum_fusion), calls=%async_computation | async-start | bytes 6291456 | tf_op jit(solution)/shard_map/all_to_all | solution.py:202
  24.5 0.1 copy.10
  24.6 0.6 reshape_squeeze.15.rb_ref
  25.2 0.1 broadcast_bitcast_fusion
  25.3 1.9 %constant_dynamic-update-slice_fusion.4 = bf16[8,128,2048]{2,1,0:T(8,128)(2,1)} fusion(bf16[1,128,2048]{2,1,0:T(8,128)(2,1)} %param.9), kind=kLoop, calls=%fused_computation.12 | loop fusion | bytes 1048576
  27.2 0.0 collective-permute-done
  27.2 1.4 collective-permute-start.6
  28.6 0.0 collective-permute-done.1
  28.6 0.4 collective-permute-done.2
  29.0 3.1 %pad_maximum_fusion.1 = bf16[4,128,2048]{2,1,0:T(8,128)(2,1)} fusion(bf16[1,128,2048]{2,1,0:T(8,128)(2,1)} %bitcast.13, bf16[1,128,2048]{2,1,0:T(8,128)(2,1)} %bitcast.12, bf16[1,128,2048]{2,1,0:T(8,128)(2,1)} %bitcast.11, bf16[1,128,2048]{2,1,0:T(8,128)(2,1)} %param.9), kind=kLoop, calls=%fused_computation.3 | loop fusion | flops 3145728 | bytes 4194304 | tf_op jit(solution)/shard_map/stack | solution.py:169
  32.2 1.9 %constant_dynamic-update-slice_fusion.3 = bf16[8,128,2048]{2,1,0:T(8,128)(2,1)} fusion(bf16[8,128,2048]{2,1,0:T(8,128)(2,1)} %constant_dynamic-update-slice_fusion.4, bf16[128,2048]{1,0:T(8,128)(2,1)} %collective-permute-done), kind=kLoop, calls=%fused_computation.11 | loop fusion | bytes 1048576
  34.1 0.0 collective-permute-done.4
  34.1 10.1 %collective-permute-done.5 = bf16[128,2048]{1,0:T(8,128)(2,1)} collective-permute-done((bf16[128,2048]{1,0:T(8,128)(2,1)}, bf16[128,2048]{1,0:T(8,128)(2,1)}, u32[]{:S(2)}, u32[]{:S(2)}) %collective-permute-start.5) | collective-permute-done | bytes 524320 | tf_op jit(solution)/shard_map/ppermute | solution.py:162
  44.2 8.6 %collective-permute-done.6 = bf16[128,2048]{1,0:T(8,128)(2,1)S(1)} collective-permute-done((bf16[128,2048]{1,0:T(8,128)(2,1)}, bf16[128,2048]{1,0:T(8,128)(2,1)S(1)}, u32[]{:S(2)}, u32[]{:S(2)}) %collective-permute-start.6) | collective-permute-done | bytes 524320 | tf_op jit(solution)/shard_map/ppermute | solution.py:162
  52.8 2.8 %pad_maximum_fusion.2 = bf16[4,128,2048]{2,1,0:T(8,128)(2,1)} fusion(bf16[1,128,2048]{2,1,0:T(8,128)(2,1)S(1)} %bitcast.48, bf16[1,128,2048]{2,1,0:T(8,128)(2,1)} %bitcast.17, bf16[1,128,2048]{2,1,0:T(8,128)(2,1)} %bitcast.16, bf16[1,128,2048]{2,1,0:T(8,128)(2,1)S(1)} %bitcast.47), kind=kLoop, calls=%fused_computation.4 | loop fusion | flops 3145728 | bytes 4194304 | tf_op jit(solution)/shard_map/stack | solution.py:166
  55.5 3.7 %gather_fusion = bf16[4,128,2048]{2,1,0:T(8,128)(2,1)} fusion(bf16[4,128,2048]{2,1,0:T(8,128)(2,1)} %pad_maximum_fusion.2, s32[1024]{0:T(1024)S(1)} %pad_clamp_fusion.1), kind=kCustom, calls=%fused_computation | custom fusion | bytes 4194320 | tf_op jit(solution)/shard_map/jit(_take)/gather | solution.py:166
  59.3 1.9 %constant_dynamic-update-slice_fusion.2 = bf16[8,128,2048]{2,1,0:T(8,128)(2,1)} fusion(bf16[8,128,2048]{2,1,0:T(8,128)(2,1)} %constant_dynamic-update-slice_fusion.3, bf16[128,2048]{1,0:T(8,128)(2,1)} %collective-permute-done.1), kind=kLoop, calls=%fused_computation.10 | loop fusion | bytes 1048576
  61.1 1.9 %constant_dynamic-update-slice_fusion.1 = bf16[8,128,2048]{2,1,0:T(8,128)(2,1)} fusion(bf16[8,128,2048]{2,1,0:T(8,128)(2,1)} %constant_dynamic-update-slice_fusion.2, bf16[128,2048]{1,0:T(8,128)(2,1)} %collective-permute-done.2), kind=kLoop, calls=%fused_computation.9 | loop fusion | bytes 1048576
  63.1 2.0 %broadcast_select_fusion = bf16[4,128,2048]{2,1,0:T(8,128)(2,1)S(1)} fusion(bf16[4,128,2048]{2,1,0:T(8,128)(2,1)} %gather_fusion, pred[4]{0:T(512)(128)(4,1)S(1)} %compare_and_fusion), kind=kLoop, calls=%fused_computation.5 | loop fusion | flops 1048576 | bytes 4194308 | tf_op jit(solution)/shard_map/jit(_take)/select_n | solution.py:166
  65.1 0.8 copy-done.6
  65.9 1.8 %constant_dynamic-update-slice_fusion = bf16[8,128,2048]{2,1,0:T(8,128)(2,1)S(1)} fusion(bf16[8,128,2048]{2,1,0:T(8,128)(2,1)S(1)} %copy-done.6, bf16[4,128,2048]{2,1,0:T(8,128)(2,1)} %collective-permute-done.3), kind=kLoop, calls=%fused_computation.8 | loop fusion | bytes 4194304 | tf_op jit(solution)/shard_map/concatenate | solution.py:174
  67.7 3.3 %convolution_convert_fusion = bf16[1024,512]{1,0:T(8,128)(2,1)} fusion(bf16[1024,2048]{1,0:T(8,128)(2,1)S(1)} %bitcast.49, bf16[512,2048]{1,0:T(8,128)(2,1)S(1)} %bitcast.42), kind=kOutput, calls=%fused_computation.6 | convolution fusion | flops 2148007936 | bytes 7340032 | tf_op jit(solution)/shard_map/dot_general | solution.py:175
  71.0 2.8 %gather_fusion.1 = bf16[8,128,512]{2,1,0:T(8,128)(2,1)} fusion(bf16[8,128,512]{2,1,0:T(8,128)(2,1)} %bitcast.46, s32[1024]{0:T(1024)S(1)} %pad_clamp_fusion), kind=kCustom, calls=%fused_computation.1 | custom fusion | bytes 2097184 | tf_op jit(solution)/shard_map/jit(_take)/gather | solution.py:184
  73.8 2.4 %bitcast_select_fusion.u_ref = bf16[1024,512]{1,0:T(8,128)(2,1)} fusion(bf16[8,128,512]{2,1,0:T(8,128)(2,1)} %gather_fusion.1, pred[1024]{0:T(1024)(128)(4,1)S(1)} %broadcast_bitcast_fusion), kind=kLoop, calls=%fused_computation.7 | loop fusion | flops 524288 | bytes 2098176 | tf_op jit(solution)/shard_map/jit(_take)/select_n | solution.py:184
  76.3 1.6 copy-done
  77.9 15.3 %shard_map.88 = bf16[8,3,128,128]{3,2,1,0:T(8,128)(2,1)} custom-call(s32[42]{0:T(128)} %reshape_squeeze.15.rb_ref, bf16[8,3,4,128,128]{4,3,2,1,0:T(8,128)(2,1)} %copy-done, bf16[1024,512]{1,0:T(8,128)(2,1)} %bitcast_select_fusion.u_ref), custom_call_target="tpu_custom_call" | custom-call | flops 905969664 | bytes 1835008 | tf_op jit(solution)/shard_map/pallas_call | solution.py:113
  93.2 3.8 %all-to-all-start.4 = ((bf16[8,3,128,128]{3,2,1,0:T(8,128)(2,1)}), bf16[8,3,128,128]{3,2,1,0:T(8,128)(2,1)S(1)}, u32[]{:S(2)}, u32[]{:S(2)}) async-start(bf16[8,3,128,128]{3,2,1,0:T(8,128)(2,1)} %shard_map.88), calls=%async_computation.4 | async-start | bytes 1572864 | tf_op jit(solution)/shard_map/all_to_all | solution.py:212
  97.0 15.3 %shard_map.87 = bf16[8,3,128,128]{3,2,1,0:T(8,128)(2,1)} custom-call(s32[42]{0:T(128)} %reshape_squeeze.15.rb_ref, bf16[8,3,4,128,128]{4,3,2,1,0:T(8,128)(2,1)} %copy-done, bf16[1024,512]{1,0:T(8,128)(2,1)} %bitcast_select_fusion.u_ref), custom_call_target="tpu_custom_call" | custom-call | flops 905969664 | bytes 1835008 | tf_op jit(solution)/shard_map/pallas_call | solution.py:113
  112.3 0.0 all-to-all-done.4.refs_3_
  112.3 4.2 %all-to-all-start.3 = ((bf16[8,3,128,128]{3,2,1,0:T(8,128)(2,1)}), bf16[8,3,128,128]{3,2,1,0:T(8,128)(2,1)S(1)}, u32[]{:S(2)}, u32[]{:S(2)}) async-start(bf16[8,3,128,128]{3,2,1,0:T(8,128)(2,1)} %shard_map.87), calls=%async_computation.3 | async-start | bytes 1572864 | tf_op jit(solution)/shard_map/all_to_all | solution.py:212
  116.5 15.3 %shard_map.86 = bf16[8,3,128,128]{3,2,1,0:T(8,128)(2,1)} custom-call(s32[42]{0:T(128)} %reshape_squeeze.15.rb_ref, bf16[8,3,4,128,128]{4,3,2,1,0:T(8,128)(2,1)} %copy-done, bf16[1024,512]{1,0:T(8,128)(2,1)} %bitcast_select_fusion.u_ref), custom_call_target="tpu_custom_call" | custom-call | flops 905969664 | bytes 1835008 | tf_op jit(solution)/shard_map/pallas_call | solution.py:113
  131.8 4.2 %all-to-all-start.2 = ((bf16[8,3,128,128]{3,2,1,0:T(8,128)(2,1)}), bf16[8,3,128,128]{3,2,1,0:T(8,128)(2,1)S(1)}, u32[]{:S(2)}, u32[]{:S(2)}) async-start(bf16[8,3,128,128]{3,2,1,0:T(8,128)(2,1)} %shard_map.86), calls=%async_computation.2 | async-start | bytes 1572864 | tf_op jit(solution)/shard_map/all_to_all | solution.py:212
  136.0 15.3 %shard_map.85 = bf16[8,3,128,128]{3,2,1,0:T(8,128)(2,1)} custom-call(s32[42]{0:T(128)} %reshape_squeeze.15.rb_ref, bf16[8,3,4,128,128]{4,3,2,1,0:T(8,128)(2,1)} %copy-done, bf16[1024,512]{1,0:T(8,128)(2,1)} %bitcast_select_fusion.u_ref), custom_call_target="tpu_custom_call" | custom-call | flops 905969664 | bytes 1835008 | tf_op jit(solution)/shard_map/pallas_call | solution.py:113
  151.3 0.0 all-to-all-done.2.refs_1_
  151.3 16.9 %all_to_all.25.refs_0_ = bf16[8,3,128,128]{3,2,1,0:T(8,128)(2,1)} all-to-all(bf16[8,3,128,128]{3,2,1,0:T(8,128)(2,1)} %shard_map.85), channel_id=1, replica_groups=mesh['dp'=4,'context'=8] {'context'}, dimensions={0} | all-to-all | bytes 1572864 | tf_op jit(solution)/shard_map/all_to_all | solution.py:212
  168.1 4.4 %shard_map.89 = (bf16[1,128,4096]{2,1,0:T(8,128)(2,1)}, bf16[1,128,4096]{2,1,0:T(8,128)(2,1)}, bf16[1,128,4096]{2,1,0:T(8,128)(2,1)}) custom-call(bf16[8,3,128,128]{3,2,1,0:T(8,128)(2,1)} %all_to_all.25.refs_0_, bf16[8,3,128,128]{3,2,1,0:T(8,128)(2,1)} %copy-done.3, bf16[8,3,128,128]{3,2,1,0:T(8,128)(2,1)} %copy-done.2, bf16[8,3,128,128]{3,2,1,0:T(8,128)(2,1)} %copy-done.1), custom_call_target="tpu_custom_call" | custom-call | tf_op jit(solution)/shard_map/pallas_call | solution.py:145
  (24 shorter events, 0.1 us)
Async XLA Ops:
  0.6 12.4 %copy-start.4 = (bf16[1,128,4096]{2,1,0:T(8,128)(2,1)S(1)}, bf16[1,128,4096]{2,1,0:T(8,128)(2,1)}, u32[]{:S(2)}) copy-start(bf16[1,128,4096]{2,1,0:T(8,128)(2,1)} %param.7) | copy-start | bytes 3145732
  0.6 26.6 %collective-permute-start = (bf16[128,2048]{1,0:T(8,128)(2,1)}, bf16[128,2048]{1,0:T(8,128)(2,1)}, u32[]{:S(2)}, u32[]{:S(2)}) collective-permute-start(bf16[128,2048]{1,0:T(8,128)(2,1)} %bitcast.43), channel_id=1, source_target_pairs={{0,2},{1,3},{2,4},{3,5},{4,6},{5,7},{6,0},{7,1},{8,10},{9,11},{10,... | collective-permute-start | bytes 1572872 | tf_op jit(solution)/shard_map/ppermute | solution.py:170
  3.6 25.0 %collective-permute-start.1 = (bf16[128,2048]{1,0:T(8,128)(2,1)}, bf16[128,2048]{1,0:T(8,128)(2,1)}, u32[]{:S(2)}, u32[]{:S(2)}) collective-permute-start(bf16[128,2048]{1,0:T(8,128)(2,1)} %bitcast.44), channel_id=1, source_target_pairs={{0,4},{1,5},{2,6},{3,7},{4,0},{5,1},{6,2},{7,3},{8,12},{9,13},{10,... | collective-permute-start | bytes 1572872 | tf_op jit(solution)/shard_map/ppermute | solution.py:170
  5.2 23.9 %collective-permute-start.2 = (bf16[128,2048]{1,0:T(8,128)(2,1)}, bf16[128,2048]{1,0:T(8,128)(2,1)}, u32[]{:S(2)}, u32[]{:S(2)}) collective-permute-start(bf16[128,2048]{1,0:T(8,128)(2,1)} %bitcast.45), channel_id=1, source_target_pairs={{0,6},{1,7},{2,0},{3,1},{4,2},{5,3},{6,4},{7,5},{8,14},{9,15},{10,... | collective-permute-start | bytes 1572872 | tf_op jit(solution)/shard_map/ppermute | solution.py:170
  6.6 27.5 %collective-permute-start.4 = (bf16[128,2048]{1,0:T(8,128)(2,1)}, bf16[128,2048]{1,0:T(8,128)(2,1)}, u32[]{:S(2)}, u32[]{:S(2)}) collective-permute-start(bf16[128,2048]{1,0:T(8,128)(2,1)} %param.10), channel_id=1, source_target_pairs={{0,8},{8,16},{16,24},{24,0},{1,9},{9,17},{17,25},{25,1},{2,10},{10... | collective-permute-start | bytes 1572872 | tf_op jit(solution)/shard_map/ppermute | solution.py:162
  8.2 36.0 %collective-permute-start.5 = (bf16[128,2048]{1,0:T(8,128)(2,1)}, bf16[128,2048]{1,0:T(8,128)(2,1)}, u32[]{:S(2)}, u32[]{:S(2)}) collective-permute-start(bf16[128,2048]{1,0:T(8,128)(2,1)} %param.10), channel_id=1, source_target_pairs={{0,16},{8,24},{16,0},{24,8},{1,17},{9,25},{17,1},{25,9},{2,18},{10... | collective-permute-start | bytes 1572872 | tf_op jit(solution)/shard_map/ppermute | solution.py:162
  20.6 3.9 %copy-start.7 = (s32[1,14,3]{1,0,2:T(1,128)S(1)}, s32[1,14,3]{1,0,2:T(1,128)}, u32[]{:S(2)}) copy-start(s32[1,14,3]{1,0,2:T(1,128)} %param.11) | copy-start | bytes 508
  20.6 55.7 %all-to-all-start = ((bf16[8,3,4,128,128]{4,3,2,1,0:T(8,128)(2,1)}), bf16[8,3,4,128,128]{4,3,2,1,0:T(8,128)(2,1)S(1)}, u32[]{:S(2)}, u32[]{:S(2)}) async-start(bf16[8,3,4,128,128]{4,3,2,1,0:T(8,128)(2,1)} %pad_maximum_fusion), calls=%async_computation | async-start | bytes 6291456 | tf_op jit(solution)/shard_map/all_to_all | solution.py:202
  27.2 25.6 %collective-permute-start.6 = (bf16[128,2048]{1,0:T(8,128)(2,1)}, bf16[128,2048]{1,0:T(8,128)(2,1)S(1)}, u32[]{:S(2)}, u32[]{:S(2)}) collective-permute-start(bf16[128,2048]{1,0:T(8,128)(2,1)} %param.10), channel_id=1, source_target_pairs={{0,24},{8,0},{16,8},{24,16},{1,25},{9,1},{17,9},{25,17},{2,26},{10... | collective-permute-start | bytes 1572872 | tf_op jit(solution)/shard_map/ppermute | solution.py:162
  29.0 23.7 %copy-start.5 = (bf16[128,2048]{1,0:T(8,128)(2,1)S(1)}, bf16[128,2048]{1,0:T(8,128)(2,1)}, u32[]{:S(2)}) copy-start(bf16[128,2048]{1,0:T(8,128)(2,1)} %param.10) | copy-start | bytes 1572868
  32.2 32.9 %collective-permute-start.3 = (bf16[4,128,2048]{2,1,0:T(8,128)(2,1)}, bf16[4,128,2048]{2,1,0:T(8,128)(2,1)}, u32[]{:S(2)}, u32[]{:S(2)}) collective-permute-start(bf16[4,128,2048]{2,1,0:T(8,128)(2,1)} %pad_maximum_fusion.1), channel_id=1, source_target_pairs={{0,1},{1,0},{2,3},{3,2},{4,5},{5,4},{6,7},{7,6},{8,9},{9,8},{10,11... | collective-permute-start | bytes 6291464 | tf_op jit(solution)/shard_map/ppermute | solution.py:173
  63.0 2.8 %copy-start.6 = (bf16[8,128,2048]{2,1,0:T(8,128)(2,1)S(1)}, bf16[8,128,2048]{2,1,0:T(8,128)(2,1)}, u32[]{:S(2)}) copy-start(bf16[8,128,2048]{2,1,0:T(8,128)(2,1)} %constant_dynamic-update-slice_fusion.1) | copy-start | bytes 12582916
  76.3 1.6 copy-start
  93.2 19.1 %all-to-all-start.4 = ((bf16[8,3,128,128]{3,2,1,0:T(8,128)(2,1)}), bf16[8,3,128,128]{3,2,1,0:T(8,128)(2,1)S(1)}, u32[]{:S(2)}, u32[]{:S(2)}) async-start(bf16[8,3,128,128]{3,2,1,0:T(8,128)(2,1)} %shard_map.88), calls=%async_computation.4 | async-start | bytes 1572864 | tf_op jit(solution)/shard_map/all_to_all | solution.py:212
  112.3 19.5 %copy-start.1 = (bf16[8,3,128,128]{3,2,1,0:T(8,128)(2,1)}, bf16[8,3,128,128]{3,2,1,0:T(8,128)(2,1)S(1)}, u32[]{:S(2)}) copy-start(bf16[8,3,128,128]{3,2,1,0:T(8,128)(2,1)S(1)} %all-to-all-done.4.refs_3_) | copy-start | bytes 2359300
  112.3 19.5 %all-to-all-start.3 = ((bf16[8,3,128,128]{3,2,1,0:T(8,128)(2,1)}), bf16[8,3,128,128]{3,2,1,0:T(8,128)(2,1)S(1)}, u32[]{:S(2)}, u32[]{:S(2)}) async-start(bf16[8,3,128,128]{3,2,1,0:T(8,128)(2,1)} %shard_map.87), calls=%async_computation.3 | async-start | bytes 1572864 | tf_op jit(solution)/shard_map/all_to_all | solution.py:212
  131.8 19.5 %copy-start.2 = (bf16[8,3,128,128]{3,2,1,0:T(8,128)(2,1)}, bf16[8,3,128,128]{3,2,1,0:T(8,128)(2,1)S(1)}, u32[]{:S(2)}) copy-start(bf16[8,3,128,128]{3,2,1,0:T(8,128)(2,1)S(1)} %all-to-all-done.3.refs_2_) | copy-start | bytes 2359300
  131.8 19.5 %all-to-all-start.2 = ((bf16[8,3,128,128]{3,2,1,0:T(8,128)(2,1)}), bf16[8,3,128,128]{3,2,1,0:T(8,128)(2,1)S(1)}, u32[]{:S(2)}, u32[]{:S(2)}) async-start(bf16[8,3,128,128]{3,2,1,0:T(8,128)(2,1)} %shard_map.86), calls=%async_computation.2 | async-start | bytes 1572864 | tf_op jit(solution)/shard_map/all_to_all | solution.py:212
  151.3 16.9 %copy-start.3 = (bf16[8,3,128,128]{3,2,1,0:T(8,128)(2,1)}, bf16[8,3,128,128]{3,2,1,0:T(8,128)(2,1)S(1)}, u32[]{:S(2)}) copy-start(bf16[8,3,128,128]{3,2,1,0:T(8,128)(2,1)S(1)} %all-to-all-done.2.refs_1_) | copy-start | bytes 2359300

commit v9 on v8

--- a/solution.py
+++ b/solution.py
@@ -59,17 +59,17 @@
 
     keys_all = x_ref[:, 1, :, :].reshape(length, HD)
     values_all = x_ref[:, 2, :, :].reshape(length, HD)
-    for index, block in enumerate((0, count - 1)):
-        qb = rows(x_ref, 0, block)[...]
-        ub = u_ref[block * BLOCK:(block + 1) * BLOCK, :]
-        query_grad, key_grad, value_grad = softmax_grads(qb, ub, keys_all, values_all, None)
-        rows(o_ref, 0, block)[...] = query_grad.astype(jnp.bfloat16)
-        if index == 0:
-            dk_acc[...] = key_grad
-            dv_acc[...] = value_grad
-        else:
-            dk_acc[...] += key_grad
-            dv_acc[...] += value_grad
+    last = count - 1
+    qb = jnp.concatenate([rows(x_ref, 0, 0)[...], rows(x_ref, 0, last)[...]], axis=0)
+    ub = jnp.concatenate(
+        [u_ref[0:BLOCK, :], u_ref[last * BLOCK:(last + 1) * BLOCK, :]], axis=0
+    )
+    query_grad, key_grad, value_grad = softmax_grads(qb, ub, keys_all, values_all, None)
+    query_grad = query_grad.astype(jnp.bfloat16)
+    rows(o_ref, 0, 0)[...] = query_grad[:BLOCK]
+    rows(o_ref, 0, last)[...] = query_grad[BLOCK:]
+    dk_acc[...] = key_grad
+    dv_acc[...] = value_grad
 
     columns = lax.broadcasted_iota(jnp.int32, (BLOCK, SLOTS * BLOCK), 1) // BLOCK
 

time: 174 us -> 170 us (0.977)
  Pallas kernels: 65.4 us -> 62.3 us
    pallas_call x4, Pallas kernels: 61.1 us -> 57.9 us  [attention_grads(): pl.pallas_call(_attention_kernel, out_shape=out, grid_spec=pltpu.Prefetch...]
  transfers between devices with their start and end apart: 11 -> 11, of which waited for: 3 -> 3; matrix products, arithmetic and copies ran while one was open for 23% -> 24% of each run, Pallas kernels for 27% -> 26%
where the time goes in v9:
time: 170 us; the launch traced here: 169 us
  Pallas kernels  62.3 us (37%)
  starting transfers between devices  27.5 us (16%)
  local copies, waits for them, and re-layouts  25.7 us (15%)
  waiting for transfers between devices  19.2 us (11%)
  blocking collectives  16.9 us (10%)
  other arithmetic  13.6 us (8%)
  matrix products  3.34 us (2%)
    pallas_call x4, Pallas kernels, attention_grads(): pl.pallas_call(_attention_kernel, out_shape=out, grid_spec=pltpu.Prefetch...  57.9 us
    ppermute x3, waiting for transfers between devices, body(): lax.ppermute(out_weight, 'dp', [(a, (a + s) % dp) for a in range(dp)])  18.7 us
    all_to_all x1, blocking collectives, body(): lax.all_to_all(grads, 'context', split_axis=0, concat_axis=0, tiled=True)  16.9 us
    unnamed x24, local copies, waits for them, and re-layouts  14 us
    all_to_all x3, starting transfers between devices, body(): lax.all_to_all(grads, 'context', split_axis=0, concat_axis=0, tiled=True)  12.3 us
    ppermute x3, starting transfers between devices, body(): lax.ppermute(local_cotangent, 'context', [(a, (a + s) % ctx) for a in ran...  5.94 us
    ppermute x3, starting transfers between devices, body(): lax.ppermute(out_weight, 'dp', [(a, (a + s) % dp) for a in range(dp)])  5.54 us
    pallas_call x1, Pallas kernels, assemble(): return pl.pallas_call(_assemble_kernel, out_shape=(out, out, out))(*pieces)  4.36 us
  transfers between devices with their start and end apart: 11, of which 3 were waited for; matrix products, arithmetic and copies ran while one was open for 24% of the time, Pallas kernels for 26%

profile of v9, /device:TPU:0, one launch (start us, length us, event | category | flops | bytes accessed | tf_op | source)
XLA Modules:
  0.0 169.4 jit_solution(11714602753302522454)
XLA Ops:
  0.6 3.0 %collective-permute-start = (bf16[128,2048]{1,0:T(8,128)(2,1)}, bf16[128,2048]{1,0:T(8,128)(2,1)}, u32[]{:S(2)}, u32[]{:S(2)}) collective-permute-start(bf16[128,2048]{1,0:T(8,128)(2,1)} %bitcast.43), channel_id=1, source_target_pairs={{0,2},{1,3},{2,4},{3,5},{4,6},{5,7},{6,0},{7,1},{8,10},{9,11},{10,... | collective-permute-start | bytes 1572872 | tf_op jit(solution)/shard_map/ppermute | solution.py:170
  3.6 1.5 collective-permute-start.1
  5.2 1.4 collective-permute-start.2
  6.6 1.6 collective-permute-start.4
  8.2 2.6 %collective-permute-start.5 = (bf16[128,2048]{1,0:T(8,128)(2,1)}, bf16[128,2048]{1,0:T(8,128)(2,1)}, u32[]{:S(2)}, u32[]{:S(2)}) collective-permute-start(bf16[128,2048]{1,0:T(8,128)(2,1)} %param.10), channel_id=1, source_target_pairs={{0,16},{8,24},{16,0},{24,8},{1,17},{9,25},{17,1},{25,9},{2,18},{10... | collective-permute-start | bytes 1572872 | tf_op jit(solution)/shard_map/ppermute | solution.py:162
  10.8 1.6 copy.11
  12.4 0.7 copy.12
  13.1 0.7 copy.13
  13.7 0.7 copy.14
  14.4 1.6 copy.15
  16.0 1.3 copy.16
  17.3 3.2 %pad_maximum_fusion = bf16[8,3,4,128,128]{4,3,2,1,0:T(8,128)(2,1)} fusion(bf16[8,1,4,128,128]{4,3,2,1,0:T(8,128)(2,1)} %bitcast.41, bf16[8,1,4,128,128]{4,3,2,1,0:T(8,128)(2,1)S(1)} %bitcast.40, bf16[8,1,4,128,128]{4,3,2,1,0:T(8,128)(2,1)S(1)} %bitcast.39), kind=kLoop, calls=%fused_computation.2 | loop fusion | flops 3145728 | bytes 6291456 | tf_op jit(solution)/shard_map/stack | solution.py:201
  20.6 3.8 %all-to-all-start = ((bf16[8,3,4,128,128]{4,3,2,1,0:T(8,128)(2,1)}), bf16[8,3,4,128,128]{4,3,2,1,0:T(8,128)(2,1)S(1)}, u32[]{:S(2)}, u32[]{:S(2)}) async-start(bf16[8,3,4,128,128]{4,3,2,1,0:T(8,128)(2,1)} %pad_maximum_fusion), calls=%async_computation | async-start | bytes 6291456 | tf_op jit(solution)/shard_map/all_to_all | solution.py:202
  24.5 0.1 copy.10
  24.6 0.6 reshape_squeeze.15.rb_ref
  25.2 0.1 broadcast_bitcast_fusion
  25.3 1.9 %constant_dynamic-update-slice_fusion.4 = bf16[8,128,2048]{2,1,0:T(8,128)(2,1)} fusion(bf16[1,128,2048]{2,1,0:T(8,128)(2,1)} %param.9), kind=kLoop, calls=%fused_computation.12 | loop fusion | bytes 1048576
  27.2 0.0 collective-permute-done
  27.2 1.4 collective-permute-start.6
  28.6 0.0 collective-permute-done.1
  28.6 0.4 collective-permute-done.2
  29.0 3.1 %pad_maximum_fusion.1 = bf16[4,128,2048]{2,1,0:T(8,128)(2,1)} fusion(bf16[1,128,2048]{2,1,0:T(8,128)(2,1)} %bitcast.13, bf16[1,128,2048]{2,1,0:T(8,128)(2,1)} %bitcast.12, bf16[1,128,2048]{2,1,0:T(8,128)(2,1)} %bitcast.11, bf16[1,128,2048]{2,1,0:T(8,128)(2,1)} %param.9), kind=kLoop, calls=%fused_computation.3 | loop fusion | flops 3145728 | bytes 4194304 | tf_op jit(solution)/shard_map/stack | solution.py:169
  32.2 0.0 collective-permute-start.3
  32.2 1.9 %constant_dynamic-update-slice_fusion.3 = bf16[8,128,2048]{2,1,0:T(8,128)(2,1)} fusion(bf16[8,128,2048]{2,1,0:T(8,128)(2,1)} %constant_dynamic-update-slice_fusion.4, bf16[128,2048]{1,0:T(8,128)(2,1)} %collective-permute-done), kind=kLoop, calls=%fused_computation.11 | loop fusion | bytes 1048576
  34.1 0.0 collective-permute-done.4
  34.1 10.1 %collective-permute-done.5 = bf16[128,2048]{1,0:T(8,128)(2,1)} collective-permute-done((bf16[128,2048]{1,0:T(8,128)(2,1)}, bf16[128,2048]{1,0:T(8,128)(2,1)}, u32[]{:S(2)}, u32[]{:S(2)}) %collective-permute-start.5) | collective-permute-done | bytes 524320 | tf_op jit(solution)/shard_map/ppermute | solution.py:162
  44.2 8.6 %collective-permute-done.6 = bf16[128,2048]{1,0:T(8,128)(2,1)S(1)} collective-permute-done((bf16[128,2048]{1,0:T(8,128)(2,1)}, bf16[128,2048]{1,0:T(8,128)(2,1)S(1)}, u32[]{:S(2)}, u32[]{:S(2)}) %collective-permute-start.6) | collective-permute-done | bytes 524320 | tf_op jit(solution)/shard_map/ppermute | solution.py:162
  52.8 2.8 %pad_maximum_fusion.2 = bf16[4,128,2048]{2,1,0:T(8,128)(2,1)} fusion(bf16[1,128,2048]{2,1,0:T(8,128)(2,1)S(1)} %bitcast.48, bf16[1,128,2048]{2,1,0:T(8,128)(2,1)} %bitcast.17, bf16[1,128,2048]{2,1,0:T(8,128)(2,1)} %bitcast.16, bf16[1,128,2048]{2,1,0:T(8,128)(2,1)S(1)} %bitcast.47), kind=kLoop, calls=%fused_computation.4 | loop fusion | flops 3145728 | bytes 4194304 | tf_op jit(solution)/shard_map/stack | solution.py:166
  55.5 3.7 %gather_fusion = bf16[4,128,2048]{2,1,0:T(8,128)(2,1)} fusion(bf16[4,128,2048]{2,1,0:T(8,128)(2,1)} %pad_maximum_fusion.2, s32[1024]{0:T(1024)S(1)} %pad_clamp_fusion.1), kind=kCustom, calls=%fused_computation | custom fusion | bytes 4194320 | tf_op jit(solution)/shard_map/jit(_take)/gather | solution.py:166
  59.3 1.9 %constant_dynamic-update-slice_fusion.2 = bf16[8,128,2048]{2,1,0:T(8,128)(2,1)} fusion(bf16[8,128,2048]{2,1,0:T(8,128)(2,1)} %constant_dynamic-update-slice_fusion.3, bf16[128,2048]{1,0:T(8,128)(2,1)} %collective-permute-done.1), kind=kLoop, calls=%fused_computation.10 | loop fusion | bytes 1048576
  61.1 1.9 %constant_dynamic-update-slice_fusion.1 = bf16[8,128,2048]{2,1,0:T(8,128)(2,1)} fusion(bf16[8,128,2048]{2,1,0:T(8,128)(2,1)} %constant_dynamic-update-slice_fusion.2, bf16[128,2048]{1,0:T(8,128)(2,1)} %collective-permute-done.2), kind=kLoop, calls=%fused_computation.9 | loop fusion | bytes 1048576
  63.1 2.0 %broadcast_select_fusion = bf16[4,128,2048]{2,1,0:T(8,128)(2,1)S(1)} fusion(bf16[4,128,2048]{2,1,0:T(8,128)(2,1)} %gather_fusion, pred[4]{0:T(512)(128)(4,1)S(1)} %compare_and_fusion), kind=kLoop, calls=%fused_computation.5 | loop fusion | flops 1048576 | bytes 4194308 | tf_op jit(solution)/shard_map/jit(_take)/select_n | solution.py:166
  65.1 0.8 copy-done.6
  65.9 1.8 %constant_dynamic-update-slice_fusion = bf16[8,128,2048]{2,1,0:T(8,128)(2,1)S(1)} fusion(bf16[8,128,2048]{2,1,0:T(8,128)(2,1)S(1)} %copy-done.6, bf16[4,128,2048]{2,1,0:T(8,128)(2,1)} %collective-permute-done.3), kind=kLoop, calls=%fused_computation.8 | loop fusion | bytes 4194304 | tf_op jit(solution)/shard_map/concatenate | solution.py:174
  67.7 3.3 %convolution_convert_fusion = bf16[1024,512]{1,0:T(8,128)(2,1)} fusion(bf16[1024,2048]{1,0:T(8,128)(2,1)S(1)} %bitcast.49, bf16[512,2048]{1,0:T(8,128)(2,1)S(1)} %bitcast.42), kind=kOutput, calls=%fused_computation.6 | convolution fusion | flops 2148007936 | bytes 7340032 | tf_op jit(solution)/shard_map/dot_general | solution.py:175
  71.0 2.8 %gather_fusion.1 = bf16[8,128,512]{2,1,0:T(8,128)(2,1)} fusion(bf16[8,128,512]{2,1,0:T(8,128)(2,1)} %bitcast.46, s32[1024]{0:T(1024)S(1)} %pad_clamp_fusion), kind=kCustom, calls=%fused_computation.1 | custom fusion | bytes 2097184 | tf_op jit(solution)/shard_map/jit(_take)/gather | solution.py:184
  73.8 2.4 %bitcast_select_fusion.u_ref = bf16[1024,512]{1,0:T(8,128)(2,1)} fusion(bf16[8,128,512]{2,1,0:T(8,128)(2,1)} %gather_fusion.1, pred[1024]{0:T(1024)(128)(4,1)S(1)} %broadcast_bitcast_fusion), kind=kLoop, calls=%fused_computation.7 | loop fusion | flops 524288 | bytes 2098176 | tf_op jit(solution)/shard_map/jit(_take)/select_n | solution.py:184
  76.3 1.6 copy-done
  77.9 14.5 %shard_map.88 = bf16[8,3,128,128]{3,2,1,0:T(8,128)(2,1)} custom-call(s32[42]{0:T(128)} %reshape_squeeze.15.rb_ref, bf16[8,3,4,128,128]{4,3,2,1,0:T(8,128)(2,1)} %copy-done, bf16[1024,512]{1,0:T(8,128)(2,1)} %bitcast_select_fusion.u_ref), custom_call_target="tpu_custom_call" | custom-call | flops 905969664 | bytes 1835008 | tf_op jit(solution)/shard_map/pallas_call | solution.py:113
  92.4 3.9 %all-to-all-start.4 = ((bf16[8,3,128,128]{3,2,1,0:T(8,128)(2,1)}), bf16[8,3,128,128]{3,2,1,0:T(8,128)(2,1)S(1)}, u32[]{:S(2)}, u32[]{:S(2)}) async-start(bf16[8,3,128,128]{3,2,1,0:T(8,128)(2,1)} %shard_map.88), calls=%async_computation.4 | async-start | bytes 1572864 | tf_op jit(solution)/shard_map/all_to_all | solution.py:212
  96.2 14.5 %shard_map.87 = bf16[8,3,128,128]{3,2,1,0:T(8,128)(2,1)} custom-call(s32[42]{0:T(128)} %reshape_squeeze.15.rb_ref, bf16[8,3,4,128,128]{4,3,2,1,0:T(8,128)(2,1)} %copy-done, bf16[1024,512]{1,0:T(8,128)(2,1)} %bitcast_select_fusion.u_ref), custom_call_target="tpu_custom_call" | custom-call | flops 905969664 | bytes 1835008 | tf_op jit(solution)/shard_map/pallas_call | solution.py:113
  110.7 0.0 all-to-all-done.4.refs_3_
  110.7 4.2 %all-to-all-start.3 = ((bf16[8,3,128,128]{3,2,1,0:T(8,128)(2,1)}), bf16[8,3,128,128]{3,2,1,0:T(8,128)(2,1)S(1)}, u32[]{:S(2)}, u32[]{:S(2)}) async-start(bf16[8,3,128,128]{3,2,1,0:T(8,128)(2,1)} %shard_map.87), calls=%async_computation.3 | async-start | bytes 1572864 | tf_op jit(solution)/shard_map/all_to_all | solution.py:212
  114.9 14.5 %shard_map.86 = bf16[8,3,128,128]{3,2,1,0:T(8,128)(2,1)} custom-call(s32[42]{0:T(128)} %reshape_squeeze.15.rb_ref, bf16[8,3,4,128,128]{4,3,2,1,0:T(8,128)(2,1)} %copy-done, bf16[1024,512]{1,0:T(8,128)(2,1)} %bitcast_select_fusion.u_ref), custom_call_target="tpu_custom_call" | custom-call | flops 905969664 | bytes 1835008 | tf_op jit(solution)/shard_map/pallas_call | solution.py:113
  129.4 4.2 %all-to-all-start.2 = ((bf16[8,3,128,128]{3,2,1,0:T(8,128)(2,1)}), bf16[8,3,128,128]{3,2,1,0:T(8,128)(2,1)S(1)}, u32[]{:S(2)}, u32[]{:S(2)}) async-start(bf16[8,3,128,128]{3,2,1,0:T(8,128)(2,1)} %shard_map.86), calls=%async_computation.2 | async-start | bytes 1572864 | tf_op jit(solution)/shard_map/all_to_all | solution.py:212
  133.6 14.5 %shard_map.85 = bf16[8,3,128,128]{3,2,1,0:T(8,128)(2,1)} custom-call(s32[42]{0:T(128)} %reshape_squeeze.15.rb_ref, bf16[8,3,4,128,128]{4,3,2,1,0:T(8,128)(2,1)} %copy-done, bf16[1024,512]{1,0:T(8,128)(2,1)} %bitcast_select_fusion.u_ref), custom_call_target="tpu_custom_call" | custom-call | flops 905969664 | bytes 1835008 | tf_op jit(solution)/shard_map/pallas_call | solution.py:113
  148.1 16.9 %all_to_all.25.refs_0_ = bf16[8,3,128,128]{3,2,1,0:T(8,128)(2,1)} all-to-all(bf16[8,3,128,128]{3,2,1,0:T(8,128)(2,1)} %shard_map.85), channel_id=1, replica_groups=mesh['dp'=4,'context'=8] {'context'}, dimensions={0} | all-to-all | bytes 1572864 | tf_op jit(solution)/shard_map/all_to_all | solution.py:212
  165.0 4.4 %shard_map.89 = (bf16[1,128,4096]{2,1,0:T(8,128)(2,1)}, bf16[1,128,4096]{2,1,0:T(8,128)(2,1)}, bf16[1,128,4096]{2,1,0:T(8,128)(2,1)}) custom-call(bf16[8,3,128,128]{3,2,1,0:T(8,128)(2,1)} %all_to_all.25.refs_0_, bf16[8,3,128,128]{3,2,1,0:T(8,128)(2,1)} %copy-done.3, bf16[8,3,128,128]{3,2,1,0:T(8,128)(2,1)} %copy-done.2, bf16[8,3,128,128]{3,2,1,0:T(8,128)(2,1)} %copy-done.1), custom_call_target="tpu_custom_call" | custom-call | tf_op jit(solution)/shard_map/pallas_call | solution.py:145
  (24 shorter events, 0.1 us)
Async XLA Ops:
  0.6 12.4 %copy-start.4 = (bf16[1,128,4096]{2,1,0:T(8,128)(2,1)S(1)}, bf16[1,128,4096]{2,1,0:T(8,128)(2,1)}, u32[]{:S(2)}) copy-start(bf16[1,128,4096]{2,1,0:T(8,128)(2,1)} %param.7) | copy-start | bytes 3145732
  0.6 26.6 %collective-permute-start = (bf16[128,2048]{1,0:T(8,128)(2,1)}, bf16[128,2048]{1,0:T(8,128)(2,1)}, u32[]{:S(2)}, u32[]{:S(2)}) collective-permute-start(bf16[128,2048]{1,0:T(8,128)(2,1)} %bitcast.43), channel_id=1, source_target_pairs={{0,2},{1,3},{2,4},{3,5},{4,6},{5,7},{6,0},{7,1},{8,10},{9,11},{10,... | collective-permute-start | bytes 1572872 | tf_op jit(solution)/shard_map/ppermute | solution.py:170
  3.6 25.0 %collective-permute-start.1 = (bf16[128,2048]{1,0:T(8,128)(2,1)}, bf16[128,2048]{1,0:T(8,128)(2,1)}, u32[]{:S(2)}, u32[]{:S(2)}) collective-permute-start(bf16[128,2048]{1,0:T(8,128)(2,1)} %bitcast.44), channel_id=1, source_target_pairs={{0,4},{1,5},{2,6},{3,7},{4,0},{5,1},{6,2},{7,3},{8,12},{9,13},{10,... | collective-permute-start | bytes 1572872 | tf_op jit(solution)/shard_map/ppermute | solution.py:170
  5.2 23.9 %collective-permute-start.2 = (bf16[128,2048]{1,0:T(8,128)(2,1)}, bf16[128,2048]{1,0:T(8,128)(2,1)}, u32[]{:S(2)}, u32[]{:S(2)}) collective-permute-start(bf16[128,2048]{1,0:T(8,128)(2,1)} %bitcast.45), channel_id=1, source_target_pairs={{0,6},{1,7},{2,0},{3,1},{4,2},{5,3},{6,4},{7,5},{8,14},{9,15},{10,... | collective-permute-start | bytes 1572872 | tf_op jit(solution)/shard_map/ppermute | solution.py:170
  6.6 27.5 %collective-permute-start.4 = (bf16[128,2048]{1,0:T(8,128)(2,1)}, bf16[128,2048]{1,0:T(8,128)(2,1)}, u32[]{:S(2)}, u32[]{:S(2)}) collective-permute-start(bf16[128,2048]{1,0:T(8,128)(2,1)} %param.10), channel_id=1, source_target_pairs={{0,8},{8,16},{16,24},{24,0},{1,9},{9,17},{17,25},{25,1},{2,10},{10... | collective-permute-start | bytes 1572872 | tf_op jit(solution)/shard_map/ppermute | solution.py:162
  8.2 36.0 %collective-permute-start.5 = (bf16[128,2048]{1,0:T(8,128)(2,1)}, bf16[128,2048]{1,0:T(8,128)(2,1)}, u32[]{:S(2)}, u32[]{:S(2)}) collective-permute-start(bf16[128,2048]{1,0:T(8,128)(2,1)} %param.10), channel_id=1, source_target_pairs={{0,16},{8,24},{16,0},{24,8},{1,17},{9,25},{17,1},{25,9},{2,18},{10... | collective-permute-start | bytes 1572872 | tf_op jit(solution)/shard_map/ppermute | solution.py:162
  20.6 3.9 %copy-start.7 = (s32[1,14,3]{1,0,2:T(1,128)S(1)}, s32[1,14,3]{1,0,2:T(1,128)}, u32[]{:S(2)}) copy-start(s32[1,14,3]{1,0,2:T(1,128)} %param.11) | copy-start | bytes 508
  20.6 55.7 %all-to-all-start = ((bf16[8,3,4,128,128]{4,3,2,1,0:T(8,128)(2,1)}), bf16[8,3,4,128,128]{4,3,2,1,0:T(8,128)(2,1)S(1)}, u32[]{:S(2)}, u32[]{:S(2)}) async-start(bf16[8,3,4,128,128]{4,3,2,1,0:T(8,128)(2,1)} %pad_maximum_fusion), calls=%async_computation | async-start | bytes 6291456 | tf_op jit(solution)/shard_map/all_to_all | solution.py:202
  27.2 25.6 %collective-permute-start.6 = (bf16[128,2048]{1,0:T(8,128)(2,1)}, bf16[128,2048]{1,0:T(8,128)(2,1)S(1)}, u32[]{:S(2)}, u32[]{:S(2)}) collective-permute-start(bf16[128,2048]{1,0:T(8,128)(2,1)} %param.10), channel_id=1, source_target_pairs={{0,24},{8,0},{16,8},{24,16},{1,25},{9,1},{17,9},{25,17},{2,26},{10... | collective-permute-start | bytes 1572872 | tf_op jit(solution)/shard_map/ppermute | solution.py:162
  29.0 23.7 %copy-start.5 = (bf16[128,2048]{1,0:T(8,128)(2,1)S(1)}, bf16[128,2048]{1,0:T(8,128)(2,1)}, u32[]{:S(2)}) copy-start(bf16[128,2048]{1,0:T(8,128)(2,1)} %param.10) | copy-start | bytes 1572868
  32.2 32.9 %collective-permute-start.3 = (bf16[4,128,2048]{2,1,0:T(8,128)(2,1)}, bf16[4,128,2048]{2,1,0:T(8,128)(2,1)}, u32[]{:S(2)}, u32[]{:S(2)}) collective-permute-start(bf16[4,128,2048]{2,1,0:T(8,128)(2,1)} %pad_maximum_fusion.1), channel_id=1, source_target_pairs={{0,1},{1,0},{2,3},{3,2},{4,5},{5,4},{6,7},{7,6},{8,9},{9,8},{10,11... | collective-permute-start | bytes 6291464 | tf_op jit(solution)/shard_map/ppermute | solution.py:173
  63.0 2.8 %copy-start.6 = (bf16[8,128,2048]{2,1,0:T(8,128)(2,1)S(1)}, bf16[8,128,2048]{2,1,0:T(8,128)(2,1)}, u32[]{:S(2)}) copy-start(bf16[8,128,2048]{2,1,0:T(8,128)(2,1)} %constant_dynamic-update-slice_fusion.1) | copy-start | bytes 12582916
  76.3 1.6 copy-start
  92.4 18.3 %all-to-all-start.4 = ((bf16[8,3,128,128]{3,2,1,0:T(8,128)(2,1)}), bf16[8,3,128,128]{3,2,1,0:T(8,128)(2,1)S(1)}, u32[]{:S(2)}, u32[]{:S(2)}) async-start(bf16[8,3,128,128]{3,2,1,0:T(8,128)(2,1)} %shard_map.88), calls=%async_computation.4 | async-start | bytes 1572864 | tf_op jit(solution)/shard_map/all_to_all | solution.py:212
  110.7 18.7 %copy-start.1 = (bf16[8,3,128,128]{3,2,1,0:T(8,128)(2,1)}, bf16[8,3,128,128]{3,2,1,0:T(8,128)(2,1)S(1)}, u32[]{:S(2)}) copy-start(bf16[8,3,128,128]{3,2,1,0:T(8,128)(2,1)S(1)} %all-to-all-done.4.refs_3_) | copy-start | bytes 2359300
  110.7 18.7 %all-to-all-start.3 = ((bf16[8,3,128,128]{3,2,1,0:T(8,128)(2,1)}), bf16[8,3,128,128]{3,2,1,0:T(8,128)(2,1)S(1)}, u32[]{:S(2)}, u32[]{:S(2)}) async-start(bf16[8,3,128,128]{3,2,1,0:T(8,128)(2,1)} %shard_map.87), calls=%async_computation.3 | async-start | bytes 1572864 | tf_op jit(solution)/shard_map/all_to_all | solution.py:212
  129.4 18.7 %copy-start.2 = (bf16[8,3,128,128]{3,2,1,0:T(8,128)(2,1)}, bf16[8,3,128,128]{3,2,1,0:T(8,128)(2,1)S(1)}, u32[]{:S(2)}) copy-start(bf16[8,3,128,128]{3,2,1,0:T(8,128)(2,1)S(1)} %all-to-all-done.3.refs_2_) | copy-start | bytes 2359300
  129.4 18.7 %all-to-all-start.2 = ((bf16[8,3,128,128]{3,2,1,0:T(8,128)(2,1)}), bf16[8,3,128,128]{3,2,1,0:T(8,128)(2,1)S(1)}, u32[]{:S(2)}, u32[]{:S(2)}) async-start(bf16[8,3,128,128]{3,2,1,0:T(8,128)(2,1)} %shard_map.86), calls=%async_computation.2 | async-start | bytes 1572864 | tf_op jit(solution)/shard_map/all_to_all | solution.py:212
  148.1 16.9 %copy-start.3 = (bf16[8,3,128,128]{3,2,1,0:T(8,128)(2,1)}, bf16[8,3,128,128]{3,2,1,0:T(8,128)(2,1)S(1)}, u32[]{:S(2)}) copy-start(bf16[8,3,128,128]{3,2,1,0:T(8,128)(2,1)S(1)} %all-to-all-done.2.refs_1_) | copy-start | bytes 2359300

commit v10 on v9

--- a/solution.py
+++ b/solution.py
@@ -131,18 +131,34 @@
 
 
 def _assemble_kernel(*refs):
-    pieces, outs = refs[:-3], refs[-3:]
+    *pieces, first, second, third, sems = refs
+    outs = (first, second, third)
     parts = pieces[0].shape[0]
+    copies = []
     for c, piece in enumerate(pieces):
         for source in range(parts):
             start = (c * parts + source) * HD
             for g, out in enumerate(outs):
-                out[0, :, start:start + HD] = piece[source, g]
+                copy = pltpu.make_async_copy(
+                    piece.at[source, g], out.at[0, :, pl.ds(start, HD)], sems.at[len(copies)]
+                )
+                copy.start()
+                copies.append(copy)
+    for copy in copies:
+        copy.wait()
 
 
 def assemble(pieces, tokens, width):
     out = jax.ShapeDtypeStruct((1, tokens, width), jnp.bfloat16)
-    return pl.pallas_call(_assemble_kernel, out_shape=(out, out, out))(*pieces)
+    total = len(pieces) * pieces[0].shape[0] * 3
+    anywhere = pl.BlockSpec(memory_space=pl.ANY)
+    return pl.pallas_call(
+        _assemble_kernel,
+        out_shape=(out, out, out),
+        in_specs=[anywhere] * len(pieces),
+        out_specs=(anywhere, anywhere, anywhere),
+        scratch_shapes=[pltpu.SemaphoreType.DMA((total,))],
+    )(*pieces)
 
 
 def body(queries, key_rows, value_rows, cotangent, out_weight, random_blocks):

time: 170 us -> 263 us (1.55)
  Pallas kernels: 62.3 us -> 155 us
    pallas_call x1, Pallas kernels: 4.36 us -> 97.3 us  [assemble(): pl.pallas_call(_assemble_kernel, out_shape=(out, out, out), in_specs=[any...]
  transfers between devices with their start and end apart: 11 -> 11, of which waited for: 3 -> 3; matrix products, arithmetic and copies ran while one was open for 24% -> 15% of each run, Pallas kernels for 26% -> 17%
where the time goes in v10:
time: 263 us; the launch traced here: 262 us
  Pallas kernels  155 us (59%)
  starting transfers between devices  27.5 us (10%)
  local copies, waits for them, and re-layouts  25.7 us (10%)
  waiting for transfers between devices  19.2 us (7%)
  blocking collectives  16.9 us (6%)
  other arithmetic  13.6 us (5%)
  matrix products  3.34 us (1%)
    pallas_call x1, Pallas kernels, assemble(): pl.pallas_call(_assemble_kernel, out_shape=(out, out, out), in_specs=[any...  97.3 us
    pallas_call x4, Pallas kernels, attention_grads(): pl.pallas_call(_attention_kernel, out_shape=out, grid_spec=pltpu.Prefetch...  57.9 us
    ppermute x3, waiting for transfers between devices, body(): lax.ppermute(out_weight, 'dp', [(a, (a + s) % dp) for a in range(dp)])  18.7 us
    all_to_all x1, blocking collectives, body(): lax.all_to_all(grads, 'context', split_axis=0, concat_axis=0, tiled=True)  16.9 us
    unnamed x24, local copies, waits for them, and re-layouts  14 us
    all_to_all x3, starting transfers between devices, body(): lax.all_to_all(grads, 'context', split_axis=0, concat_axis=0, tiled=True)  12.3 us
    ppermute x3, starting transfers between devices, body(): lax.ppermute(local_cotangent, 'context', [(a, (a + s) % ctx) for a in ran...  5.94 us
    ppermute x3, starting transfers between devices, body(): lax.ppermute(out_weight, 'dp', [(a, (a + s) % dp) for a in range(dp)])  5.54 us
  transfers between devices with their start and end apart: 11, of which 3 were waited for; matrix products, arithmetic and copies ran while one was open for 15% of the time, Pallas kernels for 17%

profile of v10, /device:TPU:0, one launch (start us, length us, event | category | flops | bytes accessed | tf_op | source)
XLA Modules:
  0.0 262.3 jit_solution(11830856687432083855)
XLA Ops:
  0.6 3.0 %collective-permute-start = (bf16[128,2048]{1,0:T(8,128)(2,1)}, bf16[128,2048]{1,0:T(8,128)(2,1)}, u32[]{:S(2)}, u32[]{:S(2)}) collective-permute-start(bf16[128,2048]{1,0:T(8,128)(2,1)} %bitcast.43), channel_id=1, source_target_pairs={{0,2},{1,3},{2,4},{3,5},{4,6},{5,7},{6,0},{7,1},{8,10},{9,11},{10,... | collective-permute-start | bytes 1572872 | tf_op jit(solution)/shard_map/ppermute | solution.py:186
  3.6 1.5 collective-permute-start.1
  5.2 1.4 collective-permute-start.2
  6.6 1.6 collective-permute-start.4
  8.2 2.6 collective-permute-start.5
  10.8 1.6 copy.11
  12.4 0.7 copy.12
  13.1 0.7 copy.13
  13.7 0.7 copy.14
  14.4 1.6 copy.15
  16.0 1.3 copy.16
  17.3 3.2 %pad_maximum_fusion = bf16[8,3,4,128,128]{4,3,2,1,0:T(8,128)(2,1)} fusion(bf16[8,1,4,128,128]{4,3,2,1,0:T(8,128)(2,1)} %bitcast.41, bf16[8,1,4,128,128]{4,3,2,1,0:T(8,128)(2,1)S(1)} %bitcast.40, bf16[8,1,4,128,128]{4,3,2,1,0:T(8,128)(2,1)S(1)} %bitcast.39), kind=kLoop, calls=%fused_computation.2 | loop fusion | flops 3145728 | bytes 6291456 | tf_op jit(solution)/shard_map/stack | solution.py:217
  20.6 3.8 %all-to-all-start = ((bf16[8,3,4,128,128]{4,3,2,1,0:T(8,128)(2,1)}), bf16[8,3,4,128,128]{4,3,2,1,0:T(8,128)(2,1)S(1)}, u32[]{:S(2)}, u32[]{:S(2)}) async-start(bf16[8,3,4,128,128]{4,3,2,1,0:T(8,128)(2,1)} %pad_maximum_fusion), calls=%async_computation | async-start | bytes 6291456 | tf_op jit(solution)/shard_map/all_to_all | solution.py:218
  24.5 0.1 copy.10
  24.6 0.6 reshape_squeeze.15.rb_ref
  25.2 0.1 broadcast_bitcast_fusion
  25.3 1.9 constant_dynamic-update-slice_fusion.4
  27.2 0.0 collective-permute-done
  27.2 1.4 collective-permute-start.6
  28.6 0.4 collective-permute-done.2
  29.0 3.1 %pad_maximum_fusion.1 = bf16[4,128,2048]{2,1,0:T(8,128)(2,1)} fusion(bf16[1,128,2048]{2,1,0:T(8,128)(2,1)} %bitcast.13, bf16[1,128,2048]{2,1,0:T(8,128)(2,1)} %bitcast.12, bf16[1,128,2048]{2,1,0:T(8,128)(2,1)} %bitcast.11, bf16[1,128,2048]{2,1,0:T(8,128)(2,1)} %param.9), kind=kLoop, calls=%fused_computation.3 | loop fusion | flops 3145728 | bytes 4194304 | tf_op jit(solution)/shard_map/stack | solution.py:185
  32.2 0.0 collective-permute-start.3
  32.2 1.9 constant_dynamic-update-slice_fusion.3
  34.1 0.0 collective-permute-done.4
  34.1 10.1 %collective-permute-done.5 = bf16[128,2048]{1,0:T(8,128)(2,1)} collective-permute-done((bf16[128,2048]{1,0:T(8,128)(2,1)}, bf16[128,2048]{1,0:T(8,128)(2,1)}, u32[]{:S(2)}, u32[]{:S(2)}) %collective-permute-start.5) | collective-permute-done | bytes 524320 | tf_op jit(solution)/shard_map/ppermute | solution.py:178
  44.2 8.6 %collective-permute-done.6 = bf16[128,2048]{1,0:T(8,128)(2,1)S(1)} collective-permute-done((bf16[128,2048]{1,0:T(8,128)(2,1)}, bf16[128,2048]{1,0:T(8,128)(2,1)S(1)}, u32[]{:S(2)}, u32[]{:S(2)}) %collective-permute-start.6) | collective-permute-done | bytes 524320 | tf_op jit(solution)/shard_map/ppermute | solution.py:178
  52.8 2.8 %pad_maximum_fusion.2 = bf16[4,128,2048]{2,1,0:T(8,128)(2,1)} fusion(bf16[1,128,2048]{2,1,0:T(8,128)(2,1)S(1)} %bitcast.48, bf16[1,128,2048]{2,1,0:T(8,128)(2,1)} %bitcast.17, bf16[1,128,2048]{2,1,0:T(8,128)(2,1)} %bitcast.16, bf16[1,128,2048]{2,1,0:T(8,128)(2,1)S(1)} %bitcast.47), kind=kLoop, calls=%fused_computation.4 | loop fusion | flops 3145728 | bytes 4194304 | tf_op jit(solution)/shard_map/stack | solution.py:182
  55.5 3.7 %gather_fusion = bf16[4,128,2048]{2,1,0:T(8,128)(2,1)} fusion(bf16[4,128,2048]{2,1,0:T(8,128)(2,1)} %pad_maximum_fusion.2, s32[1024]{0:T(1024)S(1)} %pad_clamp_fusion.1), kind=kCustom, calls=%fused_computation | custom fusion | bytes 4194320 | tf_op jit(solution)/shard_map/jit(_take)/gather | solution.py:182
  59.3 1.9 constant_dynamic-update-slice_fusion.2
  61.1 1.9 constant_dynamic-update-slice_fusion.1
  63.1 2.0 broadcast_select_fusion
  65.1 0.0 collective-permute-done.3
  65.1 0.8 copy-done.6
  65.9 1.8 constant_dynamic-update-slice_fusion
  67.7 3.3 %convolution_convert_fusion = bf16[1024,512]{1,0:T(8,128)(2,1)} fusion(bf16[1024,2048]{1,0:T(8,128)(2,1)S(1)} %bitcast.49, bf16[512,2048]{1,0:T(8,128)(2,1)S(1)} %bitcast.42), kind=kOutput, calls=%fused_computation.6 | convolution fusion | flops 2148007936 | bytes 7340032 | tf_op jit(solution)/shard_map/dot_general | solution.py:191
  71.0 2.8 %gather_fusion.1 = bf16[8,128,512]{2,1,0:T(8,128)(2,1)} fusion(bf16[8,128,512]{2,1,0:T(8,128)(2,1)} %bitcast.46, s32[1024]{0:T(1024)S(1)} %pad_clamp_fusion), kind=kCustom, calls=%fused_computation.1 | custom fusion | bytes 2097184 | tf_op jit(solution)/shard_map/jit(_take)/gather | solution.py:200
  73.8 2.4 bitcast_select_fusion.u_ref
  76.2 0.0 all-to-all-done.x_ref
  76.3 1.6 copy-done
  77.9 14.5 %shard_map.88 = bf16[8,3,128,128]{3,2,1,0:T(8,128)(2,1)} custom-call(s32[42]{0:T(128)} %reshape_squeeze.15.rb_ref, bf16[8,3,4,128,128]{4,3,2,1,0:T(8,128)(2,1)} %copy-done, bf16[1024,512]{1,0:T(8,128)(2,1)} %bitcast_select_fusion.u_ref), custom_call_target="tpu_custom_call" | custom-call | flops 905969664 | bytes 1835008 | tf_op jit(solution)/shard_map/pallas_call | solution.py:113
  92.4 3.9 %all-to-all-start.4 = ((bf16[8,3,128,128]{3,2,1,0:T(8,128)(2,1)}), bf16[8,3,128,128]{3,2,1,0:T(8,128)(2,1)S(1)}, u32[]{:S(2)}, u32[]{:S(2)}) async-start(bf16[8,3,128,128]{3,2,1,0:T(8,128)(2,1)} %shard_map.88), calls=%async_computation.4 | async-start | bytes 1572864 | tf_op jit(solution)/shard_map/all_to_all | solution.py:228
  96.2 14.5 %shard_map.87 = bf16[8,3,128,128]{3,2,1,0:T(8,128)(2,1)} custom-call(s32[42]{0:T(128)} %reshape_squeeze.15.rb_ref, bf16[8,3,4,128,128]{4,3,2,1,0:T(8,128)(2,1)} %copy-done, bf16[1024,512]{1,0:T(8,128)(2,1)} %bitcast_select_fusion.u_ref), custom_call_target="tpu_custom_call" | custom-call | flops 905969664 | bytes 1835008 | tf_op jit(solution)/shard_map/pallas_call | solution.py:113
  110.7 4.2 %all-to-all-start.3 = ((bf16[8,3,128,128]{3,2,1,0:T(8,128)(2,1)}), bf16[8,3,128,128]{3,2,1,0:T(8,128)(2,1)S(1)}, u32[]{:S(2)}, u32[]{:S(2)}) async-start(bf16[8,3,128,128]{3,2,1,0:T(8,128)(2,1)} %shard_map.87), calls=%async_computation.3 | async-start | bytes 1572864 | tf_op jit(solution)/shard_map/all_to_all | solution.py:228
  114.9 14.5 %shard_map.86 = bf16[8,3,128,128]{3,2,1,0:T(8,128)(2,1)} custom-call(s32[42]{0:T(128)} %reshape_squeeze.15.rb_ref, bf16[8,3,4,128,128]{4,3,2,1,0:T(8,128)(2,1)} %copy-done, bf16[1024,512]{1,0:T(8,128)(2,1)} %bitcast_select_fusion.u_ref), custom_call_target="tpu_custom_call" | custom-call | flops 905969664 | bytes 1835008 | tf_op jit(solution)/shard_map/pallas_call | solution.py:113
  129.4 4.2 %all-to-all-start.2 = ((bf16[8,3,128,128]{3,2,1,0:T(8,128)(2,1)}), bf16[8,3,128,128]{3,2,1,0:T(8,128)(2,1)S(1)}, u32[]{:S(2)}, u32[]{:S(2)}) async-start(bf16[8,3,128,128]{3,2,1,0:T(8,128)(2,1)} %shard_map.86), calls=%async_computation.2 | async-start | bytes 1572864 | tf_op jit(solution)/shard_map/all_to_all | solution.py:228
  133.6 14.5 %shard_map.85 = bf16[8,3,128,128]{3,2,1,0:T(8,128)(2,1)} custom-call(s32[42]{0:T(128)} %reshape_squeeze.15.rb_ref, bf16[8,3,4,128,128]{4,3,2,1,0:T(8,128)(2,1)} %copy-done, bf16[1024,512]{1,0:T(8,128)(2,1)} %bitcast_select_fusion.u_ref), custom_call_target="tpu_custom_call" | custom-call | flops 905969664 | bytes 1835008 | tf_op jit(solution)/shard_map/pallas_call | solution.py:113
  148.1 16.9 %all_to_all.25.refs_0_ = bf16[8,3,128,128]{3,2,1,0:T(8,128)(2,1)} all-to-all(bf16[8,3,128,128]{3,2,1,0:T(8,128)(2,1)} %shard_map.85), channel_id=1, replica_groups=mesh['dp'=4,'context'=8] {'context'}, dimensions={0} | all-to-all | bytes 1572864 | tf_op jit(solution)/shard_map/all_to_all | solution.py:228
  165.0 97.3 %shard_map.89 = (bf16[1,128,4096]{2,1,0:T(8,128)(2,1)}, bf16[1,128,4096]{2,1,0:T(8,128)(2,1)}, bf16[1,128,4096]{2,1,0:T(8,128)(2,1)}) custom-call(bf16[8,3,128,128]{3,2,1,0:T(8,128)(2,1)} %all_to_all.25.refs_0_, bf16[8,3,128,128]{3,2,1,0:T(8,128)(2,1)} %copy-done.3, bf16[8,3,128,128]{3,2,1,0:T(8,128)(2,1)} %copy-done.2, bf16[8,3,128,128]{3,2,1,0:T(8,128)(2,1)} %copy-done.1), custom_call_target="tpu_custom_call" | custom-call | tf_op jit(solution)/shard_map/pallas_call | solution.py:155
  (24 shorter events, 0.1 us)
Async XLA Ops:
  0.6 12.4 %copy-start.4 = (bf16[1,128,4096]{2,1,0:T(8,128)(2,1)S(1)}, bf16[1,128,4096]{2,1,0:T(8,128)(2,1)}, u32[]{:S(2)}) copy-start(bf16[1,128,4096]{2,1,0:T(8,128)(2,1)} %param.7) | copy-start | bytes 3145732
  0.6 26.6 %collective-permute-start = (bf16[128,2048]{1,0:T(8,128)(2,1)}, bf16[128,2048]{1,0:T(8,128)(2,1)}, u32[]{:S(2)}, u32[]{:S(2)}) collective-permute-start(bf16[128,2048]{1,0:T(8,128)(2,1)} %bitcast.43), channel_id=1, source_target_pairs={{0,2},{1,3},{2,4},{3,5},{4,6},{5,7},{6,0},{7,1},{8,10},{9,11},{10,... | collective-permute-start | bytes 1572872 | tf_op jit(solution)/shard_map/ppermute | solution.py:186
  3.6 25.0 %collective-permute-start.1 = (bf16[128,2048]{1,0:T(8,128)(2,1)}, bf16[128,2048]{1,0:T(8,128)(2,1)}, u32[]{:S(2)}, u32[]{:S(2)}) collective-permute-start(bf16[128,2048]{1,0:T(8,128)(2,1)} %bitcast.44), channel_id=1, source_target_pairs={{0,4},{1,5},{2,6},{3,7},{4,0},{5,1},{6,2},{7,3},{8,12},{9,13},{10,... | collective-permute-start | bytes 1572872 | tf_op jit(solution)/shard_map/ppermute | solution.py:186
  5.2 23.9 %collective-permute-start.2 = (bf16[128,2048]{1,0:T(8,128)(2,1)}, bf16[128,2048]{1,0:T(8,128)(2,1)}, u32[]{:S(2)}, u32[]{:S(2)}) collective-permute-start(bf16[128,2048]{1,0:T(8,128)(2,1)} %bitcast.45), channel_id=1, source_target_pairs={{0,6},{1,7},{2,0},{3,1},{4,2},{5,3},{6,4},{7,5},{8,14},{9,15},{10,... | collective-permute-start | bytes 1572872 | tf_op jit(solution)/shard_map/ppermute | solution.py:186
  6.6 27.5 %collective-permute-start.4 = (bf16[128,2048]{1,0:T(8,128)(2,1)}, bf16[128,2048]{1,0:T(8,128)(2,1)}, u32[]{:S(2)}, u32[]{:S(2)}) collective-permute-start(bf16[128,2048]{1,0:T(8,128)(2,1)} %param.10), channel_id=1, source_target_pairs={{0,8},{8,16},{16,24},{24,0},{1,9},{9,17},{17,25},{25,1},{2,10},{10... | collective-permute-start | bytes 1572872 | tf_op jit(solution)/shard_map/ppermute | solution.py:178
  8.2 36.0 %collective-permute-start.5 = (bf16[128,2048]{1,0:T(8,128)(2,1)}, bf16[128,2048]{1,0:T(8,128)(2,1)}, u32[]{:S(2)}, u32[]{:S(2)}) collective-permute-start(bf16[128,2048]{1,0:T(8,128)(2,1)} %param.10), channel_id=1, source_target_pairs={{0,16},{8,24},{16,0},{24,8},{1,17},{9,25},{17,1},{25,9},{2,18},{10... | collective-permute-start | bytes 1572872 | tf_op jit(solution)/shard_map/ppermute | solution.py:178
  20.6 3.9 %copy-start.7 = (s32[1,14,3]{1,0,2:T(1,128)S(1)}, s32[1,14,3]{1,0,2:T(1,128)}, u32[]{:S(2)}) copy-start(s32[1,14,3]{1,0,2:T(1,128)} %param.11) | copy-start | bytes 508
  20.6 55.7 %all-to-all-start = ((bf16[8,3,4,128,128]{4,3,2,1,0:T(8,128)(2,1)}), bf16[8,3,4,128,128]{4,3,2,1,0:T(8,128)(2,1)S(1)}, u32[]{:S(2)}, u32[]{:S(2)}) async-start(bf16[8,3,4,128,128]{4,3,2,1,0:T(8,128)(2,1)} %pad_maximum_fusion), calls=%async_computation | async-start | bytes 6291456 | tf_op jit(solution)/shard_map/all_to_all | solution.py:218
  27.2 25.6 %collective-permute-start.6 = (bf16[128,2048]{1,0:T(8,128)(2,1)}, bf16[128,2048]{1,0:T(8,128)(2,1)S(1)}, u32[]{:S(2)}, u32[]{:S(2)}) collective-permute-start(bf16[128,2048]{1,0:T(8,128)(2,1)} %param.10), channel_id=1, source_target_pairs={{0,24},{8,0},{16,8},{24,16},{1,25},{9,1},{17,9},{25,17},{2,26},{10... | collective-permute-start | bytes 1572872 | tf_op jit(solution)/shard_map/ppermute | solution.py:178
  29.0 23.7 %copy-start.5 = (bf16[128,2048]{1,0:T(8,128)(2,1)S(1)}, bf16[128,2048]{1,0:T(8,128)(2,1)}, u32[]{:S(2)}) copy-start(bf16[128,2048]{1,0:T(8,128)(2,1)} %param.10) | copy-start | bytes 1572868
  32.2 32.9 %collective-permute-start.3 = (bf16[4,128,2048]{2,1,0:T(8,128)(2,1)}, bf16[4,128,2048]{2,1,0:T(8,128)(2,1)}, u32[]{:S(2)}, u32[]{:S(2)}) collective-permute-start(bf16[4,128,2048]{2,1,0:T(8,128)(2,1)} %pad_maximum_fusion.1), channel_id=1, source_target_pairs={{0,1},{1,0},{2,3},{3,2},{4,5},{5,4},{6,7},{7,6},{8,9},{9,8},{10,11... | collective-permute-start | bytes 6291464 | tf_op jit(solution)/shard_map/ppermute | solution.py:189
  63.0 2.8 %copy-start.6 = (bf16[8,128,2048]{2,1,0:T(8,128)(2,1)S(1)}, bf16[8,128,2048]{2,1,0:T(8,128)(2,1)}, u32[]{:S(2)}) copy-start(bf16[8,128,2048]{2,1,0:T(8,128)(2,1)} %constant_dynamic-update-slice_fusion.1) | copy-start | bytes 12582916
  76.2 1.6 copy-start
  92.4 18.3 %all-to-all-start.4 = ((bf16[8,3,128,128]{3,2,1,0:T(8,128)(2,1)}), bf16[8,3,128,128]{3,2,1,0:T(8,128)(2,1)S(1)}, u32[]{:S(2)}, u32[]{:S(2)}) async-start(bf16[8,3,128,128]{3,2,1,0:T(8,128)(2,1)} %shard_map.88), calls=%async_computation.4 | async-start | bytes 1572864 | tf_op jit(solution)/shard_map/all_to_all | solution.py:228
  110.7 18.7 %copy-start.1 = (bf16[8,3,128,128]{3,2,1,0:T(8,128)(2,1)}, bf16[8,3,128,128]{3,2,1,0:T(8,128)(2,1)S(1)}, u32[]{:S(2)}) copy-start(bf16[8,3,128,128]{3,2,1,0:T(8,128)(2,1)S(1)} %all-to-all-done.4.refs_3_) | copy-start | bytes 2359300
  110.7 18.7 %all-to-all-start.3 = ((bf16[8,3,128,128]{3,2,1,0:T(8,128)(2,1)}), bf16[8,3,128,128]{3,2,1,0:T(8,128)(2,1)S(1)}, u32[]{:S(2)}, u32[]{:S(2)}) async-start(bf16[8,3,128,128]{3,2,1,0:T(8,128)(2,1)} %shard_map.87), calls=%async_computation.3 | async-start | bytes 1572864 | tf_op jit(solution)/shard_map/all_to_all | solution.py:228
  129.4 18.7 %copy-start.2 = (bf16[8,3,128,128]{3,2,1,0:T(8,128)(2,1)}, bf16[8,3,128,128]{3,2,1,0:T(8,128)(2,1)S(1)}, u32[]{:S(2)}) copy-start(bf16[8,3,128,128]{3,2,1,0:T(8,128)(2,1)S(1)} %all-to-all-done.3.refs_2_) | copy-start | bytes 2359300
  129.4 18.7 %all-to-all-start.2 = ((bf16[8,3,128,128]{3,2,1,0:T(8,128)(2,1)}), bf16[8,3,128,128]{3,2,1,0:T(8,128)(2,1)S(1)}, u32[]{:S(2)}, u32[]{:S(2)}) async-start(bf16[8,3,128,128]{3,2,1,0:T(8,128)(2,1)} %shard_map.86), calls=%async_computation.2 | async-start | bytes 1572864 | tf_op jit(solution)/shard_map/all_to_all | solution.py:228
  148.1 16.9 %copy-start.3 = (bf16[8,3,128,128]{3,2,1,0:T(8,128)(2,1)}, bf16[8,3,128,128]{3,2,1,0:T(8,128)(2,1)S(1)}, u32[]{:S(2)}) copy-start(bf16[8,3,128,128]{3,2,1,0:T(8,128)(2,1)S(1)} %all-to-all-done.2.refs_1_) | copy-start | bytes 2359300

commit v11 on v9

--- a/solution.py
+++ b/solution.py
@@ -130,7 +130,7 @@
     )(random_ids.reshape(-1), stacked, upstream)
 
 
-def _assemble_kernel(*refs):
+def _assemble_kernel(*refs, first_head):
     pieces, outs = refs[:-3], refs[-3:]
     parts = pieces[0].shape[0]
     for c, piece in enumerate(pieces):
@@ -142,7 +142,33 @@
 
 def assemble(pieces, tokens, width):
     out = jax.ShapeDtypeStruct((1, tokens, width), jnp.bfloat16)
-    return pl.pallas_call(_assemble_kernel, out_shape=(out, out, out))(*pieces)
+    span = pieces[0].shape[0] * HD
+    early = len(pieces) - 1
+    whole = pl.BlockSpec(memory_space=pltpu.VMEM)
+    head_spec = pl.BlockSpec((1, tokens, early * span), lambda i: (0, 0, 0))
+    partial = pl.pallas_call(
+        functools.partial(_assemble_kernel, first_head=0),
+        out_shape=(out, out, out),
+        grid=(1,),
+        in_specs=[whole] * early,
+        out_specs=(head_spec, head_spec, head_spec),
+    )(*pieces[:early])
+    last_spec = pl.BlockSpec((1, tokens, span), lambda i: (0, 0, early))
+    return pl.pallas_call(
+        _assemble_last_kernel,
+        out_shape=(out, out, out),
+        grid=(1,),
+        in_specs=[whole, last_spec, last_spec, last_spec],
+        out_specs=(last_spec, last_spec, last_spec),
+        input_output_aliases={1: 0, 2: 1, 3: 2},
+    )(pieces[early], *partial)
+
+
+def _assemble_last_kernel(piece, _first, _second, _third, *outs):
+    parts = piece.shape[0]
+    for source in range(parts):
+        for g, out in enumerate(outs):
+            out[0, :, source * HD:(source + 1) * HD] = piece[source, g]
 
 
 def body(queries, key_rows, value_rows, cotangent, out_weight, random_blocks):

time: 170 us -> 169 us (level)
  blocking collectives: 16.9 us -> 0 us
  waiting for transfers between devices: 19.2 us -> 28.1 us
  starting transfers between devices: 27.5 us -> 31.8 us
  Pallas kernels: 62.3 us -> 64 us
    all_to_all x1 -> x0, blocking collectives: 16.9 us -> none  [body(): lax.all_to_all(grads, 'context', split_axis=0, concat_axis=0, tiled=True)]
    all_to_all x3 -> x4, waiting for transfers between devices: 0.01 us -> 8.96 us  [body(): lax.all_to_all(grads, 'context', split_axis=0, concat_axis=0, tiled=True)]
    all_to_all x3 -> x4, starting transfers between devices: 12.3 us -> 16.5 us  [body(): lax.all_to_all(grads, 'context', split_axis=0, concat_axis=0, tiled=True)]
    pallas_call x1 -> x2, Pallas kernels: 4.36 us -> 6.08 us  [the longest x1 3.64 us: assemble(): pl.pallas_call(functools.partial(_assemble_kernel, first_head=0), out_sha...]
    unnamed x24 -> x26, local copies, waits for them, and re-layouts: 14 us -> 14.9 us
  transfers between devices with their start and end apart: 11 -> 12, of which waited for: 3 -> 4; matrix products, arithmetic and copies ran while one was open for 24% -> 24% of each run, Pallas kernels for 26% -> 28%
where the time goes in v11:
time: 169 us; the launch traced here: 168 us
  Pallas kernels  64 us (38%)
  starting transfers between devices  31.8 us (19%)
  waiting for transfers between devices  28.1 us (17%)
  local copies, waits for them, and re-layouts  26.6 us (16%)
  other arithmetic  13.7 us (8%)
  matrix products  3.34 us (2%)
    pallas_call x4, Pallas kernels, attention_grads(): pl.pallas_call(_attention_kernel, out_shape=out, grid_spec=pltpu.Prefetch...  58 us
    ppermute x3, waiting for transfers between devices, body(): lax.ppermute(out_weight, 'dp', [(a, (a + s) % dp) for a in range(dp)])  18.7 us
    all_to_all x4, starting transfers between devices, body(): lax.all_to_all(grads, 'context', split_axis=0, concat_axis=0, tiled=True)  16.5 us
    unnamed x26, local copies, waits for them, and re-layouts  14.9 us
    all_to_all x4, waiting for transfers between devices, body(): lax.all_to_all(grads, 'context', split_axis=0, concat_axis=0, tiled=True)  8.96 us
    ppermute x3, starting transfers between devices, body(): lax.ppermute(local_cotangent, 'context', [(a, (a + s) % ctx) for a in ran...  5.94 us
    ppermute x3, starting transfers between devices, body(): lax.ppermute(out_weight, 'dp', [(a, (a + s) % dp) for a in range(dp)])  5.54 us
    all_to_all x1, starting transfers between devices, body(): lax.all_to_all(stacked, 'context', split_axis=0, concat_axis=0, tiled=True)  3.78 us
  transfers between devices with their start and end apart: 12, of which 4 were waited for; matrix products, arithmetic and copies ran while one was open for 24% of the time, Pallas kernels for 28%

profile of v11, /device:TPU:0, one launch (start us, length us, event | category | flops | bytes accessed | tf_op | source)
XLA Modules:
  0.0 168.3 jit_solution(9198369173305841569)
XLA Ops:
  0.6 3.0 %collective-permute-start = (bf16[128,2048]{1,0:T(8,128)(2,1)}, bf16[128,2048]{1,0:T(8,128)(2,1)}, u32[]{:S(2)}, u32[]{:S(2)}) collective-permute-start(bf16[128,2048]{1,0:T(8,128)(2,1)} %bitcast.43), channel_id=1, source_target_pairs={{0,2},{1,3},{2,4},{3,5},{4,6},{5,7},{6,0},{7,1},{8,10},{9,11},{10,... | collective-permute-start | bytes 1572872 | tf_op jit(solution)/shard_map/ppermute | solution.py:196
  3.6 1.5 collective-permute-start.1
  5.2 1.4 collective-permute-start.2
  6.6 1.6 collective-permute-start.4
  8.2 2.6 %collective-permute-start.5 = (bf16[128,2048]{1,0:T(8,128)(2,1)}, bf16[128,2048]{1,0:T(8,128)(2,1)}, u32[]{:S(2)}, u32[]{:S(2)}) collective-permute-start(bf16[128,2048]{1,0:T(8,128)(2,1)} %param.10), channel_id=1, source_target_pairs={{0,16},{8,24},{16,0},{24,8},{1,17},{9,25},{17,1},{25,9},{2,18},{10... | collective-permute-start | bytes 1572872 | tf_op jit(solution)/shard_map/ppermute | solution.py:188
  10.8 1.6 copy.14
  12.4 0.7 copy.15
  13.1 0.7 copy.16
  13.7 0.7 copy.17
  14.4 1.6 copy.18
  16.0 1.3 copy.19
  17.3 3.2 %pad_maximum_fusion = bf16[8,3,4,128,128]{4,3,2,1,0:T(8,128)(2,1)} fusion(bf16[8,1,4,128,128]{4,3,2,1,0:T(8,128)(2,1)} %bitcast.41, bf16[8,1,4,128,128]{4,3,2,1,0:T(8,128)(2,1)S(1)} %bitcast.40, bf16[8,1,4,128,128]{4,3,2,1,0:T(8,128)(2,1)S(1)} %bitcast.39), kind=kLoop, calls=%fused_computation.2 | loop fusion | flops 3145728 | bytes 6291456 | tf_op jit(solution)/shard_map/stack | solution.py:227
  20.6 3.8 %all-to-all-start = ((bf16[8,3,4,128,128]{4,3,2,1,0:T(8,128)(2,1)}), bf16[8,3,4,128,128]{4,3,2,1,0:T(8,128)(2,1)S(1)}, u32[]{:S(2)}, u32[]{:S(2)}) async-start(bf16[8,3,4,128,128]{4,3,2,1,0:T(8,128)(2,1)} %pad_maximum_fusion), calls=%async_computation | async-start | bytes 6291456 | tf_op jit(solution)/shard_map/all_to_all | solution.py:228
  24.5 0.1 copy.13
  24.6 0.7 reshape_squeeze.15.rb_ref
  25.3 0.1 broadcast_bitcast_fusion
  25.4 1.9 %constant_dynamic-update-slice_fusion.4 = bf16[8,128,2048]{2,1,0:T(8,128)(2,1)} fusion(bf16[1,128,2048]{2,1,0:T(8,128)(2,1)} %param.9), kind=kLoop, calls=%fused_computation.12 | loop fusion | bytes 1048576
  27.2 0.0 collective-permute-done
  27.2 1.4 collective-permute-start.6
  28.6 0.4 collective-permute-done.2
  29.0 3.1 %pad_maximum_fusion.1 = bf16[4,128,2048]{2,1,0:T(8,128)(2,1)} fusion(bf16[1,128,2048]{2,1,0:T(8,128)(2,1)} %bitcast.13, bf16[1,128,2048]{2,1,0:T(8,128)(2,1)} %bitcast.12, bf16[1,128,2048]{2,1,0:T(8,128)(2,1)} %bitcast.11, bf16[1,128,2048]{2,1,0:T(8,128)(2,1)} %param.9), kind=kLoop, calls=%fused_computation.3 | loop fusion | flops 3145728 | bytes 4194304 | tf_op jit(solution)/shard_map/stack | solution.py:195
  32.2 1.9 %constant_dynamic-update-slice_fusion.3 = bf16[8,128,2048]{2,1,0:T(8,128)(2,1)} fusion(bf16[8,128,2048]{2,1,0:T(8,128)(2,1)} %constant_dynamic-update-slice_fusion.4, bf16[128,2048]{1,0:T(8,128)(2,1)} %collective-permute-done), kind=kLoop, calls=%fused_computation.11 | loop fusion | bytes 1048576
  34.1 10.1 %collective-permute-done.5 = bf16[128,2048]{1,0:T(8,128)(2,1)} collective-permute-done((bf16[128,2048]{1,0:T(8,128)(2,1)}, bf16[128,2048]{1,0:T(8,128)(2,1)}, u32[]{:S(2)}, u32[]{:S(2)}) %collective-permute-start.5) | collective-permute-done | bytes 524320 | tf_op jit(solution)/shard_map/ppermute | solution.py:188
  44.2 8.6 %collective-permute-done.6 = bf16[128,2048]{1,0:T(8,128)(2,1)S(1)} collective-permute-done((bf16[128,2048]{1,0:T(8,128)(2,1)}, bf16[128,2048]{1,0:T(8,128)(2,1)S(1)}, u32[]{:S(2)}, u32[]{:S(2)}) %collective-permute-start.6) | collective-permute-done | bytes 524320 | tf_op jit(solution)/shard_map/ppermute | solution.py:188
  52.8 2.8 %pad_maximum_fusion.2 = bf16[4,128,2048]{2,1,0:T(8,128)(2,1)} fusion(bf16[1,128,2048]{2,1,0:T(8,128)(2,1)S(1)} %bitcast.48, bf16[1,128,2048]{2,1,0:T(8,128)(2,1)} %bitcast.17, bf16[1,128,2048]{2,1,0:T(8,128)(2,1)} %bitcast.16, bf16[1,128,2048]{2,1,0:T(8,128)(2,1)S(1)} %bitcast.47), kind=kLoop, calls=%fused_computation.4 | loop fusion | flops 3145728 | bytes 4194304 | tf_op jit(solution)/shard_map/stack | solution.py:192
  55.6 3.7 %gather_fusion = bf16[4,128,2048]{2,1,0:T(8,128)(2,1)} fusion(bf16[4,128,2048]{2,1,0:T(8,128)(2,1)} %pad_maximum_fusion.2, s32[1024]{0:T(1024)S(1)} %pad_clamp_fusion.1), kind=kCustom, calls=%fused_computation | custom fusion | bytes 4194320 | tf_op jit(solution)/shard_map/jit(_take)/gather | solution.py:192
  59.3 1.9 %constant_dynamic-update-slice_fusion.2 = bf16[8,128,2048]{2,1,0:T(8,128)(2,1)} fusion(bf16[8,128,2048]{2,1,0:T(8,128)(2,1)} %constant_dynamic-update-slice_fusion.3, bf16[128,2048]{1,0:T(8,128)(2,1)} %collective-permute-done.1), kind=kLoop, calls=%fused_computation.10 | loop fusion | bytes 1048576
  61.2 1.9 %constant_dynamic-update-slice_fusion.1 = bf16[8,128,2048]{2,1,0:T(8,128)(2,1)} fusion(bf16[8,128,2048]{2,1,0:T(8,128)(2,1)} %constant_dynamic-update-slice_fusion.2, bf16[128,2048]{1,0:T(8,128)(2,1)} %collective-permute-done.2), kind=kLoop, calls=%fused_computation.9 | loop fusion | bytes 1048576
  63.1 2.0 %broadcast_select_fusion = bf16[4,128,2048]{2,1,0:T(8,128)(2,1)S(1)} fusion(bf16[4,128,2048]{2,1,0:T(8,128)(2,1)} %gather_fusion, pred[4]{0:T(512)(128)(4,1)S(1)} %compare_and_fusion), kind=kLoop, calls=%fused_computation.5 | loop fusion | flops 1048576 | bytes 4194308 | tf_op jit(solution)/shard_map/jit(_take)/select_n | solution.py:192
  65.1 0.0 collective-permute-done.3
  65.1 0.8 copy-done.7
  65.9 1.8 %constant_dynamic-update-slice_fusion = bf16[8,128,2048]{2,1,0:T(8,128)(2,1)S(1)} fusion(bf16[8,128,2048]{2,1,0:T(8,128)(2,1)S(1)} %copy-done.7, bf16[4,128,2048]{2,1,0:T(8,128)(2,1)} %collective-permute-done.3), kind=kLoop, calls=%fused_computation.8 | loop fusion | bytes 4194304 | tf_op jit(solution)/shard_map/concatenate | solution.py:200
  67.8 3.3 %convolution_convert_fusion = bf16[1024,512]{1,0:T(8,128)(2,1)} fusion(bf16[1024,2048]{1,0:T(8,128)(2,1)S(1)} %bitcast.49, bf16[512,2048]{1,0:T(8,128)(2,1)S(1)} %bitcast.42), kind=kOutput, calls=%fused_computation.6 | convolution fusion | flops 2148007936 | bytes 7340032 | tf_op jit(solution)/shard_map/dot_general | solution.py:201
  71.1 2.8 %gather_fusion.1 = bf16[8,128,512]{2,1,0:T(8,128)(2,1)} fusion(bf16[8,128,512]{2,1,0:T(8,128)(2,1)} %bitcast.46, s32[1024]{0:T(1024)S(1)} %pad_clamp_fusion), kind=kCustom, calls=%fused_computation.1 | custom fusion | bytes 2097184 | tf_op jit(solution)/shard_map/jit(_take)/gather | solution.py:210
  73.9 2.4 %bitcast_select_fusion.u_ref = bf16[1024,512]{1,0:T(8,128)(2,1)} fusion(bf16[8,128,512]{2,1,0:T(8,128)(2,1)} %gather_fusion.1, pred[1024]{0:T(1024)(128)(4,1)S(1)} %broadcast_bitcast_fusion), kind=kLoop, calls=%fused_computation.7 | loop fusion | flops 524288 | bytes 2098176 | tf_op jit(solution)/shard_map/jit(_take)/select_n | solution.py:210
  76.3 1.6 copy-done
  77.9 14.5 %shard_map.88 = bf16[8,3,128,128]{3,2,1,0:T(8,128)(2,1)} custom-call(s32[42]{0:T(128)} %reshape_squeeze.15.rb_ref, bf16[8,3,4,128,128]{4,3,2,1,0:T(8,128)(2,1)} %copy-done, bf16[1024,512]{1,0:T(8,128)(2,1)} %bitcast_select_fusion.u_ref), custom_call_target="tpu_custom_call" | custom-call | flops 905969664 | bytes 1835008 | tf_op jit(solution)/shard_map/pallas_call | solution.py:113
  92.4 3.8 %all-to-all-start.4 = ((bf16[8,3,128,128]{3,2,1,0:T(8,128)(2,1)}), bf16[8,3,128,128]{3,2,1,0:T(8,128)(2,1)S(1)}, u32[]{:S(2)}, u32[]{:S(2)}) async-start(bf16[8,3,128,128]{3,2,1,0:T(8,128)(2,1)} %shard_map.88), calls=%async_computation.4 | async-start | bytes 1572864 | tf_op jit(solution)/shard_map/all_to_all | solution.py:238
  96.3 14.5 %shard_map.87 = bf16[8,3,128,128]{3,2,1,0:T(8,128)(2,1)} custom-call(s32[42]{0:T(128)} %reshape_squeeze.15.rb_ref, bf16[8,3,4,128,128]{4,3,2,1,0:T(8,128)(2,1)} %copy-done, bf16[1024,512]{1,0:T(8,128)(2,1)} %bitcast_select_fusion.u_ref), custom_call_target="tpu_custom_call" | custom-call | flops 905969664 | bytes 1835008 | tf_op jit(solution)/shard_map/pallas_call | solution.py:113
  110.8 4.2 %all-to-all-start.3 = ((bf16[8,3,128,128]{3,2,1,0:T(8,128)(2,1)}), bf16[8,3,128,128]{3,2,1,0:T(8,128)(2,1)S(1)}, u32[]{:S(2)}, u32[]{:S(2)}) async-start(bf16[8,3,128,128]{3,2,1,0:T(8,128)(2,1)} %shard_map.87), calls=%async_computation.3 | async-start | bytes 1572864 | tf_op jit(solution)/shard_map/all_to_all | solution.py:238
  115.0 14.5 %shard_map.86 = bf16[8,3,128,128]{3,2,1,0:T(8,128)(2,1)} custom-call(s32[42]{0:T(128)} %reshape_squeeze.15.rb_ref, bf16[8,3,4,128,128]{4,3,2,1,0:T(8,128)(2,1)} %copy-done, bf16[1024,512]{1,0:T(8,128)(2,1)} %bitcast_select_fusion.u_ref), custom_call_target="tpu_custom_call" | custom-call | flops 905969664 | bytes 1835008 | tf_op jit(solution)/shard_map/pallas_call | solution.py:113
  129.5 4.2 %all-to-all-start.2 = ((bf16[8,3,128,128]{3,2,1,0:T(8,128)(2,1)}), bf16[8,3,128,128]{3,2,1,0:T(8,128)(2,1)S(1)}, u32[]{:S(2)}, u32[]{:S(2)}) async-start(bf16[8,3,128,128]{3,2,1,0:T(8,128)(2,1)} %shard_map.86), calls=%async_computation.2 | async-start | bytes 1572864 | tf_op jit(solution)/shard_map/all_to_all | solution.py:238
  133.7 14.5 %shard_map.85 = bf16[8,3,128,128]{3,2,1,0:T(8,128)(2,1)} custom-call(s32[42]{0:T(128)} %reshape_squeeze.15.rb_ref, bf16[8,3,4,128,128]{4,3,2,1,0:T(8,128)(2,1)} %copy-done, bf16[1024,512]{1,0:T(8,128)(2,1)} %bitcast_select_fusion.u_ref), custom_call_target="tpu_custom_call" | custom-call | flops 905969664 | bytes 1835008 | tf_op jit(solution)/shard_map/pallas_call | solution.py:113
  148.2 4.2 %all-to-all-start.1 = ((bf16[8,3,128,128]{3,2,1,0:T(8,128)(2,1)}), bf16[8,3,128,128]{3,2,1,0:T(8,128)(2,1)S(1)}, u32[]{:S(2)}, u32[]{:S(2)}) async-start(bf16[8,3,128,128]{3,2,1,0:T(8,128)(2,1)} %shard_map.85), calls=%async_computation.1 | async-start | bytes 1572864 | tf_op jit(solution)/shard_map/all_to_all | solution.py:238
  152.4 3.6 %shard_map.89 = (bf16[1,128,4096]{2,1,0:T(8,128)(2,1)}, bf16[1,128,4096]{2,1,0:T(8,128)(2,1)}, bf16[1,128,4096]{2,1,0:T(8,128)(2,1)}) custom-call(bf16[8,3,128,128]{3,2,1,0:T(8,128)(2,1)} %copy-done.3, bf16[8,3,128,128]{3,2,1,0:T(8,128)(2,1)} %copy-done.2, bf16[8,3,128,128]{3,2,1,0:T(8,128)(2,1)} %copy-done.1), custom_call_target="tpu_custom_call" | custom-call | tf_op jit(solution)/shard_map/pallas_call | solution.py:149
  156.1 9.0 %all-to-all-done.1.piece = bf16[8,3,128,128]{3,2,1,0:T(8,128)(2,1)S(1)} async-done(((bf16[8,3,128,128]{3,2,1,0:T(8,128)(2,1)}), bf16[8,3,128,128]{3,2,1,0:T(8,128)(2,1)S(1)}, u32[]{:S(2)}, u32[]{:S(2)}) %all-to-all-start.1) | async-done | bytes 786464 | tf_op jit(solution)/shard_map/all_to_all | solution.py:238
  165.0 0.9 copy-done.4
  165.9 2.4 %shard_map.90 = (bf16[1,128,4096]{2,1,0:T(8,128)(2,1)}, bf16[1,128,4096]{2,1,0:T(8,128)(2,1)}, bf16[1,128,4096]{2,1,0:T(8,128)(2,1)}) custom-call(bf16[8,3,128,128]{3,2,1,0:T(8,128)(2,1)} %copy-done.4, bf16[1,128,4096]{2,1,0:T(8,128)(2,1)} %get-tuple-element.6._first, ...), custom_call_target="tpu_custom_call", output_to_operand_aliasing={{0}: (1, {}), {1}: (2, {}), {2}: (3, {})} | custom-call | tf_op jit(solution)/shard_map/pallas_call | solution.py:157
  (28 shorter events, 0.1 us)
Async XLA Ops:
  0.6 12.4 %copy-start.5 = (bf16[1,128,4096]{2,1,0:T(8,128)(2,1)S(1)}, bf16[1,128,4096]{2,1,0:T(8,128)(2,1)}, u32[]{:S(2)}) copy-start(bf16[1,128,4096]{2,1,0:T(8,128)(2,1)} %param.7) | copy-start | bytes 3145732
  0.6 26.6 %collective-permute-start = (bf16[128,2048]{1,0:T(8,128)(2,1)}, bf16[128,2048]{1,0:T(8,128)(2,1)}, u32[]{:S(2)}, u32[]{:S(2)}) collective-permute-start(bf16[128,2048]{1,0:T(8,128)(2,1)} %bitcast.43), channel_id=1, source_target_pairs={{0,2},{1,3},{2,4},{3,5},{4,6},{5,7},{6,0},{7,1},{8,10},{9,11},{10,... | collective-permute-start | bytes 1572872 | tf_op jit(solution)/shard_map/ppermute | solution.py:196
  3.6 25.0 %collective-permute-start.1 = (bf16[128,2048]{1,0:T(8,128)(2,1)}, bf16[128,2048]{1,0:T(8,128)(2,1)}, u32[]{:S(2)}, u32[]{:S(2)}) collective-permute-start(bf16[128,2048]{1,0:T(8,128)(2,1)} %bitcast.44), channel_id=1, source_target_pairs={{0,4},{1,5},{2,6},{3,7},{4,0},{5,1},{6,2},{7,3},{8,12},{9,13},{10,... | collective-permute-start | bytes 1572872 | tf_op jit(solution)/shard_map/ppermute | solution.py:196
  5.2 23.9 %collective-permute-start.2 = (bf16[128,2048]{1,0:T(8,128)(2,1)}, bf16[128,2048]{1,0:T(8,128)(2,1)}, u32[]{:S(2)}, u32[]{:S(2)}) collective-permute-start(bf16[128,2048]{1,0:T(8,128)(2,1)} %bitcast.45), channel_id=1, source_target_pairs={{0,6},{1,7},{2,0},{3,1},{4,2},{5,3},{6,4},{7,5},{8,14},{9,15},{10,... | collective-permute-start | bytes 1572872 | tf_op jit(solution)/shard_map/ppermute | solution.py:196
  6.6 27.5 %collective-permute-start.4 = (bf16[128,2048]{1,0:T(8,128)(2,1)}, bf16[128,2048]{1,0:T(8,128)(2,1)}, u32[]{:S(2)}, u32[]{:S(2)}) collective-permute-start(bf16[128,2048]{1,0:T(8,128)(2,1)} %param.10), channel_id=1, source_target_pairs={{0,8},{8,16},{16,24},{24,0},{1,9},{9,17},{17,25},{25,1},{2,10},{10... | collective-permute-start | bytes 1572872 | tf_op jit(solution)/shard_map/ppermute | solution.py:188
  8.2 36.0 %collective-permute-start.5 = (bf16[128,2048]{1,0:T(8,128)(2,1)}, bf16[128,2048]{1,0:T(8,128)(2,1)}, u32[]{:S(2)}, u32[]{:S(2)}) collective-permute-start(bf16[128,2048]{1,0:T(8,128)(2,1)} %param.10), channel_id=1, source_target_pairs={{0,16},{8,24},{16,0},{24,8},{1,17},{9,25},{17,1},{25,9},{2,18},{10... | collective-permute-start | bytes 1572872 | tf_op jit(solution)/shard_map/ppermute | solution.py:188
  20.6 3.9 %copy-start.8 = (s32[1,14,3]{1,0,2:T(1,128)S(1)}, s32[1,14,3]{1,0,2:T(1,128)}, u32[]{:S(2)}) copy-start(s32[1,14,3]{1,0,2:T(1,128)} %param.11) | copy-start | bytes 508
  20.6 55.7 %all-to-all-start = ((bf16[8,3,4,128,128]{4,3,2,1,0:T(8,128)(2,1)}), bf16[8,3,4,128,128]{4,3,2,1,0:T(8,128)(2,1)S(1)}, u32[]{:S(2)}, u32[]{:S(2)}) async-start(bf16[8,3,4,128,128]{4,3,2,1,0:T(8,128)(2,1)} %pad_maximum_fusion), calls=%async_computation | async-start | bytes 6291456 | tf_op jit(solution)/shard_map/all_to_all | solution.py:228
  27.2 25.6 %collective-permute-start.6 = (bf16[128,2048]{1,0:T(8,128)(2,1)}, bf16[128,2048]{1,0:T(8,128)(2,1)S(1)}, u32[]{:S(2)}, u32[]{:S(2)}) collective-permute-start(bf16[128,2048]{1,0:T(8,128)(2,1)} %param.10), channel_id=1, source_target_pairs={{0,24},{8,0},{16,8},{24,16},{1,25},{9,1},{17,9},{25,17},{2,26},{10... | collective-permute-start | bytes 1572872 | tf_op jit(solution)/shard_map/ppermute | solution.py:188
  29.0 23.8 %copy-start.6 = (bf16[128,2048]{1,0:T(8,128)(2,1)S(1)}, bf16[128,2048]{1,0:T(8,128)(2,1)}, u32[]{:S(2)}) copy-start(bf16[128,2048]{1,0:T(8,128)(2,1)} %param.10) | copy-start | bytes 1572868
  32.2 32.9 %collective-permute-start.3 = (bf16[4,128,2048]{2,1,0:T(8,128)(2,1)}, bf16[4,128,2048]{2,1,0:T(8,128)(2,1)}, u32[]{:S(2)}, u32[]{:S(2)}) collective-permute-start(bf16[4,128,2048]{2,1,0:T(8,128)(2,1)} %pad_maximum_fusion.1), channel_id=1, source_target_pairs={{0,1},{1,0},{2,3},{3,2},{4,5},{5,4},{6,7},{7,6},{8,9},{9,8},{10,11... | collective-permute-start | bytes 6291464 | tf_op jit(solution)/shard_map/ppermute | solution.py:199
  63.1 2.8 %copy-start.7 = (bf16[8,128,2048]{2,1,0:T(8,128)(2,1)S(1)}, bf16[8,128,2048]{2,1,0:T(8,128)(2,1)}, u32[]{:S(2)}) copy-start(bf16[8,128,2048]{2,1,0:T(8,128)(2,1)} %constant_dynamic-update-slice_fusion.1) | copy-start | bytes 12582916
  76.3 1.6 copy-start
  92.4 18.3 %all-to-all-start.4 = ((bf16[8,3,128,128]{3,2,1,0:T(8,128)(2,1)}), bf16[8,3,128,128]{3,2,1,0:T(8,128)(2,1)S(1)}, u32[]{:S(2)}, u32[]{:S(2)}) async-start(bf16[8,3,128,128]{3,2,1,0:T(8,128)(2,1)} %shard_map.88), calls=%async_computation.4 | async-start | bytes 1572864 | tf_op jit(solution)/shard_map/all_to_all | solution.py:238
  110.8 18.7 %copy-start.1 = (bf16[8,3,128,128]{3,2,1,0:T(8,128)(2,1)}, bf16[8,3,128,128]{3,2,1,0:T(8,128)(2,1)S(1)}, u32[]{:S(2)}) copy-start(bf16[8,3,128,128]{3,2,1,0:T(8,128)(2,1)S(1)} %all-to-all-done.4.refs_2_) | copy-start | bytes 2359300
  110.8 18.7 %all-to-all-start.3 = ((bf16[8,3,128,128]{3,2,1,0:T(8,128)(2,1)}), bf16[8,3,128,128]{3,2,1,0:T(8,128)(2,1)S(1)}, u32[]{:S(2)}, u32[]{:S(2)}) async-start(bf16[8,3,128,128]{3,2,1,0:T(8,128)(2,1)} %shard_map.87), calls=%async_computation.3 | async-start | bytes 1572864 | tf_op jit(solution)/shard_map/all_to_all | solution.py:238
  129.5 18.7 %copy-start.2 = (bf16[8,3,128,128]{3,2,1,0:T(8,128)(2,1)}, bf16[8,3,128,128]{3,2,1,0:T(8,128)(2,1)S(1)}, u32[]{:S(2)}) copy-start(bf16[8,3,128,128]{3,2,1,0:T(8,128)(2,1)S(1)} %all-to-all-done.3.refs_1_) | copy-start | bytes 2359300
  129.5 18.7 %all-to-all-start.2 = ((bf16[8,3,128,128]{3,2,1,0:T(8,128)(2,1)}), bf16[8,3,128,128]{3,2,1,0:T(8,128)(2,1)S(1)}, u32[]{:S(2)}, u32[]{:S(2)}) async-start(bf16[8,3,128,128]{3,2,1,0:T(8,128)(2,1)} %shard_map.86), calls=%async_computation.2 | async-start | bytes 1572864 | tf_op jit(solution)/shard_map/all_to_all | solution.py:238
  148.2 4.2 %copy-start.3 = (bf16[8,3,128,128]{3,2,1,0:T(8,128)(2,1)}, bf16[8,3,128,128]{3,2,1,0:T(8,128)(2,1)S(1)}, u32[]{:S(2)}) copy-start(bf16[8,3,128,128]{3,2,1,0:T(8,128)(2,1)S(1)} %all-to-all-done.2.refs_0_) | copy-start | bytes 2359300
  148.2 16.8 %all-to-all-start.1 = ((bf16[8,3,128,128]{3,2,1,0:T(8,128)(2,1)}), bf16[8,3,128,128]{3,2,1,0:T(8,128)(2,1)S(1)}, u32[]{:S(2)}, u32[]{:S(2)}) async-start(bf16[8,3,128,128]{3,2,1,0:T(8,128)(2,1)} %shard_map.85), calls=%async_computation.1 | async-start | bytes 1572864 | tf_op jit(solution)/shard_map/all_to_all | solution.py:238
  165.0 0.9 copy-start.4

commit v12 on v11

--- a/solution.py
+++ b/solution.py
@@ -26,7 +26,7 @@
     return lax.dot_general(a, b, (((1,), (0,)), ((), ())), preferred_element_type=jnp.float32)
 
 
-def _attention_kernel(rb_ref, x_ref, u_ref, o_ref, dk_acc, dv_acc, kg_ref, vg_ref):
+def _attention_kernel(rb_ref, pos_ref, x_ref, u_ref, o_ref, dk_acc, dv_acc, kg_ref, vg_ref):
     parts, _, tokens, _ = x_ref.shape
     per_part = tokens // BLOCK
     length = parts * tokens
@@ -39,6 +39,10 @@
         else:
             offset = pl.multiple_of((block % per_part) * BLOCK, BLOCK)
         return ref.at[block // per_part, which, pl.ds(offset, BLOCK), :]
+
+    def upstream_rows(block):
+        offset = pos_ref[block // per_part] * tokens + (block % per_part) * BLOCK
+        return u_ref[pl.ds(pl.multiple_of(offset, BLOCK), BLOCK), :]
 
     def softmax_grads(qb, ub, keys, values, mask):
         scores = _nt(qb, keys) * factor
@@ -61,9 +65,7 @@
     values_all = x_ref[:, 2, :, :].reshape(length, HD)
     last = count - 1
     qb = jnp.concatenate([rows(x_ref, 0, 0)[...], rows(x_ref, 0, last)[...]], axis=0)
-    ub = jnp.concatenate(
-        [u_ref[0:BLOCK, :], u_ref[last * BLOCK:(last + 1) * BLOCK, :]], axis=0
-    )
+    ub = jnp.concatenate([upstream_rows(0), upstream_rows(last)], axis=0)
     query_grad, key_grad, value_grad = softmax_grads(qb, ub, keys_all, values_all, None)
     query_grad = query_grad.astype(jnp.bfloat16)
     rows(o_ref, 0, 0)[...] = query_grad[:BLOCK]
@@ -83,7 +85,7 @@
             vg_ref[slot * BLOCK:(slot + 1) * BLOCK, :] = rows(x_ref, 2, block)[...]
         start = pl.multiple_of(m * BLOCK, BLOCK)
         qb = rows(x_ref, 0, m)[...]
-        ub = u_ref[pl.ds(start, BLOCK), :]
+        ub = upstream_rows(m)
         mask = ((columns == 2) & (m == 1)) | ((columns == 4) & (m == count - 2))
         query_grad, key_grad, value_grad = softmax_grads(qb, ub, kg_ref[...], vg_ref[...], mask)
         rows(o_ref, 0, m)[...] = query_grad.astype(jnp.bfloat16)
@@ -98,13 +100,13 @@
     o_ref[:, 2, :, :] = dv_acc[...].reshape(parts, tokens, HD).astype(jnp.bfloat16)
 
 
-def attention_grads(stacked, upstream, head, random_ids):
+def attention_grads(stacked, upstream, head, positions, random_ids):
     parts, _, _, tokens, _ = stacked.shape
     length = parts * tokens
     count = length // BLOCK
-    source = pl.BlockSpec((parts, 3, None, tokens, HD), lambda h, rb: (0, 0, head, 0, 0))
-    whole = pl.BlockSpec((parts, 3, tokens, HD), lambda h, rb: (0, 0, 0, 0))
-    spec = pl.BlockSpec((length, HD), lambda h, rb: (0, head))
+    source = pl.BlockSpec((parts, 3, None, tokens, HD), lambda h, rb, ps: (0, 0, head, 0, 0))
+    whole = pl.BlockSpec((parts, 3, tokens, HD), lambda h, rb, ps: (0, 0, 0, 0))
+    spec = pl.BlockSpec((length, HD), lambda h, rb, ps: (0, head))
     out = jax.ShapeDtypeStruct((parts, 3, tokens, HD), jnp.bfloat16)
     pairs = 2 * BLOCK * length + (count - 2) * BLOCK * SLOTS * BLOCK
     cost = pl.CostEstimate(
@@ -114,7 +116,7 @@
         _attention_kernel,
         out_shape=out,
         grid_spec=pltpu.PrefetchScalarGridSpec(
-            num_scalar_prefetch=1,
+            num_scalar_prefetch=2,
             grid=(1,),
             in_specs=[source, spec],
             out_specs=whole,
@@ -127,7 +129,7 @@
         ),
         compiler_params=pltpu.CompilerParams(dimension_semantics=("arbitrary",)),
         cost_estimate=cost,
-    )(random_ids.reshape(-1), stacked, upstream)
+    )(random_ids.reshape(-1), positions, stacked, upstream)
 
 
 def _assemble_kernel(*refs, first_head):
@@ -207,8 +209,7 @@
         position = jnp.where(
             same, ((j - source) % ctx) // 2, ctx // 2 + (((j ^ 1) - source) % ctx) // 2
         )
-        upstream = jnp.take(upstream.reshape(ctx, tokens, -1), position, axis=0)
-        upstream = upstream.reshape(ctx * tokens, -1)
+        positions = position.astype(jnp.int32)
 
         def chunk(array):
             return array.reshape(tokens, dp, ctx, HD).transpose(2, 1, 0, 3)
@@ -220,6 +221,7 @@
             preferred_element_type=jnp.float32,
         ).astype(jnp.bfloat16)
         local = local + (upstream,)
+        positions = jnp.arange(ctx, dtype=jnp.int32)
 
         def chunk(array):
             return array.reshape(tokens, ctx, local_heads, HD).transpose(1, 2, 0, 3)
@@ -232,9 +234,9 @@
     pieces = []
     for c in range(local_heads):
         if strided:
-            grads = attention_grads(moved, upstream, c, random_blocks[0])
+            grads = attention_grads(moved, upstream, c, positions, random_blocks[0])
         else:
-            grads = attention_grads(moved, head_upstream[c], 0, random_blocks[0])
+            grads = attention_grads(moved, head_upstream[c], 0, positions, random_blocks[0])
         back = lax.all_to_all(grads, "context", split_axis=0, concat_axis=0, tiled=True)
         pieces.append(back if strided else back.transpose(1, 2, 0, 3))
 

time: 169 us -> 166 us (0.982); the launches traced: 168 us -> 163 us
  other arithmetic: 13.7 us -> 10.1 us
    gather x1 -> x0, local copies, waits for them, and re-layouts: 2.81 us -> none  [body(): upstream = jnp.take(upstream.reshape(ctx, tokens, -1), position, axis=0)]
    unnamed x26, local copies, waits for them, and re-layouts: 14.9 us -> 17.1 us
    select_n x2 -> x1, other arithmetic: 2.43 us -> 0.5 us  [body(): jnp.where(same, (j - source) % ctx // 2, ctx // 2 + ((j ^ 1) - source) %...]
    select_n x2, other arithmetic: 2.01 us -> 0.27 us  [body(): head_weight = jnp.take(jnp.stack(got), order, axis=0).reshape(dp * HD, -1)]
  transfers between devices with their start and end apart: 12 -> 12, of which waited for: 4 -> 3; matrix products, arithmetic and copies ran while one was open for 24% -> 21% of each run, Pallas kernels for 28% -> 29%
where the time goes in v12:
time: 166 us; the launch traced here: 163 us
  Pallas kernels  64.2 us (39%)
  starting transfers between devices  31.9 us (19%)
  waiting for transfers between devices  26.9 us (16%)
  local copies, waits for them, and re-layouts  25.9 us (16%)
  other arithmetic  10.1 us (6%)
  matrix products  3.34 us (2%)
    pallas_call x4, Pallas kernels, attention_grads(): pl.pallas_call(_attention_kernel, out_shape=out, grid_spec=pltpu.Prefetch...  58.1 us
    ppermute x3, waiting for transfers between devices, body(): lax.ppermute(out_weight, 'dp', [(a, (a + s) % dp) for a in range(dp)])  17.9 us
    unnamed x26, local copies, waits for them, and re-layouts  17.1 us
    all_to_all x4, starting transfers between devices, body(): lax.all_to_all(grads, 'context', split_axis=0, concat_axis=0, tiled=True)  16.5 us
    all_to_all x4, waiting for transfers between devices, body(): lax.all_to_all(grads, 'context', split_axis=0, concat_axis=0, tiled=True)  8.96 us
    ppermute x3, starting transfers between devices, body(): lax.ppermute(local_cotangent, 'context', [(a, (a + s) % ctx) for a in ran...  5.94 us
    ppermute x3, starting transfers between devices, body(): lax.ppermute(out_weight, 'dp', [(a, (a + s) % dp) for a in range(dp)])  5.59 us
    all_to_all x1, starting transfers between devices, body(): lax.all_to_all(stacked, 'context', split_axis=0, concat_axis=0, tiled=True)  3.78 us
  transfers between devices with their start and end apart: 12, of which 3 were waited for; matrix products, arithmetic and copies ran while one was open for 21% of the time, Pallas kernels for 29%

profile of v12, /device:TPU:0, one launch (start us, length us, event | category | flops | bytes accessed | tf_op | source)
XLA Modules:
  0.0 163.2 jit_solution(11877176425159338668)
XLA Ops:
  0.6 3.0 %collective-permute-start = (bf16[128,2048]{1,0:T(8,128)(2,1)}, bf16[128,2048]{1,0:T(8,128)(2,1)}, u32[]{:S(2)}, u32[]{:S(2)}) collective-permute-start(bf16[128,2048]{1,0:T(8,128)(2,1)} %bitcast.36), channel_id=1, source_target_pairs={{0,2},{1,3},{2,4},{3,5},{4,6},{5,7},{6,0},{7,1},{8,10},{9,11},{10,... | collective-permute-start | bytes 1572872 | tf_op jit(solution)/shard_map/ppermute | solution.py:198
  3.6 1.5 collective-permute-start.1
  5.1 1.4 collective-permute-start.2
  6.6 1.6 collective-permute-start.4
  8.2 2.6 %collective-permute-start.5 = (bf16[128,2048]{1,0:T(8,128)(2,1)}, bf16[128,2048]{1,0:T(8,128)(2,1)}, u32[]{:S(2)}, u32[]{:S(2)}) collective-permute-start(bf16[128,2048]{1,0:T(8,128)(2,1)} %param.10), channel_id=1, source_target_pairs={{0,16},{8,24},{16,0},{24,8},{1,17},{9,25},{17,1},{25,9},{2,18},{10... | collective-permute-start | bytes 1572872 | tf_op jit(solution)/shard_map/ppermute | solution.py:190
  10.7 1.6 copy.14
  12.4 0.7 copy.15
  13.0 1.6 copy.16
  14.7 0.7 copy.17
  15.3 1.6 copy.18
  17.0 1.3 copy.19
  18.3 3.2 %pad_maximum_fusion = bf16[8,3,4,128,128]{4,3,2,1,0:T(8,128)(2,1)} fusion(bf16[8,1,4,128,128]{4,3,2,1,0:T(8,128)(2,1)} %bitcast.34, bf16[8,1,4,128,128]{4,3,2,1,0:T(8,128)(2,1)S(1)} %bitcast.33, bf16[8,1,4,128,128]{4,3,2,1,0:T(8,128)(2,1)S(1)} %bitcast.32), kind=kLoop, calls=%fused_computation.1 | loop fusion | flops 3145728 | bytes 6291456 | tf_op jit(solution)/shard_map/stack | solution.py:229
  21.5 3.8 %all-to-all-start = ((bf16[8,3,4,128,128]{4,3,2,1,0:T(8,128)(2,1)}), bf16[8,3,4,128,128]{4,3,2,1,0:T(8,128)(2,1)S(1)}, u32[]{:S(2)}, u32[]{:S(2)}) async-start(bf16[8,3,4,128,128]{4,3,2,1,0:T(8,128)(2,1)} %pad_maximum_fusion), calls=%async_computation | async-start | bytes 6291456 | tf_op jit(solution)/shard_map/all_to_all | solution.py:230
  25.4 1.4 collective-permute-start.6
  26.8 0.5 compare_select_fusion.10.pos_ref
  27.3 0.1 copy.13
  27.4 0.7 reshape_squeeze.15.rb_ref
  28.1 1.9 %constant_dynamic-update-slice_fusion.4 = bf16[8,128,2048]{2,1,0:T(8,128)(2,1)} fusion(bf16[1,128,2048]{2,1,0:T(8,128)(2,1)} %param.9), kind=kLoop, calls=%fused_computation.10 | loop fusion | bytes 1048576
  29.9 3.1 %pad_maximum_fusion.1 = bf16[4,128,2048]{2,1,0:T(8,128)(2,1)} fusion(bf16[1,128,2048]{2,1,0:T(8,128)(2,1)} %bitcast.12, bf16[1,128,2048]{2,1,0:T(8,128)(2,1)} %bitcast.11, bf16[1,128,2048]{2,1,0:T(8,128)(2,1)} %bitcast.10, bf16[1,128,2048]{2,1,0:T(8,128)(2,1)} %param.9), kind=kLoop, calls=%fused_computation.2 | loop fusion | flops 3145728 | bytes 4194304 | tf_op jit(solution)/shard_map/stack | solution.py:197
  33.1 0.1 collective-permute-start.3
  33.2 11.0 %collective-permute-done.5 = bf16[128,2048]{1,0:T(8,128)(2,1)} collective-permute-done((bf16[128,2048]{1,0:T(8,128)(2,1)}, bf16[128,2048]{1,0:T(8,128)(2,1)}, u32[]{:S(2)}, u32[]{:S(2)}) %collective-permute-start.5) | collective-permute-done | bytes 524320 | tf_op jit(solution)/shard_map/ppermute | solution.py:190
  44.2 6.9 %collective-permute-done.6 = bf16[128,2048]{1,0:T(8,128)(2,1)} collective-permute-done((bf16[128,2048]{1,0:T(8,128)(2,1)}, bf16[128,2048]{1,0:T(8,128)(2,1)}, u32[]{:S(2)}, u32[]{:S(2)}) %collective-permute-start.6) | collective-permute-done | bytes 524320 | tf_op jit(solution)/shard_map/ppermute | solution.py:190
  51.1 3.0 %pad_maximum_fusion.2 = bf16[4,128,2048]{2,1,0:T(8,128)(2,1)} fusion(bf16[1,128,2048]{2,1,0:T(8,128)(2,1)} %bitcast.17, bf16[1,128,2048]{2,1,0:T(8,128)(2,1)} %bitcast.16, bf16[1,128,2048]{2,1,0:T(8,128)(2,1)} %bitcast.15, bf16[1,128,2048]{2,1,0:T(8,128)(2,1)S(1)} %bitcast.39), kind=kLoop, calls=%fused_computation.3 | loop fusion | flops 3145728 | bytes 4194304 | tf_op jit(solution)/shard_map/stack | solution.py:194
  54.0 3.7 %gather_fusion = bf16[4,128,2048]{2,1,0:T(8,128)(2,1)} fusion(bf16[4,128,2048]{2,1,0:T(8,128)(2,1)} %pad_maximum_fusion.2, s32[1024]{0:T(1024)S(1)} %pad_clamp_fusion), kind=kCustom, calls=%fused_computation | custom fusion | bytes 4194320 | tf_op jit(solution)/shard_map/jit(_take)/gather | solution.py:194
  57.8 2.0 %constant_dynamic-update-slice_fusion.3 = bf16[8,128,2048]{2,1,0:T(8,128)(2,1)} fusion(bf16[8,128,2048]{2,1,0:T(8,128)(2,1)} %constant_dynamic-update-slice_fusion.4, bf16[128,2048]{1,0:T(8,128)(2,1)} %collective-permute-done), kind=kLoop, calls=%fused_computation.9 | loop fusion | bytes 1048576
  59.8 1.9 %constant_dynamic-update-slice_fusion.2 = bf16[8,128,2048]{2,1,0:T(8,128)(2,1)} fusion(bf16[8,128,2048]{2,1,0:T(8,128)(2,1)} %constant_dynamic-update-slice_fusion.3, bf16[128,2048]{1,0:T(8,128)(2,1)} %collective-permute-done.1), kind=kLoop, calls=%fused_computation.8 | loop fusion | bytes 1048576
  61.7 1.9 %constant_dynamic-update-slice_fusion.1 = bf16[8,128,2048]{2,1,0:T(8,128)(2,1)} fusion(bf16[8,128,2048]{2,1,0:T(8,128)(2,1)} %constant_dynamic-update-slice_fusion.2, bf16[128,2048]{1,0:T(8,128)(2,1)} %collective-permute-done.2), kind=kLoop, calls=%fused_computation.7 | loop fusion | bytes 1048576
  63.6 0.3 broadcast_select_fusion
  63.9 0.0 collective-permute-done.3
  63.9 1.9 %copy-done.7 = bf16[8,128,2048]{2,1,0:T(8,128)(2,1)S(1)} copy-done((bf16[8,128,2048]{2,1,0:T(8,128)(2,1)S(1)}, bf16[8,128,2048]{2,1,0:T(8,128)(2,1)}, u32[]{:S(2)}) %copy-start.7) | copy-done | bytes 4194328
  65.8 1.8 %constant_dynamic-update-slice_fusion = bf16[8,128,2048]{2,1,0:T(8,128)(2,1)S(1)} fusion(bf16[8,128,2048]{2,1,0:T(8,128)(2,1)S(1)} %copy-done.7, bf16[4,128,2048]{2,1,0:T(8,128)(2,1)} %collective-permute-done.3), kind=kLoop, calls=%fused_computation.6 | loop fusion | bytes 4194304 | tf_op jit(solution)/shard_map/concatenate | solution.py:202
  67.6 3.3 %convolution_convert_fusion.u_ref = bf16[1024,512]{1,0:T(8,128)(2,1)} fusion(bf16[1024,2048]{1,0:T(8,128)(2,1)S(1)} %bitcast.40, bf16[512,2048]{1,0:T(8,128)(2,1)S(1)} %bitcast.35), kind=kOutput, calls=%fused_computation.5 | convolution fusion | flops 2148007936 | bytes 7340032 | tf_op jit(solution)/shard_map/dot_general | solution.py:203
  70.9 0.0 all-to-all-done.x_ref
  71.0 1.6 copy-done
  72.6 14.5 %shard_map.88 = bf16[8,3,128,128]{3,2,1,0:T(8,128)(2,1)} custom-call(s32[42]{0:T(128)} %reshape_squeeze.15.rb_ref, s32[8]{0:T(128)} %compare_select_fusion.10.pos_ref, bf16[8,3,4,128,128]{4,3,2,1,0:T(8,128)(2,1)} %copy-done, bf16[1024,512]{1,0:T(8,128)(2,1)} %convolution_convert_fusion.u_ref), custom_call_target="tpu_custom_call" | custom-call | flops 905969664 | bytes 1835008 | tf_op jit(solution)/shard_map/pallas_call | solution.py:115
  87.1 3.9 %all-to-all-start.4 = ((bf16[8,3,128,128]{3,2,1,0:T(8,128)(2,1)}), bf16[8,3,128,128]{3,2,1,0:T(8,128)(2,1)S(1)}, u32[]{:S(2)}, u32[]{:S(2)}) async-start(bf16[8,3,128,128]{3,2,1,0:T(8,128)(2,1)} %shard_map.88), calls=%async_computation.4 | async-start | bytes 1572864 | tf_op jit(solution)/shard_map/all_to_all | solution.py:240
  91.0 14.5 %shard_map.87 = bf16[8,3,128,128]{3,2,1,0:T(8,128)(2,1)} custom-call(s32[42]{0:T(128)} %reshape_squeeze.15.rb_ref, s32[8]{0:T(128)} %compare_select_fusion.10.pos_ref, bf16[8,3,4,128,128]{4,3,2,1,0:T(8,128)(2,1)} %copy-done, bf16[1024,512]{1,0:T(8,128)(2,1)} %convolution_convert_fusion.u_ref), custom_call_target="tpu_custom_call" | custom-call | flops 905969664 | bytes 1835008 | tf_op jit(solution)/shard_map/pallas_call | solution.py:115
  105.5 0.0 all-to-all-done.4.refs_2_
  105.5 4.2 %all-to-all-start.3 = ((bf16[8,3,128,128]{3,2,1,0:T(8,128)(2,1)}), bf16[8,3,128,128]{3,2,1,0:T(8,128)(2,1)S(1)}, u32[]{:S(2)}, u32[]{:S(2)}) async-start(bf16[8,3,128,128]{3,2,1,0:T(8,128)(2,1)} %shard_map.87), calls=%async_computation.3 | async-start | bytes 1572864 | tf_op jit(solution)/shard_map/all_to_all | solution.py:240
  109.7 14.5 %shard_map.86 = bf16[8,3,128,128]{3,2,1,0:T(8,128)(2,1)} custom-call(s32[42]{0:T(128)} %reshape_squeeze.15.rb_ref, s32[8]{0:T(128)} %compare_select_fusion.10.pos_ref, bf16[8,3,4,128,128]{4,3,2,1,0:T(8,128)(2,1)} %copy-done, bf16[1024,512]{1,0:T(8,128)(2,1)} %convolution_convert_fusion.u_ref), custom_call_target="tpu_custom_call" | custom-call | flops 905969664 | bytes 1835008 | tf_op jit(solution)/shard_map/pallas_call | solution.py:115
  124.2 0.0 all-to-all-done.3.refs_1_
  124.3 4.2 %all-to-all-start.2 = ((bf16[8,3,128,128]{3,2,1,0:T(8,128)(2,1)}), bf16[8,3,128,128]{3,2,1,0:T(8,128)(2,1)S(1)}, u32[]{:S(2)}, u32[]{:S(2)}) async-start(bf16[8,3,128,128]{3,2,1,0:T(8,128)(2,1)} %shard_map.86), calls=%async_computation.2 | async-start | bytes 1572864 | tf_op jit(solution)/shard_map/all_to_all | solution.py:240
  128.5 14.5 %shard_map.85 = bf16[8,3,128,128]{3,2,1,0:T(8,128)(2,1)} custom-call(s32[42]{0:T(128)} %reshape_squeeze.15.rb_ref, s32[8]{0:T(128)} %compare_select_fusion.10.pos_ref, bf16[8,3,4,128,128]{4,3,2,1,0:T(8,128)(2,1)} %copy-done, bf16[1024,512]{1,0:T(8,128)(2,1)} %convolution_convert_fusion.u_ref), custom_call_target="tpu_custom_call" | custom-call | flops 905969664 | bytes 1835008 | tf_op jit(solution)/shard_map/pallas_call | solution.py:115
  143.0 4.2 %all-to-all-start.1 = ((bf16[8,3,128,128]{3,2,1,0:T(8,128)(2,1)}), bf16[8,3,128,128]{3,2,1,0:T(8,128)(2,1)S(1)}, u32[]{:S(2)}, u32[]{:S(2)}) async-start(bf16[8,3,128,128]{3,2,1,0:T(8,128)(2,1)} %shard_map.85), calls=%async_computation.1 | async-start | bytes 1572864 | tf_op jit(solution)/shard_map/all_to_all | solution.py:240
  147.2 3.6 %shard_map.89 = (bf16[1,128,4096]{2,1,0:T(8,128)(2,1)}, bf16[1,128,4096]{2,1,0:T(8,128)(2,1)}, bf16[1,128,4096]{2,1,0:T(8,128)(2,1)}) custom-call(bf16[8,3,128,128]{3,2,1,0:T(8,128)(2,1)} %copy-done.4, bf16[8,3,128,128]{3,2,1,0:T(8,128)(2,1)} %copy-done.3, bf16[8,3,128,128]{3,2,1,0:T(8,128)(2,1)} %copy-done.2), custom_call_target="tpu_custom_call" | custom-call | tf_op jit(solution)/shard_map/pallas_call | solution.py:151
  150.9 9.0 %all-to-all-done.1.piece = bf16[8,3,128,128]{3,2,1,0:T(8,128)(2,1)S(1)} async-done(((bf16[8,3,128,128]{3,2,1,0:T(8,128)(2,1)}), bf16[8,3,128,128]{3,2,1,0:T(8,128)(2,1)S(1)}, u32[]{:S(2)}, u32[]{:S(2)}) %all-to-all-start.1) | async-done | bytes 786464 | tf_op jit(solution)/shard_map/all_to_all | solution.py:240
  159.8 0.9 copy-done.5
  160.7 2.4 %shard_map.90 = (bf16[1,128,4096]{2,1,0:T(8,128)(2,1)}, bf16[1,128,4096]{2,1,0:T(8,128)(2,1)}, bf16[1,128,4096]{2,1,0:T(8,128)(2,1)}) custom-call(bf16[8,3,128,128]{3,2,1,0:T(8,128)(2,1)} %copy-done.5, bf16[1,128,4096]{2,1,0:T(8,128)(2,1)} %get-tuple-element.6._first, ...), custom_call_target="tpu_custom_call", output_to_operand_aliasing={{0}: (1, {}), {1}: (2, {}), {2}: (3, {})} | custom-call | tf_op jit(solution)/shard_map/pallas_call | solution.py:159
  (23 shorter events, 0.1 us)
Async XLA Ops:
  0.6 24.7 %collective-permute-start = (bf16[128,2048]{1,0:T(8,128)(2,1)}, bf16[128,2048]{1,0:T(8,128)(2,1)}, u32[]{:S(2)}, u32[]{:S(2)}) collective-permute-start(bf16[128,2048]{1,0:T(8,128)(2,1)} %bitcast.36), channel_id=1, source_target_pairs={{0,2},{1,3},{2,4},{3,5},{4,6},{5,7},{6,0},{7,1},{8,10},{9,11},{10,... | collective-permute-start | bytes 1572872 | tf_op jit(solution)/shard_map/ppermute | solution.py:198
  3.6 26.3 %collective-permute-start.1 = (bf16[128,2048]{1,0:T(8,128)(2,1)}, bf16[128,2048]{1,0:T(8,128)(2,1)}, u32[]{:S(2)}, u32[]{:S(2)}) collective-permute-start(bf16[128,2048]{1,0:T(8,128)(2,1)} %bitcast.37), channel_id=1, source_target_pairs={{0,4},{1,5},{2,6},{3,7},{4,0},{5,1},{6,2},{7,3},{8,12},{9,13},{10,... | collective-permute-start | bytes 1572872 | tf_op jit(solution)/shard_map/ppermute | solution.py:198
  5.1 24.8 %collective-permute-start.2 = (bf16[128,2048]{1,0:T(8,128)(2,1)}, bf16[128,2048]{1,0:T(8,128)(2,1)}, u32[]{:S(2)}, u32[]{:S(2)}) collective-permute-start(bf16[128,2048]{1,0:T(8,128)(2,1)} %bitcast.38), channel_id=1, source_target_pairs={{0,6},{1,7},{2,0},{3,1},{4,2},{5,3},{6,4},{7,5},{8,14},{9,15},{10,... | collective-permute-start | bytes 1572872 | tf_op jit(solution)/shard_map/ppermute | solution.py:198
  6.6 26.6 %collective-permute-start.4 = (bf16[128,2048]{1,0:T(8,128)(2,1)}, bf16[128,2048]{1,0:T(8,128)(2,1)}, u32[]{:S(2)}, u32[]{:S(2)}) collective-permute-start(bf16[128,2048]{1,0:T(8,128)(2,1)} %param.10), channel_id=1, source_target_pairs={{0,8},{8,16},{16,24},{24,0},{1,9},{9,17},{17,25},{25,1},{2,10},{10... | collective-permute-start | bytes 1572872 | tf_op jit(solution)/shard_map/ppermute | solution.py:190
  8.2 36.0 %collective-permute-start.5 = (bf16[128,2048]{1,0:T(8,128)(2,1)}, bf16[128,2048]{1,0:T(8,128)(2,1)}, u32[]{:S(2)}, u32[]{:S(2)}) collective-permute-start(bf16[128,2048]{1,0:T(8,128)(2,1)} %param.10), channel_id=1, source_target_pairs={{0,16},{8,24},{16,0},{24,8},{1,17},{9,25},{17,1},{25,9},{2,18},{10... | collective-permute-start | bytes 1572872 | tf_op jit(solution)/shard_map/ppermute | solution.py:190
  21.5 5.8 %copy-start.8 = (s32[1,14,3]{1,0,2:T(1,128)S(1)}, s32[1,14,3]{1,0,2:T(1,128)}, u32[]{:S(2)}) copy-start(s32[1,14,3]{1,0,2:T(1,128)} %param.11) | copy-start | bytes 508
  21.5 49.4 %all-to-all-start = ((bf16[8,3,4,128,128]{4,3,2,1,0:T(8,128)(2,1)}), bf16[8,3,4,128,128]{4,3,2,1,0:T(8,128)(2,1)S(1)}, u32[]{:S(2)}, u32[]{:S(2)}) async-start(bf16[8,3,4,128,128]{4,3,2,1,0:T(8,128)(2,1)} %pad_maximum_fusion), calls=%async_computation | async-start | bytes 6291456 | tf_op jit(solution)/shard_map/all_to_all | solution.py:230
  25.4 25.7 %collective-permute-start.6 = (bf16[128,2048]{1,0:T(8,128)(2,1)}, bf16[128,2048]{1,0:T(8,128)(2,1)}, u32[]{:S(2)}, u32[]{:S(2)}) collective-permute-start(bf16[128,2048]{1,0:T(8,128)(2,1)} %param.10), channel_id=1, source_target_pairs={{0,24},{8,0},{16,8},{24,16},{1,25},{9,1},{17,9},{25,17},{2,26},{10... | collective-permute-start | bytes 1572872 | tf_op jit(solution)/shard_map/ppermute | solution.py:190
  29.9 21.1 %copy-start.6 = (bf16[128,2048]{1,0:T(8,128)(2,1)S(1)}, bf16[128,2048]{1,0:T(8,128)(2,1)}, u32[]{:S(2)}) copy-start(bf16[128,2048]{1,0:T(8,128)(2,1)} %param.10) | copy-start | bytes 1572868
  33.1 30.8 %collective-permute-start.3 = (bf16[4,128,2048]{2,1,0:T(8,128)(2,1)}, bf16[4,128,2048]{2,1,0:T(8,128)(2,1)}, u32[]{:S(2)}, u32[]{:S(2)}) collective-permute-start(bf16[4,128,2048]{2,1,0:T(8,128)(2,1)} %pad_maximum_fusion.1), channel_id=1, source_target_pairs={{0,1},{1,0},{2,3},{3,2},{4,5},{5,4},{6,7},{7,6},{8,9},{9,8},{10,11... | collective-permute-start | bytes 6291464 | tf_op jit(solution)/shard_map/ppermute | solution.py:201
  57.8 5.8 %copy-start.1 = (bf16[4,128,2048]{2,1,0:T(8,128)(2,1)S(1)}, bf16[4,128,2048]{2,1,0:T(8,128)(2,1)}, u32[]{:S(2)}) copy-start(bf16[4,128,2048]{2,1,0:T(8,128)(2,1)} %gather_fusion) | copy-start | bytes 6291460
  63.6 2.2 %copy-start.7 = (bf16[8,128,2048]{2,1,0:T(8,128)(2,1)S(1)}, bf16[8,128,2048]{2,1,0:T(8,128)(2,1)}, u32[]{:S(2)}) copy-start(bf16[8,128,2048]{2,1,0:T(8,128)(2,1)} %constant_dynamic-update-slice_fusion.1) | copy-start | bytes 12582916
  70.9 1.6 copy-start
  87.1 18.4 %all-to-all-start.4 = ((bf16[8,3,128,128]{3,2,1,0:T(8,128)(2,1)}), bf16[8,3,128,128]{3,2,1,0:T(8,128)(2,1)S(1)}, u32[]{:S(2)}, u32[]{:S(2)}) async-start(bf16[8,3,128,128]{3,2,1,0:T(8,128)(2,1)} %shard_map.88), calls=%async_computation.4 | async-start | bytes 1572864 | tf_op jit(solution)/shard_map/all_to_all | solution.py:240
  105.5 18.7 %copy-start.2 = (bf16[8,3,128,128]{3,2,1,0:T(8,128)(2,1)}, bf16[8,3,128,128]{3,2,1,0:T(8,128)(2,1)S(1)}, u32[]{:S(2)}) copy-start(bf16[8,3,128,128]{3,2,1,0:T(8,128)(2,1)S(1)} %all-to-all-done.4.refs_2_) | copy-start | bytes 2359300
  105.5 18.7 %all-to-all-start.3 = ((bf16[8,3,128,128]{3,2,1,0:T(8,128)(2,1)}), bf16[8,3,128,128]{3,2,1,0:T(8,128)(2,1)S(1)}, u32[]{:S(2)}, u32[]{:S(2)}) async-start(bf16[8,3,128,128]{3,2,1,0:T(8,128)(2,1)} %shard_map.87), calls=%async_computation.3 | async-start | bytes 1572864 | tf_op jit(solution)/shard_map/all_to_all | solution.py:240
  124.3 18.8 %copy-start.3 = (bf16[8,3,128,128]{3,2,1,0:T(8,128)(2,1)}, bf16[8,3,128,128]{3,2,1,0:T(8,128)(2,1)S(1)}, u32[]{:S(2)}) copy-start(bf16[8,3,128,128]{3,2,1,0:T(8,128)(2,1)S(1)} %all-to-all-done.3.refs_1_) | copy-start | bytes 2359300
  124.3 18.8 %all-to-all-start.2 = ((bf16[8,3,128,128]{3,2,1,0:T(8,128)(2,1)}), bf16[8,3,128,128]{3,2,1,0:T(8,128)(2,1)S(1)}, u32[]{:S(2)}, u32[]{:S(2)}) async-start(bf16[8,3,128,128]{3,2,1,0:T(8,128)(2,1)} %shard_map.86), calls=%async_computation.2 | async-start | bytes 1572864 | tf_op jit(solution)/shard_map/all_to_all | solution.py:240
  143.0 4.2 %copy-start.4 = (bf16[8,3,128,128]{3,2,1,0:T(8,128)(2,1)}, bf16[8,3,128,128]{3,2,1,0:T(8,128)(2,1)S(1)}, u32[]{:S(2)}) copy-start(bf16[8,3,128,128]{3,2,1,0:T(8,128)(2,1)S(1)} %all-to-all-done.2.refs_0_) | copy-start | bytes 2359300
  143.0 16.8 %all-to-all-start.1 = ((bf16[8,3,128,128]{3,2,1,0:T(8,128)(2,1)}), bf16[8,3,128,128]{3,2,1,0:T(8,128)(2,1)S(1)}, u32[]{:S(2)}, u32[]{:S(2)}) async-start(bf16[8,3,128,128]{3,2,1,0:T(8,128)(2,1)} %shard_map.85), calls=%async_computation.1 | async-start | bytes 1572864 | tf_op jit(solution)/shard_map/all_to_all | solution.py:240
  159.8 0.9 copy-start.5

commit v13 on v12

--- a/solution.py
+++ b/solution.py
@@ -26,7 +26,8 @@
     return lax.dot_general(a, b, (((1,), (0,)), ((), ())), preferred_element_type=jnp.float32)
 
 
-def _attention_kernel(rb_ref, pos_ref, x_ref, u_ref, o_ref, dk_acc, dv_acc, kg_ref, vg_ref):
+def _attention_kernel(rb_ref, pos_ref, x_ref, u_ref, *refs):
+    *_, o_ref, dk_acc, dv_acc, kg_ref, vg_ref = refs
     parts, _, tokens, _ = x_ref.shape
     per_part = tokens // BLOCK
     length = parts * tokens
@@ -100,14 +101,16 @@
     o_ref[:, 2, :, :] = dv_acc[...].reshape(parts, tokens, HD).astype(jnp.bfloat16)
 
 
-def attention_grads(stacked, upstream, head, positions, random_ids):
+def attention_grads(stacked, upstream, head, positions, random_ids, slots=1, slot=0, into=None):
     parts, _, _, tokens, _ = stacked.shape
     length = parts * tokens
     count = length // BLOCK
     source = pl.BlockSpec((parts, 3, None, tokens, HD), lambda h, rb, ps: (0, 0, head, 0, 0))
-    whole = pl.BlockSpec((parts, 3, tokens, HD), lambda h, rb, ps: (0, 0, 0, 0))
+    whole = pl.BlockSpec((parts, 3, None, tokens, HD), lambda h, rb, ps: (0, 0, slot, 0, 0))
     spec = pl.BlockSpec((length, HD), lambda h, rb, ps: (0, head))
-    out = jax.ShapeDtypeStruct((parts, 3, tokens, HD), jnp.bfloat16)
+    out = jax.ShapeDtypeStruct((parts, 3, slots, tokens, HD), jnp.bfloat16)
+    extra = () if into is None else (into,)
+    aliases = {} if into is None else {4: 0}
     pairs = 2 * BLOCK * length + (count - 2) * BLOCK * SLOTS * BLOCK
     cost = pl.CostEstimate(
         flops=12 * pairs * HD, transcendentals=pairs, bytes_accessed=14 * length * HD
@@ -118,7 +121,7 @@
         grid_spec=pltpu.PrefetchScalarGridSpec(
             num_scalar_prefetch=2,
             grid=(1,),
-            in_specs=[source, spec],
+            in_specs=[source, spec] + [pl.BlockSpec(memory_space=pl.ANY)] * len(extra),
             out_specs=whole,
             scratch_shapes=[
                 pltpu.VMEM((length, HD), jnp.float32),
@@ -129,32 +132,41 @@
         ),
         compiler_params=pltpu.CompilerParams(dimension_semantics=("arbitrary",)),
         cost_estimate=cost,
-    )(random_ids.reshape(-1), positions, stacked, upstream)
-
-
-def _assemble_kernel(*refs, first_head):
-    pieces, outs = refs[:-3], refs[-3:]
+        input_output_aliases=aliases,
+    )(random_ids.reshape(-1), positions, stacked, upstream, *extra)
+
+
+def _assemble_kernel(*refs, heads):
+    pieces, outs = refs[:len(heads)], refs[len(heads):]
     parts = pieces[0].shape[0]
-    for c, piece in enumerate(pieces):
-        for source in range(parts):
-            start = (c * parts + source) * HD
-            for g, out in enumerate(outs):
-                out[0, :, start:start + HD] = piece[source, g]
-
-
-def assemble(pieces, tokens, width):
+    for piece, group in zip(pieces, heads):
+        for k, c in enumerate(group):
+            for source in range(parts):
+                start = (c * parts + source) * HD
+                for g, out in enumerate(outs):
+                    out[0, :, start:start + HD] = piece[source, g, k]
+
+
+def _assemble_last_kernel(piece, _first, _second, _third, *outs):
+    parts = piece.shape[0]
+    for source in range(parts):
+        for g, out in enumerate(outs):
+            out[0, :, source * HD:(source + 1) * HD] = piece[source, g, 0]
+
+
+def assemble(pieces, heads, tokens, width):
     out = jax.ShapeDtypeStruct((1, tokens, width), jnp.bfloat16)
     span = pieces[0].shape[0] * HD
-    early = len(pieces) - 1
+    early = heads[-1][0]
     whole = pl.BlockSpec(memory_space=pltpu.VMEM)
     head_spec = pl.BlockSpec((1, tokens, early * span), lambda i: (0, 0, 0))
     partial = pl.pallas_call(
-        functools.partial(_assemble_kernel, first_head=0),
+        functools.partial(_assemble_kernel, heads=heads[:-1]),
         out_shape=(out, out, out),
         grid=(1,),
-        in_specs=[whole] * early,
+        in_specs=[whole] * (len(pieces) - 1),
         out_specs=(head_spec, head_spec, head_spec),
-    )(*pieces[:early])
+    )(*pieces[:-1])
     last_spec = pl.BlockSpec((1, tokens, span), lambda i: (0, 0, early))
     return pl.pallas_call(
         _assemble_last_kernel,
@@ -163,14 +175,7 @@
         in_specs=[whole, last_spec, last_spec, last_spec],
         out_specs=(last_spec, last_spec, last_spec),
         input_output_aliases={1: 0, 2: 1, 3: 2},
-    )(pieces[early], *partial)
-
-
-def _assemble_last_kernel(piece, _first, _second, _third, *outs):
-    parts = piece.shape[0]
-    for source in range(parts):
-        for g, out in enumerate(outs):
-            out[0, :, source * HD:(source + 1) * HD] = piece[source, g]
+    )(pieces[-1], *partial)
 
 
 def body(queries, key_rows, value_rows, cotangent, out_weight, random_blocks):
@@ -231,17 +236,25 @@
     if not strided:
         head_upstream = moved[:, 3].transpose(1, 0, 2, 3).reshape(local_heads, tokens * ctx, HD)
         moved = moved[:, :3]
+    if strided and local_heads >= 3:
+        heads = [[0, 1]] + [[c] for c in range(2, local_heads)]
+    else:
+        heads = [[c] for c in range(local_heads)]
     pieces = []
-    for c in range(local_heads):
-        if strided:
-            grads = attention_grads(moved, upstream, c, positions, random_blocks[0])
-        else:
-            grads = attention_grads(moved, head_upstream[c], 0, positions, random_blocks[0])
+    for group in heads:
+        grads = None
+        for k, c in enumerate(group):
+            if strided:
+                grads = attention_grads(
+                    moved, upstream, c, positions, random_blocks[0], len(group), k, grads
+                )
+            else:
+                grads = attention_grads(moved, head_upstream[c], 0, positions, random_blocks[0])
         back = lax.all_to_all(grads, "context", split_axis=0, concat_axis=0, tiled=True)
-        pieces.append(back if strided else back.transpose(1, 2, 0, 3))
+        pieces.append(back if strided else back[:, :, 0].transpose(1, 2, 0, 3))
 
     if strided:
-        return assemble(pieces, tokens, width)
+        return assemble(pieces, heads, tokens, width)
     outs = []
     for g in range(3):
         joined = jnp.stack([piece[g] for piece in pieces], axis=1 if strided else 2)

time: 166 us -> 167 us (level)
  waiting for transfers between devices: 26.9 us -> 33.3 us
  starting transfers between devices: 31.9 us -> 27 us
    all_to_all x4 -> x3, waiting for transfers between devices: 8.96 us -> 15.4 us  [body(): lax.all_to_all(grads, 'context', split_axis=0, concat_axis=0, tiled=True)]
    all_to_all x4 -> x3, starting transfers between devices: 16.5 us -> 11.6 us  [body(): lax.all_to_all(grads, 'context', split_axis=0, concat_axis=0, tiled=True)]
    unnamed x26 -> x24, local copies, waits for them, and re-layouts: 17.1 us -> 17.1 us
  transfers between devices with their start and end apart: 12 -> 11, of which waited for: 3 -> 4; matrix products, arithmetic and copies ran while one was open for 21% -> 21% of each run, Pallas kernels for 29% -> 29%
where the time goes in v13:
time: 167 us; the launch traced here: 165 us
  Pallas kernels  64.2 us (38%)
  waiting for transfers between devices  33.3 us (20%)
  starting transfers between devices  27 us (16%)
  local copies, waits for them, and re-layouts  25.9 us (16%)
  other arithmetic  10.2 us (6%)
  matrix products  3.34 us (2%)
    pallas_call x4, Pallas kernels, attention_grads(): pl.pallas_call(_attention_kernel, out_shape=out, grid_spec=pltpu.Prefetch...  58.1 us
    ppermute x3, waiting for transfers between devices, body(): lax.ppermute(out_weight, 'dp', [(a, (a + s) % dp) for a in range(dp)])  17.9 us
    unnamed x24, local copies, waits for them, and re-layouts  17.1 us
    all_to_all x3, waiting for transfers between devices, body(): lax.all_to_all(grads, 'context', split_axis=0, concat_axis=0, tiled=True)  15.4 us
    all_to_all x3, starting transfers between devices, body(): lax.all_to_all(grads, 'context', split_axis=0, concat_axis=0, tiled=True)  11.6 us
    ppermute x3, starting transfers between devices, body(): lax.ppermute(local_cotangent, 'context', [(a, (a + s) % ctx) for a in ran...  5.94 us
    ppermute x3, starting transfers between devices, body(): lax.ppermute(out_weight, 'dp', [(a, (a + s) % dp) for a in range(dp)])  5.59 us
    all_to_all x1, starting transfers between devices, body(): lax.all_to_all(stacked, 'context', split_axis=0, concat_axis=0, tiled=True)  3.78 us
  transfers between devices with their start and end apart: 11, of which 4 were waited for; matrix products, arithmetic and copies ran while one was open for 21% of the time, Pallas kernels for 29%

profile of v13, /device:TPU:0, one launch (start us, length us, event | category | flops | bytes accessed | tf_op | source)
XLA Modules:
  0.0 164.7 jit_solution(15789346278983253528)
XLA Ops:
  0.6 3.0 %collective-permute-start = (bf16[128,2048]{1,0:T(8,128)(2,1)}, bf16[128,2048]{1,0:T(8,128)(2,1)}, u32[]{:S(2)}, u32[]{:S(2)}) collective-permute-start(bf16[128,2048]{1,0:T(8,128)(2,1)} %bitcast.36), channel_id=1, source_target_pairs={{0,2},{1,3},{2,4},{3,5},{4,6},{5,7},{6,0},{7,1},{8,10},{9,11},{10,... | collective-permute-start | bytes 1572872 | tf_op jit(solution)/shard_map/ppermute | solution.py:203
  3.6 1.5 collective-permute-start.1
  5.1 1.4 collective-permute-start.2
  6.6 1.6 collective-permute-start.4
  8.2 2.6 %collective-permute-start.5 = (bf16[128,2048]{1,0:T(8,128)(2,1)}, bf16[128,2048]{1,0:T(8,128)(2,1)}, u32[]{:S(2)}, u32[]{:S(2)}) collective-permute-start(bf16[128,2048]{1,0:T(8,128)(2,1)} %param.10), channel_id=1, source_target_pairs={{0,16},{8,24},{16,0},{24,8},{1,17},{9,25},{17,1},{25,9},{2,18},{10... | collective-permute-start | bytes 1572872 | tf_op jit(solution)/shard_map/ppermute | solution.py:195
  10.7 1.6 copy.15
  12.4 0.7 copy.16
  13.0 1.6 copy.17
  14.7 0.7 copy.18
  15.3 1.6 copy.19
  17.0 1.3 copy.20
  18.3 3.2 %pad_maximum_fusion = bf16[8,3,4,128,128]{4,3,2,1,0:T(8,128)(2,1)} fusion(bf16[8,1,4,128,128]{4,3,2,1,0:T(8,128)(2,1)} %bitcast.34, bf16[8,1,4,128,128]{4,3,2,1,0:T(8,128)(2,1)S(1)} %bitcast.33, bf16[8,1,4,128,128]{4,3,2,1,0:T(8,128)(2,1)S(1)} %bitcast.32), kind=kLoop, calls=%fused_computation.1 | loop fusion | flops 3145728 | bytes 6291456 | tf_op jit(solution)/shard_map/stack | solution.py:234
  21.5 3.8 %all-to-all-start = ((bf16[8,3,4,128,128]{4,3,2,1,0:T(8,128)(2,1)}), bf16[8,3,4,128,128]{4,3,2,1,0:T(8,128)(2,1)S(1)}, u32[]{:S(2)}, u32[]{:S(2)}) async-start(bf16[8,3,4,128,128]{4,3,2,1,0:T(8,128)(2,1)} %pad_maximum_fusion), calls=%async_computation | async-start | bytes 6291456 | tf_op jit(solution)/shard_map/all_to_all | solution.py:235
  25.4 0.0 collective-permute-done
  25.4 1.4 collective-permute-start.6
  26.8 0.6 compare_select_fusion.10.pos_ref
  27.4 0.1 copy.14
  27.5 0.6 reshape_squeeze.15.rb_ref
  28.1 1.9 %constant_dynamic-update-slice_fusion.4 = bf16[8,128,2048]{2,1,0:T(8,128)(2,1)} fusion(bf16[1,128,2048]{2,1,0:T(8,128)(2,1)} %param.9), kind=kLoop, calls=%fused_computation.10 | loop fusion | bytes 1048576
  30.0 0.0 collective-permute-done.1
  30.0 0.0 collective-permute-done.2
  30.0 3.1 %pad_maximum_fusion.1 = bf16[4,128,2048]{2,1,0:T(8,128)(2,1)} fusion(bf16[1,128,2048]{2,1,0:T(8,128)(2,1)} %bitcast.12, bf16[1,128,2048]{2,1,0:T(8,128)(2,1)} %bitcast.11, bf16[1,128,2048]{2,1,0:T(8,128)(2,1)} %bitcast.10, bf16[1,128,2048]{2,1,0:T(8,128)(2,1)} %param.9), kind=kLoop, calls=%fused_computation.2 | loop fusion | flops 3145728 | bytes 4194304 | tf_op jit(solution)/shard_map/stack | solution.py:202
  33.1 0.1 collective-permute-start.3
  33.2 0.0 collective-permute-done.4
  33.2 11.0 %collective-permute-done.5 = bf16[128,2048]{1,0:T(8,128)(2,1)} collective-permute-done((bf16[128,2048]{1,0:T(8,128)(2,1)}, bf16[128,2048]{1,0:T(8,128)(2,1)}, u32[]{:S(2)}, u32[]{:S(2)}) %collective-permute-start.5) | collective-permute-done | bytes 524320 | tf_op jit(solution)/shard_map/ppermute | solution.py:195
  44.2 6.9 %collective-permute-done.6 = bf16[128,2048]{1,0:T(8,128)(2,1)} collective-permute-done((bf16[128,2048]{1,0:T(8,128)(2,1)}, bf16[128,2048]{1,0:T(8,128)(2,1)}, u32[]{:S(2)}, u32[]{:S(2)}) %collective-permute-start.6) | collective-permute-done | bytes 524320 | tf_op jit(solution)/shard_map/ppermute | solution.py:195
  51.1 2.9 %pad_maximum_fusion.2 = bf16[4,128,2048]{2,1,0:T(8,128)(2,1)} fusion(bf16[1,128,2048]{2,1,0:T(8,128)(2,1)} %bitcast.17, bf16[1,128,2048]{2,1,0:T(8,128)(2,1)} %bitcast.16, bf16[1,128,2048]{2,1,0:T(8,128)(2,1)} %bitcast.15, bf16[1,128,2048]{2,1,0:T(8,128)(2,1)S(1)} %bitcast.39), kind=kLoop, calls=%fused_computation.3 | loop fusion | flops 3145728 | bytes 4194304 | tf_op jit(solution)/shard_map/stack | solution.py:199
  54.0 3.7 %gather_fusion = bf16[4,128,2048]{2,1,0:T(8,128)(2,1)} fusion(bf16[4,128,2048]{2,1,0:T(8,128)(2,1)} %pad_maximum_fusion.2, s32[1024]{0:T(1024)S(1)} %pad_clamp_fusion), kind=kCustom, calls=%fused_computation | custom fusion | bytes 4194320 | tf_op jit(solution)/shard_map/jit(_take)/gather | solution.py:199
  57.7 2.0 %constant_dynamic-update-slice_fusion.3 = bf16[8,128,2048]{2,1,0:T(8,128)(2,1)} fusion(bf16[8,128,2048]{2,1,0:T(8,128)(2,1)} %constant_dynamic-update-slice_fusion.4, bf16[128,2048]{1,0:T(8,128)(2,1)} %collective-permute-done), kind=kLoop, calls=%fused_computation.9 | loop fusion | bytes 1048576
  59.8 1.9 %constant_dynamic-update-slice_fusion.2 = bf16[8,128,2048]{2,1,0:T(8,128)(2,1)} fusion(bf16[8,128,2048]{2,1,0:T(8,128)(2,1)} %constant_dynamic-update-slice_fusion.3, bf16[128,2048]{1,0:T(8,128)(2,1)} %collective-permute-done.1), kind=kLoop, calls=%fused_computation.8 | loop fusion | bytes 1048576
  61.7 1.9 %constant_dynamic-update-slice_fusion.1 = bf16[8,128,2048]{2,1,0:T(8,128)(2,1)} fusion(bf16[8,128,2048]{2,1,0:T(8,128)(2,1)} %constant_dynamic-update-slice_fusion.2, bf16[128,2048]{1,0:T(8,128)(2,1)} %collective-permute-done.2), kind=kLoop, calls=%fused_computation.7 | loop fusion | bytes 1048576
  63.6 0.3 broadcast_select_fusion
  63.8 1.9 %copy-done.6 = bf16[8,128,2048]{2,1,0:T(8,128)(2,1)S(1)} copy-done((bf16[8,128,2048]{2,1,0:T(8,128)(2,1)S(1)}, bf16[8,128,2048]{2,1,0:T(8,128)(2,1)}, u32[]{:S(2)}) %copy-start.6) | copy-done | bytes 4194328
  65.7 1.8 %constant_dynamic-update-slice_fusion = bf16[8,128,2048]{2,1,0:T(8,128)(2,1)S(1)} fusion(bf16[8,128,2048]{2,1,0:T(8,128)(2,1)S(1)} %copy-done.6, bf16[4,128,2048]{2,1,0:T(8,128)(2,1)} %collective-permute-done.3), kind=kLoop, calls=%fused_computation.6 | loop fusion | bytes 4194304 | tf_op jit(solution)/shard_map/concatenate | solution.py:207
  67.6 3.3 %convolution_convert_fusion.u_ref = bf16[1024,512]{1,0:T(8,128)(2,1)} fusion(bf16[1024,2048]{1,0:T(8,128)(2,1)S(1)} %bitcast.40, bf16[512,2048]{1,0:T(8,128)(2,1)S(1)} %bitcast.35), kind=kOutput, calls=%fused_computation.5 | convolution fusion | flops 2148007936 | bytes 7340032 | tf_op jit(solution)/shard_map/dot_general | solution.py:208
  70.9 1.6 copy-done
  72.6 14.5 %shard_map.88 = bf16[8,3,1,128,128]{4,3,2,1,0:T(8,128)(2,1)} custom-call(s32[42]{0:T(128)} %reshape_squeeze.15.rb_ref, s32[8]{0:T(128)} %compare_select_fusion.10.pos_ref, bf16[8,3,4,128,128]{4,3,2,1,0:T(8,128)(2,1)} %copy-done, bf16[1024,512]{1,0:T(8,128)(2,1)} %convolution_convert_fusion.u_ref), custom_call_target="tpu_custom_call" | custom-call | flops 905969664 | bytes 1835008 | tf_op jit(solution)/shard_map/pallas_call | solution.py:118
  87.1 3.9 %all-to-all-start.3 = ((bf16[8,3,1,128,128]{4,3,2,1,0:T(8,128)(2,1)}), bf16[8,3,1,128,128]{4,3,2,1,0:T(8,128)(2,1)S(1)}, u32[]{:S(2)}, u32[]{:S(2)}) async-start(bf16[8,3,1,128,128]{4,3,2,1,0:T(8,128)(2,1)} %shard_map.88), calls=%async_computation.3 | async-start | bytes 1572864 | tf_op jit(solution)/shard_map/all_to_all | solution.py:253
  91.0 14.6 %shard_map.86.refs_0_ = bf16[8,3,2,128,128]{4,3,2,1,0:T(8,128)(2,1)} custom-call(s32[42]{0:T(128)} %reshape_squeeze.15.rb_ref, s32[8]{0:T(128)} %compare_select_fusion.10.pos_ref, bf16[8,3,4,128,128]{4,3,2,1,0:T(8,128)(2,1)} %copy-done, bf16[1024,512]{1,0:T(8,128)(2,1)} %convolution_convert_fusion.u_ref), custom_call_target="tpu_custom_call" | custom-call | flops 905969664 | bytes 1835008 | tf_op jit(solution)/shard_map/pallas_call | solution.py:118
  105.5 14.5 %shard_map.87 = bf16[8,3,2,128,128]{4,3,2,1,0:T(8,128)(2,1)} custom-call(s32[42]{0:T(128)} %reshape_squeeze.15.rb_ref, s32[8]{0:T(128)} %compare_select_fusion.10.pos_ref, bf16[8,3,4,128,128]{4,3,2,1,0:T(8,128)(2,1)} %copy-done, bf16[1024,512]{1,0:T(8,128)(2,1)} %convolution_convert_fusion.u_ref, ...), custom_call_target="tpu_custom_call", output_to_operand_aliasing={{}: (4, {})} | custom-call | flops 905969664 | bytes 1835008 | tf_op jit(solution)/shard_map/pallas_call | solution.py:118
  120.1 4.2 %all-to-all-start.2 = ((bf16[8,3,2,128,128]{4,3,2,1,0:T(8,128)(2,1)}), bf16[8,3,2,128,128]{4,3,2,1,0:T(8,128)(2,1)S(1)}, u32[]{:S(2)}, u32[]{:S(2)}) async-start(bf16[8,3,2,128,128]{4,3,2,1,0:T(8,128)(2,1)} %shard_map.87), calls=%async_computation.2 | async-start | bytes 3145728 | tf_op jit(solution)/shard_map/all_to_all | solution.py:253
  124.3 14.5 %shard_map.85 = bf16[8,3,1,128,128]{4,3,2,1,0:T(8,128)(2,1)} custom-call(s32[42]{0:T(128)} %reshape_squeeze.15.rb_ref, s32[8]{0:T(128)} %compare_select_fusion.10.pos_ref, bf16[8,3,4,128,128]{4,3,2,1,0:T(8,128)(2,1)} %copy-done, bf16[1024,512]{1,0:T(8,128)(2,1)} %convolution_convert_fusion.u_ref), custom_call_target="tpu_custom_call" | custom-call | flops 905969664 | bytes 1835008 | tf_op jit(solution)/shard_map/pallas_call | solution.py:118
  138.8 6.5 %all-to-all-done.2.refs_0_ = bf16[8,3,2,128,128]{4,3,2,1,0:T(8,128)(2,1)S(1)} async-done(((bf16[8,3,2,128,128]{4,3,2,1,0:T(8,128)(2,1)}), bf16[8,3,2,128,128]{4,3,2,1,0:T(8,128)(2,1)S(1)}, u32[]{:S(2)}, u32[]{:S(2)}) %all-to-all-start.2) | async-done | bytes 1572896 | tf_op jit(solution)/shard_map/all_to_all | solution.py:253
  145.3 3.5 %all-to-all-start.1 = ((bf16[8,3,1,128,128]{4,3,2,1,0:T(8,128)(2,1)}), bf16[8,3,1,128,128]{4,3,2,1,0:T(8,128)(2,1)S(1)}, u32[]{:S(2)}, u32[]{:S(2)}) async-start(bf16[8,3,1,128,128]{4,3,2,1,0:T(8,128)(2,1)} %shard_map.85), calls=%async_computation.1 | async-start | bytes 1572864 | tf_op jit(solution)/shard_map/all_to_all | solution.py:253
  148.9 3.6 %shard_map.89 = (bf16[1,128,4096]{2,1,0:T(8,128)(2,1)}, bf16[1,128,4096]{2,1,0:T(8,128)(2,1)}, bf16[1,128,4096]{2,1,0:T(8,128)(2,1)}) custom-call(bf16[8,3,2,128,128]{4,3,2,1,0:T(8,128)(2,1)} %copy-done.2, bf16[8,3,1,128,128]{4,3,2,1,0:T(8,128)(2,1)} %copy-done.3), custom_call_target="tpu_custom_call" | custom-call | tf_op jit(solution)/shard_map/pallas_call | solution.py:163
  152.5 8.9 %all-to-all-done.1.piece = bf16[8,3,1,128,128]{4,3,2,1,0:T(8,128)(2,1)S(1)} async-done(((bf16[8,3,1,128,128]{4,3,2,1,0:T(8,128)(2,1)}), bf16[8,3,1,128,128]{4,3,2,1,0:T(8,128)(2,1)S(1)}, u32[]{:S(2)}, u32[]{:S(2)}) %all-to-all-start.1) | async-done | bytes 786464 | tf_op jit(solution)/shard_map/all_to_all | solution.py:253
  161.4 0.9 copy-done.4
  162.3 2.4 %shard_map.90 = (bf16[1,128,4096]{2,1,0:T(8,128)(2,1)}, bf16[1,128,4096]{2,1,0:T(8,128)(2,1)}, bf16[1,128,4096]{2,1,0:T(8,128)(2,1)}) custom-call(bf16[8,3,1,128,128]{4,3,2,1,0:T(8,128)(2,1)} %copy-done.4, bf16[1,128,4096]{2,1,0:T(8,128)(2,1)} %get-tuple-element.6._first, ...), custom_call_target="tpu_custom_call", output_to_operand_aliasing={{0}: (1, {}), {1}: (2, {}), {2}: (3, {})} | custom-call | tf_op jit(solution)/shard_map/pallas_call | solution.py:171
  (19 shorter events, 0.1 us)
Async XLA Ops:
  0.6 24.7 %collective-permute-start = (bf16[128,2048]{1,0:T(8,128)(2,1)}, bf16[128,2048]{1,0:T(8,128)(2,1)}, u32[]{:S(2)}, u32[]{:S(2)}) collective-permute-start(bf16[128,2048]{1,0:T(8,128)(2,1)} %bitcast.36), channel_id=1, source_target_pairs={{0,2},{1,3},{2,4},{3,5},{4,6},{5,7},{6,0},{7,1},{8,10},{9,11},{10,... | collective-permute-start | bytes 1572872 | tf_op jit(solution)/shard_map/ppermute | solution.py:203
  3.6 26.4 %collective-permute-start.1 = (bf16[128,2048]{1,0:T(8,128)(2,1)}, bf16[128,2048]{1,0:T(8,128)(2,1)}, u32[]{:S(2)}, u32[]{:S(2)}) collective-permute-start(bf16[128,2048]{1,0:T(8,128)(2,1)} %bitcast.37), channel_id=1, source_target_pairs={{0,4},{1,5},{2,6},{3,7},{4,0},{5,1},{6,2},{7,3},{8,12},{9,13},{10,... | collective-permute-start | bytes 1572872 | tf_op jit(solution)/shard_map/ppermute | solution.py:203
  5.1 24.9 %collective-permute-start.2 = (bf16[128,2048]{1,0:T(8,128)(2,1)}, bf16[128,2048]{1,0:T(8,128)(2,1)}, u32[]{:S(2)}, u32[]{:S(2)}) collective-permute-start(bf16[128,2048]{1,0:T(8,128)(2,1)} %bitcast.38), channel_id=1, source_target_pairs={{0,6},{1,7},{2,0},{3,1},{4,2},{5,3},{6,4},{7,5},{8,14},{9,15},{10,... | collective-permute-start | bytes 1572872 | tf_op jit(solution)/shard_map/ppermute | solution.py:203
  6.6 26.7 %collective-permute-start.4 = (bf16[128,2048]{1,0:T(8,128)(2,1)}, bf16[128,2048]{1,0:T(8,128)(2,1)}, u32[]{:S(2)}, u32[]{:S(2)}) collective-permute-start(bf16[128,2048]{1,0:T(8,128)(2,1)} %param.10), channel_id=1, source_target_pairs={{0,8},{8,16},{16,24},{24,0},{1,9},{9,17},{17,25},{25,1},{2,10},{10... | collective-permute-start | bytes 1572872 | tf_op jit(solution)/shard_map/ppermute | solution.py:195
  8.2 36.0 %collective-permute-start.5 = (bf16[128,2048]{1,0:T(8,128)(2,1)}, bf16[128,2048]{1,0:T(8,128)(2,1)}, u32[]{:S(2)}, u32[]{:S(2)}) collective-permute-start(bf16[128,2048]{1,0:T(8,128)(2,1)} %param.10), channel_id=1, source_target_pairs={{0,16},{8,24},{16,0},{24,8},{1,17},{9,25},{17,1},{25,9},{2,18},{10... | collective-permute-start | bytes 1572872 | tf_op jit(solution)/shard_map/ppermute | solution.py:195
  21.5 5.9 %copy-start.7 = (s32[1,14,3]{1,0,2:T(1,128)S(1)}, s32[1,14,3]{1,0,2:T(1,128)}, u32[]{:S(2)}) copy-start(s32[1,14,3]{1,0,2:T(1,128)} %param.11) | copy-start | bytes 508
  21.5 49.4 %all-to-all-start = ((bf16[8,3,4,128,128]{4,3,2,1,0:T(8,128)(2,1)}), bf16[8,3,4,128,128]{4,3,2,1,0:T(8,128)(2,1)S(1)}, u32[]{:S(2)}, u32[]{:S(2)}) async-start(bf16[8,3,4,128,128]{4,3,2,1,0:T(8,128)(2,1)} %pad_maximum_fusion), calls=%async_computation | async-start | bytes 6291456 | tf_op jit(solution)/shard_map/all_to_all | solution.py:235
  25.4 25.7 %collective-permute-start.6 = (bf16[128,2048]{1,0:T(8,128)(2,1)}, bf16[128,2048]{1,0:T(8,128)(2,1)}, u32[]{:S(2)}, u32[]{:S(2)}) collective-permute-start(bf16[128,2048]{1,0:T(8,128)(2,1)} %param.10), channel_id=1, source_target_pairs={{0,24},{8,0},{16,8},{24,16},{1,25},{9,1},{17,9},{25,17},{2,26},{10... | collective-permute-start | bytes 1572872 | tf_op jit(solution)/shard_map/ppermute | solution.py:195
  30.0 21.1 %copy-start.5 = (bf16[128,2048]{1,0:T(8,128)(2,1)S(1)}, bf16[128,2048]{1,0:T(8,128)(2,1)}, u32[]{:S(2)}) copy-start(bf16[128,2048]{1,0:T(8,128)(2,1)} %param.10) | copy-start | bytes 1572868
  33.1 30.7 %collective-permute-start.3 = (bf16[4,128,2048]{2,1,0:T(8,128)(2,1)}, bf16[4,128,2048]{2,1,0:T(8,128)(2,1)}, u32[]{:S(2)}, u32[]{:S(2)}) collective-permute-start(bf16[4,128,2048]{2,1,0:T(8,128)(2,1)} %pad_maximum_fusion.1), channel_id=1, source_target_pairs={{0,1},{1,0},{2,3},{3,2},{4,5},{5,4},{6,7},{7,6},{8,9},{9,8},{10,11... | collective-permute-start | bytes 6291464 | tf_op jit(solution)/shard_map/ppermute | solution.py:206
  57.7 5.8 %copy-start.1 = (bf16[4,128,2048]{2,1,0:T(8,128)(2,1)S(1)}, bf16[4,128,2048]{2,1,0:T(8,128)(2,1)}, u32[]{:S(2)}) copy-start(bf16[4,128,2048]{2,1,0:T(8,128)(2,1)} %gather_fusion) | copy-start | bytes 6291460
  63.6 2.2 %copy-start.6 = (bf16[8,128,2048]{2,1,0:T(8,128)(2,1)S(1)}, bf16[8,128,2048]{2,1,0:T(8,128)(2,1)}, u32[]{:S(2)}) copy-start(bf16[8,128,2048]{2,1,0:T(8,128)(2,1)} %constant_dynamic-update-slice_fusion.1) | copy-start | bytes 12582916
  70.9 1.6 copy-start
  87.1 33.0 %all-to-all-start.3 = ((bf16[8,3,1,128,128]{4,3,2,1,0:T(8,128)(2,1)}), bf16[8,3,1,128,128]{4,3,2,1,0:T(8,128)(2,1)S(1)}, u32[]{:S(2)}, u32[]{:S(2)}) async-start(bf16[8,3,1,128,128]{4,3,2,1,0:T(8,128)(2,1)} %shard_map.88), calls=%async_computation.3 | async-start | bytes 1572864 | tf_op jit(solution)/shard_map/all_to_all | solution.py:253
  120.1 18.7 %copy-start.3 = (bf16[8,3,1,128,128]{4,3,2,1,0:T(8,128)(2,1)}, bf16[8,3,1,128,128]{4,3,2,1,0:T(8,128)(2,1)S(1)}, u32[]{:S(2)}) copy-start(bf16[8,3,1,128,128]{4,3,2,1,0:T(8,128)(2,1)S(1)} %all-to-all-done.3.refs_1_) | copy-start | bytes 2359300
  120.1 25.2 %all-to-all-start.2 = ((bf16[8,3,2,128,128]{4,3,2,1,0:T(8,128)(2,1)}), bf16[8,3,2,128,128]{4,3,2,1,0:T(8,128)(2,1)S(1)}, u32[]{:S(2)}, u32[]{:S(2)}) async-start(bf16[8,3,2,128,128]{4,3,2,1,0:T(8,128)(2,1)} %shard_map.87), calls=%async_computation.2 | async-start | bytes 3145728 | tf_op jit(solution)/shard_map/all_to_all | solution.py:253
  145.3 3.6 %copy-start.2 = (bf16[8,3,2,128,128]{4,3,2,1,0:T(8,128)(2,1)}, bf16[8,3,2,128,128]{4,3,2,1,0:T(8,128)(2,1)S(1)}, u32[]{:S(2)}) copy-start(bf16[8,3,2,128,128]{4,3,2,1,0:T(8,128)(2,1)S(1)} %all-to-all-done.2.refs_0_) | copy-start | bytes 4718596
  145.3 16.1 %all-to-all-start.1 = ((bf16[8,3,1,128,128]{4,3,2,1,0:T(8,128)(2,1)}), bf16[8,3,1,128,128]{4,3,2,1,0:T(8,128)(2,1)S(1)}, u32[]{:S(2)}, u32[]{:S(2)}) async-start(bf16[8,3,1,128,128]{4,3,2,1,0:T(8,128)(2,1)} %shard_map.85), calls=%async_computation.1 | async-start | bytes 1572864 | tf_op jit(solution)/shard_map/all_to_all | solution.py:253
  161.4 0.9 copy-start.4

commit v14 on v12

--- a/solution.py
+++ b/solution.py
@@ -95,7 +95,7 @@
             dv_acc[pl.ds(row, BLOCK), :] += value_grad[slot * BLOCK:(slot + 1) * BLOCK, :]
         return carry
 
-    lax.fori_loop(1, count - 1, mid_step, 0, unroll=2)
+    lax.fori_loop(1, count - 1, mid_step, 0, unroll=7)
     o_ref[:, 1, :, :] = dk_acc[...].reshape(parts, tokens, HD).astype(jnp.bfloat16)
     o_ref[:, 2, :, :] = dv_acc[...].reshape(parts, tokens, HD).astype(jnp.bfloat16)
 

time: 166 us -> 161 us (0.970)
  Pallas kernels: 64.2 us -> 59.7 us
    pallas_call x4, Pallas kernels: 58.1 us -> 53.6 us  [attention_grads(): pl.pallas_call(_attention_kernel, out_shape=out, grid_spec=pltpu.Prefetch...]
  transfers between devices with their start and end apart: 12 -> 12, of which waited for: 3 -> 3; matrix products, arithmetic and copies ran while one was open for 21% -> 22% of each run, Pallas kernels for 29% -> 28%
where the time goes in v14:
time: 161 us; the launch traced here: 159 us
  Pallas kernels  59.7 us (37%)
  starting transfers between devices  31.9 us (20%)
  waiting for transfers between devices  26.9 us (17%)
  local copies, waits for them, and re-layouts  25.9 us (16%)
  other arithmetic  10.1 us (6%)
  matrix products  3.34 us (2%)
    pallas_call x4, Pallas kernels, attention_grads(): pl.pallas_call(_attention_kernel, out_shape=out, grid_spec=pltpu.Prefetch...  53.6 us
    ppermute x3, waiting for transfers between devices, body(): lax.ppermute(out_weight, 'dp', [(a, (a + s) % dp) for a in range(dp)])  17.9 us
    unnamed x26, local copies, waits for them, and re-layouts  17.1 us
    all_to_all x4, starting transfers between devices, body(): lax.all_to_all(grads, 'context', split_axis=0, concat_axis=0, tiled=True)  16.5 us
    all_to_all x4, waiting for transfers between devices, body(): lax.all_to_all(grads, 'context', split_axis=0, concat_axis=0, tiled=True)  8.96 us
    ppermute x3, starting transfers between devices, body(): lax.ppermute(local_cotangent, 'context', [(a, (a + s) % ctx) for a in ran...  5.94 us
    ppermute x3, starting transfers between devices, body(): lax.ppermute(out_weight, 'dp', [(a, (a + s) % dp) for a in range(dp)])  5.59 us
    all_to_all x1, starting transfers between devices, body(): lax.all_to_all(stacked, 'context', split_axis=0, concat_axis=0, tiled=True)  3.78 us
  transfers between devices with their start and end apart: 12, of which 3 were waited for; matrix products, arithmetic and copies ran while one was open for 22% of the time, Pallas kernels for 28%

profile of v14, /device:TPU:0, one launch (start us, length us, event | category | flops | bytes accessed | tf_op | source)
XLA Modules:
  0.0 158.7 jit_solution(14430176900740592207)
XLA Ops:
  0.6 3.0 %collective-permute-start = (bf16[128,2048]{1,0:T(8,128)(2,1)}, bf16[128,2048]{1,0:T(8,128)(2,1)}, u32[]{:S(2)}, u32[]{:S(2)}) collective-permute-start(bf16[128,2048]{1,0:T(8,128)(2,1)} %bitcast.36), channel_id=1, source_target_pairs={{0,2},{1,3},{2,4},{3,5},{4,6},{5,7},{6,0},{7,1},{8,10},{9,11},{10,... | collective-permute-start | bytes 1572872 | tf_op jit(solution)/shard_map/ppermute | solution.py:198
  3.6 1.5 collective-permute-start.1
  5.1 1.4 collective-permute-start.2
  6.6 1.6 collective-permute-start.4
  8.2 2.6 %collective-permute-start.5 = (bf16[128,2048]{1,0:T(8,128)(2,1)}, bf16[128,2048]{1,0:T(8,128)(2,1)}, u32[]{:S(2)}, u32[]{:S(2)}) collective-permute-start(bf16[128,2048]{1,0:T(8,128)(2,1)} %param.10), channel_id=1, source_target_pairs={{0,16},{8,24},{16,0},{24,8},{1,17},{9,25},{17,1},{25,9},{2,18},{10... | collective-permute-start | bytes 1572872 | tf_op jit(solution)/shard_map/ppermute | solution.py:190
  10.7 1.6 %copy.14 = bf16[1,128,4096]{1,2,0:T(8,128)(2,1)S(1)} copy(bf16[1,128,4096]{2,1,0:T(8,128)(2,1)} %param.6) | data formatting | bytes 2097152 | tf_op args[0]
  12.4 0.7 copy.15
  13.0 1.6 %copy.16 = bf16[1,128,4096]{1,2,0:T(8,128)(2,1)S(1)} copy(bf16[1,128,4096]{2,1,0:T(8,128)(2,1)} %param.7) | data formatting | bytes 2097152 | tf_op args[1]
  14.7 0.7 copy.17
  15.3 1.6 %copy.18 = bf16[1,128,4096]{1,2,0:T(8,128)(2,1)S(1)} copy(bf16[1,128,4096]{2,1,0:T(8,128)(2,1)} %param.8) | data formatting | bytes 2097152 | tf_op args[2]
  17.0 1.3 copy.19
  18.3 3.2 %pad_maximum_fusion = bf16[8,3,4,128,128]{4,3,2,1,0:T(8,128)(2,1)} fusion(bf16[8,1,4,128,128]{4,3,2,1,0:T(8,128)(2,1)} %bitcast.34, bf16[8,1,4,128,128]{4,3,2,1,0:T(8,128)(2,1)S(1)} %bitcast.33, bf16[8,1,4,128,128]{4,3,2,1,0:T(8,128)(2,1)S(1)} %bitcast.32), kind=kLoop, calls=%fused_computation.1 | loop fusion | flops 3145728 | bytes 6291456 | tf_op jit(solution)/shard_map/stack | solution.py:229
  21.5 3.8 %all-to-all-start = ((bf16[8,3,4,128,128]{4,3,2,1,0:T(8,128)(2,1)}), bf16[8,3,4,128,128]{4,3,2,1,0:T(8,128)(2,1)S(1)}, u32[]{:S(2)}, u32[]{:S(2)}) async-start(bf16[8,3,4,128,128]{4,3,2,1,0:T(8,128)(2,1)} %pad_maximum_fusion), calls=%async_computation | async-start | bytes 6291456 | tf_op jit(solution)/shard_map/all_to_all | solution.py:230
  25.4 0.0 collective-permute-done
  25.4 1.4 collective-permute-start.6
  26.8 0.5 compare_select_fusion.10.pos_ref
  27.3 0.1 copy.13
  27.4 0.7 reshape_squeeze.15.rb_ref
  28.1 1.9 %constant_dynamic-update-slice_fusion.4 = bf16[8,128,2048]{2,1,0:T(8,128)(2,1)} fusion(bf16[1,128,2048]{2,1,0:T(8,128)(2,1)} %param.9), kind=kLoop, calls=%fused_computation.10 | loop fusion | bytes 1048576
  29.9 3.1 %pad_maximum_fusion.1 = bf16[4,128,2048]{2,1,0:T(8,128)(2,1)} fusion(bf16[1,128,2048]{2,1,0:T(8,128)(2,1)} %bitcast.12, bf16[1,128,2048]{2,1,0:T(8,128)(2,1)} %bitcast.11, bf16[1,128,2048]{2,1,0:T(8,128)(2,1)} %bitcast.10, bf16[1,128,2048]{2,1,0:T(8,128)(2,1)} %param.9), kind=kLoop, calls=%fused_computation.2 | loop fusion | flops 3145728 | bytes 4194304 | tf_op jit(solution)/shard_map/stack | solution.py:197
  33.1 0.1 collective-permute-start.3
  33.2 11.0 %collective-permute-done.5 = bf16[128,2048]{1,0:T(8,128)(2,1)} collective-permute-done((bf16[128,2048]{1,0:T(8,128)(2,1)}, bf16[128,2048]{1,0:T(8,128)(2,1)}, u32[]{:S(2)}, u32[]{:S(2)}) %collective-permute-start.5) | collective-permute-done | bytes 524320 | tf_op jit(solution)/shard_map/ppermute | solution.py:190
  44.2 6.9 %collective-permute-done.6 = bf16[128,2048]{1,0:T(8,128)(2,1)} collective-permute-done((bf16[128,2048]{1,0:T(8,128)(2,1)}, bf16[128,2048]{1,0:T(8,128)(2,1)}, u32[]{:S(2)}, u32[]{:S(2)}) %collective-permute-start.6) | collective-permute-done | bytes 524320 | tf_op jit(solution)/shard_map/ppermute | solution.py:190
  51.1 3.0 %pad_maximum_fusion.2 = bf16[4,128,2048]{2,1,0:T(8,128)(2,1)} fusion(bf16[1,128,2048]{2,1,0:T(8,128)(2,1)} %bitcast.17, bf16[1,128,2048]{2,1,0:T(8,128)(2,1)} %bitcast.16, bf16[1,128,2048]{2,1,0:T(8,128)(2,1)} %bitcast.15, bf16[1,128,2048]{2,1,0:T(8,128)(2,1)S(1)} %bitcast.39), kind=kLoop, calls=%fused_computation.3 | loop fusion | flops 3145728 | bytes 4194304 | tf_op jit(solution)/shard_map/stack | solution.py:194
  54.0 3.7 %gather_fusion = bf16[4,128,2048]{2,1,0:T(8,128)(2,1)} fusion(bf16[4,128,2048]{2,1,0:T(8,128)(2,1)} %pad_maximum_fusion.2, s32[1024]{0:T(1024)S(1)} %pad_clamp_fusion), kind=kCustom, calls=%fused_computation | custom fusion | bytes 4194320 | tf_op jit(solution)/shard_map/jit(_take)/gather | solution.py:194
  57.8 2.0 %constant_dynamic-update-slice_fusion.3 = bf16[8,128,2048]{2,1,0:T(8,128)(2,1)} fusion(bf16[8,128,2048]{2,1,0:T(8,128)(2,1)} %constant_dynamic-update-slice_fusion.4, bf16[128,2048]{1,0:T(8,128)(2,1)} %collective-permute-done), kind=kLoop, calls=%fused_computation.9 | loop fusion | bytes 1048576
  59.8 1.9 %constant_dynamic-update-slice_fusion.2 = bf16[8,128,2048]{2,1,0:T(8,128)(2,1)} fusion(bf16[8,128,2048]{2,1,0:T(8,128)(2,1)} %constant_dynamic-update-slice_fusion.3, bf16[128,2048]{1,0:T(8,128)(2,1)} %collective-permute-done.1), kind=kLoop, calls=%fused_computation.8 | loop fusion | bytes 1048576
  61.7 1.9 %constant_dynamic-update-slice_fusion.1 = bf16[8,128,2048]{2,1,0:T(8,128)(2,1)} fusion(bf16[8,128,2048]{2,1,0:T(8,128)(2,1)} %constant_dynamic-update-slice_fusion.2, bf16[128,2048]{1,0:T(8,128)(2,1)} %collective-permute-done.2), kind=kLoop, calls=%fused_computation.7 | loop fusion | bytes 1048576
  63.6 0.3 broadcast_select_fusion
  63.9 0.0 collective-permute-done.3
  63.9 1.9 %copy-done.7 = bf16[8,128,2048]{2,1,0:T(8,128)(2,1)S(1)} copy-done((bf16[8,128,2048]{2,1,0:T(8,128)(2,1)S(1)}, bf16[8,128,2048]{2,1,0:T(8,128)(2,1)}, u32[]{:S(2)}) %copy-start.7) | copy-done | bytes 4194328
  65.8 1.8 %constant_dynamic-update-slice_fusion = bf16[8,128,2048]{2,1,0:T(8,128)(2,1)S(1)} fusion(bf16[8,128,2048]{2,1,0:T(8,128)(2,1)S(1)} %copy-done.7, bf16[4,128,2048]{2,1,0:T(8,128)(2,1)} %collective-permute-done.3), kind=kLoop, calls=%fused_computation.6 | loop fusion | bytes 4194304 | tf_op jit(solution)/shard_map/concatenate | solution.py:202
  67.6 3.3 %convolution_convert_fusion.u_ref = bf16[1024,512]{1,0:T(8,128)(2,1)} fusion(bf16[1024,2048]{1,0:T(8,128)(2,1)S(1)} %bitcast.40, bf16[512,2048]{1,0:T(8,128)(2,1)S(1)} %bitcast.35), kind=kOutput, calls=%fused_computation.5 | convolution fusion | flops 2148007936 | bytes 7340032 | tf_op jit(solution)/shard_map/dot_general | solution.py:203
  70.9 0.0 all-to-all-done.x_ref
  71.0 1.6 %copy-done = bf16[8,3,4,128,128]{4,3,2,1,0:T(8,128)(2,1)} copy-done((bf16[8,3,4,128,128]{4,3,2,1,0:T(8,128)(2,1)}, bf16[8,3,4,128,128]{4,3,2,1,0:T(8,128)(2,1)S(1)}, u32[]{:S(2)}) %copy-start) | copy-done | bytes 3145752
  72.6 13.4 %shard_map.88 = bf16[8,3,128,128]{3,2,1,0:T(8,128)(2,1)} custom-call(s32[42]{0:T(128)} %reshape_squeeze.15.rb_ref, s32[8]{0:T(128)} %compare_select_fusion.10.pos_ref, bf16[8,3,4,128,128]{4,3,2,1,0:T(8,128)(2,1)} %copy-done, bf16[1024,512]{1,0:T(8,128)(2,1)} %convolution_convert_fusion.u_ref), custom_call_target="tpu_custom_call" | custom-call | flops 905969664 | bytes 1835008 | tf_op jit(solution)/shard_map/pallas_call | solution.py:115
  86.0 3.9 %all-to-all-start.4 = ((bf16[8,3,128,128]{3,2,1,0:T(8,128)(2,1)}), bf16[8,3,128,128]{3,2,1,0:T(8,128)(2,1)S(1)}, u32[]{:S(2)}, u32[]{:S(2)}) async-start(bf16[8,3,128,128]{3,2,1,0:T(8,128)(2,1)} %shard_map.88), calls=%async_computation.4 | async-start | bytes 1572864 | tf_op jit(solution)/shard_map/all_to_all | solution.py:240
  89.9 13.4 %shard_map.87 = bf16[8,3,128,128]{3,2,1,0:T(8,128)(2,1)} custom-call(s32[42]{0:T(128)} %reshape_squeeze.15.rb_ref, s32[8]{0:T(128)} %compare_select_fusion.10.pos_ref, bf16[8,3,4,128,128]{4,3,2,1,0:T(8,128)(2,1)} %copy-done, bf16[1024,512]{1,0:T(8,128)(2,1)} %convolution_convert_fusion.u_ref), custom_call_target="tpu_custom_call" | custom-call | flops 905969664 | bytes 1835008 | tf_op jit(solution)/shard_map/pallas_call | solution.py:115
  103.3 0.0 all-to-all-done.4.refs_2_
  103.3 4.2 %all-to-all-start.3 = ((bf16[8,3,128,128]{3,2,1,0:T(8,128)(2,1)}), bf16[8,3,128,128]{3,2,1,0:T(8,128)(2,1)S(1)}, u32[]{:S(2)}, u32[]{:S(2)}) async-start(bf16[8,3,128,128]{3,2,1,0:T(8,128)(2,1)} %shard_map.87), calls=%async_computation.3 | async-start | bytes 1572864 | tf_op jit(solution)/shard_map/all_to_all | solution.py:240
  107.5 13.4 %shard_map.86 = bf16[8,3,128,128]{3,2,1,0:T(8,128)(2,1)} custom-call(s32[42]{0:T(128)} %reshape_squeeze.15.rb_ref, s32[8]{0:T(128)} %compare_select_fusion.10.pos_ref, bf16[8,3,4,128,128]{4,3,2,1,0:T(8,128)(2,1)} %copy-done, bf16[1024,512]{1,0:T(8,128)(2,1)} %convolution_convert_fusion.u_ref), custom_call_target="tpu_custom_call" | custom-call | flops 905969664 | bytes 1835008 | tf_op jit(solution)/shard_map/pallas_call | solution.py:115
  120.9 4.2 %all-to-all-start.2 = ((bf16[8,3,128,128]{3,2,1,0:T(8,128)(2,1)}), bf16[8,3,128,128]{3,2,1,0:T(8,128)(2,1)S(1)}, u32[]{:S(2)}, u32[]{:S(2)}) async-start(bf16[8,3,128,128]{3,2,1,0:T(8,128)(2,1)} %shard_map.86), calls=%async_computation.2 | async-start | bytes 1572864 | tf_op jit(solution)/shard_map/all_to_all | solution.py:240
  125.1 13.4 %shard_map.85 = bf16[8,3,128,128]{3,2,1,0:T(8,128)(2,1)} custom-call(s32[42]{0:T(128)} %reshape_squeeze.15.rb_ref, s32[8]{0:T(128)} %compare_select_fusion.10.pos_ref, bf16[8,3,4,128,128]{4,3,2,1,0:T(8,128)(2,1)} %copy-done, bf16[1024,512]{1,0:T(8,128)(2,1)} %convolution_convert_fusion.u_ref), custom_call_target="tpu_custom_call" | custom-call | flops 905969664 | bytes 1835008 | tf_op jit(solution)/shard_map/pallas_call | solution.py:115
  138.5 4.2 %all-to-all-start.1 = ((bf16[8,3,128,128]{3,2,1,0:T(8,128)(2,1)}), bf16[8,3,128,128]{3,2,1,0:T(8,128)(2,1)S(1)}, u32[]{:S(2)}, u32[]{:S(2)}) async-start(bf16[8,3,128,128]{3,2,1,0:T(8,128)(2,1)} %shard_map.85), calls=%async_computation.1 | async-start | bytes 1572864 | tf_op jit(solution)/shard_map/all_to_all | solution.py:240
  142.7 3.6 %shard_map.89 = (bf16[1,128,4096]{2,1,0:T(8,128)(2,1)}, bf16[1,128,4096]{2,1,0:T(8,128)(2,1)}, bf16[1,128,4096]{2,1,0:T(8,128)(2,1)}) custom-call(bf16[8,3,128,128]{3,2,1,0:T(8,128)(2,1)} %copy-done.4, bf16[8,3,128,128]{3,2,1,0:T(8,128)(2,1)} %copy-done.3, bf16[8,3,128,128]{3,2,1,0:T(8,128)(2,1)} %copy-done.2), custom_call_target="tpu_custom_call" | custom-call | tf_op jit(solution)/shard_map/pallas_call | solution.py:151
  146.4 9.0 %all-to-all-done.1.piece = bf16[8,3,128,128]{3,2,1,0:T(8,128)(2,1)S(1)} async-done(((bf16[8,3,128,128]{3,2,1,0:T(8,128)(2,1)}), bf16[8,3,128,128]{3,2,1,0:T(8,128)(2,1)S(1)}, u32[]{:S(2)}, u32[]{:S(2)}) %all-to-all-start.1) | async-done | bytes 786464 | tf_op jit(solution)/shard_map/all_to_all | solution.py:240
  155.3 0.9 copy-done.5
  156.2 2.4 %shard_map.90 = (bf16[1,128,4096]{2,1,0:T(8,128)(2,1)}, bf16[1,128,4096]{2,1,0:T(8,128)(2,1)}, bf16[1,128,4096]{2,1,0:T(8,128)(2,1)}) custom-call(bf16[8,3,128,128]{3,2,1,0:T(8,128)(2,1)} %copy-done.5, bf16[1,128,4096]{2,1,0:T(8,128)(2,1)} %get-tuple-element.6._first, ...), custom_call_target="tpu_custom_call", output_to_operand_aliasing={{0}: (1, {}), {1}: (2, {}), {2}: (3, {})} | custom-call | tf_op jit(solution)/shard_map/pallas_call | solution.py:159
  (23 shorter events, 0.1 us)
Async XLA Ops:
  0.6 24.7 %collective-permute-start = (bf16[128,2048]{1,0:T(8,128)(2,1)}, bf16[128,2048]{1,0:T(8,128)(2,1)}, u32[]{:S(2)}, u32[]{:S(2)}) collective-permute-start(bf16[128,2048]{1,0:T(8,128)(2,1)} %bitcast.36), channel_id=1, source_target_pairs={{0,2},{1,3},{2,4},{3,5},{4,6},{5,7},{6,0},{7,1},{8,10},{9,11},{10,... | collective-permute-start | bytes 1572872 | tf_op jit(solution)/shard_map/ppermute | solution.py:198
  3.6 26.3 %collective-permute-start.1 = (bf16[128,2048]{1,0:T(8,128)(2,1)}, bf16[128,2048]{1,0:T(8,128)(2,1)}, u32[]{:S(2)}, u32[]{:S(2)}) collective-permute-start(bf16[128,2048]{1,0:T(8,128)(2,1)} %bitcast.37), channel_id=1, source_target_pairs={{0,4},{1,5},{2,6},{3,7},{4,0},{5,1},{6,2},{7,3},{8,12},{9,13},{10,... | collective-permute-start | bytes 1572872 | tf_op jit(solution)/shard_map/ppermute | solution.py:198
  5.1 24.8 %collective-permute-start.2 = (bf16[128,2048]{1,0:T(8,128)(2,1)}, bf16[128,2048]{1,0:T(8,128)(2,1)}, u32[]{:S(2)}, u32[]{:S(2)}) collective-permute-start(bf16[128,2048]{1,0:T(8,128)(2,1)} %bitcast.38), channel_id=1, source_target_pairs={{0,6},{1,7},{2,0},{3,1},{4,2},{5,3},{6,4},{7,5},{8,14},{9,15},{10,... | collective-permute-start | bytes 1572872 | tf_op jit(solution)/shard_map/ppermute | solution.py:198
  6.6 26.6 %collective-permute-start.4 = (bf16[128,2048]{1,0:T(8,128)(2,1)}, bf16[128,2048]{1,0:T(8,128)(2,1)}, u32[]{:S(2)}, u32[]{:S(2)}) collective-permute-start(bf16[128,2048]{1,0:T(8,128)(2,1)} %param.10), channel_id=1, source_target_pairs={{0,8},{8,16},{16,24},{24,0},{1,9},{9,17},{17,25},{25,1},{2,10},{10... | collective-permute-start | bytes 1572872 | tf_op jit(solution)/shard_map/ppermute | solution.py:190
  8.2 36.0 %collective-permute-start.5 = (bf16[128,2048]{1,0:T(8,128)(2,1)}, bf16[128,2048]{1,0:T(8,128)(2,1)}, u32[]{:S(2)}, u32[]{:S(2)}) collective-permute-start(bf16[128,2048]{1,0:T(8,128)(2,1)} %param.10), channel_id=1, source_target_pairs={{0,16},{8,24},{16,0},{24,8},{1,17},{9,25},{17,1},{25,9},{2,18},{10... | collective-permute-start | bytes 1572872 | tf_op jit(solution)/shard_map/ppermute | solution.py:190
  21.5 5.8 %copy-start.8 = (s32[1,14,3]{1,0,2:T(1,128)S(1)}, s32[1,14,3]{1,0,2:T(1,128)}, u32[]{:S(2)}) copy-start(s32[1,14,3]{1,0,2:T(1,128)} %param.11) | copy-start | bytes 508
  21.5 49.4 %all-to-all-start = ((bf16[8,3,4,128,128]{4,3,2,1,0:T(8,128)(2,1)}), bf16[8,3,4,128,128]{4,3,2,1,0:T(8,128)(2,1)S(1)}, u32[]{:S(2)}, u32[]{:S(2)}) async-start(bf16[8,3,4,128,128]{4,3,2,1,0:T(8,128)(2,1)} %pad_maximum_fusion), calls=%async_computation | async-start | bytes 6291456 | tf_op jit(solution)/shard_map/all_to_all | solution.py:230
  25.4 25.7 %collective-permute-start.6 = (bf16[128,2048]{1,0:T(8,128)(2,1)}, bf16[128,2048]{1,0:T(8,128)(2,1)}, u32[]{:S(2)}, u32[]{:S(2)}) collective-permute-start(bf16[128,2048]{1,0:T(8,128)(2,1)} %param.10), channel_id=1, source_target_pairs={{0,24},{8,0},{16,8},{24,16},{1,25},{9,1},{17,9},{25,17},{2,26},{10... | collective-permute-start | bytes 1572872 | tf_op jit(solution)/shard_map/ppermute | solution.py:190
  29.9 21.1 %copy-start.6 = (bf16[128,2048]{1,0:T(8,128)(2,1)S(1)}, bf16[128,2048]{1,0:T(8,128)(2,1)}, u32[]{:S(2)}) copy-start(bf16[128,2048]{1,0:T(8,128)(2,1)} %param.10) | copy-start | bytes 1572868
  33.1 30.8 %collective-permute-start.3 = (bf16[4,128,2048]{2,1,0:T(8,128)(2,1)}, bf16[4,128,2048]{2,1,0:T(8,128)(2,1)}, u32[]{:S(2)}, u32[]{:S(2)}) collective-permute-start(bf16[4,128,2048]{2,1,0:T(8,128)(2,1)} %pad_maximum_fusion.1), channel_id=1, source_target_pairs={{0,1},{1,0},{2,3},{3,2},{4,5},{5,4},{6,7},{7,6},{8,9},{9,8},{10,11... | collective-permute-start | bytes 6291464 | tf_op jit(solution)/shard_map/ppermute | solution.py:201
  57.8 5.8 %copy-start.1 = (bf16[4,128,2048]{2,1,0:T(8,128)(2,1)S(1)}, bf16[4,128,2048]{2,1,0:T(8,128)(2,1)}, u32[]{:S(2)}) copy-start(bf16[4,128,2048]{2,1,0:T(8,128)(2,1)} %gather_fusion) | copy-start | bytes 6291460
  63.6 2.2 %copy-start.7 = (bf16[8,128,2048]{2,1,0:T(8,128)(2,1)S(1)}, bf16[8,128,2048]{2,1,0:T(8,128)(2,1)}, u32[]{:S(2)}) copy-start(bf16[8,128,2048]{2,1,0:T(8,128)(2,1)} %constant_dynamic-update-slice_fusion.1) | copy-start | bytes 12582916
  70.9 1.6 %copy-start = (bf16[8,3,4,128,128]{4,3,2,1,0:T(8,128)(2,1)}, bf16[8,3,4,128,128]{4,3,2,1,0:T(8,128)(2,1)S(1)}, u32[]{:S(2)}) copy-start(bf16[8,3,4,128,128]{4,3,2,1,0:T(8,128)(2,1)S(1)} %all-to-all-done.x_ref) | copy-start | bytes 9437188
  86.0 17.3 %all-to-all-start.4 = ((bf16[8,3,128,128]{3,2,1,0:T(8,128)(2,1)}), bf16[8,3,128,128]{3,2,1,0:T(8,128)(2,1)S(1)}, u32[]{:S(2)}, u32[]{:S(2)}) async-start(bf16[8,3,128,128]{3,2,1,0:T(8,128)(2,1)} %shard_map.88), calls=%async_computation.4 | async-start | bytes 1572864 | tf_op jit(solution)/shard_map/all_to_all | solution.py:240
  103.3 17.6 %copy-start.2 = (bf16[8,3,128,128]{3,2,1,0:T(8,128)(2,1)}, bf16[8,3,128,128]{3,2,1,0:T(8,128)(2,1)S(1)}, u32[]{:S(2)}) copy-start(bf16[8,3,128,128]{3,2,1,0:T(8,128)(2,1)S(1)} %all-to-all-done.4.refs_2_) | copy-start | bytes 2359300
  103.3 17.6 %all-to-all-start.3 = ((bf16[8,3,128,128]{3,2,1,0:T(8,128)(2,1)}), bf16[8,3,128,128]{3,2,1,0:T(8,128)(2,1)S(1)}, u32[]{:S(2)}, u32[]{:S(2)}) async-start(bf16[8,3,128,128]{3,2,1,0:T(8,128)(2,1)} %shard_map.87), calls=%async_computation.3 | async-start | bytes 1572864 | tf_op jit(solution)/shard_map/all_to_all | solution.py:240
  120.9 17.6 %copy-start.3 = (bf16[8,3,128,128]{3,2,1,0:T(8,128)(2,1)}, bf16[8,3,128,128]{3,2,1,0:T(8,128)(2,1)S(1)}, u32[]{:S(2)}) copy-start(bf16[8,3,128,128]{3,2,1,0:T(8,128)(2,1)S(1)} %all-to-all-done.3.refs_1_) | copy-start | bytes 2359300
  120.9 17.6 %all-to-all-start.2 = ((bf16[8,3,128,128]{3,2,1,0:T(8,128)(2,1)}), bf16[8,3,128,128]{3,2,1,0:T(8,128)(2,1)S(1)}, u32[]{:S(2)}, u32[]{:S(2)}) async-start(bf16[8,3,128,128]{3,2,1,0:T(8,128)(2,1)} %shard_map.86), calls=%async_computation.2 | async-start | bytes 1572864 | tf_op jit(solution)/shard_map/all_to_all | solution.py:240
  138.5 4.2 %copy-start.4 = (bf16[8,3,128,128]{3,2,1,0:T(8,128)(2,1)}, bf16[8,3,128,128]{3,2,1,0:T(8,128)(2,1)S(1)}, u32[]{:S(2)}) copy-start(bf16[8,3,128,128]{3,2,1,0:T(8,128)(2,1)S(1)} %all-to-all-done.2.refs_0_) | copy-start | bytes 2359300
  138.5 16.8 %all-to-all-start.1 = ((bf16[8,3,128,128]{3,2,1,0:T(8,128)(2,1)}), bf16[8,3,128,128]{3,2,1,0:T(8,128)(2,1)S(1)}, u32[]{:S(2)}, u32[]{:S(2)}) async-start(bf16[8,3,128,128]{3,2,1,0:T(8,128)(2,1)} %shard_map.85), calls=%async_computation.1 | async-start | bytes 1572864 | tf_op jit(solution)/shard_map/all_to_all | solution.py:240
  155.3 0.9 copy-start.5

commit v15 on v14

--- a/solution.py
+++ b/solution.py
@@ -191,7 +191,10 @@
             for s in range(1, dp)
         ]
         order = (me - jnp.arange(dp)) % dp
-        head_weight = jnp.take(jnp.stack(got), order, axis=0).reshape(dp * HD, -1)
+        spread = jnp.stack(got)
+        head_weight = jnp.concatenate(
+            [lax.dynamic_index_in_dim(spread, order[c], 0, keepdims=False) for c in range(dp)]
+        )
         j = lax.axis_index("context")
         shifts = list(range(0, ctx, 2))
         mine = jnp.stack([local_cotangent] + [

time: 161 us -> 156 us (0.969)
  between operations: 0.77 us -> 8.71 us
  waiting for transfers between devices: 26.9 us -> 20 us
  local copies, waits for them, and re-layouts: 25.9 us -> 20.5 us
  starting transfers between devices: 31.9 us -> 33.8 us
    ppermute x3, waiting for transfers between devices: 17.9 us -> 11 us  [body(): lax.ppermute(out_weight, 'dp', [(a, (a + s) % dp) for a in range(dp)])]
    gather x1 -> x0, local copies, waits for them, and re-layouts: 3.7 us -> none  [body(): head_weight = jnp.take(jnp.stack(got), order, axis=0).reshape(dp * HD, -1)]
    unnamed x26 -> x22, local copies, waits for them, and re-layouts: 17.1 us -> 14.6 us
    all_to_all x4, starting transfers between devices: 16.5 us -> 18.5 us  [body(): lax.all_to_all(grads, 'context', split_axis=0, concat_axis=0, tiled=True)]
  transfers between devices with their start and end apart: 12 -> 12, of which waited for: 3 -> 3; matrix products, arithmetic and copies ran while one was open for 22% -> 18% of each run, Pallas kernels for 28% -> 28%
where the time goes in v15:
time: 156 us; the launch traced here: 155 us
  Pallas kernels  59.7 us (38%)
  starting transfers between devices  33.8 us (22%)
  local copies, waits for them, and re-layouts  20.5 us (13%)
  waiting for transfers between devices  20 us (13%)
  other arithmetic  8.83 us (6%)
  between operations  8.71 us (6%)
  matrix products  3.34 us (2%)
    pallas_call x4, Pallas kernels, attention_grads(): pl.pallas_call(_attention_kernel, out_shape=out, grid_spec=pltpu.Prefetch...  53.6 us
    all_to_all x4, starting transfers between devices, body(): lax.all_to_all(grads, 'context', split_axis=0, concat_axis=0, tiled=True)  18.5 us
    unnamed x22, local copies, waits for them, and re-layouts  14.6 us
    ppermute x3, waiting for transfers between devices, body(): lax.ppermute(out_weight, 'dp', [(a, (a + s) % dp) for a in range(dp)])  11 us
    all_to_all x4, waiting for transfers between devices, body(): lax.all_to_all(grads, 'context', split_axis=0, concat_axis=0, tiled=True)  8.96 us
    ppermute x3, starting transfers between devices, body(): lax.ppermute(local_cotangent, 'context', [(a, (a + s) % ctx) for a in ran...  5.94 us
    ppermute x3, starting transfers between devices, body(): lax.ppermute(out_weight, 'dp', [(a, (a + s) % dp) for a in range(dp)])  5.51 us
    all_to_all x1, starting transfers between devices, body(): lax.all_to_all(stacked, 'context', split_axis=0, concat_axis=0, tiled=True)  3.65 us
  transfers between devices with their start and end apart: 12, of which 3 were waited for; matrix products, arithmetic and copies ran while one was open for 18% of the time, Pallas kernels for 28%

profile of v15, /device:TPU:0, one launch (start us, length us, event | category | flops | bytes accessed | tf_op | source)
XLA Modules:
  0.0 154.9 jit_solution(12128534822372345207)
XLA Ops:
  0.6 3.0 %collective-permute-start = (bf16[128,2048]{1,0:T(8,128)(2,1)}, bf16[128,2048]{1,0:T(8,128)(2,1)}, u32[]{:S(2)}, u32[]{:S(2)}) collective-permute-start(bf16[128,2048]{1,0:T(8,128)(2,1)} %bitcast.43), channel_id=1, source_target_pairs={{0,2},{1,3},{2,4},{3,5},{4,6},{5,7},{6,0},{7,1},{8,10},{9,11},{10,... | collective-permute-start | bytes 1572872 | tf_op jit(solution)/shard_map/ppermute | solution.py:201
  3.6 1.6 %collective-permute-start.4 = (bf16[128,2048]{1,0:T(8,128)(2,1)}, bf16[128,2048]{1,0:T(8,128)(2,1)}, u32[]{:S(2)}, u32[]{:S(2)}) collective-permute-start(bf16[128,2048]{1,0:T(8,128)(2,1)} %param.10), channel_id=1, source_target_pairs={{0,8},{8,16},{16,24},{24,0},{1,9},{9,17},{17,25},{25,1},{2,10},{10... | collective-permute-start | bytes 1572872 | tf_op jit(solution)/shard_map/ppermute | solution.py:190
  5.2 2.6 %collective-permute-start.5 = (bf16[128,2048]{1,0:T(8,128)(2,1)}, bf16[128,2048]{1,0:T(8,128)(2,1)}, u32[]{:S(2)}, u32[]{:S(2)}) collective-permute-start(bf16[128,2048]{1,0:T(8,128)(2,1)} %param.10), channel_id=1, source_target_pairs={{0,16},{8,24},{16,0},{24,8},{1,17},{9,25},{17,1},{25,9},{2,18},{10... | collective-permute-start | bytes 1572872 | tf_op jit(solution)/shard_map/ppermute | solution.py:190
  7.8 1.5 collective-permute-start.1
  9.3 1.4 collective-permute-start.2
  10.7 1.6 %copy.14 = bf16[1,128,4096]{1,2,0:T(8,128)(2,1)S(1)} copy(bf16[1,128,4096]{2,1,0:T(8,128)(2,1)} %param.6) | data formatting | bytes 2097152 | tf_op args[0]
  12.4 0.7 copy.15
  13.0 1.6 %copy.16 = bf16[1,128,4096]{1,2,0:T(8,128)(2,1)S(1)} copy(bf16[1,128,4096]{2,1,0:T(8,128)(2,1)} %param.7) | data formatting | bytes 2097152 | tf_op args[1]
  14.7 0.7 copy.17
  15.3 1.6 %copy.18 = bf16[1,128,4096]{1,2,0:T(8,128)(2,1)S(1)} copy(bf16[1,128,4096]{2,1,0:T(8,128)(2,1)} %param.8) | data formatting | bytes 2097152 | tf_op args[2]
  17.0 1.3 copy.19
  18.3 3.2 %pad_maximum_fusion = bf16[8,3,4,128,128]{4,3,2,1,0:T(8,128)(2,1)} fusion(bf16[8,1,4,128,128]{4,3,2,1,0:T(8,128)(2,1)} %bitcast.42, bf16[8,1,4,128,128]{4,3,2,1,0:T(8,128)(2,1)S(1)} %bitcast.41, bf16[8,1,4,128,128]{4,3,2,1,0:T(8,128)(2,1)S(1)} %bitcast.40), kind=kLoop, calls=%fused_computation | loop fusion | flops 3145728 | bytes 6291456 | tf_op jit(solution)/shard_map/stack | solution.py:232
  21.5 3.6 %all-to-all-start = ((bf16[8,3,4,128,128]{4,3,2,1,0:T(8,128)(2,1)}), bf16[8,3,4,128,128]{4,3,2,1,0:T(8,128)(2,1)S(1)}, u32[]{:S(2)}, u32[]{:S(2)}) async-start(bf16[8,3,4,128,128]{4,3,2,1,0:T(8,128)(2,1)} %pad_maximum_fusion), calls=%async_computation | async-start | bytes 6291456 | tf_op jit(solution)/shard_map/all_to_all | solution.py:233
  25.2 0.0 copy-start.6
  25.2 1.9 %constant_dynamic-update-slice_fusion.4 = bf16[8,128,2048]{2,1,0:T(8,128)(2,1)} fusion(bf16[1,128,2048]{2,1,0:T(8,128)(2,1)} %param.9), kind=kLoop, calls=%fused_computation.20 | loop fusion | bytes 1048576
  27.1 1.3 collective-permute-start.6
  28.4 0.0 collective-permute-done.2
  28.4 3.2 %pad_maximum_fusion.1 = bf16[4,128,2048]{2,1,0:T(8,128)(2,1)} fusion(bf16[1,128,2048]{2,1,0:T(8,128)(2,1)} %bitcast.12, bf16[1,128,2048]{2,1,0:T(8,128)(2,1)} %bitcast.11, bf16[1,128,2048]{2,1,0:T(8,128)(2,1)} %bitcast.10, bf16[1,128,2048]{2,1,0:T(8,128)(2,1)} %param.9), kind=kLoop, calls=%fused_computation.1 | loop fusion | flops 3145728 | bytes 4194304 | tf_op jit(solution)/shard_map/stack | solution.py:200
  31.6 0.1 collective-permute-start.3
  31.8 0.7 fusion.15
  37.7 0.1 copy.13
  37.8 0.6 reshape_squeeze.15.rb_ref
  41.1 0.6 compare_select_fusion.6.pos_ref
  41.7 0.1 collective-permute-done.5
  41.8 11.0 %collective-permute-done.6 = bf16[128,2048]{1,0:T(8,128)(2,1)} collective-permute-done((bf16[128,2048]{1,0:T(8,128)(2,1)}, bf16[128,2048]{1,0:T(8,128)(2,1)}, u32[]{:S(2)}, u32[]{:S(2)}) %collective-permute-start.6) | collective-permute-done | bytes 524320 | tf_op jit(solution)/shard_map/ppermute | solution.py:190
  52.7 1.8 %pad_maximum_fusion.2 = bf16[4,128,2048]{2,1,0:T(8,128)(2,1)S(1)} fusion(bf16[1,128,2048]{2,1,0:T(8,128)(2,1)} %bitcast.17, bf16[1,128,2048]{2,1,0:T(8,128)(2,1)} %bitcast.16, bf16[1,128,2048]{2,1,0:T(8,128)(2,1)} %bitcast.15, bf16[1,128,2048]{2,1,0:T(8,128)(2,1)} %bitcast.46), kind=kLoop, calls=%fused_computation.2 | loop fusion | flops 3145728 | bytes 4194304 | tf_op jit(solution)/shard_map/stack | solution.py:194
  54.5 0.1 dynamic-slice_bitcast_fusion.3
  54.7 2.0 %copy-done.5 = bf16[8,128,2048]{2,1,0:T(8,128)(2,1)S(1)} copy-done((bf16[8,128,2048]{2,1,0:T(8,128)(2,1)S(1)}, bf16[8,128,2048]{2,1,0:T(8,128)(2,1)}, u32[]{:S(2)}) %copy-start.5) | copy-done | bytes 4194328
  56.7 1.1 constant_dynamic-update-slice_fusion.3
  57.8 1.1 constant_dynamic-update-slice_fusion.2
  58.9 1.1 constant_dynamic-update-slice_fusion.1
  60.0 0.0 collective-permute-done.3
  60.0 1.8 %constant_dynamic-update-slice_fusion = bf16[8,128,2048]{2,1,0:T(8,128)(2,1)S(1)} fusion(bf16[8,128,2048]{2,1,0:T(8,128)(2,1)S(1)} %constant_dynamic-update-slice_fusion.1, bf16[4,128,2048]{2,1,0:T(8,128)(2,1)} %collective-permute-done.3), kind=kLoop, calls=%fused_computation.16 | loop fusion | bytes 4194304 | tf_op jit(solution)/shard_map/concatenate | solution.py:205
  61.8 3.3 %fusion.8.u_ref = bf16[1024,512]{1,0:T(8,128)(2,1)} fusion(bf16[1024,2048]{1,0:T(8,128)(2,1)S(1)} %bitcast.47, bf16[128,2048]{1,0:T(8,128)(2,1)S(1)} %get-tuple-element.10, bf16[128,2048]{1,0:T(8,128)(2,1)S(1)} %get-tuple-element.11, bf16[128,2048]{1,0:T(8,128)(2,1)S(1)} %get-tuple-element.12, bf16[128,2048]{1,0:T(8,128)(2,1)S(1)} %get-tuple-element.9), kind=kOutput, calls=%fused_computation.11 | convolution fusion | flops 2156396544 | bytes 7340032 | tf_op jit(solution)/shard_map/dot_general | solution.py:206
  65.2 1.6 %copy-done = bf16[8,3,4,128,128]{4,3,2,1,0:T(8,128)(2,1)} copy-done((bf16[8,3,4,128,128]{4,3,2,1,0:T(8,128)(2,1)}, bf16[8,3,4,128,128]{4,3,2,1,0:T(8,128)(2,1)S(1)}, u32[]{:S(2)}) %copy-start) | copy-done | bytes 3145752
  66.8 13.4 %shard_map.88 = bf16[8,3,128,128]{3,2,1,0:T(8,128)(2,1)} custom-call(s32[42]{0:T(128)} %reshape_squeeze.15.rb_ref, s32[8]{0:T(128)} %compare_select_fusion.6.pos_ref, bf16[8,3,4,128,128]{4,3,2,1,0:T(8,128)(2,1)} %copy-done, bf16[1024,512]{1,0:T(8,128)(2,1)} %fusion.8.u_ref), custom_call_target="tpu_custom_call" | custom-call | flops 905969664 | bytes 1835008 | tf_op jit(solution)/shard_map/pallas_call | solution.py:115
  80.2 5.9 %all-to-all-start.4 = ((bf16[8,3,128,128]{3,2,1,0:T(8,128)(2,1)}), bf16[8,3,128,128]{3,2,1,0:T(8,128)(2,1)S(1)}, u32[]{:S(2)}, u32[]{:S(2)}) async-start(bf16[8,3,128,128]{3,2,1,0:T(8,128)(2,1)} %shard_map.88), calls=%async_computation.4 | async-start | bytes 1572864 | tf_op jit(solution)/shard_map/all_to_all | solution.py:243
  86.1 13.4 %shard_map.87 = bf16[8,3,128,128]{3,2,1,0:T(8,128)(2,1)} custom-call(s32[42]{0:T(128)} %reshape_squeeze.15.rb_ref, s32[8]{0:T(128)} %compare_select_fusion.6.pos_ref, bf16[8,3,4,128,128]{4,3,2,1,0:T(8,128)(2,1)} %copy-done, bf16[1024,512]{1,0:T(8,128)(2,1)} %fusion.8.u_ref), custom_call_target="tpu_custom_call" | custom-call | flops 905969664 | bytes 1835008 | tf_op jit(solution)/shard_map/pallas_call | solution.py:115
  99.5 4.2 %all-to-all-start.3 = ((bf16[8,3,128,128]{3,2,1,0:T(8,128)(2,1)}), bf16[8,3,128,128]{3,2,1,0:T(8,128)(2,1)S(1)}, u32[]{:S(2)}, u32[]{:S(2)}) async-start(bf16[8,3,128,128]{3,2,1,0:T(8,128)(2,1)} %shard_map.87), calls=%async_computation.3 | async-start | bytes 1572864 | tf_op jit(solution)/shard_map/all_to_all | solution.py:243
  103.7 13.4 %shard_map.86 = bf16[8,3,128,128]{3,2,1,0:T(8,128)(2,1)} custom-call(s32[42]{0:T(128)} %reshape_squeeze.15.rb_ref, s32[8]{0:T(128)} %compare_select_fusion.6.pos_ref, bf16[8,3,4,128,128]{4,3,2,1,0:T(8,128)(2,1)} %copy-done, bf16[1024,512]{1,0:T(8,128)(2,1)} %fusion.8.u_ref), custom_call_target="tpu_custom_call" | custom-call | flops 905969664 | bytes 1835008 | tf_op jit(solution)/shard_map/pallas_call | solution.py:115
  117.1 0.0 all-to-all-done.3.refs_1_
  117.1 4.2 %all-to-all-start.2 = ((bf16[8,3,128,128]{3,2,1,0:T(8,128)(2,1)}), bf16[8,3,128,128]{3,2,1,0:T(8,128)(2,1)S(1)}, u32[]{:S(2)}, u32[]{:S(2)}) async-start(bf16[8,3,128,128]{3,2,1,0:T(8,128)(2,1)} %shard_map.86), calls=%async_computation.2 | async-start | bytes 1572864 | tf_op jit(solution)/shard_map/all_to_all | solution.py:243
  121.3 13.4 %shard_map.85 = bf16[8,3,128,128]{3,2,1,0:T(8,128)(2,1)} custom-call(s32[42]{0:T(128)} %reshape_squeeze.15.rb_ref, s32[8]{0:T(128)} %compare_select_fusion.6.pos_ref, bf16[8,3,4,128,128]{4,3,2,1,0:T(8,128)(2,1)} %copy-done, bf16[1024,512]{1,0:T(8,128)(2,1)} %fusion.8.u_ref), custom_call_target="tpu_custom_call" | custom-call | flops 905969664 | bytes 1835008 | tf_op jit(solution)/shard_map/pallas_call | solution.py:115
  134.8 4.2 %all-to-all-start.1 = ((bf16[8,3,128,128]{3,2,1,0:T(8,128)(2,1)}), bf16[8,3,128,128]{3,2,1,0:T(8,128)(2,1)S(1)}, u32[]{:S(2)}, u32[]{:S(2)}) async-start(bf16[8,3,128,128]{3,2,1,0:T(8,128)(2,1)} %shard_map.85), calls=%async_computation.1 | async-start | bytes 1572864 | tf_op jit(solution)/shard_map/all_to_all | solution.py:243
  139.0 3.6 %shard_map.89 = (bf16[1,128,4096]{2,1,0:T(8,128)(2,1)}, bf16[1,128,4096]{2,1,0:T(8,128)(2,1)}, bf16[1,128,4096]{2,1,0:T(8,128)(2,1)}) custom-call(bf16[8,3,128,128]{3,2,1,0:T(8,128)(2,1)} %copy-done.3, bf16[8,3,128,128]{3,2,1,0:T(8,128)(2,1)} %copy-done.2, bf16[8,3,128,128]{3,2,1,0:T(8,128)(2,1)} %copy-done.1), custom_call_target="tpu_custom_call" | custom-call | tf_op jit(solution)/shard_map/pallas_call | solution.py:151
  142.6 9.0 %all-to-all-done.1.piece = bf16[8,3,128,128]{3,2,1,0:T(8,128)(2,1)S(1)} async-done(((bf16[8,3,128,128]{3,2,1,0:T(8,128)(2,1)}), bf16[8,3,128,128]{3,2,1,0:T(8,128)(2,1)S(1)}, u32[]{:S(2)}, u32[]{:S(2)}) %all-to-all-start.1) | async-done | bytes 786464 | tf_op jit(solution)/shard_map/all_to_all | solution.py:243
  151.6 0.9 copy-done.4
  152.5 2.4 %shard_map.90 = (bf16[1,128,4096]{2,1,0:T(8,128)(2,1)}, bf16[1,128,4096]{2,1,0:T(8,128)(2,1)}, bf16[1,128,4096]{2,1,0:T(8,128)(2,1)}) custom-call(bf16[8,3,128,128]{3,2,1,0:T(8,128)(2,1)} %copy-done.4, bf16[1,128,4096]{2,1,0:T(8,128)(2,1)} %get-tuple-element.6._first, ...), custom_call_target="tpu_custom_call", output_to_operand_aliasing={{0}: (1, {}), {1}: (2, {}), {2}: (3, {})} | custom-call | tf_op jit(solution)/shard_map/pallas_call | solution.py:159
  (17 shorter events, 0.0 us)
Async XLA Ops:
  0.6 26.4 %collective-permute-start = (bf16[128,2048]{1,0:T(8,128)(2,1)}, bf16[128,2048]{1,0:T(8,128)(2,1)}, u32[]{:S(2)}, u32[]{:S(2)}) collective-permute-start(bf16[128,2048]{1,0:T(8,128)(2,1)} %bitcast.43), channel_id=1, source_target_pairs={{0,2},{1,3},{2,4},{3,5},{4,6},{5,7},{6,0},{7,1},{8,10},{9,11},{10,... | collective-permute-start | bytes 1572872 | tf_op jit(solution)/shard_map/ppermute | solution.py:201
  3.6 38.1 %collective-permute-start.4 = (bf16[128,2048]{1,0:T(8,128)(2,1)}, bf16[128,2048]{1,0:T(8,128)(2,1)}, u32[]{:S(2)}, u32[]{:S(2)}) collective-permute-start(bf16[128,2048]{1,0:T(8,128)(2,1)} %param.10), channel_id=1, source_target_pairs={{0,8},{8,16},{16,24},{24,0},{1,9},{9,17},{17,25},{25,1},{2,10},{10... | collective-permute-start | bytes 1572872 | tf_op jit(solution)/shard_map/ppermute | solution.py:190
  5.2 36.6 %collective-permute-start.5 = (bf16[128,2048]{1,0:T(8,128)(2,1)}, bf16[128,2048]{1,0:T(8,128)(2,1)}, u32[]{:S(2)}, u32[]{:S(2)}) collective-permute-start(bf16[128,2048]{1,0:T(8,128)(2,1)} %param.10), channel_id=1, source_target_pairs={{0,16},{8,24},{16,0},{24,8},{1,17},{9,25},{17,1},{25,9},{2,18},{10... | collective-permute-start | bytes 1572872 | tf_op jit(solution)/shard_map/ppermute | solution.py:190
  7.8 20.6 %collective-permute-start.1 = (bf16[128,2048]{1,0:T(8,128)(2,1)}, bf16[128,2048]{1,0:T(8,128)(2,1)}, u32[]{:S(2)}, u32[]{:S(2)}) collective-permute-start(bf16[128,2048]{1,0:T(8,128)(2,1)} %bitcast.44), channel_id=1, source_target_pairs={{0,4},{1,5},{2,6},{3,7},{4,0},{5,1},{6,2},{7,3},{8,12},{9,13},{10,... | collective-permute-start | bytes 1572872 | tf_op jit(solution)/shard_map/ppermute | solution.py:201
  9.3 19.1 %collective-permute-start.2 = (bf16[128,2048]{1,0:T(8,128)(2,1)}, bf16[128,2048]{1,0:T(8,128)(2,1)}, u32[]{:S(2)}, u32[]{:S(2)}) collective-permute-start(bf16[128,2048]{1,0:T(8,128)(2,1)} %bitcast.45), channel_id=1, source_target_pairs={{0,6},{1,7},{2,0},{3,1},{4,2},{5,3},{6,4},{7,5},{8,14},{9,15},{10,... | collective-permute-start | bytes 1572872 | tf_op jit(solution)/shard_map/ppermute | solution.py:201
  21.5 43.7 %all-to-all-start = ((bf16[8,3,4,128,128]{4,3,2,1,0:T(8,128)(2,1)}), bf16[8,3,4,128,128]{4,3,2,1,0:T(8,128)(2,1)S(1)}, u32[]{:S(2)}, u32[]{:S(2)}) async-start(bf16[8,3,4,128,128]{4,3,2,1,0:T(8,128)(2,1)} %pad_maximum_fusion), calls=%async_computation | async-start | bytes 6291456 | tf_op jit(solution)/shard_map/all_to_all | solution.py:233
  25.2 12.6 %copy-start.6 = (s32[1,14,3]{1,0,2:T(1,128)S(1)}, s32[1,14,3]{1,0,2:T(1,128)}, u32[]{:S(2)}) copy-start(s32[1,14,3]{1,0,2:T(1,128)} %param.11) | copy-start | bytes 508
  27.1 25.7 %collective-permute-start.6 = (bf16[128,2048]{1,0:T(8,128)(2,1)}, bf16[128,2048]{1,0:T(8,128)(2,1)}, u32[]{:S(2)}, u32[]{:S(2)}) collective-permute-start(bf16[128,2048]{1,0:T(8,128)(2,1)} %param.10), channel_id=1, source_target_pairs={{0,24},{8,0},{16,8},{24,16},{1,25},{9,1},{17,9},{25,17},{2,26},{10... | collective-permute-start | bytes 1572872 | tf_op jit(solution)/shard_map/ppermute | solution.py:190
  31.6 28.4 %collective-permute-start.3 = (bf16[4,128,2048]{2,1,0:T(8,128)(2,1)}, bf16[4,128,2048]{2,1,0:T(8,128)(2,1)}, u32[]{:S(2)}, u32[]{:S(2)}) collective-permute-start(bf16[4,128,2048]{2,1,0:T(8,128)(2,1)} %pad_maximum_fusion.1), channel_id=1, source_target_pairs={{0,1},{1,0},{2,3},{3,2},{4,5},{5,4},{6,7},{7,6},{8,9},{9,8},{10,11... | collective-permute-start | bytes 6291464 | tf_op jit(solution)/shard_map/ppermute | solution.py:204
  54.5 2.2 %copy-start.5 = (bf16[8,128,2048]{2,1,0:T(8,128)(2,1)S(1)}, bf16[8,128,2048]{2,1,0:T(8,128)(2,1)}, u32[]{:S(2)}) copy-start(bf16[8,128,2048]{2,1,0:T(8,128)(2,1)} %constant_dynamic-update-slice_fusion.4) | copy-start | bytes 12582916
  65.2 1.6 %copy-start = (bf16[8,3,4,128,128]{4,3,2,1,0:T(8,128)(2,1)}, bf16[8,3,4,128,128]{4,3,2,1,0:T(8,128)(2,1)S(1)}, u32[]{:S(2)}) copy-start(bf16[8,3,4,128,128]{4,3,2,1,0:T(8,128)(2,1)S(1)} %all-to-all-done.x_ref) | copy-start | bytes 9437188
  80.2 19.3 %all-to-all-start.4 = ((bf16[8,3,128,128]{3,2,1,0:T(8,128)(2,1)}), bf16[8,3,128,128]{3,2,1,0:T(8,128)(2,1)S(1)}, u32[]{:S(2)}, u32[]{:S(2)}) async-start(bf16[8,3,128,128]{3,2,1,0:T(8,128)(2,1)} %shard_map.88), calls=%async_computation.4 | async-start | bytes 1572864 | tf_op jit(solution)/shard_map/all_to_all | solution.py:243
  99.5 17.6 %copy-start.1 = (bf16[8,3,128,128]{3,2,1,0:T(8,128)(2,1)}, bf16[8,3,128,128]{3,2,1,0:T(8,128)(2,1)S(1)}, u32[]{:S(2)}) copy-start(bf16[8,3,128,128]{3,2,1,0:T(8,128)(2,1)S(1)} %all-to-all-done.4.refs_2_) | copy-start | bytes 2359300
  99.5 17.6 %all-to-all-start.3 = ((bf16[8,3,128,128]{3,2,1,0:T(8,128)(2,1)}), bf16[8,3,128,128]{3,2,1,0:T(8,128)(2,1)S(1)}, u32[]{:S(2)}, u32[]{:S(2)}) async-start(bf16[8,3,128,128]{3,2,1,0:T(8,128)(2,1)} %shard_map.87), calls=%async_computation.3 | async-start | bytes 1572864 | tf_op jit(solution)/shard_map/all_to_all | solution.py:243
  117.1 17.6 %copy-start.2 = (bf16[8,3,128,128]{3,2,1,0:T(8,128)(2,1)}, bf16[8,3,128,128]{3,2,1,0:T(8,128)(2,1)S(1)}, u32[]{:S(2)}) copy-start(bf16[8,3,128,128]{3,2,1,0:T(8,128)(2,1)S(1)} %all-to-all-done.3.refs_1_) | copy-start | bytes 2359300
  117.1 17.6 %all-to-all-start.2 = ((bf16[8,3,128,128]{3,2,1,0:T(8,128)(2,1)}), bf16[8,3,128,128]{3,2,1,0:T(8,128)(2,1)S(1)}, u32[]{:S(2)}, u32[]{:S(2)}) async-start(bf16[8,3,128,128]{3,2,1,0:T(8,128)(2,1)} %shard_map.86), calls=%async_computation.2 | async-start | bytes 1572864 | tf_op jit(solution)/shard_map/all_to_all | solution.py:243
  134.8 4.2 %copy-start.3 = (bf16[8,3,128,128]{3,2,1,0:T(8,128)(2,1)}, bf16[8,3,128,128]{3,2,1,0:T(8,128)(2,1)S(1)}, u32[]{:S(2)}) copy-start(bf16[8,3,128,128]{3,2,1,0:T(8,128)(2,1)S(1)} %all-to-all-done.2.refs_0_) | copy-start | bytes 2359300
  134.8 16.8 %all-to-all-start.1 = ((bf16[8,3,128,128]{3,2,1,0:T(8,128)(2,1)}), bf16[8,3,128,128]{3,2,1,0:T(8,128)(2,1)S(1)}, u32[]{:S(2)}, u32[]{:S(2)}) async-start(bf16[8,3,128,128]{3,2,1,0:T(8,128)(2,1)} %shard_map.85), calls=%async_computation.1 | async-start | bytes 1572864 | tf_op jit(solution)/shard_map/all_to_all | solution.py:243
  151.6 0.9 copy-start.4

commit v16 on v15

--- a/solution.py
+++ b/solution.py
@@ -95,7 +95,7 @@
             dv_acc[pl.ds(row, BLOCK), :] += value_grad[slot * BLOCK:(slot + 1) * BLOCK, :]
         return carry
 
-    lax.fori_loop(1, count - 1, mid_step, 0, unroll=7)
+    lax.fori_loop(1, count - 1, mid_step, 0, unroll=14)
     o_ref[:, 1, :, :] = dk_acc[...].reshape(parts, tokens, HD).astype(jnp.bfloat16)
     o_ref[:, 2, :, :] = dv_acc[...].reshape(parts, tokens, HD).astype(jnp.bfloat16)
 

time: 156 us -> 154 us (0.987)
  Pallas kernels: 59.7 us -> 58.1 us
    pallas_call x4, Pallas kernels: 53.6 us -> 52 us  [attention_grads(): pl.pallas_call(_attention_kernel, out_shape=out, grid_spec=pltpu.Prefetch...]
where the time goes in v16:
time: 154 us; the launch traced here: 153 us
  Pallas kernels  58.1 us (38%)
  starting transfers between devices  33.8 us (22%)
  local copies, waits for them, and re-layouts  20.5 us (13%)
  waiting for transfers between devices  20 us (13%)
  other arithmetic  8.83 us (6%)
  between operations  8.71 us (6%)
  matrix products  3.34 us (2%)
    pallas_call x4, Pallas kernels, attention_grads(): pl.pallas_call(_attention_kernel, out_shape=out, grid_spec=pltpu.Prefetch...  52 us
    all_to_all x4, starting transfers between devices, body(): lax.all_to_all(grads, 'context', split_axis=0, concat_axis=0, tiled=True)  18.5 us
    unnamed x22, local copies, waits for them, and re-layouts  14.6 us
    ppermute x3, waiting for transfers between devices, body(): lax.ppermute(out_weight, 'dp', [(a, (a + s) % dp) for a in range(dp)])  11 us
    all_to_all x4, waiting for transfers between devices, body(): lax.all_to_all(grads, 'context', split_axis=0, concat_axis=0, tiled=True)  8.96 us
    ppermute x3, starting transfers between devices, body(): lax.ppermute(local_cotangent, 'context', [(a, (a + s) % ctx) for a in ran...  5.94 us
    ppermute x3, starting transfers between devices, body(): lax.ppermute(out_weight, 'dp', [(a, (a + s) % dp) for a in range(dp)])  5.51 us
    all_to_all x1, starting transfers between devices, body(): lax.all_to_all(stacked, 'context', split_axis=0, concat_axis=0, tiled=True)  3.65 us
  transfers between devices with their start and end apart: 12, of which 3 were waited for; matrix products, arithmetic and copies ran while one was open for 18% of the time, Pallas kernels for 28%

profile of v16, /device:TPU:0, one launch (start us, length us, event | category | flops | bytes accessed | tf_op | source)
XLA Modules:
  0.0 153.3 jit_solution(3530558090992028517)
XLA Ops:
  0.6 3.0 %collective-permute-start = (bf16[128,2048]{1,0:T(8,128)(2,1)}, bf16[128,2048]{1,0:T(8,128)(2,1)}, u32[]{:S(2)}, u32[]{:S(2)}) collective-permute-start(bf16[128,2048]{1,0:T(8,128)(2,1)} %bitcast.43), channel_id=1, source_target_pairs={{0,2},{1,3},{2,4},{3,5},{4,6},{5,7},{6,0},{7,1},{8,10},{9,11},{10,... | collective-permute-start | bytes 1572872 | tf_op jit(solution)/shard_map/ppermute | solution.py:201
  3.6 1.6 %collective-permute-start.4 = (bf16[128,2048]{1,0:T(8,128)(2,1)}, bf16[128,2048]{1,0:T(8,128)(2,1)}, u32[]{:S(2)}, u32[]{:S(2)}) collective-permute-start(bf16[128,2048]{1,0:T(8,128)(2,1)} %param.10), channel_id=1, source_target_pairs={{0,8},{8,16},{16,24},{24,0},{1,9},{9,17},{17,25},{25,1},{2,10},{10... | collective-permute-start | bytes 1572872 | tf_op jit(solution)/shard_map/ppermute | solution.py:190
  5.2 2.6 %collective-permute-start.5 = (bf16[128,2048]{1,0:T(8,128)(2,1)}, bf16[128,2048]{1,0:T(8,128)(2,1)}, u32[]{:S(2)}, u32[]{:S(2)}) collective-permute-start(bf16[128,2048]{1,0:T(8,128)(2,1)} %param.10), channel_id=1, source_target_pairs={{0,16},{8,24},{16,0},{24,8},{1,17},{9,25},{17,1},{25,9},{2,18},{10... | collective-permute-start | bytes 1572872 | tf_op jit(solution)/shard_map/ppermute | solution.py:190
  7.8 1.5 collective-permute-start.1
  9.3 1.4 collective-permute-start.2
  10.7 1.6 %copy.14 = bf16[1,128,4096]{1,2,0:T(8,128)(2,1)S(1)} copy(bf16[1,128,4096]{2,1,0:T(8,128)(2,1)} %param.6) | data formatting | bytes 2097152 | tf_op args[0]
  12.4 0.7 copy.15
  13.0 1.6 %copy.16 = bf16[1,128,4096]{1,2,0:T(8,128)(2,1)S(1)} copy(bf16[1,128,4096]{2,1,0:T(8,128)(2,1)} %param.7) | data formatting | bytes 2097152 | tf_op args[1]
  14.7 0.7 copy.17
  15.3 1.6 %copy.18 = bf16[1,128,4096]{1,2,0:T(8,128)(2,1)S(1)} copy(bf16[1,128,4096]{2,1,0:T(8,128)(2,1)} %param.8) | data formatting | bytes 2097152 | tf_op args[2]
  17.0 1.3 copy.19
  18.3 3.2 %pad_maximum_fusion = bf16[8,3,4,128,128]{4,3,2,1,0:T(8,128)(2,1)} fusion(bf16[8,1,4,128,128]{4,3,2,1,0:T(8,128)(2,1)} %bitcast.42, bf16[8,1,4,128,128]{4,3,2,1,0:T(8,128)(2,1)S(1)} %bitcast.41, bf16[8,1,4,128,128]{4,3,2,1,0:T(8,128)(2,1)S(1)} %bitcast.40), kind=kLoop, calls=%fused_computation | loop fusion | flops 3145728 | bytes 6291456 | tf_op jit(solution)/shard_map/stack | solution.py:232
  21.5 3.6 %all-to-all-start = ((bf16[8,3,4,128,128]{4,3,2,1,0:T(8,128)(2,1)}), bf16[8,3,4,128,128]{4,3,2,1,0:T(8,128)(2,1)S(1)}, u32[]{:S(2)}, u32[]{:S(2)}) async-start(bf16[8,3,4,128,128]{4,3,2,1,0:T(8,128)(2,1)} %pad_maximum_fusion), calls=%async_computation | async-start | bytes 6291456 | tf_op jit(solution)/shard_map/all_to_all | solution.py:233
  25.2 0.0 copy-start.6
  25.2 1.9 %constant_dynamic-update-slice_fusion.4 = bf16[8,128,2048]{2,1,0:T(8,128)(2,1)} fusion(bf16[1,128,2048]{2,1,0:T(8,128)(2,1)} %param.9), kind=kLoop, calls=%fused_computation.20 | loop fusion | bytes 1048576
  27.1 1.3 collective-permute-start.6
  28.4 0.0 collective-permute-done.2
  28.4 3.2 %pad_maximum_fusion.1 = bf16[4,128,2048]{2,1,0:T(8,128)(2,1)} fusion(bf16[1,128,2048]{2,1,0:T(8,128)(2,1)} %bitcast.12, bf16[1,128,2048]{2,1,0:T(8,128)(2,1)} %bitcast.11, bf16[1,128,2048]{2,1,0:T(8,128)(2,1)} %bitcast.10, bf16[1,128,2048]{2,1,0:T(8,128)(2,1)} %param.9), kind=kLoop, calls=%fused_computation.1 | loop fusion | flops 3145728 | bytes 4194304 | tf_op jit(solution)/shard_map/stack | solution.py:200
  31.6 0.1 collective-permute-start.3
  31.8 0.7 fusion.15
  37.7 0.1 copy.13
  37.8 0.6 reshape_squeeze.15.rb_ref
  41.1 0.6 compare_select_fusion.6.pos_ref
  41.7 0.1 collective-permute-done.5
  41.8 11.0 %collective-permute-done.6 = bf16[128,2048]{1,0:T(8,128)(2,1)} collective-permute-done((bf16[128,2048]{1,0:T(8,128)(2,1)}, bf16[128,2048]{1,0:T(8,128)(2,1)}, u32[]{:S(2)}, u32[]{:S(2)}) %collective-permute-start.6) | collective-permute-done | bytes 524320 | tf_op jit(solution)/shard_map/ppermute | solution.py:190
  52.7 1.8 %pad_maximum_fusion.2 = bf16[4,128,2048]{2,1,0:T(8,128)(2,1)S(1)} fusion(bf16[1,128,2048]{2,1,0:T(8,128)(2,1)} %bitcast.17, bf16[1,128,2048]{2,1,0:T(8,128)(2,1)} %bitcast.16, bf16[1,128,2048]{2,1,0:T(8,128)(2,1)} %bitcast.15, bf16[1,128,2048]{2,1,0:T(8,128)(2,1)} %bitcast.46), kind=kLoop, calls=%fused_computation.2 | loop fusion | flops 3145728 | bytes 4194304 | tf_op jit(solution)/shard_map/stack | solution.py:194
  54.5 0.1 dynamic-slice_bitcast_fusion.3
  54.7 2.0 %copy-done.5 = bf16[8,128,2048]{2,1,0:T(8,128)(2,1)S(1)} copy-done((bf16[8,128,2048]{2,1,0:T(8,128)(2,1)S(1)}, bf16[8,128,2048]{2,1,0:T(8,128)(2,1)}, u32[]{:S(2)}) %copy-start.5) | copy-done | bytes 4194328
  56.7 1.1 constant_dynamic-update-slice_fusion.3
  57.8 1.1 constant_dynamic-update-slice_fusion.2
  58.9 1.1 constant_dynamic-update-slice_fusion.1
  60.0 0.0 collective-permute-done.3
  60.0 1.8 %constant_dynamic-update-slice_fusion = bf16[8,128,2048]{2,1,0:T(8,128)(2,1)S(1)} fusion(bf16[8,128,2048]{2,1,0:T(8,128)(2,1)S(1)} %constant_dynamic-update-slice_fusion.1, bf16[4,128,2048]{2,1,0:T(8,128)(2,1)} %collective-permute-done.3), kind=kLoop, calls=%fused_computation.16 | loop fusion | bytes 4194304 | tf_op jit(solution)/shard_map/concatenate | solution.py:205
  61.8 3.3 %fusion.8.u_ref = bf16[1024,512]{1,0:T(8,128)(2,1)} fusion(bf16[1024,2048]{1,0:T(8,128)(2,1)S(1)} %bitcast.47, bf16[128,2048]{1,0:T(8,128)(2,1)S(1)} %get-tuple-element.10, bf16[128,2048]{1,0:T(8,128)(2,1)S(1)} %get-tuple-element.11, bf16[128,2048]{1,0:T(8,128)(2,1)S(1)} %get-tuple-element.12, bf16[128,2048]{1,0:T(8,128)(2,1)S(1)} %get-tuple-element.9), kind=kOutput, calls=%fused_computation.11 | convolution fusion | flops 2156396544 | bytes 7340032 | tf_op jit(solution)/shard_map/dot_general | solution.py:206
  65.2 1.6 %copy-done = bf16[8,3,4,128,128]{4,3,2,1,0:T(8,128)(2,1)} copy-done((bf16[8,3,4,128,128]{4,3,2,1,0:T(8,128)(2,1)}, bf16[8,3,4,128,128]{4,3,2,1,0:T(8,128)(2,1)S(1)}, u32[]{:S(2)}) %copy-start) | copy-done | bytes 3145752
  66.8 13.0 %shard_map.88 = bf16[8,3,128,128]{3,2,1,0:T(8,128)(2,1)} custom-call(s32[42]{0:T(128)} %reshape_squeeze.15.rb_ref, s32[8]{0:T(128)} %compare_select_fusion.6.pos_ref, bf16[8,3,4,128,128]{4,3,2,1,0:T(8,128)(2,1)} %copy-done, bf16[1024,512]{1,0:T(8,128)(2,1)} %fusion.8.u_ref), custom_call_target="tpu_custom_call" | custom-call | flops 905969664 | bytes 1835008 | tf_op jit(solution)/shard_map/pallas_call | solution.py:115
  79.8 5.9 %all-to-all-start.4 = ((bf16[8,3,128,128]{3,2,1,0:T(8,128)(2,1)}), bf16[8,3,128,128]{3,2,1,0:T(8,128)(2,1)S(1)}, u32[]{:S(2)}, u32[]{:S(2)}) async-start(bf16[8,3,128,128]{3,2,1,0:T(8,128)(2,1)} %shard_map.88), calls=%async_computation.4 | async-start | bytes 1572864 | tf_op jit(solution)/shard_map/all_to_all | solution.py:243
  85.7 13.0 %shard_map.87 = bf16[8,3,128,128]{3,2,1,0:T(8,128)(2,1)} custom-call(s32[42]{0:T(128)} %reshape_squeeze.15.rb_ref, s32[8]{0:T(128)} %compare_select_fusion.6.pos_ref, bf16[8,3,4,128,128]{4,3,2,1,0:T(8,128)(2,1)} %copy-done, bf16[1024,512]{1,0:T(8,128)(2,1)} %fusion.8.u_ref), custom_call_target="tpu_custom_call" | custom-call | flops 905969664 | bytes 1835008 | tf_op jit(solution)/shard_map/pallas_call | solution.py:115
  98.7 4.2 %all-to-all-start.3 = ((bf16[8,3,128,128]{3,2,1,0:T(8,128)(2,1)}), bf16[8,3,128,128]{3,2,1,0:T(8,128)(2,1)S(1)}, u32[]{:S(2)}, u32[]{:S(2)}) async-start(bf16[8,3,128,128]{3,2,1,0:T(8,128)(2,1)} %shard_map.87), calls=%async_computation.3 | async-start | bytes 1572864 | tf_op jit(solution)/shard_map/all_to_all | solution.py:243
  102.9 13.0 %shard_map.86 = bf16[8,3,128,128]{3,2,1,0:T(8,128)(2,1)} custom-call(s32[42]{0:T(128)} %reshape_squeeze.15.rb_ref, s32[8]{0:T(128)} %compare_select_fusion.6.pos_ref, bf16[8,3,4,128,128]{4,3,2,1,0:T(8,128)(2,1)} %copy-done, bf16[1024,512]{1,0:T(8,128)(2,1)} %fusion.8.u_ref), custom_call_target="tpu_custom_call" | custom-call | flops 905969664 | bytes 1835008 | tf_op jit(solution)/shard_map/pallas_call | solution.py:115
  115.9 0.0 all-to-all-done.3.refs_1_
  115.9 4.2 %all-to-all-start.2 = ((bf16[8,3,128,128]{3,2,1,0:T(8,128)(2,1)}), bf16[8,3,128,128]{3,2,1,0:T(8,128)(2,1)S(1)}, u32[]{:S(2)}, u32[]{:S(2)}) async-start(bf16[8,3,128,128]{3,2,1,0:T(8,128)(2,1)} %shard_map.86), calls=%async_computation.2 | async-start | bytes 1572864 | tf_op jit(solution)/shard_map/all_to_all | solution.py:243
  120.1 13.0 %shard_map.85 = bf16[8,3,128,128]{3,2,1,0:T(8,128)(2,1)} custom-call(s32[42]{0:T(128)} %reshape_squeeze.15.rb_ref, s32[8]{0:T(128)} %compare_select_fusion.6.pos_ref, bf16[8,3,4,128,128]{4,3,2,1,0:T(8,128)(2,1)} %copy-done, bf16[1024,512]{1,0:T(8,128)(2,1)} %fusion.8.u_ref), custom_call_target="tpu_custom_call" | custom-call | flops 905969664 | bytes 1835008 | tf_op jit(solution)/shard_map/pallas_call | solution.py:115
  133.2 4.2 %all-to-all-start.1 = ((bf16[8,3,128,128]{3,2,1,0:T(8,128)(2,1)}), bf16[8,3,128,128]{3,2,1,0:T(8,128)(2,1)S(1)}, u32[]{:S(2)}, u32[]{:S(2)}) async-start(bf16[8,3,128,128]{3,2,1,0:T(8,128)(2,1)} %shard_map.85), calls=%async_computation.1 | async-start | bytes 1572864 | tf_op jit(solution)/shard_map/all_to_all | solution.py:243
  137.4 3.6 %shard_map.89 = (bf16[1,128,4096]{2,1,0:T(8,128)(2,1)}, bf16[1,128,4096]{2,1,0:T(8,128)(2,1)}, bf16[1,128,4096]{2,1,0:T(8,128)(2,1)}) custom-call(bf16[8,3,128,128]{3,2,1,0:T(8,128)(2,1)} %copy-done.3, bf16[8,3,128,128]{3,2,1,0:T(8,128)(2,1)} %copy-done.2, bf16[8,3,128,128]{3,2,1,0:T(8,128)(2,1)} %copy-done.1), custom_call_target="tpu_custom_call" | custom-call | tf_op jit(solution)/shard_map/pallas_call | solution.py:151
  141.0 9.0 %all-to-all-done.1.piece = bf16[8,3,128,128]{3,2,1,0:T(8,128)(2,1)S(1)} async-done(((bf16[8,3,128,128]{3,2,1,0:T(8,128)(2,1)}), bf16[8,3,128,128]{3,2,1,0:T(8,128)(2,1)S(1)}, u32[]{:S(2)}, u32[]{:S(2)}) %all-to-all-start.1) | async-done | bytes 786464 | tf_op jit(solution)/shard_map/all_to_all | solution.py:243
  150.0 0.9 copy-done.4
  150.9 2.4 %shard_map.90 = (bf16[1,128,4096]{2,1,0:T(8,128)(2,1)}, bf16[1,128,4096]{2,1,0:T(8,128)(2,1)}, bf16[1,128,4096]{2,1,0:T(8,128)(2,1)}) custom-call(bf16[8,3,128,128]{3,2,1,0:T(8,128)(2,1)} %copy-done.4, bf16[1,128,4096]{2,1,0:T(8,128)(2,1)} %get-tuple-element.6._first, ...), custom_call_target="tpu_custom_call", output_to_operand_aliasing={{0}: (1, {}), {1}: (2, {}), {2}: (3, {})} | custom-call | tf_op jit(solution)/shard_map/pallas_call | solution.py:159
  (17 shorter events, 0.0 us)
Async XLA Ops:
  0.6 26.4 %collective-permute-start = (bf16[128,2048]{1,0:T(8,128)(2,1)}, bf16[128,2048]{1,0:T(8,128)(2,1)}, u32[]{:S(2)}, u32[]{:S(2)}) collective-permute-start(bf16[128,2048]{1,0:T(8,128)(2,1)} %bitcast.43), channel_id=1, source_target_pairs={{0,2},{1,3},{2,4},{3,5},{4,6},{5,7},{6,0},{7,1},{8,10},{9,11},{10,... | collective-permute-start | bytes 1572872 | tf_op jit(solution)/shard_map/ppermute | solution.py:201
  3.6 38.1 %collective-permute-start.4 = (bf16[128,2048]{1,0:T(8,128)(2,1)}, bf16[128,2048]{1,0:T(8,128)(2,1)}, u32[]{:S(2)}, u32[]{:S(2)}) collective-permute-start(bf16[128,2048]{1,0:T(8,128)(2,1)} %param.10), channel_id=1, source_target_pairs={{0,8},{8,16},{16,24},{24,0},{1,9},{9,17},{17,25},{25,1},{2,10},{10... | collective-permute-start | bytes 1572872 | tf_op jit(solution)/shard_map/ppermute | solution.py:190
  5.2 36.6 %collective-permute-start.5 = (bf16[128,2048]{1,0:T(8,128)(2,1)}, bf16[128,2048]{1,0:T(8,128)(2,1)}, u32[]{:S(2)}, u32[]{:S(2)}) collective-permute-start(bf16[128,2048]{1,0:T(8,128)(2,1)} %param.10), channel_id=1, source_target_pairs={{0,16},{8,24},{16,0},{24,8},{1,17},{9,25},{17,1},{25,9},{2,18},{10... | collective-permute-start | bytes 1572872 | tf_op jit(solution)/shard_map/ppermute | solution.py:190
  7.8 20.6 %collective-permute-start.1 = (bf16[128,2048]{1,0:T(8,128)(2,1)}, bf16[128,2048]{1,0:T(8,128)(2,1)}, u32[]{:S(2)}, u32[]{:S(2)}) collective-permute-start(bf16[128,2048]{1,0:T(8,128)(2,1)} %bitcast.44), channel_id=1, source_target_pairs={{0,4},{1,5},{2,6},{3,7},{4,0},{5,1},{6,2},{7,3},{8,12},{9,13},{10,... | collective-permute-start | bytes 1572872 | tf_op jit(solution)/shard_map/ppermute | solution.py:201
  9.3 19.1 %collective-permute-start.2 = (bf16[128,2048]{1,0:T(8,128)(2,1)}, bf16[128,2048]{1,0:T(8,128)(2,1)}, u32[]{:S(2)}, u32[]{:S(2)}) collective-permute-start(bf16[128,2048]{1,0:T(8,128)(2,1)} %bitcast.45), channel_id=1, source_target_pairs={{0,6},{1,7},{2,0},{3,1},{4,2},{5,3},{6,4},{7,5},{8,14},{9,15},{10,... | collective-permute-start | bytes 1572872 | tf_op jit(solution)/shard_map/ppermute | solution.py:201
  21.5 43.7 %all-to-all-start = ((bf16[8,3,4,128,128]{4,3,2,1,0:T(8,128)(2,1)}), bf16[8,3,4,128,128]{4,3,2,1,0:T(8,128)(2,1)S(1)}, u32[]{:S(2)}, u32[]{:S(2)}) async-start(bf16[8,3,4,128,128]{4,3,2,1,0:T(8,128)(2,1)} %pad_maximum_fusion), calls=%async_computation | async-start | bytes 6291456 | tf_op jit(solution)/shard_map/all_to_all | solution.py:233
  25.2 12.6 %copy-start.6 = (s32[1,14,3]{1,0,2:T(1,128)S(1)}, s32[1,14,3]{1,0,2:T(1,128)}, u32[]{:S(2)}) copy-start(s32[1,14,3]{1,0,2:T(1,128)} %param.11) | copy-start | bytes 508
  27.1 25.7 %collective-permute-start.6 = (bf16[128,2048]{1,0:T(8,128)(2,1)}, bf16[128,2048]{1,0:T(8,128)(2,1)}, u32[]{:S(2)}, u32[]{:S(2)}) collective-permute-start(bf16[128,2048]{1,0:T(8,128)(2,1)} %param.10), channel_id=1, source_target_pairs={{0,24},{8,0},{16,8},{24,16},{1,25},{9,1},{17,9},{25,17},{2,26},{10... | collective-permute-start | bytes 1572872 | tf_op jit(solution)/shard_map/ppermute | solution.py:190
  31.6 28.4 %collective-permute-start.3 = (bf16[4,128,2048]{2,1,0:T(8,128)(2,1)}, bf16[4,128,2048]{2,1,0:T(8,128)(2,1)}, u32[]{:S(2)}, u32[]{:S(2)}) collective-permute-start(bf16[4,128,2048]{2,1,0:T(8,128)(2,1)} %pad_maximum_fusion.1), channel_id=1, source_target_pairs={{0,1},{1,0},{2,3},{3,2},{4,5},{5,4},{6,7},{7,6},{8,9},{9,8},{10,11... | collective-permute-start | bytes 6291464 | tf_op jit(solution)/shard_map/ppermute | solution.py:204
  54.5 2.2 %copy-start.5 = (bf16[8,128,2048]{2,1,0:T(8,128)(2,1)S(1)}, bf16[8,128,2048]{2,1,0:T(8,128)(2,1)}, u32[]{:S(2)}) copy-start(bf16[8,128,2048]{2,1,0:T(8,128)(2,1)} %constant_dynamic-update-slice_fusion.4) | copy-start | bytes 12582916
  65.2 1.6 %copy-start = (bf16[8,3,4,128,128]{4,3,2,1,0:T(8,128)(2,1)}, bf16[8,3,4,128,128]{4,3,2,1,0:T(8,128)(2,1)S(1)}, u32[]{:S(2)}) copy-start(bf16[8,3,4,128,128]{4,3,2,1,0:T(8,128)(2,1)S(1)} %all-to-all-done.x_ref) | copy-start | bytes 9437188
  79.8 18.9 %all-to-all-start.4 = ((bf16[8,3,128,128]{3,2,1,0:T(8,128)(2,1)}), bf16[8,3,128,128]{3,2,1,0:T(8,128)(2,1)S(1)}, u32[]{:S(2)}, u32[]{:S(2)}) async-start(bf16[8,3,128,128]{3,2,1,0:T(8,128)(2,1)} %shard_map.88), calls=%async_computation.4 | async-start | bytes 1572864 | tf_op jit(solution)/shard_map/all_to_all | solution.py:243
  98.7 17.2 %copy-start.1 = (bf16[8,3,128,128]{3,2,1,0:T(8,128)(2,1)}, bf16[8,3,128,128]{3,2,1,0:T(8,128)(2,1)S(1)}, u32[]{:S(2)}) copy-start(bf16[8,3,128,128]{3,2,1,0:T(8,128)(2,1)S(1)} %all-to-all-done.4.refs_2_) | copy-start | bytes 2359300
  98.7 17.2 %all-to-all-start.3 = ((bf16[8,3,128,128]{3,2,1,0:T(8,128)(2,1)}), bf16[8,3,128,128]{3,2,1,0:T(8,128)(2,1)S(1)}, u32[]{:S(2)}, u32[]{:S(2)}) async-start(bf16[8,3,128,128]{3,2,1,0:T(8,128)(2,1)} %shard_map.87), calls=%async_computation.3 | async-start | bytes 1572864 | tf_op jit(solution)/shard_map/all_to_all | solution.py:243
  115.9 17.2 %copy-start.2 = (bf16[8,3,128,128]{3,2,1,0:T(8,128)(2,1)}, bf16[8,3,128,128]{3,2,1,0:T(8,128)(2,1)S(1)}, u32[]{:S(2)}) copy-start(bf16[8,3,128,128]{3,2,1,0:T(8,128)(2,1)S(1)} %all-to-all-done.3.refs_1_) | copy-start | bytes 2359300
  115.9 17.2 %all-to-all-start.2 = ((bf16[8,3,128,128]{3,2,1,0:T(8,128)(2,1)}), bf16[8,3,128,128]{3,2,1,0:T(8,128)(2,1)S(1)}, u32[]{:S(2)}, u32[]{:S(2)}) async-start(bf16[8,3,128,128]{3,2,1,0:T(8,128)(2,1)} %shard_map.86), calls=%async_computation.2 | async-start | bytes 1572864 | tf_op jit(solution)/shard_map/all_to_all | solution.py:243
  133.2 4.2 %copy-start.3 = (bf16[8,3,128,128]{3,2,1,0:T(8,128)(2,1)}, bf16[8,3,128,128]{3,2,1,0:T(8,128)(2,1)S(1)}, u32[]{:S(2)}) copy-start(bf16[8,3,128,128]{3,2,1,0:T(8,128)(2,1)S(1)} %all-to-all-done.2.refs_0_) | copy-start | bytes 2359300
  133.2 16.8 %all-to-all-start.1 = ((bf16[8,3,128,128]{3,2,1,0:T(8,128)(2,1)}), bf16[8,3,128,128]{3,2,1,0:T(8,128)(2,1)S(1)}, u32[]{:S(2)}, u32[]{:S(2)}) async-start(bf16[8,3,128,128]{3,2,1,0:T(8,128)(2,1)} %shard_map.85), calls=%async_computation.1 | async-start | bytes 1572864 | tf_op jit(solution)/shard_map/all_to_all | solution.py:243
  150.0 0.9 copy-start.4

commit v17 on v16

--- a/solution.py
+++ b/solution.py
@@ -74,13 +74,16 @@
     dv_acc[...] = value_grad
 
     columns = lax.broadcasted_iota(jnp.int32, (BLOCK, SLOTS * BLOCK), 1) // BLOCK
+    for slot, block in enumerate((0, last)):
+        kg_ref[slot * BLOCK:(slot + 1) * BLOCK, :] = rows(x_ref, 1, block)[...]
+        vg_ref[slot * BLOCK:(slot + 1) * BLOCK, :] = rows(x_ref, 2, block)[...]
 
     def mid_step(m, carry):
         base = (m - 1) * RAND
         lower = jnp.where(m - 1 >= 1, m - 1, m)
         upper = jnp.where(m + 1 <= count - 2, m + 1, m)
         ids = [0, count - 1, lower, m, upper] + [rb_ref[base + r] for r in range(RAND)]
-        for slot, block in enumerate(ids):
+        for slot, block in enumerate(ids[2:], start=2):
             kg_ref[slot * BLOCK:(slot + 1) * BLOCK, :] = rows(x_ref, 1, block)[...]
             vg_ref[slot * BLOCK:(slot + 1) * BLOCK, :] = rows(x_ref, 2, block)[...]
         start = pl.multiple_of(m * BLOCK, BLOCK)
@@ -160,7 +163,7 @@
         _assemble_last_kernel,
         out_shape=(out, out, out),
         grid=(1,),
-        in_specs=[whole, last_spec, last_spec, last_spec],
+        in_specs=[whole] + [pl.BlockSpec(memory_space=pl.ANY)] * 3,
         out_specs=(last_spec, last_spec, last_spec),
         input_output_aliases={1: 0, 2: 1, 3: 2},
     )(pieces[early], *partial)

time: 154 us -> 154 us (level)
  no operation moved by 1% of the time
where the time goes in v17:
time: 154 us; the launch traced here: 153 us
  Pallas kernels  58 us (38%)
  starting transfers between devices  33.8 us (22%)
  local copies, waits for them, and re-layouts  20.5 us (13%)
  waiting for transfers between devices  20 us (13%)
  other arithmetic  8.83 us (6%)
  between operations  8.71 us (6%)
  matrix products  3.34 us (2%)
    pallas_call x4, Pallas kernels, attention_grads(): pl.pallas_call(_attention_kernel, out_shape=out, grid_spec=pltpu.Prefetch...  52.1 us
    all_to_all x4, starting transfers between devices, body(): lax.all_to_all(grads, 'context', split_axis=0, concat_axis=0, tiled=True)  18.5 us
    unnamed x22, local copies, waits for them, and re-layouts  14.6 us
    ppermute x3, waiting for transfers between devices, body(): lax.ppermute(out_weight, 'dp', [(a, (a + s) % dp) for a in range(dp)])  11 us
    all_to_all x4, waiting for transfers between devices, body(): lax.all_to_all(grads, 'context', split_axis=0, concat_axis=0, tiled=True)  8.96 us
    ppermute x3, starting transfers between devices, body(): lax.ppermute(local_cotangent, 'context', [(a, (a + s) % ctx) for a in ran...  5.94 us
    ppermute x3, starting transfers between devices, body(): lax.ppermute(out_weight, 'dp', [(a, (a + s) % dp) for a in range(dp)])  5.51 us
    all_to_all x1, starting transfers between devices, body(): lax.all_to_all(stacked, 'context', split_axis=0, concat_axis=0, tiled=True)  3.65 us
  transfers between devices with their start and end apart: 12, of which 3 were waited for; matrix products, arithmetic and copies ran while one was open for 18% of the time, Pallas kernels for 28%

profile of v17, /device:TPU:0, one launch (start us, length us, event | category | flops | bytes accessed | tf_op | source)
XLA Modules:
  0.0 153.2 jit_solution(17626162966034905060)
XLA Ops:
  0.6 3.0 %collective-permute-start = (bf16[128,2048]{1,0:T(8,128)(2,1)}, bf16[128,2048]{1,0:T(8,128)(2,1)}, u32[]{:S(2)}, u32[]{:S(2)}) collective-permute-start(bf16[128,2048]{1,0:T(8,128)(2,1)} %bitcast.43), channel_id=1, source_target_pairs={{0,2},{1,3},{2,4},{3,5},{4,6},{5,7},{6,0},{7,1},{8,10},{9,11},{10,... | collective-permute-start | bytes 1572872 | tf_op jit(solution)/shard_map/ppermute | solution.py:204
  3.6 1.6 %collective-permute-start.4 = (bf16[128,2048]{1,0:T(8,128)(2,1)}, bf16[128,2048]{1,0:T(8,128)(2,1)}, u32[]{:S(2)}, u32[]{:S(2)}) collective-permute-start(bf16[128,2048]{1,0:T(8,128)(2,1)} %param.10), channel_id=1, source_target_pairs={{0,8},{8,16},{16,24},{24,0},{1,9},{9,17},{17,25},{25,1},{2,10},{10... | collective-permute-start | bytes 1572872 | tf_op jit(solution)/shard_map/ppermute | solution.py:193
  5.2 2.6 %collective-permute-start.5 = (bf16[128,2048]{1,0:T(8,128)(2,1)}, bf16[128,2048]{1,0:T(8,128)(2,1)}, u32[]{:S(2)}, u32[]{:S(2)}) collective-permute-start(bf16[128,2048]{1,0:T(8,128)(2,1)} %param.10), channel_id=1, source_target_pairs={{0,16},{8,24},{16,0},{24,8},{1,17},{9,25},{17,1},{25,9},{2,18},{10... | collective-permute-start | bytes 1572872 | tf_op jit(solution)/shard_map/ppermute | solution.py:193
  7.8 1.5 collective-permute-start.1
  9.3 1.4 collective-permute-start.2
  10.7 1.6 %copy.14 = bf16[1,128,4096]{1,2,0:T(8,128)(2,1)S(1)} copy(bf16[1,128,4096]{2,1,0:T(8,128)(2,1)} %param.6) | data formatting | bytes 2097152 | tf_op args[0]
  12.4 0.7 copy.15
  13.0 1.6 %copy.16 = bf16[1,128,4096]{1,2,0:T(8,128)(2,1)S(1)} copy(bf16[1,128,4096]{2,1,0:T(8,128)(2,1)} %param.7) | data formatting | bytes 2097152 | tf_op args[1]
  14.7 0.7 copy.17
  15.3 1.6 %copy.18 = bf16[1,128,4096]{1,2,0:T(8,128)(2,1)S(1)} copy(bf16[1,128,4096]{2,1,0:T(8,128)(2,1)} %param.8) | data formatting | bytes 2097152 | tf_op args[2]
  17.0 1.3 copy.19
  18.3 3.2 %pad_maximum_fusion = bf16[8,3,4,128,128]{4,3,2,1,0:T(8,128)(2,1)} fusion(bf16[8,1,4,128,128]{4,3,2,1,0:T(8,128)(2,1)} %bitcast.42, bf16[8,1,4,128,128]{4,3,2,1,0:T(8,128)(2,1)S(1)} %bitcast.41, bf16[8,1,4,128,128]{4,3,2,1,0:T(8,128)(2,1)S(1)} %bitcast.40), kind=kLoop, calls=%fused_computation | loop fusion | flops 3145728 | bytes 6291456 | tf_op jit(solution)/shard_map/stack | solution.py:235
  21.5 3.6 %all-to-all-start = ((bf16[8,3,4,128,128]{4,3,2,1,0:T(8,128)(2,1)}), bf16[8,3,4,128,128]{4,3,2,1,0:T(8,128)(2,1)S(1)}, u32[]{:S(2)}, u32[]{:S(2)}) async-start(bf16[8,3,4,128,128]{4,3,2,1,0:T(8,128)(2,1)} %pad_maximum_fusion), calls=%async_computation | async-start | bytes 6291456 | tf_op jit(solution)/shard_map/all_to_all | solution.py:236
  25.2 0.0 copy-start.6
  25.2 1.9 %constant_dynamic-update-slice_fusion.4 = bf16[8,128,2048]{2,1,0:T(8,128)(2,1)} fusion(bf16[1,128,2048]{2,1,0:T(8,128)(2,1)} %param.9), kind=kLoop, calls=%fused_computation.20 | loop fusion | bytes 1048576
  27.1 1.3 collective-permute-start.6
  28.4 0.0 collective-permute-done.2
  28.4 3.2 %pad_maximum_fusion.1 = bf16[4,128,2048]{2,1,0:T(8,128)(2,1)} fusion(bf16[1,128,2048]{2,1,0:T(8,128)(2,1)} %bitcast.12, bf16[1,128,2048]{2,1,0:T(8,128)(2,1)} %bitcast.11, bf16[1,128,2048]{2,1,0:T(8,128)(2,1)} %bitcast.10, bf16[1,128,2048]{2,1,0:T(8,128)(2,1)} %param.9), kind=kLoop, calls=%fused_computation.1 | loop fusion | flops 3145728 | bytes 4194304 | tf_op jit(solution)/shard_map/stack | solution.py:203
  31.6 0.1 collective-permute-start.3
  31.8 0.7 fusion.15
  37.7 0.1 copy.13
  37.8 0.6 reshape_squeeze.15.rb_ref
  41.1 0.6 compare_select_fusion.6.pos_ref
  41.7 0.1 collective-permute-done.5
  41.8 11.0 %collective-permute-done.6 = bf16[128,2048]{1,0:T(8,128)(2,1)} collective-permute-done((bf16[128,2048]{1,0:T(8,128)(2,1)}, bf16[128,2048]{1,0:T(8,128)(2,1)}, u32[]{:S(2)}, u32[]{:S(2)}) %collective-permute-start.6) | collective-permute-done | bytes 524320 | tf_op jit(solution)/shard_map/ppermute | solution.py:193
  52.7 1.8 %pad_maximum_fusion.2 = bf16[4,128,2048]{2,1,0:T(8,128)(2,1)S(1)} fusion(bf16[1,128,2048]{2,1,0:T(8,128)(2,1)} %bitcast.17, bf16[1,128,2048]{2,1,0:T(8,128)(2,1)} %bitcast.16, bf16[1,128,2048]{2,1,0:T(8,128)(2,1)} %bitcast.15, bf16[1,128,2048]{2,1,0:T(8,128)(2,1)} %bitcast.46), kind=kLoop, calls=%fused_computation.2 | loop fusion | flops 3145728 | bytes 4194304 | tf_op jit(solution)/shard_map/stack | solution.py:197
  54.5 0.1 dynamic-slice_bitcast_fusion.3
  54.7 2.0 %copy-done.5 = bf16[8,128,2048]{2,1,0:T(8,128)(2,1)S(1)} copy-done((bf16[8,128,2048]{2,1,0:T(8,128)(2,1)S(1)}, bf16[8,128,2048]{2,1,0:T(8,128)(2,1)}, u32[]{:S(2)}) %copy-start.5) | copy-done | bytes 4194328
  56.7 1.1 constant_dynamic-update-slice_fusion.3
  57.8 1.1 constant_dynamic-update-slice_fusion.2
  58.9 1.1 constant_dynamic-update-slice_fusion.1
  60.0 0.0 collective-permute-done.3
  60.0 1.8 %constant_dynamic-update-slice_fusion = bf16[8,128,2048]{2,1,0:T(8,128)(2,1)S(1)} fusion(bf16[8,128,2048]{2,1,0:T(8,128)(2,1)S(1)} %constant_dynamic-update-slice_fusion.1, bf16[4,128,2048]{2,1,0:T(8,128)(2,1)} %collective-permute-done.3), kind=kLoop, calls=%fused_computation.16 | loop fusion | bytes 4194304 | tf_op jit(solution)/shard_map/concatenate | solution.py:208
  61.8 3.3 %fusion.8.u_ref = bf16[1024,512]{1,0:T(8,128)(2,1)} fusion(bf16[1024,2048]{1,0:T(8,128)(2,1)S(1)} %bitcast.47, bf16[128,2048]{1,0:T(8,128)(2,1)S(1)} %get-tuple-element.10, bf16[128,2048]{1,0:T(8,128)(2,1)S(1)} %get-tuple-element.11, bf16[128,2048]{1,0:T(8,128)(2,1)S(1)} %get-tuple-element.12, bf16[128,2048]{1,0:T(8,128)(2,1)S(1)} %get-tuple-element.9), kind=kOutput, calls=%fused_computation.11 | convolution fusion | flops 2156396544 | bytes 7340032 | tf_op jit(solution)/shard_map/dot_general | solution.py:209
  65.2 1.6 %copy-done = bf16[8,3,4,128,128]{4,3,2,1,0:T(8,128)(2,1)} copy-done((bf16[8,3,4,128,128]{4,3,2,1,0:T(8,128)(2,1)}, bf16[8,3,4,128,128]{4,3,2,1,0:T(8,128)(2,1)S(1)}, u32[]{:S(2)}) %copy-start) | copy-done | bytes 3145752
  66.8 13.0 %shard_map.88 = bf16[8,3,128,128]{3,2,1,0:T(8,128)(2,1)} custom-call(s32[42]{0:T(128)} %reshape_squeeze.15.rb_ref, s32[8]{0:T(128)} %compare_select_fusion.6.pos_ref, bf16[8,3,4,128,128]{4,3,2,1,0:T(8,128)(2,1)} %copy-done, bf16[1024,512]{1,0:T(8,128)(2,1)} %fusion.8.u_ref), custom_call_target="tpu_custom_call" | custom-call | flops 905969664 | bytes 1835008 | tf_op jit(solution)/shard_map/pallas_call | solution.py:118
  79.8 5.9 %all-to-all-start.4 = ((bf16[8,3,128,128]{3,2,1,0:T(8,128)(2,1)}), bf16[8,3,128,128]{3,2,1,0:T(8,128)(2,1)S(1)}, u32[]{:S(2)}, u32[]{:S(2)}) async-start(bf16[8,3,128,128]{3,2,1,0:T(8,128)(2,1)} %shard_map.88), calls=%async_computation.4 | async-start | bytes 1572864 | tf_op jit(solution)/shard_map/all_to_all | solution.py:246
  85.7 13.0 %shard_map.87 = bf16[8,3,128,128]{3,2,1,0:T(8,128)(2,1)} custom-call(s32[42]{0:T(128)} %reshape_squeeze.15.rb_ref, s32[8]{0:T(128)} %compare_select_fusion.6.pos_ref, bf16[8,3,4,128,128]{4,3,2,1,0:T(8,128)(2,1)} %copy-done, bf16[1024,512]{1,0:T(8,128)(2,1)} %fusion.8.u_ref), custom_call_target="tpu_custom_call" | custom-call | flops 905969664 | bytes 1835008 | tf_op jit(solution)/shard_map/pallas_call | solution.py:118
  98.8 0.0 all-to-all-done.4.refs_2_
  98.8 4.2 %all-to-all-start.3 = ((bf16[8,3,128,128]{3,2,1,0:T(8,128)(2,1)}), bf16[8,3,128,128]{3,2,1,0:T(8,128)(2,1)S(1)}, u32[]{:S(2)}, u32[]{:S(2)}) async-start(bf16[8,3,128,128]{3,2,1,0:T(8,128)(2,1)} %shard_map.87), calls=%async_computation.3 | async-start | bytes 1572864 | tf_op jit(solution)/shard_map/all_to_all | solution.py:246
  103.0 13.0 %shard_map.86 = bf16[8,3,128,128]{3,2,1,0:T(8,128)(2,1)} custom-call(s32[42]{0:T(128)} %reshape_squeeze.15.rb_ref, s32[8]{0:T(128)} %compare_select_fusion.6.pos_ref, bf16[8,3,4,128,128]{4,3,2,1,0:T(8,128)(2,1)} %copy-done, bf16[1024,512]{1,0:T(8,128)(2,1)} %fusion.8.u_ref), custom_call_target="tpu_custom_call" | custom-call | flops 905969664 | bytes 1835008 | tf_op jit(solution)/shard_map/pallas_call | solution.py:118
  116.0 4.2 %all-to-all-start.2 = ((bf16[8,3,128,128]{3,2,1,0:T(8,128)(2,1)}), bf16[8,3,128,128]{3,2,1,0:T(8,128)(2,1)S(1)}, u32[]{:S(2)}, u32[]{:S(2)}) async-start(bf16[8,3,128,128]{3,2,1,0:T(8,128)(2,1)} %shard_map.86), calls=%async_computation.2 | async-start | bytes 1572864 | tf_op jit(solution)/shard_map/all_to_all | solution.py:246
  120.2 13.0 %shard_map.85 = bf16[8,3,128,128]{3,2,1,0:T(8,128)(2,1)} custom-call(s32[42]{0:T(128)} %reshape_squeeze.15.rb_ref, s32[8]{0:T(128)} %compare_select_fusion.6.pos_ref, bf16[8,3,4,128,128]{4,3,2,1,0:T(8,128)(2,1)} %copy-done, bf16[1024,512]{1,0:T(8,128)(2,1)} %fusion.8.u_ref), custom_call_target="tpu_custom_call" | custom-call | flops 905969664 | bytes 1835008 | tf_op jit(solution)/shard_map/pallas_call | solution.py:118
  133.2 4.2 %all-to-all-start.1 = ((bf16[8,3,128,128]{3,2,1,0:T(8,128)(2,1)}), bf16[8,3,128,128]{3,2,1,0:T(8,128)(2,1)S(1)}, u32[]{:S(2)}, u32[]{:S(2)}) async-start(bf16[8,3,128,128]{3,2,1,0:T(8,128)(2,1)} %shard_map.85), calls=%async_computation.1 | async-start | bytes 1572864 | tf_op jit(solution)/shard_map/all_to_all | solution.py:246
  137.5 3.6 %shard_map.89 = (bf16[1,128,4096]{2,1,0:T(8,128)(2,1)}, bf16[1,128,4096]{2,1,0:T(8,128)(2,1)}, bf16[1,128,4096]{2,1,0:T(8,128)(2,1)}) custom-call(bf16[8,3,128,128]{3,2,1,0:T(8,128)(2,1)} %copy-done.3, bf16[8,3,128,128]{3,2,1,0:T(8,128)(2,1)} %copy-done.2, bf16[8,3,128,128]{3,2,1,0:T(8,128)(2,1)} %copy-done.1), custom_call_target="tpu_custom_call" | custom-call | tf_op jit(solution)/shard_map/pallas_call | solution.py:154
  141.1 9.0 %all-to-all-done.1.piece = bf16[8,3,128,128]{3,2,1,0:T(8,128)(2,1)S(1)} async-done(((bf16[8,3,128,128]{3,2,1,0:T(8,128)(2,1)}), bf16[8,3,128,128]{3,2,1,0:T(8,128)(2,1)S(1)}, u32[]{:S(2)}, u32[]{:S(2)}) %all-to-all-start.1) | async-done | bytes 786464 | tf_op jit(solution)/shard_map/all_to_all | solution.py:246
  150.1 0.9 copy-done.4
  150.9 2.2 %shard_map.90 = (bf16[1,128,4096]{2,1,0:T(8,128)(2,1)}, bf16[1,128,4096]{2,1,0:T(8,128)(2,1)}, bf16[1,128,4096]{2,1,0:T(8,128)(2,1)}) custom-call(bf16[8,3,128,128]{3,2,1,0:T(8,128)(2,1)} %copy-done.4, bf16[1,128,4096]{2,1,0:T(8,128)(2,1)} %get-tuple-element.6._first, ...), custom_call_target="tpu_custom_call", output_to_operand_aliasing={{0}: (1, {}), {1}: (2, {}), {2}: (3, {})} | custom-call | tf_op jit(solution)/shard_map/pallas_call | solution.py:162
  (17 shorter events, 0.0 us)
Async XLA Ops:
  0.6 26.4 %collective-permute-start = (bf16[128,2048]{1,0:T(8,128)(2,1)}, bf16[128,2048]{1,0:T(8,128)(2,1)}, u32[]{:S(2)}, u32[]{:S(2)}) collective-permute-start(bf16[128,2048]{1,0:T(8,128)(2,1)} %bitcast.43), channel_id=1, source_target_pairs={{0,2},{1,3},{2,4},{3,5},{4,6},{5,7},{6,0},{7,1},{8,10},{9,11},{10,... | collective-permute-start | bytes 1572872 | tf_op jit(solution)/shard_map/ppermute | solution.py:204
  3.6 38.1 %collective-permute-start.4 = (bf16[128,2048]{1,0:T(8,128)(2,1)}, bf16[128,2048]{1,0:T(8,128)(2,1)}, u32[]{:S(2)}, u32[]{:S(2)}) collective-permute-start(bf16[128,2048]{1,0:T(8,128)(2,1)} %param.10), channel_id=1, source_target_pairs={{0,8},{8,16},{16,24},{24,0},{1,9},{9,17},{17,25},{25,1},{2,10},{10... | collective-permute-start | bytes 1572872 | tf_op jit(solution)/shard_map/ppermute | solution.py:193
  5.2 36.6 %collective-permute-start.5 = (bf16[128,2048]{1,0:T(8,128)(2,1)}, bf16[128,2048]{1,0:T(8,128)(2,1)}, u32[]{:S(2)}, u32[]{:S(2)}) collective-permute-start(bf16[128,2048]{1,0:T(8,128)(2,1)} %param.10), channel_id=1, source_target_pairs={{0,16},{8,24},{16,0},{24,8},{1,17},{9,25},{17,1},{25,9},{2,18},{10... | collective-permute-start | bytes 1572872 | tf_op jit(solution)/shard_map/ppermute | solution.py:193
  7.8 20.6 %collective-permute-start.1 = (bf16[128,2048]{1,0:T(8,128)(2,1)}, bf16[128,2048]{1,0:T(8,128)(2,1)}, u32[]{:S(2)}, u32[]{:S(2)}) collective-permute-start(bf16[128,2048]{1,0:T(8,128)(2,1)} %bitcast.44), channel_id=1, source_target_pairs={{0,4},{1,5},{2,6},{3,7},{4,0},{5,1},{6,2},{7,3},{8,12},{9,13},{10,... | collective-permute-start | bytes 1572872 | tf_op jit(solution)/shard_map/ppermute | solution.py:204
  9.3 19.1 %collective-permute-start.2 = (bf16[128,2048]{1,0:T(8,128)(2,1)}, bf16[128,2048]{1,0:T(8,128)(2,1)}, u32[]{:S(2)}, u32[]{:S(2)}) collective-permute-start(bf16[128,2048]{1,0:T(8,128)(2,1)} %bitcast.45), channel_id=1, source_target_pairs={{0,6},{1,7},{2,0},{3,1},{4,2},{5,3},{6,4},{7,5},{8,14},{9,15},{10,... | collective-permute-start | bytes 1572872 | tf_op jit(solution)/shard_map/ppermute | solution.py:204
  21.5 43.7 %all-to-all-start = ((bf16[8,3,4,128,128]{4,3,2,1,0:T(8,128)(2,1)}), bf16[8,3,4,128,128]{4,3,2,1,0:T(8,128)(2,1)S(1)}, u32[]{:S(2)}, u32[]{:S(2)}) async-start(bf16[8,3,4,128,128]{4,3,2,1,0:T(8,128)(2,1)} %pad_maximum_fusion), calls=%async_computation | async-start | bytes 6291456 | tf_op jit(solution)/shard_map/all_to_all | solution.py:236
  25.2 12.6 %copy-start.6 = (s32[1,14,3]{1,0,2:T(1,128)S(1)}, s32[1,14,3]{1,0,2:T(1,128)}, u32[]{:S(2)}) copy-start(s32[1,14,3]{1,0,2:T(1,128)} %param.11) | copy-start | bytes 508
  27.1 25.7 %collective-permute-start.6 = (bf16[128,2048]{1,0:T(8,128)(2,1)}, bf16[128,2048]{1,0:T(8,128)(2,1)}, u32[]{:S(2)}, u32[]{:S(2)}) collective-permute-start(bf16[128,2048]{1,0:T(8,128)(2,1)} %param.10), channel_id=1, source_target_pairs={{0,24},{8,0},{16,8},{24,16},{1,25},{9,1},{17,9},{25,17},{2,26},{10... | collective-permute-start | bytes 1572872 | tf_op jit(solution)/shard_map/ppermute | solution.py:193
  31.6 28.4 %collective-permute-start.3 = (bf16[4,128,2048]{2,1,0:T(8,128)(2,1)}, bf16[4,128,2048]{2,1,0:T(8,128)(2,1)}, u32[]{:S(2)}, u32[]{:S(2)}) collective-permute-start(bf16[4,128,2048]{2,1,0:T(8,128)(2,1)} %pad_maximum_fusion.1), channel_id=1, source_target_pairs={{0,1},{1,0},{2,3},{3,2},{4,5},{5,4},{6,7},{7,6},{8,9},{9,8},{10,11... | collective-permute-start | bytes 6291464 | tf_op jit(solution)/shard_map/ppermute | solution.py:207
  54.5 2.2 %copy-start.5 = (bf16[8,128,2048]{2,1,0:T(8,128)(2,1)S(1)}, bf16[8,128,2048]{2,1,0:T(8,128)(2,1)}, u32[]{:S(2)}) copy-start(bf16[8,128,2048]{2,1,0:T(8,128)(2,1)} %constant_dynamic-update-slice_fusion.4) | copy-start | bytes 12582916
  65.2 1.6 %copy-start = (bf16[8,3,4,128,128]{4,3,2,1,0:T(8,128)(2,1)}, bf16[8,3,4,128,128]{4,3,2,1,0:T(8,128)(2,1)S(1)}, u32[]{:S(2)}) copy-start(bf16[8,3,4,128,128]{4,3,2,1,0:T(8,128)(2,1)S(1)} %all-to-all-done.x_ref) | copy-start | bytes 9437188
  79.8 18.9 %all-to-all-start.4 = ((bf16[8,3,128,128]{3,2,1,0:T(8,128)(2,1)}), bf16[8,3,128,128]{3,2,1,0:T(8,128)(2,1)S(1)}, u32[]{:S(2)}, u32[]{:S(2)}) async-start(bf16[8,3,128,128]{3,2,1,0:T(8,128)(2,1)} %shard_map.88), calls=%async_computation.4 | async-start | bytes 1572864 | tf_op jit(solution)/shard_map/all_to_all | solution.py:246
  98.8 17.2 %copy-start.1 = (bf16[8,3,128,128]{3,2,1,0:T(8,128)(2,1)}, bf16[8,3,128,128]{3,2,1,0:T(8,128)(2,1)S(1)}, u32[]{:S(2)}) copy-start(bf16[8,3,128,128]{3,2,1,0:T(8,128)(2,1)S(1)} %all-to-all-done.4.refs_2_) | copy-start | bytes 2359300
  98.8 17.2 %all-to-all-start.3 = ((bf16[8,3,128,128]{3,2,1,0:T(8,128)(2,1)}), bf16[8,3,128,128]{3,2,1,0:T(8,128)(2,1)S(1)}, u32[]{:S(2)}, u32[]{:S(2)}) async-start(bf16[8,3,128,128]{3,2,1,0:T(8,128)(2,1)} %shard_map.87), calls=%async_computation.3 | async-start | bytes 1572864 | tf_op jit(solution)/shard_map/all_to_all | solution.py:246
  116.0 17.3 %copy-start.2 = (bf16[8,3,128,128]{3,2,1,0:T(8,128)(2,1)}, bf16[8,3,128,128]{3,2,1,0:T(8,128)(2,1)S(1)}, u32[]{:S(2)}) copy-start(bf16[8,3,128,128]{3,2,1,0:T(8,128)(2,1)S(1)} %all-to-all-done.3.refs_1_) | copy-start | bytes 2359300
  116.0 17.3 %all-to-all-start.2 = ((bf16[8,3,128,128]{3,2,1,0:T(8,128)(2,1)}), bf16[8,3,128,128]{3,2,1,0:T(8,128)(2,1)S(1)}, u32[]{:S(2)}, u32[]{:S(2)}) async-start(bf16[8,3,128,128]{3,2,1,0:T(8,128)(2,1)} %shard_map.86), calls=%async_computation.2 | async-start | bytes 1572864 | tf_op jit(solution)/shard_map/all_to_all | solution.py:246
  133.2 4.2 %copy-start.3 = (bf16[8,3,128,128]{3,2,1,0:T(8,128)(2,1)}, bf16[8,3,128,128]{3,2,1,0:T(8,128)(2,1)S(1)}, u32[]{:S(2)}) copy-start(bf16[8,3,128,128]{3,2,1,0:T(8,128)(2,1)S(1)} %all-to-all-done.2.refs_0_) | copy-start | bytes 2359300
  133.2 16.8 %all-to-all-start.1 = ((bf16[8,3,128,128]{3,2,1,0:T(8,128)(2,1)}), bf16[8,3,128,128]{3,2,1,0:T(8,128)(2,1)S(1)}, u32[]{:S(2)}, u32[]{:S(2)}) async-start(bf16[8,3,128,128]{3,2,1,0:T(8,128)(2,1)} %shard_map.85), calls=%async_computation.1 | async-start | bytes 1572864 | tf_op jit(solution)/shard_map/all_to_all | solution.py:246
  150.1 0.9 copy-start.4
